TPU v7x, 32 devices: a whole 2x2x4 slice. The times are simulated.
32 devices in a mesh: req: 8 (over y, x, core), exp: 4 (over z).
Axes of the slice: x: 2, y: 2, z: 4, core: 2. Of those that a mesh axis runs over, the one named last changes fastest.
Arguments:
- tokens: bfloat16 [4096, 1024], P(('req', 'exp'))
- norm_attn: bfloat16 [1024], replicated, may hold values from 0.099609375 to 1.8984375
- w_query: bfloat16 [1024, 1024], replicated
- w_key: bfloat16 [1024, 512], replicated
- w_value: bfloat16 [1024, 512], replicated, may hold values from -0.1875 to 0.1875
- w_out: bfloat16 [1024, 1024], P('exp'), may hold values from -0.1875 to 0.1875
- norm_moe: bfloat16 [1024], replicated, may hold values from 0.099609375 to 1.8984375
- w_router: bfloat16 [1024, 32], replicated
- w_gate: bfloat16 [32, 1024, 512], P('exp'), may hold values from -0.1875 to 0.1875
- w_up: bfloat16 [32, 1024, 512], P('exp'), may hold values from -0.1875 to 0.1875
- w_down: bfloat16 [32, 512, 1024], P('exp')
- segment_ids: int32 [8, 512], P('req'), may hold values from 0 to 3, never falling along the last dimension, each value on 1 to 256 neighbouring positions
- page_order: int32 [8, 512], P('req'), may hold values from 0 to 511, each once within a row
- expert_ids: int32 [4096, 8], P(('req', 'exp')), may hold values from 0 to 31, all different within a row; in each aligned block of 128 rows (0 to 127, 128 to 255, ...) at most 64 rows name the same one
Outputs:
- mixed: bfloat16 [4096, 1024], P(('req', 'exp'))
- kv_cache: bfloat16 [4096, 8, 128], P('req', 'exp')
Inputs may be any that keep to these rules, and one draw needn't show every extreme that they name: `segment_ids`: along each row, request numbers never fall; every pack holds 4 requests of 1 to 256 positions, one of exactly 256. `page_order`: each row is a permutation of the pack's 512 positions. `expert_ids`: A token's 8 experts differ. Within the rows of one device no expert is named by more than 64 rows, and in some device's rows an expert is named by exactly 64.
All inputs are finite; a program needn't handle non-finite values.
Results may differ from a plain program's by a relative error of at most 0.0055.
Values may be sent and summed in bfloat16 or wider, within the bound.
No kernel may reach another device: no remote copies, remote signals or barrier semaphores. Data moves between devices by JAX's collectives and lax.ppermute only.
A program may use at most 128 MiB of HBM per device.

v0:
```python
import jax
import jax.numpy as jnp
from jax import lax
from jax.sharding import PartitionSpec as P

HD = 64
CAP = 64


def rms_scale(rows, gain):
    rows = rows.astype(jnp.float32)
    inverse = lax.rsqrt(jnp.mean(rows * rows, axis=-1, keepdims=True) + 1e-06)
    return (rows * inverse * gain.astype(jnp.float32)).astype(jnp.bfloat16)


def positions(seg):
    index = jnp.arange(seg.shape[0], dtype=jnp.int32)
    starts = jnp.concatenate([jnp.ones((1,), dtype=bool), seg[1:] != seg[:-1]])
    first = lax.cummax(jnp.where(starts, index, 0), axis=0)
    return index - first


def rotate(values, pos):
    half = values.shape[-1] // 2
    freq = 10000.0 ** (-jnp.arange(half, dtype=jnp.float32) / half)
    angle = pos.astype(jnp.float32)[:, None] * freq[None, :]
    cosine = jnp.cos(angle)[:, None, :]
    sine = jnp.sin(angle)[:, None, :]
    front = values[..., :half]
    back = values[..., half:]
    return jnp.concatenate([front * cosine - back * sine, back * cosine + front * sine], axis=-1)


def attend(query, keyval, seg):
    plen, groups, width = query.shape
    half = width // 2
    block = min(512, plen)
    blocks = plen // block
    queries = query.reshape(blocks, block, groups, 2, half)
    keys = keyval[..., :half]
    values = keyval[..., half:]
    key_pos = jnp.arange(plen, dtype=jnp.int32)
    query_pos = key_pos.reshape(blocks, block)
    query_seg = seg.reshape(blocks, block)

    def one_block(args):
        qblock, qpos, qseg = args
        score = (
            jnp.einsum("qkgd,tkd->kgqt", qblock, keys, preferred_element_type=jnp.float32) * 0.125
        )
        allowed = (qseg[:, None] == seg[None, :]) & (key_pos[None, :] <= qpos[:, None])
        score = jnp.where(allowed[None, None], score, -1e30)
        top = jnp.max(score, axis=-1, keepdims=True)
        expo = jnp.exp(score - top)
        probs = (expo / jnp.sum(expo, axis=-1, keepdims=True)).astype(jnp.bfloat16)
        out = jnp.einsum("kgqt,tkd->qkgd", probs, values, preferred_element_type=jnp.float32)
        return out.astype(jnp.bfloat16)

    outs = lax.map(one_block, (queries, query_pos, query_seg))
    return outs.reshape(plen, groups * width)


def expert_apply(received, w_gate, w_up, w_down):
    gate = jnp.einsum("pend,edf->penf", received, w_gate, preferred_element_type=jnp.float32)
    upward = jnp.einsum("pend,edf->penf", received, w_up, preferred_element_type=jnp.float32)
    hidden = (jax.nn.silu(gate) * upward).astype(jnp.bfloat16)
    result = jnp.einsum("penf,efd->pend", hidden, w_down, preferred_element_type=jnp.float32)
    return result.astype(jnp.bfloat16)


def shards(
    tokens,
    norm_attn,
    w_query,
    w_key,
    w_value,
    w_out,
    norm_moe,
    w_router,
    w_gate,
    w_up,
    w_down,
    segment_ids,
    page_order,
    expert_ids,
):
    rows, width = tokens.shape
    seg = segment_ids[0]
    groups = w_key.shape[1] // HD
    here = lax.axis_index("exp")
    pos = lax.dynamic_slice_in_dim(positions(seg), here * rows, rows)
    normed = rms_scale(tokens, norm_attn)
    query = jnp.dot(normed, w_query, preferred_element_type=jnp.float32).reshape(
        rows, 2 * groups, HD
    )
    query = rotate(query, pos).astype(jnp.bfloat16).reshape(rows, groups, 2 * HD)
    keys = jnp.dot(normed, w_key, preferred_element_type=jnp.float32).reshape(rows, groups, HD)
    keys = rotate(keys, pos).astype(jnp.bfloat16)
    values = (
        jnp.dot(normed, w_value, preferred_element_type=jnp.float32)
        .astype(jnp.bfloat16)
        .reshape(rows, groups, HD)
    )
    keyval = jnp.concatenate([keys, values], axis=-1)
    query_heads, keyval_heads = (
        lax.all_to_all(query, "exp", split_axis=1, concat_axis=0, tiled=True),
        lax.all_to_all(keyval, "exp", split_axis=1, concat_axis=0, tiled=True),
    )
    kv_cache = jnp.zeros_like(keyval_heads).at[page_order[0]].set(keyval_heads)
    heads_out = attend(query_heads, keyval_heads, seg)
    attention = lax.psum_scatter(
        jnp.dot(heads_out, w_out, preferred_element_type=jnp.float32),
        "exp",
        scatter_dimension=0,
        tiled=True,
    )
    resid = tokens.astype(jnp.float32) + attention
    normed2 = rms_scale(resid, norm_moe)
    topk = expert_ids.shape[1]
    experts = w_router.shape[1]
    local = w_gate.shape[0]
    owners = lax.axis_size("exp")
    logits = jnp.dot(normed2, w_router, preferred_element_type=jnp.float32)
    weights = jax.nn.softmax(jnp.take_along_axis(logits, expert_ids, axis=1), axis=-1)
    flat = expert_ids.reshape(-1)
    hits = (flat[:, None] == jnp.arange(experts, dtype=jnp.int32)[None, :]).astype(jnp.int32)
    slot = jnp.sum(jnp.cumsum(hits, axis=0) * hits, axis=1) - 1
    source = jnp.arange(flat.shape[0], dtype=jnp.int32) // topk
    sending = normed2[source]
    copies = lax.axis_size("req")
    share = CAP // copies
    target = (
        (slot % copies * owners + flat // local) * local + flat % local
    ) * share + slot // copies
    buffer = jnp.zeros((experts * CAP, width), jnp.bfloat16).at[target].set(sending)
    buffer = buffer.reshape(copies * owners, local, share, width)
    returned = lax.all_to_all(
        expert_apply(
            lax.all_to_all(buffer, ("req", "exp"), split_axis=0, concat_axis=0, tiled=True),
            w_gate,
            w_up,
            w_down,
        ),
        ("req", "exp"),
        split_axis=0,
        concat_axis=0,
        tiled=True,
    )
    gathered = returned.reshape(experts * CAP, width)[target].reshape(rows, topk, width)
    moe = jnp.sum(weights[:, :, None] * gathered.astype(jnp.float32), axis=1)
    mixed = (resid + moe).astype(jnp.bfloat16)
    return (mixed, kv_cache)


def solution(mesh):
    placed = (
        P(("req", "exp"), None),
        P(),
        P(),
        P(),
        P(),
        P("exp", None),
        P(),
        P(),
        P("exp", None, None),
        P("exp", None, None),
        P("exp", None, None),
        P("req", None),
        P("req", None),
        P(("req", "exp"), None),
    )
    return jax.shard_map(
        shards,
        mesh=mesh,
        in_specs=placed,
        out_specs=(P(("req", "exp"), None), P("req", "exp", None)),
        check_vma=False,
    )
```

profile of v0, /device:TPU:0, one launch (start us, length us, event | category | flops | bytes accessed | tf_op | source)
XLA Modules:
  0.0 352.3 jit_solution(7622006813359838821)
XLA Ops:
  7.2 0.9 compare_reduce_fusion
  8.2 1.1 fusion.36
  9.2 0.1 add_select_fusion
  9.3 0.3 reduce-window.15
  9.6 0.1 slice.42
  9.7 0.1 slice_reduce_fusion
  9.9 0.1 bitcast_subtract_fusion
  9.9 0.7 convert_element_type.64
  10.6 1.7 convolution_convert_fusion
  12.3 0.1 copy.61
  12.4 1.9 fusion.57
  14.4 0.1 dynamic-slice_convert_fusion
  14.4 0.1 multiply_cosine_fusion
  14.6 0.7 pad_maximum_fusion
  15.4 6.3 %all-to-all-start = ((bf16[128,8,128]{0,2,1:T(8,128)(2,1)}), bf16[128,8,128]{0,2,1:T(8,128)(2,1)S(1)}, u32[]{:S(2)}, u32[]{:S(2)}) async-start(bf16[128,8,128]{0,2,1:T(8,128)(2,1)} %pad_maximum_fusion), calls=%async_computation | async-start | bytes 524288 | tf_op jit(solution)/shard_map/all_to_all | solution.py:107
  21.7 1.0 fusion.54
  22.7 0.1 subtract_convert_fusion
  22.8 0.7 pad_maximum_fusion.1
  23.5 7.1 %all-to-all-done = bf16[128,8,128]{0,2,1:T(8,128)(2,1)S(1)} async-done(((bf16[128,8,128]{0,2,1:T(8,128)(2,1)}), bf16[128,8,128]{0,2,1:T(8,128)(2,1)S(1)}, u32[]{:S(2)}, u32[]{:S(2)}) %all-to-all-start) | async-done | bytes 262176 | tf_op jit(solution)/shard_map/all_to_all | solution.py:107
  30.6 3.4 all-to-all-start.1
  34.0 0.2 reduce-scatter.2.cloned.1.call-start
  34.3 0.2 fusion.35
  34.5 0.2 copy.99
  34.7 0.1 reshape.526
  34.8 6.2 %all-to-all-done.1 = bf16[128,8,128]{0,2,1:T(8,128)(2,1)S(1)} async-done(((bf16[128,8,128]{0,2,1:T(8,128)(2,1)}), bf16[128,8,128]{0,2,1:T(8,128)(2,1)S(1)}, u32[]{:S(2)}, u32[]{:S(2)}) %all-to-all-start.1) | async-done | bytes 262176 | tf_op jit(solution)/shard_map/all_to_all | solution.py:106
  41.0 0.2 copy.65
  41.3 0.1 squeeze.14
  41.4 3.6 %fusion.59 = (f32[2,2,512]{2,1,0:T(2,128)S(1)}, f32[2,2,512,512]{2,3,1,0:T(8,128)}) fusion(pred[512,512]{0,1:T(8,128)(4,1)S(1)} %fusion.35, bf16[512,2,2,64]{0,3,2,1:T(8,128)(2,1)S(1)} %squeeze.14, bf16[512,2,128]{0,2,1:T(8,128)(2,1)S(1)} %reshape.526), kind=kOutput, calls=%fused_computation.113 | convolution fusion | flops 138412544 | bytes 4857856 | tf_op jit(solution)/shard_map/while/body/eval_jaxpr/sub | solution.py:54
  44.9 2.8 fusion.34
  47.7 1.8 fusion.60
  49.6 0.0 reduce-scatter.2.cloned.1.call-update
  49.6 0.1 copy.70
  49.7 0.1 reshape.488
  49.8 0.1 eq.62
  49.9 0.1 eq.58
  50.0 9.0 %reduce-window.19 = s32[32,8,128]{2,1,0:T(8,128)S(1)} reduce-window(s32[32,8,128]{2,1,0:T(8,128)S(1)} %fusion.43, s32[]{:T(128)} %constant.117.clone.1), window={size=1x1x128 pad=0_0x0_0x127_0}, to_apply=%region_9.10 | reduce-window | flops 4161536 | bytes 262148 | tf_op jit(solution)/shard_map/reduce-window.2
  59.0 0.1 slice.63
  59.1 0.1 copy.72
  59.3 0.1 copy.73
  59.4 0.1 broadcast_add_fusion
  59.6 0.1 compare_select_fusion.1
  59.6 33.3 %reduce-scatter.2.cloned.1.call-done = f32[128,1024]{1,0:T(8,128)} async-done(((f32[512,1024]{1,0:T(8,128)}), f32[128,1024]{1,0:T(8,128)}) %reduce-scatter.2.cloned.1.call-update) | async-done | bytes 524304 | tf_op jit(solution)/shard_map/reduce_scatter | solution.py:111
  93.0 1.2 multiply_reduce_fusion
  94.2 1.2 multiply_convert_fusion
  95.3 15.3 %scatter_custom_fusion = bf16[2048,1024]{1,0:T(8,128)(2,1)} fusion(s32[1024]{0:T(1024)S(1)} %bitcast.148, bf16[128,1024]{1,0:T(8,128)(2,1)S(1)} %multiply_convert_fusion, s32[1024]{0:T(1024)S(1)} %broadcast_clamp_fusion.1, bf16[]{:T(256)} %constant.129.clone.1), kind=kCustom, calls=%fused_computation.28 | custom fusion | bytes 4194306 | tf_op jit(solution)/shard_map/scatter | solution.py:135
  110.6 96.2 %all_to_all.43 = bf16[32,8,8,1024]{3,2,1,0:T(8,128)(2,1)S(1)} all-to-all(bf16[32,8,8,1024]{3,2,1,0:T(8,128)(2,1)} %bitcast.137), channel_id=1, replica_groups=mesh['req'=8,'exp'=4] {'req','exp'}, dimensions={0} | all-to-all | bytes 8388608 | tf_op jit(solution)/shard_map/all_to_all | solution.py:139
  206.8 2.0 copy-done.2
  208.8 7.7 %fusion.3 = f32[8,32,8,512]{3,2,1,0:T(8,128)} fusion(bf16[8,1024,512]{2,1,0:T(8,128)(2,1)} %param.23, bf16[32,8,8,1024]{3,2,1,0:T(8,128)(2,1)S(1)} %all_to_all.43), kind=kOutput, calls=%fused_computation.8 | convolution fusion | flops 2147483648 | bytes 16777216 | tf_op jit(solution)/shard_map/pend,edf->penf/dot_general | solution.py:65
  216.5 14.7 %convert_bitcast_fusion = bf16[32,8,8,1024]{3,2,0,1:T(8,128)(2,1)} fusion(bf16[8,512,1024]{2,1,0:T(8,128)(2,1)} %param.24, f32[8,32,8,512]{3,2,1,0:T(8,128)} %fusion.3, bf16[8,1024,512]{2,1,0:T(8,128)(2,1)} %param.22, bf16[32,8,8,1024]{3,2,1,0:T(8,128)(2,1)} %copy-done.2), kind=kOutput, calls=%fused_computation.22 | convolution fusion | flops 4303355904 | bytes 29360128 | tf_op jit(solution)/shard_map/penf,efd->pend/dot_general | solution.py:67
  231.1 4.8 %copy.77 = bf16[32,8,8,1024]{3,2,1,0:T(8,128)(2,1)} copy(bf16[32,8,8,1024]{3,2,0,1:T(8,128)(2,1)} %convert_bitcast_fusion) | data formatting | bytes 8388608 | tf_op jit(solution)/shard_map/convert_element_type | solution.py:68
  235.9 4.9 %all-to-all-start.3 = ((bf16[32,8,8,1024]{3,2,1,0:T(8,128)(2,1)}), bf16[32,8,8,1024]{3,2,1,0:T(8,128)(2,1)}, u32[]{:S(2)}, u32[]{:S(2)}) async-start(bf16[32,8,8,1024]{3,2,1,0:T(8,128)(2,1)} %copy.77), calls=%async_computation.4 | async-start | bytes 8388608 | tf_op jit(solution)/shard_map/all_to_all | solution.py:137
  240.9 0.1 copy.67
  241.0 0.1 reshape.508
  241.1 0.2 copy.78
  241.3 0.1 broadcast_in_dim.73
  241.4 14.2 %scatter_fusion = bf16[512,2,128]{2,1,0:T(2,128)(2,1)S(1)} fusion(bf16[512,2,128]{2,1,0:T(2,128)(2,1)S(1)} %broadcast_in_dim.73, s32[512]{0:T(512)S(1)} %bitcast.152, bf16[512,2,128]{2,1,0:T(2,128)(2,1)S(1)} %copy.78), kind=kCustom, calls=%fused_computation.4 | custom fusion | bytes 788480 | tf_op jit(solution)/shard_map/scatter | solution.py:109
  255.7 0.2 fusion.61
  255.8 7.0 %gather_fusion.1 = f32[1024]{0:T(1024)S(1)} fusion(f32[128,32]{0,1:T(8,128)S(1)} %fusion.61, s32[1024]{0:T(1024)S(1)} %reshape.508), kind=kCustom, calls=%fused_computation.2 | custom fusion | bytes 16384 | tf_op jit(solution)/shard_map/jit(take_along_axis)/gather | solution.py:124
  262.9 0.1 reshape.511
  263.1 0.1 copy.69
  263.2 69.6 %all-to-all-done.3 = bf16[32,8,8,1024]{3,2,1,0:T(8,128)(2,1)} async-done(((bf16[32,8,8,1024]{3,2,1,0:T(8,128)(2,1)}), bf16[32,8,8,1024]{3,2,1,0:T(8,128)(2,1)}, u32[]{:S(2)}, u32[]{:S(2)}) %all-to-all-start.3) | async-done | bytes 4194336 | tf_op jit(solution)/shard_map/all_to_all | solution.py:137
  332.8 8.9 %gather_fusion = bf16[1024,1024]{1,0:T(8,128)(2,1)} fusion(bf16[2048,1024]{1,0:T(8,128)(2,1)} %bitcast.35, s32[1024]{0:T(1024)S(1)} %broadcast_clamp_fusion), kind=kCustom, calls=%fused_computation.1 | custom fusion | bytes 4198400 | tf_op jit(solution)/shard_map/gather | solution.py:149
  341.7 2.9 fusion.7
  344.7 0.8 add_convert_fusion
  (43 shorter events, 0.4 us)
Async XLA Ops:
  7.2 14.5 %copy-start = (bf16[1024,1024]{1,0:T(8,128)(2,1)S(1)}, bf16[1024,1024]{1,0:T(8,128)(2,1)}, u32[]{:S(2)}) copy-start(bf16[1024,1024]{1,0:T(8,128)(2,1)} %param.16) | copy-start | bytes 6291460
  7.2 14.5 %copy-start.3 = (bf16[128,1024]{1,0:T(8,128)(2,1)S(1)}, bf16[128,1024]{1,0:T(8,128)(2,1)}, u32[]{:S(2)}) copy-start(bf16[128,1024]{1,0:T(8,128)(2,1)} %param.14) | copy-start | bytes 786436
  12.3 22.0 %copy-start.9 = (s32[1,512]{1,0:T(1,128)S(1)}, s32[1,512]{1,0:T(1,128)}, u32[]{:S(2)}) copy-start(s32[1,512]{1,0:T(1,128)} %param.25) | copy-start | bytes 6148
  15.4 15.3 %all-to-all-start = ((bf16[128,8,128]{0,2,1:T(8,128)(2,1)}), bf16[128,8,128]{0,2,1:T(8,128)(2,1)S(1)}, u32[]{:S(2)}, u32[]{:S(2)}) async-start(bf16[128,8,128]{0,2,1:T(8,128)(2,1)} %pad_maximum_fusion), calls=%async_computation | async-start | bytes 524288 | tf_op jit(solution)/shard_map/all_to_all | solution.py:107
  30.6 10.4 %all-to-all-start.1 = ((bf16[128,8,128]{0,2,1:T(8,128)(2,1)}), bf16[128,8,128]{0,2,1:T(8,128)(2,1)S(1)}, u32[]{:S(2)}, u32[]{:S(2)}) async-start(bf16[128,8,128]{0,2,1:T(8,128)(2,1)} %bitcast.12), calls=%async_computation.1 | async-start | bytes 524288 | tf_op jit(solution)/shard_map/all_to_all | solution.py:106
  34.0 58.9 %reduce-scatter.2.cloned.1.call-start = ((), (), s32[]{:S(2)}) async-start(), calls=%async_computation.5 | async-start | bytes 2621440 | tf_op jit(solution)/shard_map/reduce_scatter | solution.py:111
  44.9 2.8 copy-start.6
  47.7 1.9 copy-start.7
  47.7 2.3 copy-start.10
  206.8 2.0 copy-start.2
  235.9 5.2 %copy-start.11 = (s32[1,512]{1,0:T(1,128)S(1)}, s32[1,512]{1,0:T(1,128)}, u32[]{:S(2)}) copy-start(s32[1,512]{1,0:T(1,128)} %param.26) | copy-start | bytes 6148
  235.9 19.7 %copy-start.8 = (bf16[1024,32]{0,1:T(8,128)(2,1)S(1)}, bf16[1024,32]{0,1:T(8,128)(2,1)}, u32[]{:S(2)}) copy-start(bf16[1024,32]{0,1:T(8,128)(2,1)} %param.21) | copy-start | bytes 196612
  235.9 96.9 %all-to-all-start.3 = ((bf16[32,8,8,1024]{3,2,1,0:T(8,128)(2,1)}), bf16[32,8,8,1024]{3,2,1,0:T(8,128)(2,1)}, u32[]{:S(2)}, u32[]{:S(2)}) async-start(bf16[32,8,8,1024]{3,2,1,0:T(8,128)(2,1)} %copy.77), calls=%async_computation.4 | async-start | bytes 8388608 | tf_op jit(solution)/shard_map/all_to_all | solution.py:137
  255.7 7.2 %copy-start.5 = (bf16[512,2,128]{2,1,0:T(2,128)(2,1)}, bf16[512,2,128]{2,1,0:T(2,128)(2,1)S(1)}, u32[]{:S(2)}) copy-start(bf16[512,2,128]{2,1,0:T(2,128)(2,1)S(1)} %scatter_fusion) | copy-start | bytes 786436
  332.8 11.9 %copy-start.4 = (f32[128,1024]{1,0:T(8,128)S(1)}, f32[128,1024]{1,0:T(8,128)}, u32[]{:S(2)}) copy-start(f32[128,1024]{1,0:T(8,128)} %reduce-scatter.2.cloned.1.call-done) | copy-start | bytes 1572868
  332.8 12.7 %copy-start.1 = (bf16[1024,1024]{1,0:T(8,128)(2,1)S(1)}, bf16[1024,1024]{1,0:T(8,128)(2,1)}, u32[]{:S(2)}) copy-start(bf16[1024,1024]{1,0:T(8,128)(2,1)} %param.16) | copy-start | bytes 6291460
Sparse Core Ops, SparseCore 0:
  49.7 43.2 reduce-scatter.1
where the time goes:
time: 354 us; the launch traced here: 352 us
  waiting for transfers between devices  116 us (33%)
  blocking collectives  96.2 us (27%)
  local copies, waits for them, and re-layouts  54.6 us (15%)
  matrix products  35.2 us (10%)
  other arithmetic  20.7 us (6%)
  starting transfers between devices  14.9 us (4%)
  between operations  14.4 us (4%)
    all_to_all x1, blocking collectives, shards(): lax.all_to_all(buffer, ('req', 'exp'), split_axis=0, concat_axis=0, tiled...  96.2 us
    all_to_all x1, waiting for transfers between devices, shards(): lax.all_to_all(expert_apply(lax.all_to_all(buffer, ('req', 'exp'), split_...  69.6 us
    reduce_scatter x1, waiting for transfers between devices, shards(): lax.psum_scatter(jnp.dot(heads_out, w_out, preferred_element_type=jnp.flo...  33.3 us
    scatter x1, local copies, waits for them, and re-layouts, shards(): jnp.zeros((experts * CAP, width), jnp.bfloat16).at[target].set(sending)  15.3 us
    dot_general x1, matrix products, expert_apply(): jnp.einsum('penf,efd->pend', hidden, w_down, preferred_element_type=jnp.f...  14.7 us
    scatter x1, local copies, waits for them, and re-layouts, shards(): kv_cache = jnp.zeros_like(keyval_heads).at[page_order[0]].set(keyval_heads)  14.2 us
    another operation x7, other arithmetic  9.6 us
    gather x1, local copies, waits for them, and re-layouts, shards(): returned.reshape(experts * CAP, width)[target].reshape(rows, topk, width)  8.93 us
  transfers between devices with their start and end apart: 4, of which 4 were waited for; matrix products, arithmetic and copies ran while one was open for 10% of the time, Pallas kernels for 0%

commit v1 on v0

--- a/solution.py
+++ b/solution.py
@@ -60,12 +60,37 @@
     return outs.reshape(plen, groups * width)
 
 
-def expert_apply(received, w_gate, w_up, w_down):
-    gate = jnp.einsum("pend,edf->penf", received, w_gate, preferred_element_type=jnp.float32)
-    upward = jnp.einsum("pend,edf->penf", received, w_up, preferred_element_type=jnp.float32)
+def expert_mix(rows_all, ids_all, w_router, w_gate, w_up, w_down):
+    tokens_all = rows_all.shape[0]
+    local = w_gate.shape[0]
+    cap = CAP * lax.axis_size("exp")
+    here = lax.axis_index("exp")
+    logits = jnp.dot(rows_all, w_router, preferred_element_type=jnp.float32)
+    weights = jax.nn.softmax(jnp.take_along_axis(logits, ids_all, axis=1), axis=-1)
+    match = (ids_all - here * local)[:, :, None] == jnp.arange(local, dtype=jnp.int32)
+    hits = jnp.any(match, axis=1)
+    mine = jnp.sum(jnp.where(match, weights[:, :, None], 0.0), axis=1)
+    order = jnp.arange(tokens_all, dtype=jnp.int32)
+    before = (order[None, :] < order[:, None]).astype(jnp.bfloat16)
+    slot = jnp.dot(before, hits.astype(jnp.bfloat16), preferred_element_type=jnp.float32)
+    slot = slot.astype(jnp.int32)
+    picks = hits.T[:, None, :] & (
+        slot.T[:, None, :] == jnp.arange(cap, dtype=jnp.int32)[None, :, None]
+    )
+    received = jnp.einsum(
+        "est,td->esd", picks.astype(jnp.bfloat16), rows_all, preferred_element_type=jnp.float32
+    ).astype(jnp.bfloat16)
+    gate = jnp.einsum("esd,edf->esf", received, w_gate, preferred_element_type=jnp.float32)
+    upward = jnp.einsum("esd,edf->esf", received, w_up, preferred_element_type=jnp.float32)
     hidden = (jax.nn.silu(gate) * upward).astype(jnp.bfloat16)
-    result = jnp.einsum("penf,efd->pend", hidden, w_down, preferred_element_type=jnp.float32)
-    return result.astype(jnp.bfloat16)
+    result = jnp.einsum("esf,efd->esd", hidden, w_down, preferred_element_type=jnp.float32)
+    result = result.astype(jnp.bfloat16)
+    combine = jnp.where(picks, mine.T[:, None, :], 0.0)
+    high = combine.astype(jnp.bfloat16)
+    low = (combine - high.astype(jnp.float32)).astype(jnp.bfloat16)
+    partial = jnp.einsum("est,esd->td", high, result, preferred_element_type=jnp.float32)
+    partial = partial + jnp.einsum("est,esd->td", low, result, preferred_element_type=jnp.float32)
+    return partial
 
 
 def shards(
@@ -88,6 +113,7 @@
     seg = segment_ids[0]
     groups = w_key.shape[1] // HD
     here = lax.axis_index("exp")
+    ids_all = lax.all_gather(expert_ids, "exp", axis=0, tiled=True)
     pos = lax.dynamic_slice_in_dim(positions(seg), here * rows, rows)
     normed = rms_scale(tokens, norm_attn)
     query = jnp.dot(normed, w_query, preferred_element_type=jnp.float32).reshape(
@@ -116,38 +142,9 @@
     )
     resid = tokens.astype(jnp.float32) + attention
     normed2 = rms_scale(resid, norm_moe)
-    topk = expert_ids.shape[1]
-    experts = w_router.shape[1]
-    local = w_gate.shape[0]
-    owners = lax.axis_size("exp")
-    logits = jnp.dot(normed2, w_router, preferred_element_type=jnp.float32)
-    weights = jax.nn.softmax(jnp.take_along_axis(logits, expert_ids, axis=1), axis=-1)
-    flat = expert_ids.reshape(-1)
-    hits = (flat[:, None] == jnp.arange(experts, dtype=jnp.int32)[None, :]).astype(jnp.int32)
-    slot = jnp.sum(jnp.cumsum(hits, axis=0) * hits, axis=1) - 1
-    source = jnp.arange(flat.shape[0], dtype=jnp.int32) // topk
-    sending = normed2[source]
-    copies = lax.axis_size("req")
-    share = CAP // copies
-    target = (
-        (slot % copies * owners + flat // local) * local + flat % local
-    ) * share + slot // copies
-    buffer = jnp.zeros((experts * CAP, width), jnp.bfloat16).at[target].set(sending)
-    buffer = buffer.reshape(copies * owners, local, share, width)
-    returned = lax.all_to_all(
-        expert_apply(
-            lax.all_to_all(buffer, ("req", "exp"), split_axis=0, concat_axis=0, tiled=True),
-            w_gate,
-            w_up,
-            w_down,
-        ),
-        ("req", "exp"),
-        split_axis=0,
-        concat_axis=0,
-        tiled=True,
-    )
-    gathered = returned.reshape(experts * CAP, width)[target].reshape(rows, topk, width)
-    moe = jnp.sum(weights[:, :, None] * gathered.astype(jnp.float32), axis=1)
+    rows_all = lax.all_gather(normed2, "exp", axis=0, tiled=True)
+    partial = expert_mix(rows_all, ids_all, w_router, w_gate, w_up, w_down)
+    moe = lax.psum_scatter(partial, "exp", scatter_dimension=0, tiled=True)
     mixed = (resid + moe).astype(jnp.bfloat16)
     return (mixed, kv_cache)
 

time: 354 us -> 251 us (0.71)
  blocking collectives: 96.2 us -> 13.3 us
  waiting for transfers between devices: 116 us -> 98.3 us
  matrix products: 35.2 us -> 51.7 us
  other arithmetic: 20.7 us -> 10.3 us
  starting transfers between devices: 14.9 us -> 9.88 us
    all_to_all x1 -> x0, blocking collectives: 96.2 us -> none  [shards(): lax.all_to_all(buffer, ('req', 'exp'), split_axis=0, concat_axis=0, tiled...]
    all_to_all x1 -> x0, waiting for transfers between devices: 69.6 us -> none  [shards(): lax.all_to_all(expert_apply(lax.all_to_all(buffer, ('req', 'exp'), split_...]
    reduce_scatter x0 -> x1, waiting for transfers between devices: none -> 28.6 us  [shards(): moe = lax.psum_scatter(partial, 'exp', scatter_dimension=0, tiled=True)]
    gather x6 -> x5, local copies, waits for them, and re-layouts: 16.3 us -> 35.4 us  [expert_mix(): jnp.take_along_axis(logits, ids_all, axis=1)]
    dot_general x3 -> x7, matrix products: 22.5 us -> 39 us  [the longest x1 14.6 us: expert_mix(): jnp.einsum('esf,efd->esd', hidden, w_down, preferred_element_type=jnp.flo...]
    scatter x1 -> x0, local copies, waits for them, and re-layouts: 15.3 us -> none  [shards(): jnp.zeros((experts * CAP, width), jnp.bfloat16).at[target].set(sending)]
    all_gather x0 -> x1, blocking collectives: none -> 13.3 us  [shards(): ids_all = lax.all_gather(expert_ids, 'exp', axis=0, tiled=True)]
    all_gather x0 -> x1, waiting for transfers between devices: none -> 12.8 us  [shards(): rows_all = lax.all_gather(normed2, 'exp', axis=0, tiled=True)]
  transfers between devices with their start and end apart: 4 -> 5, of which waited for: 4 -> 5; matrix products, arithmetic and copies ran while one was open for 10% -> 7% of each run, Pallas kernels for 0% -> 0%
where the time goes in v1:
time: 251 us; the launch traced here: 250 us
  waiting for transfers between devices  98.3 us (39%)
  local copies, waits for them, and re-layouts  52.9 us (21%)
  matrix products  51.7 us (21%)
  between operations  14.1 us (6%)
  blocking collectives  13.3 us (5%)
  other arithmetic  10.3 us (4%)
  starting transfers between devices  9.88 us (4%)
    reduce_scatter x1, waiting for transfers between devices, shards(): lax.psum_scatter(jnp.dot(heads_out, w_out, preferred_element_type=jnp.flo...  43.3 us
    gather x5, local copies, waits for them, and re-layouts, expert_mix(): jnp.take_along_axis(logits, ids_all, axis=1)  35.4 us
    reduce_scatter x1, waiting for transfers between devices, shards(): moe = lax.psum_scatter(partial, 'exp', scatter_dimension=0, tiled=True)  28.6 us
    dot_general x1, matrix products, expert_mix(): jnp.einsum('esf,efd->esd', hidden, w_down, preferred_element_type=jnp.flo...  14.6 us
    scatter x1, local copies, waits for them, and re-layouts, shards(): kv_cache = jnp.zeros_like(keyval_heads).at[page_order[0]].set(keyval_heads)  14.2 us
    all_gather x1, blocking collectives, shards(): ids_all = lax.all_gather(expert_ids, 'exp', axis=0, tiled=True)  13.3 us
    all_gather x1, waiting for transfers between devices, shards(): rows_all = lax.all_gather(normed2, 'exp', axis=0, tiled=True)  12.8 us
    dot_general x1, matrix products, expert_mix(): jnp.einsum('esd,edf->esf', received, w_gate, preferred_element_type=jnp.f...  7.68 us
  transfers between devices with their start and end apart: 5, of which 5 were waited for; matrix products, arithmetic and copies ran while one was open for 7% of the time, Pallas kernels for 0%

profile of v1, /device:TPU:0, one launch (start us, length us, event | category | flops | bytes accessed | tf_op | source)
XLA Modules:
  0.0 250.5 jit_solution(3685987123882004109)
XLA Ops:
  7.2 0.0 copy-start
  7.2 0.9 compare_reduce_fusion
  8.2 1.1 fusion.31
  9.2 0.1 add_select_fusion
  9.3 0.3 reduce-window.9
  9.6 0.1 slice.36
  9.7 0.1 slice_reduce_fusion
  9.9 0.1 bitcast_subtract_fusion
  9.9 0.7 convert_element_type.69
  10.6 1.7 convolution_convert_fusion.1
  12.3 0.0 copy-start.10
  12.3 0.1 copy.44
  12.4 1.9 fusion.49
  14.4 0.1 dynamic-slice_convert_fusion
  14.4 0.1 multiply_cosine_fusion
  14.6 0.7 pad_maximum_fusion
  15.4 6.3 %all-to-all-start = ((bf16[128,8,128]{0,2,1:T(8,128)(2,1)}), bf16[128,8,128]{0,2,1:T(8,128)(2,1)S(1)}, u32[]{:S(2)}, u32[]{:S(2)}) async-start(bf16[128,8,128]{0,2,1:T(8,128)(2,1)} %pad_maximum_fusion), calls=%async_computation | async-start | bytes 524288 | tf_op jit(solution)/shard_map/all_to_all | solution.py:133
  21.7 1.0 fusion.46
  22.7 0.1 subtract_convert_fusion
  22.8 0.7 pad_maximum_fusion.1
  23.5 7.1 %all-to-all-done = bf16[128,8,128]{0,2,1:T(8,128)(2,1)S(1)} async-done(((bf16[128,8,128]{0,2,1:T(8,128)(2,1)}), bf16[128,8,128]{0,2,1:T(8,128)(2,1)S(1)}, u32[]{:S(2)}, u32[]{:S(2)}) %all-to-all-start) | async-done | bytes 262176 | tf_op jit(solution)/shard_map/all_to_all | solution.py:133
  30.6 3.4 %all-to-all-start.1 = ((bf16[128,8,128]{0,2,1:T(8,128)(2,1)}), bf16[128,8,128]{0,2,1:T(8,128)(2,1)S(1)}, u32[]{:S(2)}, u32[]{:S(2)}) async-start(bf16[128,8,128]{0,2,1:T(8,128)(2,1)} %bitcast.12), calls=%async_computation.1 | async-start | bytes 524288 | tf_op jit(solution)/shard_map/all_to_all | solution.py:132
  34.0 0.0 reduce-scatter.3.cloned.1.call-start
  34.1 0.2 fusion.30
  34.3 0.2 copy.62
  34.5 0.1 reshape.234
  34.6 0.0 copy-start.6
  34.6 6.4 %all-to-all-done.1 = bf16[128,8,128]{0,2,1:T(8,128)(2,1)S(1)} async-done(((bf16[128,8,128]{0,2,1:T(8,128)(2,1)}), bf16[128,8,128]{0,2,1:T(8,128)(2,1)S(1)}, u32[]{:S(2)}, u32[]{:S(2)}) %all-to-all-start.1) | async-done | bytes 262176 | tf_op jit(solution)/shard_map/all_to_all | solution.py:132
  41.0 0.2 copy.48
  41.2 0.1 squeeze.14
  41.3 3.6 %fusion.51 = (f32[2,2,512]{2,1,0:T(2,128)S(1)}, f32[2,2,512,512]{2,3,1,0:T(8,128)}) fusion(pred[512,512]{0,1:T(8,128)(4,1)S(1)} %fusion.30, bf16[512,2,2,64]{0,3,2,1:T(8,128)(2,1)S(1)} %squeeze.14, bf16[512,2,128]{0,2,1:T(8,128)(2,1)S(1)} %reshape.234), kind=kOutput, calls=%fused_computation.90 | convolution fusion | flops 138412544 | bytes 4857856 | tf_op jit(solution)/shard_map/while/body/eval_jaxpr/sub | solution.py:54
  44.9 2.7 %fusion.28 = bf16[2,64,2,512]{3,1,2,0:T(8,128)(2,1)S(1)} fusion(f32[2,2,512,512]{2,3,1,0:T(8,128)} %get-tuple-element.33, f32[2,2,512]{2,1,0:T(2,128)S(1)} %get-tuple-element.32, bf16[512,2,128]{0,2,1:T(8,128)(2,1)S(1)} %reshape.234), kind=kOutput, calls=%fused_computation.33 | convolution fusion | flops 136445952 | bytes 4595712 | tf_op jit(solution)/shard_map/while/body/eval_jaxpr/kgqt,tkd->qkgd/dot_general | solution.py:56
  47.7 0.0 copy-start.12
  47.7 0.0 copy-start.11
  47.7 1.8 fusion.52
  49.5 0.0 reduce-scatter.3.cloned.1.call-update
  49.5 0.0 all-gather.2.cloned.1.call-start
  49.6 43.3 %reduce-scatter.3.cloned.1.call-done = f32[128,1024]{1,0:T(8,128)} async-done(((f32[512,1024]{1,0:T(8,128)}), f32[128,1024]{1,0:T(8,128)}) %reduce-scatter.3.cloned.1.call-update) | async-done | bytes 524304 | tf_op jit(solution)/shard_map/reduce_scatter | solution.py:137
  92.9 1.2 multiply_reduce_fusion
  94.1 1.9 multiply_convert_fusion.1
  96.0 0.0 all-gather.2.cloned.1.call-update
  96.0 0.0 reduce-scatter.5.cloned.1.call-start
  96.1 13.3 %all_gather.6 = s32[512,8]{0,1:T(8,128)S(1)} all-gather(s32[128,8]{0,1:T(8,128)S(1)} %copy-done.11), channel_id=1, replica_groups=mesh['req'=8,'exp'=4] {'exp'}, dimensions={0}, use_global_device_ids=true | all-gather | bytes 20480 | tf_op jit(solution)/shard_map/all_gather | solution.py:116
  109.4 0.1 copy.50
  109.6 0.2 reshape.224
  109.8 0.9 convolution_convert_fusion.2
  110.6 12.8 %all-gather.2.cloned.1.call-done = bf16[512,1024]{1,0:T(8,128)(2,1)} async-done(((bf16[128,1024]{1,0:T(8,128)(2,1)}), bf16[512,1024]{1,0:T(8,128)(2,1)}) %all-gather.2.cloned.1.call-update) | async-done | bytes 1048592 | tf_op jit(solution)/shard_map/all_gather | solution.py:145
  123.4 1.6 fusion.53
  125.0 0.0 copy-start.5
  125.1 33.2 %gather_fusion = f32[4096]{0:T(1024)S(1)} fusion(f32[512,32]{0,1:T(8,128)S(1)} %fusion.53, s32[4096]{0:T(1024)S(1)} %reshape.224), kind=kCustom, calls=%fused_computation | custom fusion | bytes 65536 | tf_op jit(solution)/shard_map/jit(take_along_axis)/gather | solution.py:69
  158.3 0.9 reshape.227
  159.1 1.0 copy.51
  160.3 4.7 %fusion.6 = bf16[8,256,1024]{2,1,0:T(8,128)(2,1)S(1)} fusion(s32[8,512]{1,0:T(8,128)} %convolution_convert_fusion.2, pred[8,512]{1,0:T(8,128)(4,1)S(1)} %bitcast.100, bf16[512,1024]{1,0:T(8,128)(2,1)S(1)} %copy-done.5), kind=kOutput, calls=%fused_computation.15 | convolution fusion | flops 2151677952 | bytes 5263360 | tf_op jit(solution)/shard_map/est,td->esd/dot_general | solution.py:80
  165.1 2.0 copy-done.2
  167.0 7.7 %fusion.54 = f32[8,256,512]{2,1,0:T(8,128)} fusion(bf16[8,256,1024]{2,1,0:T(8,128)(2,1)S(1)} %fusion.6, bf16[8,1024,512]{2,1,0:T(8,128)(2,1)} %param.22), kind=kOutput, calls=%fused_computation.93 | convolution fusion | flops 2147483648 | bytes 16777216 | tf_op jit(solution)/shard_map/esd,edf->esf/dot_general | solution.py:83
  174.7 14.6 %convolution_convert_fusion = bf16[8,256,1024]{2,1,0:T(8,128)(2,1)} fusion(bf16[8,512,1024]{2,1,0:T(8,128)(2,1)} %param.24, f32[8,256,512]{2,1,0:T(8,128)} %fusion.54, bf16[8,256,1024]{2,1,0:T(8,128)(2,1)} %copy-done.2, bf16[8,1024,512]{2,1,0:T(8,128)(2,1)} %param.23), kind=kOutput, calls=%fused_computation.14 | convolution fusion | flops 4303355904 | bytes 29360128 | tf_op jit(solution)/shard_map/esf,efd->esd/dot_general | solution.py:86
  189.3 5.3 %fusion.9 = f32[512,1024,1]{1,0,2:T(8,128)S(1)} fusion(bf16[8,256,1024]{2,1,0:T(8,128)(2,1)} %convolution_convert_fusion, f32[8,512]{1,0:T(8,128)S(1)} %bitcast.97, s32[8,512]{1,0:T(8,128)S(1)} %copy-done.14, pred[8,512]{1,0:T(8,128)(4,1)S(1)} %bitcast.101), kind=kOutput, calls=%fused_computation.16 | convolution fusion | flops 2150629376 | bytes 6328320 | tf_op jit(solution)/shard_map/est,esd->td/dot_general | solution.py:91
  194.7 4.2 %bitcast_add_fusion = f32[512,1024]{1,0:T(8,128)} fusion(f32[512,1024,1]{1,0,2:T(8,128)S(1)} %fusion.9, bf16[8,256,1024]{2,1,0:T(8,128)(2,1)S(1)} %copy-done.15, f32[8,512]{1,0:T(8,128)S(1)} %bitcast.98, s32[8,512]{1,0:T(8,128)S(1)} %copy-done.14, pred[8,512]{1,0:T(8,128)(4,1)S(1)} %bitcast.102), kind=kOutput, calls=%fused_computation.18 | convolution fusion | flops 2155347968 | bytes 8425472 | tf_op jit(solution)/shard_map/est,esd->td/dot_general | solution.py:92
  198.9 0.0 reduce-scatter.5.cloned.1.call-update
  198.9 0.2 copy.53
  199.1 0.1 broadcast_in_dim.101
  199.3 14.2 %scatter_fusion = bf16[512,2,128]{2,1,0:T(2,128)(2,1)S(1)} fusion(bf16[512,2,128]{2,1,0:T(2,128)(2,1)S(1)} %broadcast_in_dim.101, s32[512]{0:T(512)S(1)} %bitcast.99, bf16[512,2,128]{2,1,0:T(2,128)(2,1)S(1)} %copy.53), kind=kCustom, calls=%fused_computation.1 | custom fusion | bytes 788480 | tf_op jit(solution)/shard_map/scatter | solution.py:135
  213.5 28.6 %reduce-scatter.5.cloned.1.call-done = f32[128,1024]{1,0:T(8,128)} async-done(((f32[512,1024]{1,0:T(8,128)}), f32[128,1024]{1,0:T(8,128)}) %reduce-scatter.5.cloned.1.call-update) | async-done | bytes 524304 | tf_op jit(solution)/shard_map/reduce_scatter | solution.py:147
  242.1 1.8 add_convert_fusion
  (39 shorter events, 0.3 us)
Async XLA Ops:
  7.2 14.6 %copy-start = (bf16[1024,1024]{1,0:T(8,128)(2,1)S(1)}, bf16[1024,1024]{1,0:T(8,128)(2,1)}, u32[]{:S(2)}) copy-start(bf16[1024,1024]{1,0:T(8,128)(2,1)} %param.16) | copy-start | bytes 6291460
  7.2 14.5 %copy-start.1 = (bf16[128,1024]{1,0:T(8,128)(2,1)S(1)}, bf16[128,1024]{1,0:T(8,128)(2,1)}, u32[]{:S(2)}) copy-start(bf16[128,1024]{1,0:T(8,128)(2,1)} %param.14) | copy-start | bytes 786436
  12.3 21.8 %copy-start.10 = (s32[1,512]{1,0:T(1,128)S(1)}, s32[1,512]{1,0:T(1,128)}, u32[]{:S(2)}) copy-start(s32[1,512]{1,0:T(1,128)} %param.25) | copy-start | bytes 6148
  15.4 15.2 %all-to-all-start = ((bf16[128,8,128]{0,2,1:T(8,128)(2,1)}), bf16[128,8,128]{0,2,1:T(8,128)(2,1)S(1)}, u32[]{:S(2)}, u32[]{:S(2)}) async-start(bf16[128,8,128]{0,2,1:T(8,128)(2,1)} %pad_maximum_fusion), calls=%async_computation | async-start | bytes 524288 | tf_op jit(solution)/shard_map/all_to_all | solution.py:133
  30.6 10.4 %all-to-all-start.1 = ((bf16[128,8,128]{0,2,1:T(8,128)(2,1)}), bf16[128,8,128]{0,2,1:T(8,128)(2,1)S(1)}, u32[]{:S(2)}, u32[]{:S(2)}) async-start(bf16[128,8,128]{0,2,1:T(8,128)(2,1)} %bitcast.12), calls=%async_computation.1 | async-start | bytes 524288 | tf_op jit(solution)/shard_map/all_to_all | solution.py:132
  34.0 58.9 %reduce-scatter.3.cloned.1.call-start = ((), (), s32[]{:S(2)}) async-start(), calls=%async_computation.4 | async-start | bytes 2621440 | tf_op jit(solution)/shard_map/reduce_scatter | solution.py:137
  34.6 10.3 %copy-start.6 = (bf16[512,2,128]{0,2,1:T(8,128)(2,1)}, bf16[512,2,128]{0,2,1:T(8,128)(2,1)S(1)}, u32[]{:S(2)}) copy-start(bf16[512,2,128]{0,2,1:T(8,128)(2,1)S(1)} %reshape.234) | copy-start | bytes 786436
  44.9 2.8 %copy-start.8 = (bf16[256,1024]{1,0:T(8,128)(2,1)S(1)}, bf16[256,1024]{1,0:T(8,128)(2,1)}, u32[]{:S(2)}) copy-start(bf16[256,1024]{1,0:T(8,128)(2,1)} %param.19) | copy-start | bytes 1572868
  47.7 1.9 copy-start.12
  47.7 48.4 %copy-start.11 = (s32[128,8]{0,1:T(8,128)S(1)}, s32[128,8]{0,1:T(8,128)}, u32[]{:S(2)}) copy-start(s32[128,8]{0,1:T(8,128)} %param.27) | copy-start | bytes 12292
  47.7 75.7 %copy-start.9 = (bf16[1024,32]{0,1:T(8,128)(2,1)S(1)}, bf16[1024,32]{0,1:T(8,128)(2,1)}, u32[]{:S(2)}) copy-start(bf16[1024,32]{0,1:T(8,128)(2,1)} %param.21) | copy-start | bytes 196612
  49.5 73.9 %all-gather.2.cloned.1.call-start = ((), (), s32[]{:S(2)}) async-start(), calls=%async_computation.5 | async-start | bytes 1310720 | tf_op jit(solution)/shard_map/all_gather | solution.py:145
  96.0 146.1 %reduce-scatter.5.cloned.1.call-start = ((), (), s32[]{:S(2)}) async-start(), calls=%async_computation.6 | async-start | bytes 2621440 | tf_op jit(solution)/shard_map/reduce_scatter | solution.py:147
  125.0 35.3 %copy-start.5 = (bf16[512,1024]{1,0:T(8,128)(2,1)S(1)}, bf16[512,1024]{1,0:T(8,128)(2,1)}, u32[]{:S(2)}) copy-start(bf16[512,1024]{1,0:T(8,128)(2,1)} %all-gather.2.cloned.1.call-done) | copy-start | bytes 3145732
  165.0 2.0 copy-start.2
  174.7 14.6 %copy-start.14 = (s32[8,512]{1,0:T(8,128)S(1)}, s32[8,512]{1,0:T(8,128)}, u32[]{:S(2)}) copy-start(s32[8,512]{1,0:T(8,128)} %convolution_convert_fusion.2) | copy-start | bytes 49156
  189.3 5.3 %copy-start.15 = (bf16[8,256,1024]{2,1,0:T(8,128)(2,1)S(1)}, bf16[8,256,1024]{2,1,0:T(8,128)(2,1)}, u32[]{:S(2)}) copy-start(bf16[8,256,1024]{2,1,0:T(8,128)(2,1)} %convolution_convert_fusion) | copy-start | bytes 12582916
  194.6 4.3 %copy-start.13 = (s32[1,512]{1,0:T(1,128)S(1)}, s32[1,512]{1,0:T(1,128)}, u32[]{:S(2)}) copy-start(s32[1,512]{1,0:T(1,128)} %param.26) | copy-start | bytes 6148
  194.6 4.3 %copy-start.7 = (bf16[512,2,128]{0,2,1:T(8,128)(2,1)S(1)}, bf16[512,2,128]{0,2,1:T(8,128)(2,1)}, u32[]{:S(2)}) copy-start(bf16[512,2,128]{0,2,1:T(8,128)(2,1)} %copy-done.6) | copy-start | bytes 786436
  194.6 47.4 %copy-start.3 = (f32[128,1024]{1,0:T(8,128)S(1)}, f32[128,1024]{1,0:T(8,128)}, u32[]{:S(2)}) copy-start(f32[128,1024]{1,0:T(8,128)} %reduce-scatter.3.cloned.1.call-done) | copy-start | bytes 1572868
  213.5 30.5 %copy-start.4 = (bf16[512,2,128]{2,1,0:T(2,128)(2,1)}, bf16[512,2,128]{2,1,0:T(2,128)(2,1)S(1)}, u32[]{:S(2)}) copy-start(bf16[512,2,128]{2,1,0:T(2,128)(2,1)S(1)} %scatter_fusion) | copy-start | bytes 786436
Sparse Core Ops, SparseCore 0:
  49.7 43.2 reduce-scatter.2
  96.1 27.2 all-gather.1
  199.0 43.0 reduce-scatter.4

commit v2 on v1

--- a/solution.py
+++ b/solution.py
@@ -60,20 +60,36 @@
     return outs.reshape(plen, groups * width)
 
 
-def expert_mix(rows_all, ids_all, w_router, w_gate, w_up, w_down):
-    tokens_all = rows_all.shape[0]
+def routing(normed2, ids, w_router):
+    experts = w_router.shape[1]
+    logits = jnp.dot(normed2, w_router, preferred_element_type=jnp.float32)
+    match = ids[:, :, None] == jnp.arange(experts, dtype=jnp.int32)
+    chosen = jnp.sum(jnp.where(match, logits[:, None, :], 0.0), axis=2)
+    weights = jax.nn.softmax(chosen, axis=-1)
+    dense = jnp.sum(jnp.where(match, weights[:, :, None], 0.0), axis=1)
+    high = dense.astype(jnp.bfloat16)
+    low = (dense - high.astype(jnp.float32)).astype(jnp.bfloat16)
+    named = jnp.any(match, axis=1).astype(jnp.bfloat16)
+    pad = (-3 * experts) % 128
+    fill = jnp.zeros((normed2.shape[0], pad), jnp.bfloat16)
+    return jnp.concatenate([normed2, high, low, named, fill], axis=1)
+
+
+def expert_mix(packed, width, experts, w_gate, w_up, w_down):
+    tokens_all = packed.shape[0]
     local = w_gate.shape[0]
     cap = CAP * lax.axis_size("exp")
     here = lax.axis_index("exp")
-    logits = jnp.dot(rows_all, w_router, preferred_element_type=jnp.float32)
-    weights = jax.nn.softmax(jnp.take_along_axis(logits, ids_all, axis=1), axis=-1)
-    match = (ids_all - here * local)[:, :, None] == jnp.arange(local, dtype=jnp.int32)
-    hits = jnp.any(match, axis=1)
-    mine = jnp.sum(jnp.where(match, weights[:, :, None], 0.0), axis=1)
+    rows_all = packed[:, :width]
+
+    def columns(block):
+        return lax.dynamic_slice_in_dim(packed, width + block * experts + here * local, local, 1)
+
+    high, low, named = columns(0), columns(1), columns(2)
+    hits = named > 0
     order = jnp.arange(tokens_all, dtype=jnp.int32)
     before = (order[None, :] < order[:, None]).astype(jnp.bfloat16)
-    slot = jnp.dot(before, hits.astype(jnp.bfloat16), preferred_element_type=jnp.float32)
-    slot = slot.astype(jnp.int32)
+    slot = jnp.dot(before, named, preferred_element_type=jnp.float32).astype(jnp.int32)
     picks = hits.T[:, None, :] & (
         slot.T[:, None, :] == jnp.arange(cap, dtype=jnp.int32)[None, :, None]
     )
@@ -85,9 +101,9 @@
     hidden = (jax.nn.silu(gate) * upward).astype(jnp.bfloat16)
     result = jnp.einsum("esf,efd->esd", hidden, w_down, preferred_element_type=jnp.float32)
     result = result.astype(jnp.bfloat16)
-    combine = jnp.where(picks, mine.T[:, None, :], 0.0)
-    high = combine.astype(jnp.bfloat16)
-    low = (combine - high.astype(jnp.float32)).astype(jnp.bfloat16)
+    zero = jnp.zeros((), jnp.bfloat16)
+    high = jnp.where(picks, high.T[:, None, :], zero)
+    low = jnp.where(picks, low.T[:, None, :], zero)
     partial = jnp.einsum("est,esd->td", high, result, preferred_element_type=jnp.float32)
     partial = partial + jnp.einsum("est,esd->td", low, result, preferred_element_type=jnp.float32)
     return partial
@@ -113,7 +129,6 @@
     seg = segment_ids[0]
     groups = w_key.shape[1] // HD
     here = lax.axis_index("exp")
-    ids_all = lax.all_gather(expert_ids, "exp", axis=0, tiled=True)
     pos = lax.dynamic_slice_in_dim(positions(seg), here * rows, rows)
     normed = rms_scale(tokens, norm_attn)
     query = jnp.dot(normed, w_query, preferred_element_type=jnp.float32).reshape(
@@ -132,7 +147,11 @@
         lax.all_to_all(query, "exp", split_axis=1, concat_axis=0, tiled=True),
         lax.all_to_all(keyval, "exp", split_axis=1, concat_axis=0, tiled=True),
     )
-    kv_cache = jnp.zeros_like(keyval_heads).at[page_order[0]].set(keyval_heads)
+    plen = keyval_heads.shape[0]
+    placing = page_order[0][None, :] == jnp.arange(plen, dtype=jnp.int32)[:, None]
+    kv_cache = jnp.einsum(
+        "rs,skd->rkd", placing.astype(jnp.bfloat16), keyval_heads, preferred_element_type=jnp.float32
+    ).astype(jnp.bfloat16)
     heads_out = attend(query_heads, keyval_heads, seg)
     attention = lax.psum_scatter(
         jnp.dot(heads_out, w_out, preferred_element_type=jnp.float32),
@@ -142,8 +161,8 @@
     )
     resid = tokens.astype(jnp.float32) + attention
     normed2 = rms_scale(resid, norm_moe)
-    rows_all = lax.all_gather(normed2, "exp", axis=0, tiled=True)
-    partial = expert_mix(rows_all, ids_all, w_router, w_gate, w_up, w_down)
+    packed = lax.all_gather(routing(normed2, expert_ids, w_router), "exp", axis=0, tiled=True)
+    partial = expert_mix(packed, width, w_router.shape[1], w_gate, w_up, w_down)
     moe = lax.psum_scatter(partial, "exp", scatter_dimension=0, tiled=True)
     mixed = (resid + moe).astype(jnp.bfloat16)
     return (mixed, kv_cache)

time: 251 us -> 222 us (0.88)
  local copies, waits for them, and re-layouts: 52.9 us -> 6.52 us
  waiting for transfers between devices: 98.3 us -> 127 us
  blocking collectives: 13.3 us -> 0 us
    gather x5 -> x0, local copies, waits for them, and re-layouts: 35.4 us -> none  [expert_mix(): jnp.take_along_axis(logits, ids_all, axis=1)]
    all_gather x1, waiting for transfers between devices: 12.8 us -> 29.4 us  [shards(): lax.all_gather(routing(normed2, expert_ids, w_router), 'exp', axis=0, til...]
    scatter x1 -> x0, local copies, waits for them, and re-layouts: 14.2 us -> none  [shards(): kv_cache = jnp.zeros_like(keyval_heads).at[page_order[0]].set(keyval_heads)]
    all_gather x1 -> x0, blocking collectives: 13.3 us -> none  [shards(): ids_all = lax.all_gather(expert_ids, 'exp', axis=0, tiled=True)]
    reduce_scatter x1, waiting for transfers between devices: 28.6 us -> 41.9 us  [shards(): moe = lax.psum_scatter(partial, 'exp', scatter_dimension=0, tiled=True)]
  transfers between devices with their start and end apart: 5 -> 5, of which waited for: 5 -> 5; matrix products, arithmetic and copies ran while one was open for 7% -> 2% of each run, Pallas kernels for 0% -> 0%
where the time goes in v2:
time: 222 us
  waiting for transfers between devices  127 us (57%)
  matrix products  52.4 us (24%)
  between operations  14.1 us (6%)
  other arithmetic  11.3 us (5%)
  starting transfers between devices  10.1 us (5%)
  local copies, waits for them, and re-layouts  6.52 us (3%)
    reduce_scatter x1, waiting for transfers between devices, shards(): lax.psum_scatter(jnp.dot(heads_out, w_out, preferred_element_type=jnp.flo...  43.2 us
    reduce_scatter x1, waiting for transfers between devices, shards(): moe = lax.psum_scatter(partial, 'exp', scatter_dimension=0, tiled=True)  41.9 us
    all_gather x1, waiting for transfers between devices, shards(): lax.all_gather(routing(normed2, expert_ids, w_router), 'exp', axis=0, til...  29.4 us
    dot_general x1, matrix products, expert_mix(): jnp.einsum('esf,efd->esd', hidden, w_down, preferred_element_type=jnp.flo...  14.7 us
    dot_general x1, matrix products, expert_mix(): jnp.einsum('esd,edf->esf', received, w_gate, preferred_element_type=jnp.f...  7.64 us
    all_to_all x1, waiting for transfers between devices, shards(): lax.all_to_all(keyval, 'exp', split_axis=1, concat_axis=0, tiled=True)  7.1 us
    all_to_all x1, starting transfers between devices, shards(): lax.all_to_all(keyval, 'exp', split_axis=1, concat_axis=0, tiled=True)  6.35 us
    all_to_all x1, waiting for transfers between devices, shards(): lax.all_to_all(query, 'exp', split_axis=1, concat_axis=0, tiled=True)  5.72 us
  transfers between devices with their start and end apart: 5, of which 5 were waited for; matrix products, arithmetic and copies ran while one was open for 2% of the time, Pallas kernels for 0%

profile of v2, /device:TPU:0, one launch (start us, length us, event | category | flops | bytes accessed | tf_op | source)
XLA Modules:
  0.0 221.7 jit_solution(15428031028679203526)
XLA Ops:
  7.2 0.0 copy-start
  7.2 0.9 compare_reduce_fusion
  8.2 1.1 fusion.34
  9.2 0.1 add_select_fusion
  9.3 0.3 reduce-window.9
  9.6 0.1 slice.39
  9.7 0.1 slice_reduce_fusion
  9.9 0.1 bitcast_subtract_fusion
  9.9 0.7 convert_element_type.75
  10.6 1.7 convolution_convert_fusion.2
  12.3 0.0 copy-start.7
  12.3 0.1 copy.58
  12.4 1.9 fusion.54
  14.4 0.1 dynamic-slice_convert_fusion
  14.4 0.1 multiply_cosine_fusion
  14.6 0.7 pad_maximum_fusion
  15.4 6.3 %all-to-all-start = ((bf16[128,8,128]{0,2,1:T(8,128)(2,1)}), bf16[128,8,128]{0,2,1:T(8,128)(2,1)S(1)}, u32[]{:S(2)}, u32[]{:S(2)}) async-start(bf16[128,8,128]{0,2,1:T(8,128)(2,1)} %pad_maximum_fusion), calls=%async_computation | async-start | bytes 524288 | tf_op jit(solution)/shard_map/all_to_all | solution.py:148
  21.7 1.0 fusion.51
  22.7 0.1 subtract_convert_fusion
  22.8 0.7 pad_maximum_fusion.1
  23.5 7.1 %all-to-all-done = bf16[128,8,128]{0,2,1:T(8,128)(2,1)S(1)} async-done(((bf16[128,8,128]{0,2,1:T(8,128)(2,1)}), bf16[128,8,128]{0,2,1:T(8,128)(2,1)S(1)}, u32[]{:S(2)}, u32[]{:S(2)}) %all-to-all-start) | async-done | bytes 262176 | tf_op jit(solution)/shard_map/all_to_all | solution.py:148
  30.6 3.4 %all-to-all-start.1 = ((bf16[128,8,128]{0,2,1:T(8,128)(2,1)}), bf16[128,8,128]{0,2,1:T(8,128)(2,1)S(1)}, u32[]{:S(2)}, u32[]{:S(2)}) async-start(bf16[128,8,128]{0,2,1:T(8,128)(2,1)} %bitcast.12), calls=%async_computation.1 | async-start | bytes 524288 | tf_op jit(solution)/shard_map/all_to_all | solution.py:147
  34.0 0.0 reduce-scatter.3.cloned.1.call-start
  34.1 0.9 fusion.31
  35.0 0.2 copy.82
  35.2 0.1 all_to_all.27
  35.3 5.7 %all-to-all-done.1 = bf16[128,8,128]{0,2,1:T(8,128)(2,1)S(1)} async-done(((bf16[128,8,128]{0,2,1:T(8,128)(2,1)}), bf16[128,8,128]{0,2,1:T(8,128)(2,1)S(1)}, u32[]{:S(2)}, u32[]{:S(2)}) %all-to-all-start.1) | async-done | bytes 262176 | tf_op jit(solution)/shard_map/all_to_all | solution.py:147
  41.0 0.2 copy.62
  41.2 0.1 squeeze.11
  41.3 4.5 %fusion.56 = (f32[2,2,512]{2,1,0:T(2,128)S(1)}, f32[2,2,512,512]{2,3,1,0:T(8,128)}) fusion(pred[512,512]{0,1:T(8,128)(4,1)} %fusion.31, bf16[512,2,2,64]{0,3,2,1:T(8,128)(2,1)S(1)} %squeeze.11, bf16[512,2,128]{0,2,1:T(8,128)(2,1)S(1)} %all_to_all.27), kind=kOutput, calls=%fused_computation.92 | convolution fusion | flops 138412544 | bytes 4857856 | tf_op jit(solution)/shard_map/while/body/eval_jaxpr/sub | solution.py:54
  45.9 2.7 %fusion.26 = bf16[2,64,2,512]{3,1,2,0:T(8,128)(2,1)S(1)} fusion(f32[2,2,512,512]{2,3,1,0:T(8,128)} %get-tuple-element.45, f32[2,2,512]{2,1,0:T(2,128)S(1)} %get-tuple-element.44, bf16[512,2,128]{0,2,1:T(8,128)(2,1)S(1)} %all_to_all.27), kind=kOutput, calls=%fused_computation.27 | convolution fusion | flops 136445952 | bytes 4595712 | tf_op jit(solution)/shard_map/while/body/eval_jaxpr/kgqt,tkd->qkgd/dot_general | solution.py:56
  48.6 0.0 copy-start.8
  48.6 1.8 fusion.57
  50.5 0.0 reduce-scatter.3.cloned.1.call-update
  50.5 0.0 all-gather.2.cloned.1.call-start
  50.6 0.1 copy.66
  50.7 43.2 %reduce-scatter.3.cloned.1.call-done = f32[128,1024]{1,0:T(8,128)} async-done(((f32[512,1024]{1,0:T(8,128)}), f32[128,1024]{1,0:T(8,128)}) %reduce-scatter.3.cloned.1.call-update) | async-done | bytes 524304 | tf_op jit(solution)/shard_map/reduce_scatter | solution.py:156
  93.9 1.2 multiply_reduce_fusion
  95.1 1.2 multiply_convert_fusion.1
  96.3 0.2 fusion.58
  96.4 0.1 select_reduce_fusion.1
  96.6 0.1 copy.65
  96.7 0.1 copy.64
  96.8 0.8 concatenate.22
  97.7 0.0 all-gather.2.cloned.1.call-update
  97.7 0.2 reduce-scatter.5.cloned.1.call-start
  97.9 29.4 %all-gather.2.cloned.1.call-done = bf16[512,1152]{1,0:T(8,128)(2,1)} async-done(((bf16[128,1152]{1,0:T(8,128)(2,1)}), bf16[512,1152]{1,0:T(8,128)(2,1)}) %all-gather.2.cloned.1.call-update) | async-done | bytes 1179664 | tf_op jit(solution)/shard_map/all_gather | solution.py:164
  127.3 1.0 compare_bitcast_fusion
  128.3 0.1 copy.67
  128.5 1.1 dynamic-slice_bitcast_fusion
  129.6 0.1 copy.70
  129.7 0.1 copy.68
  129.7 1.2 convolution_convert_fusion.3
  131.0 5.2 %fusion.7 = bf16[8,256,1024]{2,1,0:T(8,128)(2,1)S(1)} fusion(s32[8,512]{1,0:T(8,128)S(1)} %convolution_convert_fusion.3, pred[8,512]{1,0:T(8,128)(4,1)S(1)} %copy.67, bf16[512,1152]{1,0:T(8,128)(2,1)} %all-gather.2.cloned.1.call-done), kind=kOutput, calls=%fused_computation.12 | convolution fusion | flops 2151677952 | bytes 5263360 | tf_op jit(solution)/shard_map/est,td->esd/dot_general | solution.py:96
  136.2 2.0 copy-done.2
  138.2 7.6 %fusion.59 = f32[8,256,512]{2,1,0:T(8,128)} fusion(bf16[8,256,1024]{2,1,0:T(8,128)(2,1)S(1)} %fusion.7, bf16[8,1024,512]{2,1,0:T(8,128)(2,1)} %param.22), kind=kOutput, calls=%fused_computation.95 | convolution fusion | flops 2147483648 | bytes 16777216 | tf_op jit(solution)/shard_map/esd,edf->esf/dot_general | solution.py:99
  145.8 14.7 %convolution_convert_fusion = bf16[8,256,1024]{2,1,0:T(8,128)(2,1)} fusion(bf16[8,512,1024]{2,1,0:T(8,128)(2,1)} %param.24, f32[8,256,512]{2,1,0:T(8,128)} %fusion.59, bf16[8,256,1024]{2,1,0:T(8,128)(2,1)} %copy-done.2, bf16[8,1024,512]{2,1,0:T(8,128)(2,1)} %param.23), kind=kOutput, calls=%fused_computation.11 | convolution fusion | flops 4303355904 | bytes 29360128 | tf_op jit(solution)/shard_map/esf,efd->esd/dot_general | solution.py:102
  160.5 5.2 %fusion.10 = f32[512,1024,1]{1,0,2:T(8,128)S(1)} fusion(bf16[8,256,1024]{2,1,0:T(8,128)(2,1)} %convolution_convert_fusion, s32[8,512]{1,0:T(8,128)S(1)} %convolution_convert_fusion.3, pred[8,512]{1,0:T(8,128)(4,1)S(1)} %copy.67, bf16[8,512]{1,0:T(8,128)(2,1)S(1)} %copy.68), kind=kOutput, calls=%fused_computation.13 | convolution fusion | flops 2150629376 | bytes 6320128 | tf_op jit(solution)/shard_map/est,esd->td/dot_general | solution.py:107
  165.8 4.3 %bitcast_add_fusion = f32[512,1024]{1,0:T(8,128)} fusion(f32[512,1024,1]{1,0,2:T(8,128)S(1)} %fusion.10, bf16[8,256,1024]{2,1,0:T(8,128)(2,1)S(1)} %copy-done.10, s32[8,512]{1,0:T(8,128)S(1)} %convolution_convert_fusion.3, pred[8,512]{1,0:T(8,128)(4,1)S(1)} %copy.67, bf16[8,512]{1,0:T(8,128)(2,1)S(1)} %copy.70), kind=kOutput, calls=%fused_computation.15 | convolution fusion | flops 2151153664 | bytes 8417280 | tf_op jit(solution)/shard_map/est,esd->td/dot_general | solution.py:108
  170.0 0.0 reduce-scatter.5.cloned.1.call-update
  170.1 0.3 convolution_convert_fusion.1
  170.4 1.0 copy.72
  171.4 41.9 %reduce-scatter.5.cloned.1.call-done = f32[128,1024]{1,0:T(8,128)} async-done(((f32[512,1024]{1,0:T(8,128)}), f32[128,1024]{1,0:T(8,128)}) %reduce-scatter.5.cloned.1.call-update) | async-done | bytes 524304 | tf_op jit(solution)/shard_map/reduce_scatter | solution.py:166
  213.3 1.8 add_convert_fusion
  (32 shorter events, 0.3 us)
Async XLA Ops:
  7.2 14.6 %copy-start = (bf16[1024,1024]{1,0:T(8,128)(2,1)S(1)}, bf16[1024,1024]{1,0:T(8,128)(2,1)}, u32[]{:S(2)}) copy-start(bf16[1024,1024]{1,0:T(8,128)(2,1)} %param.16) | copy-start | bytes 6291460
  7.2 14.5 %copy-start.1 = (bf16[128,1024]{1,0:T(8,128)(2,1)S(1)}, bf16[128,1024]{1,0:T(8,128)(2,1)}, u32[]{:S(2)}) copy-start(bf16[128,1024]{1,0:T(8,128)(2,1)} %param.14) | copy-start | bytes 786436
  12.3 21.8 %copy-start.7 = (s32[1,512]{1,0:T(1,128)S(1)}, s32[1,512]{1,0:T(1,128)}, u32[]{:S(2)}) copy-start(s32[1,512]{1,0:T(1,128)} %param.25) | copy-start | bytes 6148
  15.4 15.2 %all-to-all-start = ((bf16[128,8,128]{0,2,1:T(8,128)(2,1)}), bf16[128,8,128]{0,2,1:T(8,128)(2,1)S(1)}, u32[]{:S(2)}, u32[]{:S(2)}) async-start(bf16[128,8,128]{0,2,1:T(8,128)(2,1)} %pad_maximum_fusion), calls=%async_computation | async-start | bytes 524288 | tf_op jit(solution)/shard_map/all_to_all | solution.py:148
  30.6 10.4 %all-to-all-start.1 = ((bf16[128,8,128]{0,2,1:T(8,128)(2,1)}), bf16[128,8,128]{0,2,1:T(8,128)(2,1)S(1)}, u32[]{:S(2)}, u32[]{:S(2)}) async-start(bf16[128,8,128]{0,2,1:T(8,128)(2,1)} %bitcast.12), calls=%async_computation.1 | async-start | bytes 524288 | tf_op jit(solution)/shard_map/all_to_all | solution.py:147
  34.0 59.9 %reduce-scatter.3.cloned.1.call-start = ((), (), s32[]{:S(2)}) async-start(), calls=%async_computation.4 | async-start | bytes 2621440 | tf_op jit(solution)/shard_map/reduce_scatter | solution.py:156
  45.9 2.8 %copy-start.4 = (bf16[256,1024]{1,0:T(8,128)(2,1)S(1)}, bf16[256,1024]{1,0:T(8,128)(2,1)}, u32[]{:S(2)}) copy-start(bf16[256,1024]{1,0:T(8,128)(2,1)} %param.19) | copy-start | bytes 1572868
  48.6 1.9 copy-start.8
  48.6 1.9 copy-start.6
  48.6 47.6 %copy-start.5 = (bf16[1024,32]{0,1:T(8,128)(2,1)S(1)}, bf16[1024,32]{0,1:T(8,128)(2,1)}, u32[]{:S(2)}) copy-start(bf16[1024,32]{0,1:T(8,128)(2,1)} %param.21) | copy-start | bytes 196612
  50.5 76.8 %all-gather.2.cloned.1.call-start = ((), (), s32[]{:S(2)}) async-start(), calls=%async_computation.5 | async-start | bytes 1474560 | tf_op jit(solution)/shard_map/all_gather | solution.py:164
  97.7 115.6 %reduce-scatter.5.cloned.1.call-start = ((), (), s32[]{:S(2)}) async-start(), calls=%async_computation.6 | async-start | bytes 2621440 | tf_op jit(solution)/shard_map/reduce_scatter | solution.py:166
  136.2 2.0 copy-start.2
  160.5 5.3 %copy-start.10 = (bf16[8,256,1024]{2,1,0:T(8,128)(2,1)S(1)}, bf16[8,256,1024]{2,1,0:T(8,128)(2,1)}, u32[]{:S(2)}) copy-start(bf16[8,256,1024]{2,1,0:T(8,128)(2,1)} %convolution_convert_fusion) | copy-start | bytes 12582916
  165.7 4.3 %copy-start.9 = (s32[1,512]{1,0:T(1,128)S(1)}, s32[1,512]{1,0:T(1,128)}, u32[]{:S(2)}) copy-start(s32[1,512]{1,0:T(1,128)} %param.26) | copy-start | bytes 6148
  165.8 47.5 %copy-start.3 = (f32[128,1024]{1,0:T(8,128)S(1)}, f32[128,1024]{1,0:T(8,128)}, u32[]{:S(2)}) copy-start(f32[128,1024]{1,0:T(8,128)} %reduce-scatter.3.cloned.1.call-done) | copy-start | bytes 1572868
Sparse Core Ops, SparseCore 0:
  50.6 43.2 reduce-scatter.2
  97.8 29.4 all-gather.1
  170.2 43.0 reduce-scatter.4

commit v3 on v2

--- a/solution.py
+++ b/solution.py
@@ -143,10 +143,10 @@
         .reshape(rows, groups, HD)
     )
     keyval = jnp.concatenate([keys, values], axis=-1)
-    query_heads, keyval_heads = (
-        lax.all_to_all(query, "exp", split_axis=1, concat_axis=0, tiled=True),
-        lax.all_to_all(keyval, "exp", split_axis=1, concat_axis=0, tiled=True),
+    both = lax.all_to_all(
+        jnp.concatenate([query, keyval], axis=-1), "exp", split_axis=1, concat_axis=0, tiled=True
     )
+    query_heads, keyval_heads = both[..., : 2 * HD], both[..., 2 * HD :]
     plen = keyval_heads.shape[0]
     placing = page_order[0][None, :] == jnp.arange(plen, dtype=jnp.int32)[:, None]
     kv_cache = jnp.einsum(
@@ -154,16 +154,17 @@
     ).astype(jnp.bfloat16)
     heads_out = attend(query_heads, keyval_heads, seg)
     attention = lax.psum_scatter(
-        jnp.dot(heads_out, w_out, preferred_element_type=jnp.float32),
+        jnp.dot(heads_out, w_out, preferred_element_type=jnp.float32).astype(jnp.bfloat16),
         "exp",
         scatter_dimension=0,
         tiled=True,
     )
-    resid = tokens.astype(jnp.float32) + attention
+    resid = tokens.astype(jnp.float32) + attention.astype(jnp.float32)
     normed2 = rms_scale(resid, norm_moe)
     packed = lax.all_gather(routing(normed2, expert_ids, w_router), "exp", axis=0, tiled=True)
     partial = expert_mix(packed, width, w_router.shape[1], w_gate, w_up, w_down)
-    moe = lax.psum_scatter(partial, "exp", scatter_dimension=0, tiled=True)
+    moe = lax.psum_scatter(partial.astype(jnp.bfloat16), "exp", scatter_dimension=0, tiled=True)
+    moe = moe.astype(jnp.float32)
     mixed = (resid + moe).astype(jnp.bfloat16)
     return (mixed, kv_cache)
 

time: 222 us -> 184 us (0.83)
  waiting for transfers between devices: 127 us -> 94.6 us
  starting transfers between devices: 10.1 us -> 6.61 us
    reduce_scatter x1, waiting for transfers between devices: 43.2 us -> 26.3 us  [shards(): lax.psum_scatter(jnp.dot(heads_out, w_out, preferred_element_type=jnp.flo...]
    reduce_scatter x1, waiting for transfers between devices: 41.9 us -> 25.3 us  [shards(): lax.psum_scatter(partial.astype(jnp.bfloat16), 'exp', scatter_dimension=0...]
    all_to_all x2 -> x1, starting transfers between devices: 9.75 us -> 6.35 us  [shards(): lax.all_to_all(jnp.concatenate([query, keyval], axis=-1), 'exp', split_ax...]
    all_to_all x2 -> x1, waiting for transfers between devices: 12.8 us -> 14.3 us  [shards(): lax.all_to_all(jnp.concatenate([query, keyval], axis=-1), 'exp', split_ax...]
  transfers between devices with their start and end apart: 5 -> 4, of which waited for: 5 -> 4; matrix products, arithmetic and copies ran while one was open for 2% -> 1% of each run, Pallas kernels for 0% -> 0%
where the time goes in v3:
time: 184 us; the launch traced here: 183 us
  waiting for transfers between devices  94.6 us (51%)
  matrix products  52.4 us (28%)
  between operations  14.1 us (8%)
  other arithmetic  9.76 us (5%)
  starting transfers between devices  6.61 us (4%)
  local copies, waits for them, and re-layouts  6 us (3%)
    all_gather x1, waiting for transfers between devices, shards(): lax.all_gather(routing(normed2, expert_ids, w_router), 'exp', axis=0, til...  28.7 us
    reduce_scatter x1, waiting for transfers between devices, shards(): lax.psum_scatter(jnp.dot(heads_out, w_out, preferred_element_type=jnp.flo...  26.3 us
    reduce_scatter x1, waiting for transfers between devices, shards(): lax.psum_scatter(partial.astype(jnp.bfloat16), 'exp', scatter_dimension=0...  25.3 us
    dot_general x1, matrix products, expert_mix(): jnp.einsum('esf,efd->esd', hidden, w_down, preferred_element_type=jnp.flo...  14.7 us
    all_to_all x1, waiting for transfers between devices, shards(): lax.all_to_all(jnp.concatenate([query, keyval], axis=-1), 'exp', split_ax...  14.3 us
    dot_general x1, matrix products, expert_mix(): jnp.einsum('esd,edf->esf', received, w_gate, preferred_element_type=jnp.f...  7.64 us
    all_to_all x1, starting transfers between devices, shards(): lax.all_to_all(jnp.concatenate([query, keyval], axis=-1), 'exp', split_ax...  6.35 us
    dot_general x1, matrix products, expert_mix(): jnp.einsum('est,esd->td', high, result, preferred_element_type=jnp.float32)  5.24 us
  transfers between devices with their start and end apart: 4, of which 4 were waited for; matrix products, arithmetic and copies ran while one was open for 1% of the time, Pallas kernels for 0%

profile of v3, /device:TPU:0, one launch (start us, length us, event | category | flops | bytes accessed | tf_op | source)
XLA Modules:
  0.0 183.4 jit_solution(10459357557374199096)
XLA Ops:
  7.2 0.0 copy-start
  7.2 0.9 compare_reduce_fusion
  8.1 1.1 fusion.35
  9.2 0.1 add_select_fusion
  9.3 0.3 reduce-window.9
  9.6 0.1 slice.47
  9.7 0.1 slice_reduce_fusion
  9.8 0.1 bitcast_subtract_fusion
  9.9 0.7 convert_element_type.87
  10.6 1.7 convolution_convert_fusion.3
  12.3 0.1 copy.56
  12.4 0.0 copy-start.7
  12.4 1.9 %fusion.54 = f32[128,512]{0,1:T(8,128)S(1)} fusion(bf16[1024,512]{1,0:T(8,128)(2,1)} %param.17, bf16[128,1024]{1,0:T(8,128)(2,1)} %param.14, f32[1024]{0:T(1024)S(1)} %convert_element_type.87, f32[128]{0:T(128)S(1)} %add_rsqrt_fusion.1), kind=kOutput, calls=%fused_computation.93 | convolution fusion | flops 134742016 | bytes 1577472 | tf_op jit(solution)/shard_map/dot_general | solution.py:138
  14.3 0.0 copy-done
  14.4 1.9 %fusion.56 = f32[128,1024]{0,1:T(8,128)S(1)} fusion(bf16[1024,1024]{1,0:T(8,128)(2,1)S(1)} %copy-done, bf16[128,1024]{1,0:T(8,128)(2,1)} %param.14, f32[1024]{0:T(1024)S(1)} %convert_element_type.87, f32[128]{0:T(128)S(1)} %add_rsqrt_fusion.1), kind=kOutput, calls=%fused_computation.94 | convolution fusion | flops 268959744 | bytes 2888192 | tf_op jit(solution)/shard_map/dot_general | solution.py:134
  16.3 0.1 dynamic-slice_convert_fusion
  16.4 0.1 multiply_cosine_fusion
  16.6 0.1 subtract_convert_fusion
  16.7 0.8 pad_maximum_fusion
  17.5 6.3 %all-to-all-start = ((bf16[128,8,256]{0,2,1:T(8,128)(2,1)}), bf16[128,8,256]{0,2,1:T(8,128)(2,1)S(1)}, u32[]{:S(2)}, u32[]{:S(2)}) async-start(bf16[128,8,256]{0,2,1:T(8,128)(2,1)} %pad_maximum_fusion), calls=%async_computation | async-start | bytes 1048576 | tf_op jit(solution)/shard_map/all_to_all | solution.py:146
  23.8 0.0 copy-done.7
  23.8 0.2 fusion.32
  24.1 14.3 %all-to-all-done = bf16[128,8,256]{0,2,1:T(8,128)(2,1)S(1)} async-done(((bf16[128,8,256]{0,2,1:T(8,128)(2,1)}), bf16[128,8,256]{0,2,1:T(8,128)(2,1)S(1)}, u32[]{:S(2)}, u32[]{:S(2)}) %all-to-all-start) | async-done | bytes 524320 | tf_op jit(solution)/shard_map/all_to_all | solution.py:146
  38.3 0.1 copy.79
  38.5 3.6 %fusion.58 = (f32[2,2,512]{2,1,0:T(2,128)S(1)}, f32[2,2,512,512]{2,3,1,0:T(8,128)}) fusion(pred[512,512]{0,1:T(8,128)(4,1)S(1)} %fusion.32, bf16[512,2,2,64]{0,3,2,1:T(8,128)(2,1)S(1)} %bitcast.97, bf16[512,2,256]{0,2,1:T(8,128)(2,1)S(1)} %bitcast.90), kind=kOutput, calls=%fused_computation.95 | convolution fusion | flops 138412544 | bytes 4857856 | tf_op jit(solution)/shard_map/while/body/eval_jaxpr/sub | solution.py:54
  42.0 0.0 copy-start.1
  42.0 2.7 %fusion.27 = bf16[2,64,2,512]{3,1,2,0:T(8,128)(2,1)S(1)} fusion(f32[2,2,512,512]{2,3,1,0:T(8,128)} %get-tuple-element.45, f32[2,2,512]{2,1,0:T(2,128)S(1)} %get-tuple-element.44, bf16[512,2,256]{0,2,1:T(8,128)(2,1)S(1)} %bitcast.91), kind=kOutput, calls=%fused_computation.29 | convolution fusion | flops 136445952 | bytes 4595712 | tf_op jit(solution)/shard_map/while/body/eval_jaxpr/kgqt,tkd->qkgd/dot_general | solution.py:56
  44.8 0.0 copy-start.5
  44.8 1.5 convolution_convert_fusion.1
  46.3 0.0 reduce-scatter.3.cloned.1.call-update
  46.3 0.0 all-gather.2.cloned.1.call-start
  46.4 0.0 copy-done.6
  46.4 0.1 copy.62
  46.5 26.3 %reduce-scatter.3.cloned.1.call-done = bf16[128,1024]{1,0:T(8,128)(2,1)} async-done(((bf16[512,1024]{1,0:T(8,128)(2,1)}), bf16[128,1024]{1,0:T(8,128)(2,1)}) %reduce-scatter.3.cloned.1.call-update) | async-done | bytes 262160 | tf_op jit(solution)/shard_map/reduce_scatter | solution.py:156
  72.8 1.1 multiply_reduce_fusion
  74.0 1.1 multiply_convert_fusion.1
  75.0 0.2 fusion.59
  75.2 0.1 select_reduce_fusion.1
  75.4 0.1 copy.61
  75.5 0.1 copy.60
  75.6 0.8 concatenate.22
  76.5 0.0 all-gather.2.cloned.1.call-update
  76.5 0.2 reduce-scatter.5.cloned.1.call-start
  76.7 28.7 %all-gather.2.cloned.1.call-done = bf16[512,1152]{1,0:T(8,128)(2,1)} async-done(((bf16[128,1152]{1,0:T(8,128)(2,1)}), bf16[512,1152]{1,0:T(8,128)(2,1)}) %all-gather.2.cloned.1.call-update) | async-done | bytes 1179664 | tf_op jit(solution)/shard_map/all_gather | solution.py:164
  105.4 1.0 compare_bitcast_fusion
  106.4 0.1 copy.63
  106.5 1.1 dynamic-slice_bitcast_fusion
  107.7 0.1 copy.66
  107.7 0.1 copy.64
  107.8 1.2 convolution_convert_fusion.4
  109.1 5.2 %fusion.7 = bf16[8,256,1024]{2,1,0:T(8,128)(2,1)S(1)} fusion(s32[8,512]{1,0:T(8,128)S(1)} %convolution_convert_fusion.4, pred[8,512]{1,0:T(8,128)(4,1)S(1)} %copy.63, bf16[512,1152]{1,0:T(8,128)(2,1)} %all-gather.2.cloned.1.call-done), kind=kOutput, calls=%fused_computation.12 | convolution fusion | flops 2151677952 | bytes 5263360 | tf_op jit(solution)/shard_map/est,td->esd/dot_general | solution.py:96
  114.3 2.0 %copy-done.2 = bf16[8,256,1024]{2,1,0:T(8,128)(2,1)} copy-done((bf16[8,256,1024]{2,1,0:T(8,128)(2,1)}, bf16[8,256,1024]{2,1,0:T(8,128)(2,1)S(1)}, u32[]{:S(2)}) %copy-start.2) | copy-done | bytes 4194328
  116.3 7.6 %fusion.60 = f32[8,256,512]{2,1,0:T(8,128)} fusion(bf16[8,256,1024]{2,1,0:T(8,128)(2,1)S(1)} %fusion.7, bf16[8,1024,512]{2,1,0:T(8,128)(2,1)} %param.22), kind=kOutput, calls=%fused_computation.97 | convolution fusion | flops 2147483648 | bytes 16777216 | tf_op jit(solution)/shard_map/esd,edf->esf/dot_general | solution.py:99
  123.9 14.7 %convolution_convert_fusion = bf16[8,256,1024]{2,1,0:T(8,128)(2,1)} fusion(bf16[8,512,1024]{2,1,0:T(8,128)(2,1)} %param.24, f32[8,256,512]{2,1,0:T(8,128)} %fusion.60, bf16[8,256,1024]{2,1,0:T(8,128)(2,1)} %copy-done.2, bf16[8,1024,512]{2,1,0:T(8,128)(2,1)} %param.23), kind=kOutput, calls=%fused_computation.11 | convolution fusion | flops 4303355904 | bytes 29360128 | tf_op jit(solution)/shard_map/esf,efd->esd/dot_general | solution.py:102
  138.6 5.2 %fusion.10 = f32[512,1024,1]{1,0,2:T(8,128)S(1)} fusion(bf16[8,256,1024]{2,1,0:T(8,128)(2,1)} %convolution_convert_fusion, s32[8,512]{1,0:T(8,128)S(1)} %convolution_convert_fusion.4, pred[8,512]{1,0:T(8,128)(4,1)S(1)} %copy.63, bf16[8,512]{1,0:T(8,128)(2,1)S(1)} %copy.64), kind=kOutput, calls=%fused_computation.13 | convolution fusion | flops 2150629376 | bytes 6320128 | tf_op jit(solution)/shard_map/est,esd->td/dot_general | solution.py:107
  143.8 0.0 copy-start.9
  143.8 0.0 copy-start.3
  143.9 4.6 %fusion.14 = bf16[512,1024]{1,0:T(8,128)(2,1)} fusion(f32[512,1024,1]{1,0,2:T(8,128)S(1)} %fusion.10, bf16[8,256,1024]{2,1,0:T(8,128)(2,1)S(1)} %copy-done.10, s32[8,512]{1,0:T(8,128)S(1)} %convolution_convert_fusion.4, pred[8,512]{1,0:T(8,128)(4,1)S(1)} %copy.63, bf16[8,512]{1,0:T(8,128)(2,1)S(1)} %copy.66), kind=kOutput, calls=%fused_computation.16 | convolution fusion | flops 2151677952 | bytes 7368704 | tf_op jit(solution)/shard_map/est,esd->td/dot_general | solution.py:108
  148.4 0.0 reduce-scatter.5.cloned.1.call-update
  148.4 0.0 copy-done.9
  148.5 0.3 convolution_convert_fusion.2
  148.8 1.0 copy.68
  149.8 25.3 %reduce-scatter.5.cloned.1.call-done = bf16[128,1024]{1,0:T(8,128)(2,1)} async-done(((bf16[512,1024]{1,0:T(8,128)(2,1)}), bf16[128,1024]{1,0:T(8,128)(2,1)}) %reduce-scatter.5.cloned.1.call-update) | async-done | bytes 262160 | tf_op jit(solution)/shard_map/reduce_scatter | solution.py:166
  175.1 1.8 add_convert_fusion
  (28 shorter events, 0.3 us)
Async XLA Ops:
  7.2 7.2 %copy-start = (bf16[1024,1024]{1,0:T(8,128)(2,1)S(1)}, bf16[1024,1024]{1,0:T(8,128)(2,1)}, u32[]{:S(2)}) copy-start(bf16[1024,1024]{1,0:T(8,128)(2,1)} %param.16) | copy-start | bytes 6291460
  12.4 11.4 %copy-start.7 = (s32[1,512]{1,0:T(1,128)S(1)}, s32[1,512]{1,0:T(1,128)}, u32[]{:S(2)}) copy-start(s32[1,512]{1,0:T(1,128)} %param.25) | copy-start | bytes 6148
  17.5 20.8 %all-to-all-start = ((bf16[128,8,256]{0,2,1:T(8,128)(2,1)}), bf16[128,8,256]{0,2,1:T(8,128)(2,1)S(1)}, u32[]{:S(2)}, u32[]{:S(2)}) async-start(bf16[128,8,256]{0,2,1:T(8,128)(2,1)} %pad_maximum_fusion), calls=%async_computation | async-start | bytes 1048576 | tf_op jit(solution)/shard_map/all_to_all | solution.py:146
  23.8 49.0 %reduce-scatter.3.cloned.1.call-start = ((), (), s32[]{:S(2)}) async-start(), calls=%async_computation.3 | async-start | bytes 1310720 | tf_op jit(solution)/shard_map/reduce_scatter | solution.py:156
  42.0 2.8 %copy-start.4 = (bf16[256,1024]{1,0:T(8,128)(2,1)S(1)}, bf16[256,1024]{1,0:T(8,128)(2,1)}, u32[]{:S(2)}) copy-start(bf16[256,1024]{1,0:T(8,128)(2,1)} %param.19) | copy-start | bytes 1572868
  42.0 4.3 %copy-start.8 = (bf16[1024]{0:T(1024)(128)(2,1)S(1)}, bf16[1024]{0:T(1024)(128)(2,1)}, u32[]{:S(2)}) copy-start(bf16[1024]{0:T(1024)(128)(2,1)} %param.20) | copy-start | bytes 6148
  42.0 4.3 %copy-start.6 = (s32[128,8]{0,1:T(8,128)S(1)}, s32[128,8]{0,1:T(8,128)}, u32[]{:S(2)}) copy-start(s32[128,8]{0,1:T(8,128)} %param.27) | copy-start | bytes 12292
  42.0 30.8 %copy-start.1 = (bf16[128,1024]{1,0:T(8,128)(2,1)S(1)}, bf16[128,1024]{1,0:T(8,128)(2,1)}, u32[]{:S(2)}) copy-start(bf16[128,1024]{1,0:T(8,128)(2,1)} %param.14) | copy-start | bytes 786436
  44.8 30.2 %copy-start.5 = (bf16[1024,32]{0,1:T(8,128)(2,1)S(1)}, bf16[1024,32]{0,1:T(8,128)(2,1)}, u32[]{:S(2)}) copy-start(bf16[1024,32]{0,1:T(8,128)(2,1)} %param.21) | copy-start | bytes 196612
  46.3 59.1 %all-gather.2.cloned.1.call-start = ((), (), s32[]{:S(2)}) async-start(), calls=%async_computation.4 | async-start | bytes 1474560 | tf_op jit(solution)/shard_map/all_gather | solution.py:164
  76.5 98.6 %reduce-scatter.5.cloned.1.call-start = ((), (), s32[]{:S(2)}) async-start(), calls=%async_computation.5 | async-start | bytes 1310720 | tf_op jit(solution)/shard_map/reduce_scatter | solution.py:166
  114.3 2.0 %copy-start.2 = (bf16[8,256,1024]{2,1,0:T(8,128)(2,1)}, bf16[8,256,1024]{2,1,0:T(8,128)(2,1)S(1)}, u32[]{:S(2)}) copy-start(bf16[8,256,1024]{2,1,0:T(8,128)(2,1)S(1)} %fusion.7) | copy-start | bytes 12582916
  138.6 5.2 %copy-start.10 = (bf16[8,256,1024]{2,1,0:T(8,128)(2,1)S(1)}, bf16[8,256,1024]{2,1,0:T(8,128)(2,1)}, u32[]{:S(2)}) copy-start(bf16[8,256,1024]{2,1,0:T(8,128)(2,1)} %convolution_convert_fusion) | copy-start | bytes 12582916
  143.8 4.6 %copy-start.9 = (s32[1,512]{1,0:T(1,128)S(1)}, s32[1,512]{1,0:T(1,128)}, u32[]{:S(2)}) copy-start(s32[1,512]{1,0:T(1,128)} %param.26) | copy-start | bytes 6148
  143.8 31.3 %copy-start.3 = (bf16[128,1024]{1,0:T(8,128)(2,1)S(1)}, bf16[128,1024]{1,0:T(8,128)(2,1)}, u32[]{:S(2)}) copy-start(bf16[128,1024]{1,0:T(8,128)(2,1)} %reduce-scatter.3.cloned.1.call-done) | copy-start | bytes 786436
Sparse Core Ops, SparseCore 0:
  46.4 26.3 reduce-scatter.2
  76.6 28.7 all-gather.1
  148.6 26.4 reduce-scatter.4

commit v4 on v3

--- a/solution.py
+++ b/solution.py
@@ -78,7 +78,7 @@
 def expert_mix(packed, width, experts, w_gate, w_up, w_down):
     tokens_all = packed.shape[0]
     local = w_gate.shape[0]
-    cap = CAP * lax.axis_size("exp")
+    cap = CAP
     here = lax.axis_index("exp")
     rows_all = packed[:, :width]
 
@@ -107,6 +107,21 @@
     partial = jnp.einsum("est,esd->td", high, result, preferred_element_type=jnp.float32)
     partial = partial + jnp.einsum("est,esd->td", low, result, preferred_element_type=jnp.float32)
     return partial
+
+
+def shifted(x, step):
+    count = lax.axis_size("exp")
+    return lax.ppermute(x, "exp", [(j, (j + step) % count) for j in range(count)])
+
+
+def exchange_sum(blocks):
+    count = blocks.shape[0]
+    here = lax.axis_index("exp")
+    total = lax.dynamic_index_in_dim(blocks, here, 0, keepdims=False).astype(jnp.float32)
+    for step in range(1, count):
+        send = lax.dynamic_index_in_dim(blocks, (here + step) % count, 0, keepdims=False)
+        total = total + shifted(send, step).astype(jnp.float32)
+    return total
 
 
 def shards(
@@ -153,18 +168,17 @@
         "rs,skd->rkd", placing.astype(jnp.bfloat16), keyval_heads, preferred_element_type=jnp.float32
     ).astype(jnp.bfloat16)
     heads_out = attend(query_heads, keyval_heads, seg)
-    attention = lax.psum_scatter(
-        jnp.dot(heads_out, w_out, preferred_element_type=jnp.float32).astype(jnp.bfloat16),
-        "exp",
-        scatter_dimension=0,
-        tiled=True,
-    )
-    resid = tokens.astype(jnp.float32) + attention.astype(jnp.float32)
+    owners = lax.axis_size("exp")
+    attention = jnp.dot(heads_out, w_out, preferred_element_type=jnp.float32).astype(jnp.bfloat16)
+    attention = exchange_sum(attention.reshape(owners, rows, width))
+    resid = tokens.astype(jnp.float32) + attention
     normed2 = rms_scale(resid, norm_moe)
-    packed = lax.all_gather(routing(normed2, expert_ids, w_router), "exp", axis=0, tiled=True)
-    partial = expert_mix(packed, width, w_router.shape[1], w_gate, w_up, w_down)
-    moe = lax.psum_scatter(partial.astype(jnp.bfloat16), "exp", scatter_dimension=0, tiled=True)
-    moe = moe.astype(jnp.float32)
+    packed = routing(normed2, expert_ids, w_router)
+    experts = w_router.shape[1]
+    moe = expert_mix(packed, width, experts, w_gate, w_up, w_down)
+    for step in range(1, owners):
+        partial = expert_mix(shifted(packed, step), width, experts, w_gate, w_up, w_down)
+        moe = moe + shifted(partial.astype(jnp.bfloat16), -step).astype(jnp.float32)
     mixed = (resid + moe).astype(jnp.bfloat16)
     return (mixed, kv_cache)
 

time: 184 us -> 176 us (0.957)
  waiting for transfers between devices: 94.6 us -> 34.9 us
  matrix products: 52.4 us -> 102 us
  between operations: 14.1 us -> 1.07 us
  starting transfers between devices: 6.61 us -> 17.9 us
  local copies, waits for them, and re-layouts: 6 us -> 8.74 us
    reduce_scatter x2 -> x0, waiting for transfers between devices: 51.6 us -> none  [the longest x1 26.3 us: shards(): lax.psum_scatter(jnp.dot(heads_out, w_out, preferred_element_type=jnp.flo...]
    all_gather x1 -> x0, waiting for transfers between devices: 28.7 us -> none  [shards(): lax.all_gather(routing(normed2, expert_ids, w_router), 'exp', axis=0, til...]
    dot_general x1 -> x4, matrix products: 14.7 us -> 40.5 us  [expert_mix(): jnp.einsum('esf,efd->esd', hidden, w_down, preferred_element_type=jnp.flo...]
    ppermute x0 -> x9, waiting for transfers between devices: none -> 20.7 us  [shifted(): lax.ppermute(x, 'exp', [(j, (j + step) % count) for j in range(count)])]
    dot_general x1 -> x4, matrix products: 7.64 us -> 23.8 us  [expert_mix(): jnp.einsum('esd,edf->esf', received, w_gate, preferred_element_type=jnp.f...]
    ppermute x0 -> x9, starting transfers between devices: none -> 11.5 us  [shifted(): lax.ppermute(x, 'exp', [(j, (j + step) % count) for j in range(count)])]
    transpose x1 -> x8, local copies, waits for them, and re-layouts: 0.09 us -> 3.94 us  [expert_mix(): high = jnp.where(picks, high.T[:, None, :], zero)]
    dot_general x1 -> x4, matrix products: 5.24 us -> 8.74 us  [expert_mix(): jnp.einsum('est,esd->td', high, result, preferred_element_type=jnp.float32)]
  transfers between devices with their start and end apart: 4 -> 10, of which waited for: 4 -> 4; matrix products, arithmetic and copies ran while one was open for 1% -> 55% of each run, Pallas kernels for 0% -> 0%
where the time goes in v4:
time: 176 us; the launch traced here: 174 us
  matrix products  102 us (58%)
  waiting for transfers between devices  34.9 us (20%)
  starting transfers between devices  17.9 us (10%)
  other arithmetic  9.7 us (6%)
  local copies, waits for them, and re-layouts  8.74 us (5%)
    dot_general x4, matrix products, expert_mix(): jnp.einsum('esf,efd->esd', hidden, w_down, preferred_element_type=jnp.flo...  40.5 us
    dot_general x4, matrix products, expert_mix(): jnp.einsum('esd,edf->esf', received, w_gate, preferred_element_type=jnp.f...  23.8 us
    ppermute x9, waiting for transfers between devices, shifted(): lax.ppermute(x, 'exp', [(j, (j + step) % count) for j in range(count)])  20.7 us
    all_to_all x1, waiting for transfers between devices, shards(): lax.all_to_all(jnp.concatenate([query, keyval], axis=-1), 'exp', split_ax...  14.3 us
    ppermute x9, starting transfers between devices, shifted(): lax.ppermute(x, 'exp', [(j, (j + step) % count) for j in range(count)])  11.5 us
    dot_general x4, matrix products, expert_mix(): jnp.einsum('est,esd->td', high, result, preferred_element_type=jnp.float32)  8.74 us
    dot_general x4, matrix products, expert_mix(): jnp.einsum('est,esd->td', low, result, preferred_element_type=jnp.float32)  6.36 us
    all_to_all x1, starting transfers between devices, shards(): lax.all_to_all(jnp.concatenate([query, keyval], axis=-1), 'exp', split_ax...  6.35 us
  transfers between devices with their start and end apart: 10, of which 4 were waited for; matrix products, arithmetic and copies ran while one was open for 55% of the time, Pallas kernels for 0%

profile of v4, /device:TPU:0, one launch (start us, length us, event | category | flops | bytes accessed | tf_op | source)
XLA Modules:
  0.0 174.2 jit_solution(7570005080290346367)
XLA Ops:
  0.7 0.8 convert_element_type.156
  1.5 1.1 fusion.33
  2.6 1.7 convolution_convert_fusion.10
  4.4 1.9 %fusion.140 = f32[128,512]{0,1:T(8,128)S(1)} fusion(bf16[1024,512]{1,0:T(8,128)(2,1)} %param.17, bf16[128,1024]{1,0:T(8,128)(2,1)} %param.14, f32[1024]{0:T(1024)S(1)} %convert_element_type.156, f32[128]{0:T(128)S(1)} %add_rsqrt_fusion.1), kind=kOutput, calls=%fused_computation.210 | convolution fusion | flops 134742016 | bytes 1577472 | tf_op jit(solution)/shard_map/dot_general | solution.py:153
  6.3 0.8 compare_reduce_fusion
  7.3 0.3 reduce-window.9
  7.9 1.9 %fusion.142 = f32[128,1024]{0,1:T(8,128)S(1)} fusion(bf16[1024,1024]{1,0:T(8,128)(2,1)S(1)} %copy-done, bf16[128,1024]{1,0:T(8,128)(2,1)} %param.14, f32[1024]{0:T(1024)S(1)} %convert_element_type.156, f32[128]{0:T(128)S(1)} %add_rsqrt_fusion.1), kind=kOutput, calls=%fused_computation.211 | convolution fusion | flops 268959744 | bytes 2888192 | tf_op jit(solution)/shard_map/dot_general | solution.py:149
  9.9 0.1 multiply_cosine_fusion
  10.2 0.8 pad_maximum_fusion
  11.0 6.3 %all-to-all-start = ((bf16[128,8,256]{0,2,1:T(8,128)(2,1)}), bf16[128,8,256]{0,2,1:T(8,128)(2,1)S(1)}, u32[]{:S(2)}, u32[]{:S(2)}) async-start(bf16[128,8,256]{0,2,1:T(8,128)(2,1)} %pad_maximum_fusion), calls=%async_computation | async-start | bytes 1048576 | tf_op jit(solution)/shard_map/all_to_all | solution.py:161
  17.4 0.2 fusion.30
  17.6 14.3 %all-to-all-done = bf16[128,8,256]{0,2,1:T(8,128)(2,1)S(1)} async-done(((bf16[128,8,256]{0,2,1:T(8,128)(2,1)}), bf16[128,8,256]{0,2,1:T(8,128)(2,1)S(1)}, u32[]{:S(2)}, u32[]{:S(2)}) %all-to-all-start) | async-done | bytes 524320 | tf_op jit(solution)/shard_map/all_to_all | solution.py:161
  32.0 3.6 %fusion.144 = (f32[2,2,512]{2,1,0:T(2,128)S(1)}, f32[2,2,512,512]{2,3,1,0:T(8,128)}) fusion(pred[512,512]{0,1:T(8,128)(4,1)S(1)} %fusion.30, bf16[512,2,2,64]{0,3,2,1:T(8,128)(2,1)S(1)} %bitcast.184, bf16[512,2,256]{0,2,1:T(8,128)(2,1)S(1)} %bitcast.177), kind=kOutput, calls=%fused_computation.212 | convolution fusion | flops 138412544 | bytes 4857856 | tf_op jit(solution)/shard_map/while/body/eval_jaxpr/sub | solution.py:54
  35.6 2.7 %fusion.17 = bf16[2,64,2,512]{3,1,2,0:T(8,128)(2,1)S(1)} fusion(f32[2,2,512,512]{2,3,1,0:T(8,128)} %get-tuple-element.56, f32[2,2,512]{2,1,0:T(2,128)S(1)} %get-tuple-element.55, bf16[512,2,256]{0,2,1:T(8,128)(2,1)S(1)} %bitcast.178), kind=kOutput, calls=%fused_computation.42 | convolution fusion | flops 136445952 | bytes 4595712 | tf_op jit(solution)/shard_map/while/body/eval_jaxpr/kgqt,tkd->qkgd/dot_general | solution.py:56
  38.4 0.5 convolution_convert_fusion.8
  38.8 0.9 dynamic-slice_bitcast_fusion.2
  39.7 1.5 collective-permute-start.2
  41.2 0.6 collective-permute-start
  41.8 0.1 copy.86
  41.9 1.3 convolution_convert_fusion.9
  43.3 1.0 copy.100
  44.2 4.8 %collective-permute-done.2 = bf16[128,1024]{1,0:T(8,128)(2,1)} collective-permute-done((bf16[128,1024]{1,0:T(8,128)(2,1)}, bf16[128,1024]{1,0:T(8,128)(2,1)}, u32[]{:S(2)}, u32[]{:S(2)}) %collective-permute-start.2) | collective-permute-done | bytes 262176 | tf_op jit(solution)/shard_map/ppermute | solution.py:114
  49.1 13.1 %collective-permute-done.1 = bf16[128,1024]{1,0:T(8,128)(2,1)} collective-permute-done((bf16[128,1024]{1,0:T(8,128)(2,1)}, bf16[128,1024]{1,0:T(8,128)(2,1)}, u32[]{:S(2)}, u32[]{:S(2)}) %collective-permute-start.1) | collective-permute-done | bytes 262176 | tf_op jit(solution)/shard_map/ppermute | solution.py:114
  62.1 1.4 multiply_reduce_fusion
  63.5 0.8 copy-done.2
  64.4 0.2 fusion.145
  65.0 0.8 concatenate.22
  65.8 3.6 %collective-permute-start.5 = (bf16[128,1152]{1,0:T(8,128)(2,1)}, bf16[128,1152]{1,0:T(8,128)(2,1)}, u32[]{:S(2)}, u32[]{:S(2)}) collective-permute-start(bf16[128,1152]{1,0:T(8,128)(2,1)} %concatenate.22), channel_id=1, source_target_pairs={{0,2},{1,3},{2,0},{3,1},{4,6},{5,7},{6,4},{7,5},{8,10},{9,11},{10,... | collective-permute-start | bytes 884744 | tf_op jit(solution)/shard_map/ppermute | solution.py:114
  69.4 2.0 %collective-permute-start.3 = (bf16[128,1152]{1,0:T(8,128)(2,1)}, bf16[128,1152]{1,0:T(8,128)(2,1)}, u32[]{:S(2)}, u32[]{:S(2)}) collective-permute-start(bf16[128,1152]{1,0:T(8,128)(2,1)} %concatenate.22), channel_id=1, source_target_pairs={{0,1},{1,2},{2,3},{3,0},{4,5},{5,6},{6,7},{7,4},{8,9},{9,10},{10,1... | collective-permute-start | bytes 884744 | tf_op jit(solution)/shard_map/ppermute | solution.py:114
  71.5 1.0 convolution_convert_fusion.14
  72.5 0.9 compare_bitcast_fusion.3
  73.4 0.4 convolution_convert_fusion.7
  73.9 6.0 %fusion.146 = f32[8,64,512]{2,1,0:T(8,128)} fusion(bf16[8,64,1024]{2,1,0:T(8,128)(2,1)S(1)} %convolution_convert_fusion.7, bf16[8,1024,512]{2,1,0:T(8,128)(2,1)} %param.22), kind=kOutput, calls=%fused_computation.214 | convolution fusion | flops 536870912 | bytes 10485760 | tf_op jit(solution)/shard_map/esd,edf->esf/dot_general | solution.py:99
  79.9 10.1 %convolution_convert_fusion.6 = bf16[8,64,1024]{2,1,0:T(8,128)(2,1)} fusion(bf16[8,512,1024]{2,1,0:T(8,128)(2,1)} %param.24, bf16[8,64,1024]{2,1,0:T(8,128)(2,1)S(1)} %convolution_convert_fusion.7, bf16[8,1024,512]{2,1,0:T(8,128)(2,1)} %param.23, f32[8,64,512]{2,1,0:T(8,128)} %fusion.146), kind=kOutput, calls=%fused_computation.15 | convolution fusion | flops 1075838976 | bytes 19922944 | tf_op jit(solution)/shard_map/esf,efd->esd/dot_general | solution.py:102
  90.0 0.8 compare_bitcast_fusion
  90.9 1.0 convolution_convert_fusion.11
  91.9 1.4 convolution_convert_fusion.1
  93.3 5.9 %fusion.149 = f32[8,64,512]{2,1,0:T(8,128)} fusion(bf16[8,64,1024]{2,1,0:T(8,128)(2,1)S(1)} %convolution_convert_fusion.1, bf16[8,1024,512]{2,1,0:T(8,128)(2,1)} %param.22), kind=kOutput, calls=%fused_computation.217 | convolution fusion | flops 536870912 | bytes 10485760 | tf_op jit(solution)/shard_map/esd,edf->esf/dot_general | solution.py:99
  99.2 10.1 %convolution_convert_fusion = bf16[8,64,1024]{2,1,0:T(8,128)(2,1)} fusion(bf16[8,512,1024]{2,1,0:T(8,128)(2,1)} %param.24, bf16[8,64,1024]{2,1,0:T(8,128)(2,1)S(1)} %convolution_convert_fusion.1, bf16[8,1024,512]{2,1,0:T(8,128)(2,1)} %param.23, f32[8,64,512]{2,1,0:T(8,128)} %fusion.149), kind=kOutput, calls=%fused_computation.9 | convolution fusion | flops 1075838976 | bytes 19922944 | tf_op jit(solution)/shard_map/esf,efd->esd/dot_general | solution.py:102
  109.4 0.9 dynamic-slice_bitcast_fusion.4
  110.3 1.6 convolution_bitcast_fusion
  112.0 2.3 %fusion.14 = bf16[128,1024]{1,0:T(8,128)(2,1)} fusion(f32[128,1024]{1,0:T(8,128)S(1)} %convolution_bitcast_fusion, bf16[8,64,1024]{2,1,0:T(8,128)(2,1)} %convolution_convert_fusion, s32[8,128]{1,0:T(8,128)S(1)} %convolution_convert_fusion.11, pred[8,128]{1,0:T(8,128)(4,1)S(1)} %copy.96, bf16[8,128]{1,0:T(8,128)(2,1)S(1)} %copy.97), kind=kOutput, calls=%fused_computation.38 | convolution fusion | flops 134676480 | bytes 1842176 | tf_op jit(solution)/shard_map/est,esd->td/dot_general | solution.py:107
  114.3 0.8 compare_bitcast_fusion.1
  115.2 1.0 convolution_convert_fusion.12
  116.3 1.4 convolution_convert_fusion.3
  117.7 5.9 %fusion.148 = f32[8,64,512]{2,1,0:T(8,128)} fusion(bf16[8,64,1024]{2,1,0:T(8,128)(2,1)S(1)} %convolution_convert_fusion.3, bf16[8,1024,512]{2,1,0:T(8,128)(2,1)} %param.22), kind=kOutput, calls=%fused_computation.216 | convolution fusion | flops 536870912 | bytes 10485760 | tf_op jit(solution)/shard_map/esd,edf->esf/dot_general | solution.py:99
  123.6 10.1 %convolution_convert_fusion.2 = bf16[8,64,1024]{2,1,0:T(8,128)(2,1)} fusion(bf16[8,512,1024]{2,1,0:T(8,128)(2,1)} %param.24, bf16[8,64,1024]{2,1,0:T(8,128)(2,1)S(1)} %convolution_convert_fusion.3, bf16[8,1024,512]{2,1,0:T(8,128)(2,1)} %param.23, f32[8,64,512]{2,1,0:T(8,128)} %fusion.148), kind=kOutput, calls=%fused_computation.11 | convolution fusion | flops 1075838976 | bytes 19922944 | tf_op jit(solution)/shard_map/esf,efd->esd/dot_general | solution.py:102
  133.7 0.9 dynamic-slice_bitcast_fusion.6
  134.7 1.6 convolution_bitcast_fusion.2
  136.4 2.3 %fusion.15 = bf16[128,1024]{1,0:T(8,128)(2,1)} fusion(f32[128,1024]{1,0:T(8,128)S(1)} %convolution_bitcast_fusion.2, bf16[8,64,1024]{2,1,0:T(8,128)(2,1)} %convolution_convert_fusion.2, s32[8,128]{1,0:T(8,128)S(1)} %convolution_convert_fusion.12, pred[8,128]{1,0:T(8,128)(4,1)S(1)} %copy.93, bf16[8,128]{1,0:T(8,128)(2,1)S(1)} %copy.94), kind=kOutput, calls=%fused_computation.39 | convolution fusion | flops 134676480 | bytes 1842176 | tf_op jit(solution)/shard_map/est,esd->td/dot_general | solution.py:107
  138.7 2.3 %collective-permute-start.6 = (bf16[128,1024]{1,0:T(8,128)(2,1)}, bf16[128,1024]{1,0:T(8,128)(2,1)}, u32[]{:S(2)}, u32[]{:S(2)}) collective-permute-start(bf16[128,1024]{1,0:T(8,128)(2,1)} %fusion.15), channel_id=1, source_target_pairs={{0,2},{1,3},{2,0},{3,1},{4,6},{5,7},{6,4},{7,5},{8,10},{9,11},{10,... | collective-permute-start | bytes 786440 | tf_op jit(solution)/shard_map/ppermute | solution.py:114
  141.0 0.8 compare_bitcast_fusion.2
  141.9 1.0 convolution_convert_fusion.13
  142.9 1.4 convolution_convert_fusion.5
  144.3 5.9 %fusion.147 = f32[8,64,512]{2,1,0:T(8,128)} fusion(bf16[8,64,1024]{2,1,0:T(8,128)(2,1)S(1)} %convolution_convert_fusion.5, bf16[8,1024,512]{2,1,0:T(8,128)(2,1)} %param.22), kind=kOutput, calls=%fused_computation.215 | convolution fusion | flops 536870912 | bytes 10485760 | tf_op jit(solution)/shard_map/esd,edf->esf/dot_general | solution.py:99
  150.3 10.1 %convolution_convert_fusion.4 = bf16[8,64,1024]{2,1,0:T(8,128)(2,1)} fusion(bf16[8,512,1024]{2,1,0:T(8,128)(2,1)} %param.24, bf16[8,64,1024]{2,1,0:T(8,128)(2,1)S(1)} %convolution_convert_fusion.5, bf16[8,1024,512]{2,1,0:T(8,128)(2,1)} %param.23, f32[8,64,512]{2,1,0:T(8,128)} %fusion.147), kind=kOutput, calls=%fused_computation.13 | convolution fusion | flops 1075838976 | bytes 19922944 | tf_op jit(solution)/shard_map/esf,efd->esd/dot_general | solution.py:102
  160.4 0.9 dynamic-slice_bitcast_fusion.8
  161.5 1.6 convolution_bitcast_fusion.4
  163.1 1.6 fusion.16
  164.7 1.5 collective-permute-start.4
  166.2 0.9 dynamic-slice_bitcast_fusion.10
  167.3 1.6 convolution_bitcast_fusion.6
  168.9 2.8 %collective-permute-done.4 = bf16[128,1024]{1,0:T(8,128)(2,1)S(1)} collective-permute-done((bf16[128,1024]{1,0:T(8,128)(2,1)S(1)}, bf16[128,1024]{1,0:T(8,128)(2,1)S(1)}, u32[]{:S(2)}, u32[]{:S(2)}) %collective-permute-start.4) | collective-permute-done | bytes 262176 | tf_op jit(solution)/shard_map/ppermute | solution.py:114
  171.6 2.5 %add_convert_fusion = bf16[128,1024]{1,0:T(8,128)(2,1)} fusion(f32[128,1024]{1,0:T(8,128)} %copy-done.2, bf16[128,1024]{1,0:T(8,128)(2,1)S(1)} %collective-permute-done.8, bf16[128,1024]{1,0:T(8,128)(2,1)} %collective-permute-done.6, bf16[128,1024]{1,0:T(8,128)(2,1)S(1)} %collective-permute-done.4, f32[128,1024]{1,0:T(8,128)S(1)} %convolution_bitcast_fusion.6, ...), kind=kOutput, calls=%fused_computation.76 | convolution fusion | flops 135593984 | bytes 3152896 | tf_op jit(solution)/shard_map/est,esd->td/dot_general | solution.py:107
  (68 shorter events, 2.2 us)
Async XLA Ops:
  0.6 7.2 %copy-start = (bf16[1024,1024]{1,0:T(8,128)(2,1)S(1)}, bf16[1024,1024]{1,0:T(8,128)(2,1)}, u32[]{:S(2)}) copy-start(bf16[1024,1024]{1,0:T(8,128)(2,1)} %param.16) | copy-start | bytes 6291460
  0.6 16.7 %copy-start.7 = (s32[1,512]{1,0:T(1,128)S(1)}, s32[1,512]{1,0:T(1,128)}, u32[]{:S(2)}) copy-start(s32[1,512]{1,0:T(1,128)} %param.25) | copy-start | bytes 6148
  11.0 20.8 %all-to-all-start = ((bf16[128,8,256]{0,2,1:T(8,128)(2,1)}), bf16[128,8,256]{0,2,1:T(8,128)(2,1)S(1)}, u32[]{:S(2)}, u32[]{:S(2)}) async-start(bf16[128,8,256]{0,2,1:T(8,128)(2,1)} %pad_maximum_fusion), calls=%async_computation | async-start | bytes 1048576 | tf_op jit(solution)/shard_map/all_to_all | solution.py:161
  31.9 6.4 %copy-start.3 = (bf16[4,2,32,8,128]{4,3,0,2,1:T(8,128)(2,1)}, bf16[4,2,32,8,128]{4,3,0,2,1:T(8,128)(2,1)S(1)}, u32[]{:S(2)}) copy-start(bf16[4,2,32,8,128]{4,3,0,2,1:T(8,128)(2,1)S(1)} %copy.110) | copy-start | bytes 1572868
  35.5 2.8 %copy-start.4 = (bf16[256,1024]{1,0:T(8,128)(2,1)S(1)}, bf16[256,1024]{1,0:T(8,128)(2,1)}, u32[]{:S(2)}) copy-start(bf16[256,1024]{1,0:T(8,128)(2,1)} %param.19) | copy-start | bytes 1572868
  35.5 6.2 %copy-start.6 = (s32[128,8]{0,1:T(8,128)S(1)}, s32[128,8]{0,1:T(8,128)}, u32[]{:S(2)}) copy-start(s32[128,8]{0,1:T(8,128)} %param.27) | copy-start | bytes 12292
  35.5 6.2 %copy-start.8 = (bf16[1024]{0:T(1024)(128)(2,1)S(1)}, bf16[1024]{0:T(1024)(128)(2,1)}, u32[]{:S(2)}) copy-start(bf16[1024]{0:T(1024)(128)(2,1)} %param.20) | copy-start | bytes 6148
  35.5 6.4 %copy-start.9 = (s32[1,512]{1,0:T(1,128)S(1)}, s32[1,512]{1,0:T(1,128)}, u32[]{:S(2)}) copy-start(s32[1,512]{1,0:T(1,128)} %param.26) | copy-start | bytes 6148
  35.6 26.6 %copy-start.1 = (bf16[128,1024]{1,0:T(8,128)(2,1)S(1)}, bf16[128,1024]{1,0:T(8,128)(2,1)}, u32[]{:S(2)}) copy-start(bf16[128,1024]{1,0:T(8,128)(2,1)} %param.14) | copy-start | bytes 786436
  35.6 28.9 %copy-start.5 = (bf16[1024,32]{0,1:T(8,128)(2,1)S(1)}, bf16[1024,32]{0,1:T(8,128)(2,1)}, u32[]{:S(2)}) copy-start(bf16[1024,32]{0,1:T(8,128)(2,1)} %param.21) | copy-start | bytes 196612
  39.7 9.3 %collective-permute-start.2 = (bf16[128,1024]{1,0:T(8,128)(2,1)}, bf16[128,1024]{1,0:T(8,128)(2,1)}, u32[]{:S(2)}, u32[]{:S(2)}) collective-permute-start(bf16[128,1024]{1,0:T(8,128)(2,1)} %get-tuple-element.39), channel_id=1, source_target_pairs={{0,3},{1,0},{2,1},{3,2},{4,7},{5,4},{6,5},{7,6},{8,11},{9,8},{10,9... | collective-permute-start | bytes 786440 | tf_op jit(solution)/shard_map/ppermute | solution.py:114
  41.2 20.9 %collective-permute-start.1 = (bf16[128,1024]{1,0:T(8,128)(2,1)}, bf16[128,1024]{1,0:T(8,128)(2,1)}, u32[]{:S(2)}, u32[]{:S(2)}) collective-permute-start(bf16[128,1024]{1,0:T(8,128)(2,1)} %get-tuple-element.40), channel_id=1, source_target_pairs={{0,2},{1,3},{2,0},{3,1},{4,6},{5,7},{6,4},{7,5},{8,10},{9,11},{10,... | collective-permute-start | bytes 786440 | tf_op jit(solution)/shard_map/ppermute | solution.py:114
  41.2 20.9 %collective-permute-start = (bf16[128,1024]{1,0:T(8,128)(2,1)}, bf16[128,1024]{1,0:T(8,128)(2,1)}, u32[]{:S(2)}, u32[]{:S(2)}) collective-permute-start(bf16[128,1024]{1,0:T(8,128)(2,1)} %get-tuple-element.38), channel_id=1, source_target_pairs={{0,1},{1,2},{2,3},{3,0},{4,5},{5,6},{6,7},{7,4},{8,9},{9,10},{10,1... | collective-permute-start | bytes 786440 | tf_op jit(solution)/shard_map/ppermute | solution.py:114
  63.5 0.8 copy-start.2
  65.8 24.1 %collective-permute-start.7 = (bf16[128,1152]{1,0:T(8,128)(2,1)}, bf16[128,1152]{1,0:T(8,128)(2,1)}, u32[]{:S(2)}, u32[]{:S(2)}) collective-permute-start(bf16[128,1152]{1,0:T(8,128)(2,1)} %concatenate.22), channel_id=1, source_target_pairs={{0,3},{1,0},{2,1},{3,2},{4,7},{5,4},{6,5},{7,6},{8,11},{9,8},{10,9... | collective-permute-start | bytes 884744 | tf_op jit(solution)/shard_map/ppermute | solution.py:114
  65.8 48.5 %collective-permute-start.5 = (bf16[128,1152]{1,0:T(8,128)(2,1)}, bf16[128,1152]{1,0:T(8,128)(2,1)}, u32[]{:S(2)}, u32[]{:S(2)}) collective-permute-start(bf16[128,1152]{1,0:T(8,128)(2,1)} %concatenate.22), channel_id=1, source_target_pairs={{0,2},{1,3},{2,0},{3,1},{4,6},{5,7},{6,4},{7,5},{8,10},{9,11},{10,... | collective-permute-start | bytes 884744 | tf_op jit(solution)/shard_map/ppermute | solution.py:114
  69.4 71.6 %collective-permute-start.3 = (bf16[128,1152]{1,0:T(8,128)(2,1)}, bf16[128,1152]{1,0:T(8,128)(2,1)}, u32[]{:S(2)}, u32[]{:S(2)}) collective-permute-start(bf16[128,1152]{1,0:T(8,128)(2,1)} %concatenate.22), channel_id=1, source_target_pairs={{0,1},{1,2},{2,3},{3,0},{4,5},{5,6},{6,7},{7,4},{8,9},{9,10},{10,1... | collective-permute-start | bytes 884744 | tf_op jit(solution)/shard_map/ppermute | solution.py:114
  114.3 54.6 %collective-permute-start.8 = (bf16[128,1024]{1,0:T(8,128)(2,1)}, bf16[128,1024]{1,0:T(8,128)(2,1)S(1)}, u32[]{:S(2)}, u32[]{:S(2)}) collective-permute-start(bf16[128,1024]{1,0:T(8,128)(2,1)} %fusion.14), channel_id=1, source_target_pairs={{0,1},{1,2},{2,3},{3,0},{4,5},{5,6},{6,7},{7,4},{8,9},{9,10},{10,1... | collective-permute-start | bytes 786440 | tf_op jit(solution)/shard_map/ppermute | solution.py:114
  138.7 30.2 %collective-permute-start.6 = (bf16[128,1024]{1,0:T(8,128)(2,1)}, bf16[128,1024]{1,0:T(8,128)(2,1)}, u32[]{:S(2)}, u32[]{:S(2)}) collective-permute-start(bf16[128,1024]{1,0:T(8,128)(2,1)} %fusion.15), channel_id=1, source_target_pairs={{0,2},{1,3},{2,0},{3,1},{4,6},{5,7},{6,4},{7,5},{8,10},{9,11},{10,... | collective-permute-start | bytes 786440 | tf_op jit(solution)/shard_map/ppermute | solution.py:114
  164.7 7.0 %collective-permute-start.4 = (bf16[128,1024]{1,0:T(8,128)(2,1)S(1)}, bf16[128,1024]{1,0:T(8,128)(2,1)S(1)}, u32[]{:S(2)}, u32[]{:S(2)}) collective-permute-start(bf16[128,1024]{1,0:T(8,128)(2,1)S(1)} %fusion.16), channel_id=1, source_target_pairs={{0,3},{1,0},{2,1},{3,2},{4,7},{5,4},{6,5},{7,6},{8,11},{9,8},{10,9... | collective-permute-start | bytes 786440 | tf_op jit(solution)/shard_map/ppermute | solution.py:114

commit v5 on v4

--- a/solution.py
+++ b/solution.py
@@ -31,33 +31,20 @@
     return jnp.concatenate([front * cosine - back * sine, back * cosine + front * sine], axis=-1)
 
 
-def attend(query, keyval, seg):
+def attend(query, keyval, seg, where_at):
     plen, groups, width = query.shape
     half = width // 2
-    block = min(512, plen)
-    blocks = plen // block
-    queries = query.reshape(blocks, block, groups, 2, half)
+    queries = query.reshape(plen, groups, 2, half)
     keys = keyval[..., :half]
     values = keyval[..., half:]
-    key_pos = jnp.arange(plen, dtype=jnp.int32)
-    query_pos = key_pos.reshape(blocks, block)
-    query_seg = seg.reshape(blocks, block)
-
-    def one_block(args):
-        qblock, qpos, qseg = args
-        score = (
-            jnp.einsum("qkgd,tkd->kgqt", qblock, keys, preferred_element_type=jnp.float32) * 0.125
-        )
-        allowed = (qseg[:, None] == seg[None, :]) & (key_pos[None, :] <= qpos[:, None])
-        score = jnp.where(allowed[None, None], score, -1e30)
-        top = jnp.max(score, axis=-1, keepdims=True)
-        expo = jnp.exp(score - top)
-        probs = (expo / jnp.sum(expo, axis=-1, keepdims=True)).astype(jnp.bfloat16)
-        out = jnp.einsum("kgqt,tkd->qkgd", probs, values, preferred_element_type=jnp.float32)
-        return out.astype(jnp.bfloat16)
-
-    outs = lax.map(one_block, (queries, query_pos, query_seg))
-    return outs.reshape(plen, groups * width)
+    score = jnp.einsum("qkgd,tkd->kgqt", queries, keys, preferred_element_type=jnp.float32) * 0.125
+    allowed = (seg[:, None] == seg[None, :]) & (where_at[None, :] <= where_at[:, None])
+    score = jnp.where(allowed[None, None], score, -1e30)
+    top = jnp.max(score, axis=-1, keepdims=True)
+    expo = jnp.exp(score - top)
+    probs = (expo / jnp.sum(expo, axis=-1, keepdims=True)).astype(jnp.bfloat16)
+    out = jnp.einsum("kgqt,tkd->qkgd", probs, values, preferred_element_type=jnp.float32)
+    return out.astype(jnp.bfloat16).reshape(plen, groups * width)
 
 
 def routing(normed2, ids, w_router):
@@ -75,10 +62,11 @@
     return jnp.concatenate([normed2, high, low, named, fill], axis=1)
 
 
-def expert_mix(packed, width, experts, w_gate, w_up, w_down):
+def expert_mix(packed, sources, width, experts, w_gate, w_up, w_down):
     tokens_all = packed.shape[0]
     local = w_gate.shape[0]
-    cap = CAP
+    rows = tokens_all // sources
+    cap = CAP * sources
     here = lax.axis_index("exp")
     rows_all = packed[:, :width]
 
@@ -88,8 +76,10 @@
     high, low, named = columns(0), columns(1), columns(2)
     hits = named > 0
     order = jnp.arange(tokens_all, dtype=jnp.int32)
-    before = (order[None, :] < order[:, None]).astype(jnp.bfloat16)
-    slot = jnp.dot(before, named, preferred_element_type=jnp.float32).astype(jnp.int32)
+    block = order // rows
+    before = (order[None, :] < order[:, None]) & (block[None, :] == block[:, None])
+    slot = jnp.dot(before.astype(jnp.bfloat16), named, preferred_element_type=jnp.float32)
+    slot = slot.astype(jnp.int32) + (block * CAP)[:, None]
     picks = hits.T[:, None, :] & (
         slot.T[:, None, :] == jnp.arange(cap, dtype=jnp.int32)[None, :, None]
     )
@@ -115,13 +105,19 @@
 
 
 def exchange_sum(blocks):
-    count = blocks.shape[0]
+    total = blocks[0].astype(jnp.float32)
+    for step in range(1, blocks.shape[0]):
+        total = total + shifted(blocks[step], -step).astype(jnp.float32)
+    return total
+
+
+def step_rows(x, rows):
+    count = lax.axis_size("exp")
     here = lax.axis_index("exp")
-    total = lax.dynamic_index_in_dim(blocks, here, 0, keepdims=False).astype(jnp.float32)
-    for step in range(1, count):
-        send = lax.dynamic_index_in_dim(blocks, (here + step) % count, 0, keepdims=False)
-        total = total + shifted(send, step).astype(jnp.float32)
-    return total
+    parts = [
+        lax.dynamic_slice_in_dim(x, (here - step) % count * rows, rows) for step in range(count)
+    ]
+    return jnp.concatenate(parts)
 
 
 def shards(
@@ -158,27 +154,34 @@
         .reshape(rows, groups, HD)
     )
     keyval = jnp.concatenate([keys, values], axis=-1)
-    both = lax.all_to_all(
-        jnp.concatenate([query, keyval], axis=-1), "exp", split_axis=1, concat_axis=0, tiled=True
-    )
+    owners = lax.axis_size("exp")
+    share = groups // owners
+    both = jnp.concatenate([query, keyval], axis=-1)
+    parts = [lax.dynamic_slice_in_dim(both, here * share, share, 1)]
+    for step in range(1, owners):
+        send = lax.dynamic_slice_in_dim(both, (here + step) % owners * share, share, 1)
+        parts.append(shifted(send, step))
+    both = jnp.concatenate(parts)
     query_heads, keyval_heads = both[..., : 2 * HD], both[..., 2 * HD :]
     plen = keyval_heads.shape[0]
-    placing = page_order[0][None, :] == jnp.arange(plen, dtype=jnp.int32)[:, None]
+    where_at = step_rows(jnp.arange(plen, dtype=jnp.int32), rows)
+    placing = step_rows(page_order[0], rows)[None, :] == jnp.arange(plen, dtype=jnp.int32)[:, None]
     kv_cache = jnp.einsum(
         "rs,skd->rkd", placing.astype(jnp.bfloat16), keyval_heads, preferred_element_type=jnp.float32
     ).astype(jnp.bfloat16)
-    heads_out = attend(query_heads, keyval_heads, seg)
-    owners = lax.axis_size("exp")
+    heads_out = attend(query_heads, keyval_heads, step_rows(seg, rows), where_at)
     attention = jnp.dot(heads_out, w_out, preferred_element_type=jnp.float32).astype(jnp.bfloat16)
     attention = exchange_sum(attention.reshape(owners, rows, width))
     resid = tokens.astype(jnp.float32) + attention
     normed2 = rms_scale(resid, norm_moe)
     packed = routing(normed2, expert_ids, w_router)
     experts = w_router.shape[1]
-    moe = expert_mix(packed, width, experts, w_gate, w_up, w_down)
+    moe = expert_mix(packed, 1, width, experts, w_gate, w_up, w_down)
+    received = jnp.concatenate([shifted(packed, step) for step in range(1, owners)])
+    others = expert_mix(received, owners - 1, width, experts, w_gate, w_up, w_down)
+    others = others.astype(jnp.bfloat16).reshape(owners - 1, rows, width)
     for step in range(1, owners):
-        partial = expert_mix(shifted(packed, step), width, experts, w_gate, w_up, w_down)
-        moe = moe + shifted(partial.astype(jnp.bfloat16), -step).astype(jnp.float32)
+        moe = moe + shifted(others[step - 1], -step).astype(jnp.float32)
     mixed = (resid + moe).astype(jnp.bfloat16)
     return (mixed, kv_cache)
 

time: 176 us -> 153 us (0.87)
  matrix products: 102 us -> 59.7 us
  waiting for transfers between devices: 34.9 us -> 51.6 us
  local copies, waits for them, and re-layouts: 8.74 us -> 12.4 us
    ppermute x9 -> x12, waiting for transfers between devices: 20.7 us -> 51.6 us  [shifted(): lax.ppermute(x, 'exp', [(j, (j + step) % count) for j in range(count)])]
    dot_general x4 -> x2, matrix products: 40.5 us -> 22.8 us  [expert_mix(): jnp.einsum('esf,efd->esd', hidden, w_down, preferred_element_type=jnp.flo...]
    all_to_all x1 -> x0, waiting for transfers between devices: 14.3 us -> none  [shards(): lax.all_to_all(jnp.concatenate([query, keyval], axis=-1), 'exp', split_ax...]
    dot_general x4 -> x2, matrix products: 23.8 us -> 12.8 us  [expert_mix(): jnp.einsum('esd,edf->esf', received, w_gate, preferred_element_type=jnp.f...]
    ppermute x9 -> x12, starting transfers between devices: 11.5 us -> 19.4 us  [shifted(): lax.ppermute(x, 'exp', [(j, (j + step) % count) for j in range(count)])]
    all_to_all x1 -> x0, starting transfers between devices: 6.35 us -> none  [shards(): lax.all_to_all(jnp.concatenate([query, keyval], axis=-1), 'exp', split_ax...]
    dot_general x4 -> x2, matrix products: 6.36 us -> 1.87 us  [expert_mix(): jnp.einsum('est,esd->td', low, result, preferred_element_type=jnp.float32)]
    unnamed x21 -> x33, local copies, waits for them, and re-layouts: 1.8 us -> 6.13 us
  transfers between devices with their start and end apart: 10 -> 12, of which waited for: 4 -> 10; matrix products, arithmetic and copies ran while one was open for 55% -> 17% of each run, Pallas kernels for 0% -> 0%
where the time goes in v5:
time: 153 us; the launch traced here: 152 us
  matrix products  59.7 us (39%)
  waiting for transfers between devices  51.6 us (34%)
  starting transfers between devices  19.4 us (13%)
  local copies, waits for them, and re-layouts  12.4 us (8%)
  other arithmetic  8.1 us (5%)
    ppermute x12, waiting for transfers between devices, shifted(): lax.ppermute(x, 'exp', [(j, (j + step) % count) for j in range(count)])  51.6 us
    dot_general x2, matrix products, expert_mix(): jnp.einsum('esf,efd->esd', hidden, w_down, preferred_element_type=jnp.flo...  22.8 us
    ppermute x12, starting transfers between devices, shifted(): lax.ppermute(x, 'exp', [(j, (j + step) % count) for j in range(count)])  19.4 us
    dot_general x2, matrix products, expert_mix(): jnp.einsum('esd,edf->esf', received, w_gate, preferred_element_type=jnp.f...  12.8 us
    unnamed x33, local copies, waits for them, and re-layouts  6.13 us
    dot_general x2, matrix products, expert_mix(): jnp.einsum('est,esd->td', high, result, preferred_element_type=jnp.float32)  5.82 us
    sub x1, matrix products, attend(): expo = jnp.exp(score - top)  3.58 us
  transfers between devices with their start and end apart: 12, of which 10 were waited for; matrix products, arithmetic and copies ran while one was open for 17% of the time, Pallas kernels for 0%

profile of v5, /device:TPU:0, one launch (start us, length us, event | category | flops | bytes accessed | tf_op | source)
XLA Modules:
  0.0 152.3 jit_solution(2214149349544012538)
XLA Ops:
  0.7 0.9 compare_reduce_fusion
  1.7 1.1 fusion.41
  2.8 0.3 reduce-window.9
  3.4 0.7 convert_element_type.115
  4.1 1.7 %convolution_convert_fusion.5 = bf16[128,512]{1,0:T(8,128)(2,1)S(1)} fusion(bf16[1024,512]{1,0:T(8,128)(2,1)} %param.18, bf16[128,1024]{1,0:T(8,128)(2,1)} %param.14, f32[1024]{0:T(1024)S(1)} %convert_element_type.115, f32[128]{0:T(128)S(1)} %add_rsqrt_fusion.1), kind=kOutput, calls=%fused_computation.36 | convolution fusion | flops 134807552 | bytes 1446400 | tf_op jit(solution)/shard_map/dot_general | solution.py:152
  5.9 1.9 %fusion.103 = f32[128,512]{0,1:T(8,128)S(1)} fusion(bf16[1024,512]{1,0:T(8,128)(2,1)} %param.17, bf16[128,1024]{1,0:T(8,128)(2,1)} %param.14, f32[1024]{0:T(1024)S(1)} %convert_element_type.115, f32[128]{0:T(128)S(1)} %add_rsqrt_fusion.1), kind=kOutput, calls=%fused_computation.176 | convolution fusion | flops 134742016 | bytes 1577472 | tf_op jit(solution)/shard_map/dot_general | solution.py:149
  7.9 1.0 fusion.105
  9.0 0.1 multiply_cosine_fusion
  9.4 5.1 %collective-permute-start.2 = (bf16[128,2,256]{0,2,1:T(8,128)(2,1)S(1)}, bf16[128,2,256]{0,2,1:T(8,128)(2,1)S(1)}, u32[]{:S(2)}, u32[]{:S(2)}) collective-permute-start(bf16[128,2,256]{0,2,1:T(8,128)(2,1)S(1)} %get-tuple-element.25), channel_id=1, source_target_pairs={{0,3},{1,0},{2,1},{3,2},{4,7},{5,4},{6,5},{7,6},{8,11},{9,8},{10,9... | collective-permute-start | bytes 393224 | tf_op jit(solution)/shard_map/ppermute | solution.py:104
  14.5 1.0 collective-permute-start
  15.5 0.6 add_select_fusion
  16.5 0.3 compare_and_fusion
  16.8 1.6 %collective-permute-done.2 = bf16[128,2,256]{0,2,1:T(8,128)(2,1)S(1)} collective-permute-done((bf16[128,2,256]{0,2,1:T(8,128)(2,1)S(1)}, bf16[128,2,256]{0,2,1:T(8,128)(2,1)S(1)}, u32[]{:S(2)}, u32[]{:S(2)}) %collective-permute-start.2) | collective-permute-done | bytes 131104 | tf_op jit(solution)/shard_map/ppermute | solution.py:104
  18.4 7.3 %collective-permute-done.1 = bf16[128,2,256]{0,2,1:T(8,128)(2,1)S(1)} collective-permute-done((bf16[128,2,256]{0,2,1:T(8,128)(2,1)S(1)}, bf16[128,2,256]{0,2,1:T(8,128)(2,1)S(1)}, u32[]{:S(2)}, u32[]{:S(2)}) %collective-permute-start.1) | collective-permute-done | bytes 131104 | tf_op jit(solution)/shard_map/ppermute | solution.py:104
  25.7 0.7 copy-done.7
  26.4 1.0 pad_maximum_fusion.1
  27.4 3.6 %fusion.109 = (f32[2,2,512]{2,1,0:T(2,128)S(1)}, f32[2,2,512,512]{2,3,1,0:T(8,128)}) fusion(pred[512,512]{0,1:T(8,128)(4,1)S(1)} %compare_and_fusion, bf16[512,2,2,64]{0,3,2,1:T(8,128)(2,1)S(1)} %bitcast.123, bf16[512,2,256]{0,2,1:T(8,128)(2,1)S(1)} %pad_maximum_fusion.1), kind=kOutput, calls=%fused_computation.180 | convolution fusion | flops 138412544 | bytes 4857856 | tf_op jit(solution)/shard_map/sub | solution.py:44
  31.0 2.7 %fusion.17 = bf16[2,64,2,512]{3,1,2,0:T(8,128)(2,1)S(1)} fusion(f32[2,2,512,512]{2,3,1,0:T(8,128)} %get-tuple-element.43, f32[2,2,512]{2,1,0:T(2,128)S(1)} %get-tuple-element.42, bf16[512,2,256]{0,2,1:T(8,128)(2,1)S(1)} %pad_maximum_fusion.1), kind=kOutput, calls=%fused_computation.28 | convolution fusion | flops 136445952 | bytes 4595712 | tf_op jit(solution)/shard_map/kgqt,tkd->qkgd/dot_general | solution.py:46
  33.7 0.5 convolution_convert_fusion.3
  34.2 0.9 fusion.107
  35.1 1.5 %collective-permute-start.3 = (bf16[128,1024]{1,0:T(8,128)(2,1)}, bf16[128,1024]{1,0:T(8,128)(2,1)}, u32[]{:S(2)}, u32[]{:S(2)}) collective-permute-start(bf16[128,1024]{1,0:T(8,128)(2,1)} %get-tuple-element.14), channel_id=1, source_target_pairs={{0,3},{1,0},{2,1},{3,2},{4,7},{5,4},{6,5},{7,6},{8,11},{9,8},{10,9... | collective-permute-start | bytes 786440 | tf_op jit(solution)/shard_map/ppermute | solution.py:104
  36.6 0.5 collective-permute-start.5
  37.1 2.6 %collective-permute-start.4 = (bf16[128,1024]{1,0:T(8,128)(2,1)}, bf16[128,1024]{1,0:T(8,128)(2,1)}, u32[]{:S(2)}, u32[]{:S(2)}) collective-permute-start(bf16[128,1024]{1,0:T(8,128)(2,1)} %get-tuple-element.16), channel_id=1, source_target_pairs={{0,2},{1,3},{2,0},{3,1},{4,6},{5,7},{6,4},{7,5},{8,10},{9,11},{10,... | collective-permute-start | bytes 786440 | tf_op jit(solution)/shard_map/ppermute | solution.py:104
  39.8 0.1 copy.68
  39.9 1.3 convolution_convert_fusion.4
  41.2 1.0 copy.76
  42.2 1.8 %collective-permute-done.3 = bf16[128,1024]{1,0:T(8,128)(2,1)} collective-permute-done((bf16[128,1024]{1,0:T(8,128)(2,1)}, bf16[128,1024]{1,0:T(8,128)(2,1)}, u32[]{:S(2)}, u32[]{:S(2)}) %collective-permute-start.3) | collective-permute-done | bytes 262176 | tf_op jit(solution)/shard_map/ppermute | solution.py:104
  44.0 8.4 %collective-permute-done.5 = bf16[128,1024]{1,0:T(8,128)(2,1)} collective-permute-done((bf16[128,1024]{1,0:T(8,128)(2,1)}, bf16[128,1024]{1,0:T(8,128)(2,1)}, u32[]{:S(2)}, u32[]{:S(2)}) %collective-permute-start.5) | collective-permute-done | bytes 262176 | tf_op jit(solution)/shard_map/ppermute | solution.py:104
  52.4 8.3 %collective-permute-done.4 = bf16[128,1024]{1,0:T(8,128)(2,1)} collective-permute-done((bf16[128,1024]{1,0:T(8,128)(2,1)}, bf16[128,1024]{1,0:T(8,128)(2,1)}, u32[]{:S(2)}, u32[]{:S(2)}) %collective-permute-start.4) | collective-permute-done | bytes 262176 | tf_op jit(solution)/shard_map/ppermute | solution.py:104
  60.7 1.4 multiply_reduce_fusion
  62.1 0.8 copy-done.4
  63.0 0.2 fusion.110
  63.3 0.1 copy.67
  63.4 0.1 copy.66
  63.6 0.8 concatenate.40
  64.4 1.6 %collective-permute-start.8 = (bf16[128,1152]{1,0:T(8,128)(2,1)}, bf16[128,1152]{1,0:T(8,128)(2,1)}, u32[]{:S(2)}, u32[]{:S(2)}) collective-permute-start(bf16[128,1152]{1,0:T(8,128)(2,1)} %concatenate.40), channel_id=1, source_target_pairs={{0,3},{1,0},{2,1},{3,2},{4,7},{5,4},{6,5},{7,6},{8,11},{9,8},{10,9... | collective-permute-start | bytes 884744 | tf_op jit(solution)/shard_map/ppermute | solution.py:104
  66.0 0.6 collective-permute-start.6
  66.6 0.9 compare_bitcast_fusion.1
  67.5 1.0 fusion.28
  68.6 0.4 convolution_convert_fusion.2
  69.0 5.9 %fusion.111 = f32[8,64,512]{2,1,0:T(8,128)} fusion(bf16[8,64,1024]{2,1,0:T(8,128)(2,1)S(1)} %convolution_convert_fusion.2, bf16[8,1024,512]{2,1,0:T(8,128)(2,1)} %param.22), kind=kOutput, calls=%fused_computation.182 | convolution fusion | flops 536870912 | bytes 10485760 | tf_op jit(solution)/shard_map/esd,edf->esf/dot_general | solution.py:89
  74.9 10.0 %convolution_convert_fusion.1 = bf16[8,64,1024]{2,1,0:T(8,128)(2,1)} fusion(bf16[8,512,1024]{2,1,0:T(8,128)(2,1)} %param.24, bf16[8,64,1024]{2,1,0:T(8,128)(2,1)S(1)} %convolution_convert_fusion.2, bf16[8,1024,512]{2,1,0:T(8,128)(2,1)} %param.23, f32[8,64,512]{2,1,0:T(8,128)} %fusion.111), kind=kOutput, calls=%fused_computation.19 | convolution fusion | flops 1075838976 | bytes 19922944 | tf_op jit(solution)/shard_map/esf,efd->esd/dot_general | solution.py:92
  85.0 1.3 collective-permute-done.6
  86.3 1.0 constant_dynamic-update-slice_fusion.2
  87.3 3.6 %collective-permute-done.7 = bf16[128,1152]{1,0:T(8,128)(2,1)} collective-permute-done((bf16[128,1152]{1,0:T(8,128)(2,1)}, bf16[128,1152]{1,0:T(8,128)(2,1)}, u32[]{:S(2)}, u32[]{:S(2)}) %collective-permute-start.7) | collective-permute-done | bytes 294944 | tf_op jit(solution)/shard_map/ppermute | solution.py:104
  90.9 1.0 constant_dynamic-update-slice_fusion.1
  91.9 1.0 constant_dynamic-update-slice_fusion
  93.1 0.1 dynamic-slice_bitcast_fusion
  93.4 0.3 fusion.27
  93.7 1.9 %fusion.7 = bf16[8,192,1024]{2,1,0:T(8,128)(2,1)S(1)} fusion(s32[8,384]{1,0:T(8,128)S(1)} %fusion.27, pred[8,384]{1,0:T(8,128)(4,1)S(1)} %copy.72, bf16[384,1152]{1,0:T(8,128)(2,1)S(1)} %constant_dynamic-update-slice_fusion), kind=kOutput, calls=%fused_computation.11 | convolution fusion | flops 1210712064 | bytes 3947520 | tf_op jit(solution)/shard_map/est,td->esd/dot_general | solution.py:86
  95.6 1.7 %copy-done.3 = bf16[8,192,1024]{2,1,0:T(8,128)(2,1)} copy-done((bf16[8,192,1024]{2,1,0:T(8,128)(2,1)}, bf16[8,192,1024]{2,1,0:T(8,128)(2,1)S(1)}, u32[]{:S(2)}) %copy-start.3) | copy-done | bytes 3145752
  97.2 6.9 %fusion.112 = f32[8,192,512]{2,1,0:T(8,128)} fusion(bf16[8,192,1024]{2,1,0:T(8,128)(2,1)S(1)} %fusion.7, bf16[8,1024,512]{2,1,0:T(8,128)(2,1)} %param.22), kind=kOutput, calls=%fused_computation.183 | convolution fusion | flops 1610612736 | bytes 14680064 | tf_op jit(solution)/shard_map/esd,edf->esf/dot_general | solution.py:89
  104.1 12.7 %convolution_convert_fusion = bf16[8,192,1024]{2,1,0:T(8,128)(2,1)} fusion(bf16[8,512,1024]{2,1,0:T(8,128)(2,1)} %param.24, f32[8,192,512]{2,1,0:T(8,128)} %fusion.112, bf16[8,192,1024]{2,1,0:T(8,128)(2,1)} %copy-done.3, bf16[8,1024,512]{2,1,0:T(8,128)(2,1)} %param.23), kind=kOutput, calls=%fused_computation.12 | convolution fusion | flops 3227516928 | bytes 26214400 | tf_op jit(solution)/shard_map/esf,efd->esd/dot_general | solution.py:92
  116.9 3.5 %fusion.18 = f32[384,1024,1]{1,0,2:T(8,128)S(1)} fusion(bf16[8,192,1024]{2,1,0:T(8,128)(2,1)} %convolution_convert_fusion, s32[8,384]{1,0:T(8,128)S(1)} %fusion.27, pred[8,384]{1,0:T(8,128)(4,1)S(1)} %copy.72, bf16[8,384]{1,0:T(8,128)(2,1)S(1)} %copy.73), kind=kOutput, calls=%fused_computation.29 | convolution fusion | flops 1209729024 | bytes 4740096 | tf_op jit(solution)/shard_map/est,esd->td/dot_general | solution.py:97
  120.4 1.5 fusion.14
  121.9 0.9 fusion.108
  122.8 2.5 %collective-permute-start.11 = (bf16[128,1024]{1,0:T(8,128)(2,1)}, bf16[128,1024]{1,0:T(8,128)(2,1)}, u32[]{:S(2)}, u32[]{:S(2)}) collective-permute-start(bf16[128,1024]{1,0:T(8,128)(2,1)} %get-tuple-element.20), channel_id=1, source_target_pairs={{0,1},{1,2},{2,3},{3,0},{4,5},{5,6},{6,7},{7,4},{8,9},{9,10},{10,1... | collective-permute-start | bytes 786440 | tf_op jit(solution)/shard_map/ppermute | solution.py:104
  125.3 3.9 %collective-permute-start.10 = (bf16[128,1024]{1,0:T(8,128)(2,1)}, bf16[128,1024]{1,0:T(8,128)(2,1)}, u32[]{:S(2)}, u32[]{:S(2)}) collective-permute-start(bf16[128,1024]{1,0:T(8,128)(2,1)} %get-tuple-element.21), channel_id=1, source_target_pairs={{0,2},{1,3},{2,0},{3,1},{4,6},{5,7},{6,4},{7,5},{8,10},{9,11},{10,... | collective-permute-start | bytes 786440 | tf_op jit(solution)/shard_map/ppermute | solution.py:104
  129.2 0.9 dynamic-slice_bitcast_fusion.3
  130.3 0.4 convolution_bitcast_fusion
  130.7 0.4 collective-permute-done.9
  131.1 10.7 %collective-permute-done.11 = bf16[128,1024]{1,0:T(8,128)(2,1)} collective-permute-done((bf16[128,1024]{1,0:T(8,128)(2,1)}, bf16[128,1024]{1,0:T(8,128)(2,1)}, u32[]{:S(2)}, u32[]{:S(2)}) %collective-permute-start.11) | collective-permute-done | bytes 262176 | tf_op jit(solution)/shard_map/ppermute | solution.py:104
  141.9 8.2 %collective-permute-done.10 = bf16[128,1024]{1,0:T(8,128)(2,1)} collective-permute-done((bf16[128,1024]{1,0:T(8,128)(2,1)}, bf16[128,1024]{1,0:T(8,128)(2,1)}, u32[]{:S(2)}, u32[]{:S(2)}) %collective-permute-start.10) | collective-permute-done | bytes 262176 | tf_op jit(solution)/shard_map/ppermute | solution.py:104
  150.0 2.3 %add_convert_fusion = bf16[128,1024]{1,0:T(8,128)(2,1)} fusion(f32[128,1024]{1,0:T(8,128)} %copy-done.4, bf16[128,1024]{1,0:T(8,128)(2,1)} %collective-permute-done.11, bf16[128,1024]{1,0:T(8,128)(2,1)} %collective-permute-done.10, bf16[128,1024]{1,0:T(8,128)(2,1)S(1)} %collective-permute-done.9, f32[128,1024]{1,0:T(8,128)S(1)} %convolution_bitcast_fusion, ...), kind=kOutput, calls=%fused_computation.64 | convolution fusion | flops 135593984 | bytes 3152896 | tf_op jit(solution)/shard_map/est,esd->td/dot_general | solution.py:97
  (79 shorter events, 2.1 us)
Async XLA Ops:
  0.6 7.2 %copy-start = (bf16[1024,1024]{1,0:T(8,128)(2,1)S(1)}, bf16[1024,1024]{1,0:T(8,128)(2,1)}, u32[]{:S(2)}) copy-start(bf16[1024,1024]{1,0:T(8,128)(2,1)} %param.16) | copy-start | bytes 6291460
  0.6 7.2 %copy-start.2 = (bf16[128,1024]{1,0:T(8,128)(2,1)S(1)}, bf16[128,1024]{1,0:T(8,128)(2,1)}, u32[]{:S(2)}) copy-start(bf16[128,1024]{1,0:T(8,128)(2,1)} %param.14) | copy-start | bytes 786436
  7.9 8.5 %copy-start.10 = (s32[1,512]{1,0:T(1,128)S(1)}, s32[1,512]{1,0:T(1,128)}, u32[]{:S(2)}) copy-start(s32[1,512]{1,0:T(1,128)} %param.25) | copy-start | bytes 6148
  7.9 8.6 %copy-start.11 = (s32[1,512]{1,0:T(1,128)S(1)}, s32[1,512]{1,0:T(1,128)}, u32[]{:S(2)}) copy-start(s32[1,512]{1,0:T(1,128)} %param.26) | copy-start | bytes 6148
  7.9 8.9 %copy-start.9 = (s32[128,8]{0,1:T(8,128)S(1)}, s32[128,8]{0,1:T(8,128)}, u32[]{:S(2)}) copy-start(s32[128,8]{0,1:T(8,128)} %param.27) | copy-start | bytes 12292
  9.4 9.0 %collective-permute-start.2 = (bf16[128,2,256]{0,2,1:T(8,128)(2,1)S(1)}, bf16[128,2,256]{0,2,1:T(8,128)(2,1)S(1)}, u32[]{:S(2)}, u32[]{:S(2)}) collective-permute-start(bf16[128,2,256]{0,2,1:T(8,128)(2,1)S(1)} %get-tuple-element.25), channel_id=1, source_target_pairs={{0,3},{1,0},{2,1},{3,2},{4,7},{5,4},{6,5},{7,6},{8,11},{9,8},{10,9... | collective-permute-start | bytes 393224 | tf_op jit(solution)/shard_map/ppermute | solution.py:104
  14.5 11.2 %collective-permute-start.1 = (bf16[128,2,256]{0,2,1:T(8,128)(2,1)S(1)}, bf16[128,2,256]{0,2,1:T(8,128)(2,1)S(1)}, u32[]{:S(2)}, u32[]{:S(2)}) collective-permute-start(bf16[128,2,256]{0,2,1:T(8,128)(2,1)S(1)} %get-tuple-element.26), channel_id=1, source_target_pairs={{0,2},{1,3},{2,0},{3,1},{4,6},{5,7},{6,4},{7,5},{8,10},{9,11},{10,... | collective-permute-start | bytes 393224 | tf_op jit(solution)/shard_map/ppermute | solution.py:104
  14.5 11.2 %collective-permute-start = (bf16[128,2,256]{0,2,1:T(8,128)(2,1)S(1)}, bf16[128,2,256]{0,2,1:T(8,128)(2,1)S(1)}, u32[]{:S(2)}, u32[]{:S(2)}) collective-permute-start(bf16[128,2,256]{0,2,1:T(8,128)(2,1)S(1)} %get-tuple-element.27), channel_id=1, source_target_pairs={{0,1},{1,2},{2,3},{3,0},{4,5},{5,6},{6,7},{7,4},{8,9},{9,10},{10,1... | collective-permute-start | bytes 393224 | tf_op jit(solution)/shard_map/ppermute | solution.py:104
  25.7 0.7 copy-start.7
  27.4 3.6 %copy-start.5 = (bf16[512,2,256]{0,2,1:T(8,128)(2,1)}, bf16[512,2,256]{0,2,1:T(8,128)(2,1)S(1)}, u32[]{:S(2)}) copy-start(bf16[512,2,256]{0,2,1:T(8,128)(2,1)S(1)} %pad_maximum_fusion.1) | copy-start | bytes 1572868
  31.0 2.8 %copy-start.6 = (bf16[256,1024]{1,0:T(8,128)(2,1)S(1)}, bf16[256,1024]{1,0:T(8,128)(2,1)}, u32[]{:S(2)}) copy-start(bf16[256,1024]{1,0:T(8,128)(2,1)} %param.19) | copy-start | bytes 1572868
  33.7 6.0 %copy-start.12 = (bf16[1024]{0:T(1024)(128)(2,1)S(1)}, bf16[1024]{0:T(1024)(128)(2,1)}, u32[]{:S(2)}) copy-start(bf16[1024]{0:T(1024)(128)(2,1)} %param.20) | copy-start | bytes 6148
  34.2 28.8 %copy-start.8 = (bf16[1024,32]{0,1:T(8,128)(2,1)S(1)}, bf16[1024,32]{0,1:T(8,128)(2,1)}, u32[]{:S(2)}) copy-start(bf16[1024,32]{0,1:T(8,128)(2,1)} %param.21) | copy-start | bytes 196612
  35.1 8.9 %collective-permute-start.3 = (bf16[128,1024]{1,0:T(8,128)(2,1)}, bf16[128,1024]{1,0:T(8,128)(2,1)}, u32[]{:S(2)}, u32[]{:S(2)}) collective-permute-start(bf16[128,1024]{1,0:T(8,128)(2,1)} %get-tuple-element.14), channel_id=1, source_target_pairs={{0,3},{1,0},{2,1},{3,2},{4,7},{5,4},{6,5},{7,6},{8,11},{9,8},{10,9... | collective-permute-start | bytes 786440 | tf_op jit(solution)/shard_map/ppermute | solution.py:104
  36.6 15.7 %collective-permute-start.5 = (bf16[128,1024]{1,0:T(8,128)(2,1)}, bf16[128,1024]{1,0:T(8,128)(2,1)}, u32[]{:S(2)}, u32[]{:S(2)}) collective-permute-start(bf16[128,1024]{1,0:T(8,128)(2,1)} %get-tuple-element.15), channel_id=1, source_target_pairs={{0,1},{1,2},{2,3},{3,0},{4,5},{5,6},{6,7},{7,4},{8,9},{9,10},{10,1... | collective-permute-start | bytes 786440 | tf_op jit(solution)/shard_map/ppermute | solution.py:104
  37.1 23.5 %collective-permute-start.4 = (bf16[128,1024]{1,0:T(8,128)(2,1)}, bf16[128,1024]{1,0:T(8,128)(2,1)}, u32[]{:S(2)}, u32[]{:S(2)}) collective-permute-start(bf16[128,1024]{1,0:T(8,128)(2,1)} %get-tuple-element.16), channel_id=1, source_target_pairs={{0,2},{1,3},{2,0},{3,1},{4,6},{5,7},{6,4},{7,5},{8,10},{9,11},{10,... | collective-permute-start | bytes 786440 | tf_op jit(solution)/shard_map/ppermute | solution.py:104
  62.0 0.8 copy-start.4
  64.4 27.5 %collective-permute-start.8 = (bf16[128,1152]{1,0:T(8,128)(2,1)}, bf16[128,1152]{1,0:T(8,128)(2,1)}, u32[]{:S(2)}, u32[]{:S(2)}) collective-permute-start(bf16[128,1152]{1,0:T(8,128)(2,1)} %concatenate.40), channel_id=1, source_target_pairs={{0,3},{1,0},{2,1},{3,2},{4,7},{5,4},{6,5},{7,6},{8,11},{9,8},{10,9... | collective-permute-start | bytes 884744 | tf_op jit(solution)/shard_map/ppermute | solution.py:104
  66.0 24.8 %collective-permute-start.7 = (bf16[128,1152]{1,0:T(8,128)(2,1)}, bf16[128,1152]{1,0:T(8,128)(2,1)}, u32[]{:S(2)}, u32[]{:S(2)}) collective-permute-start(bf16[128,1152]{1,0:T(8,128)(2,1)} %concatenate.40), channel_id=1, source_target_pairs={{0,2},{1,3},{2,0},{3,1},{4,6},{5,7},{6,4},{7,5},{8,10},{9,11},{10,... | collective-permute-start | bytes 884744 | tf_op jit(solution)/shard_map/ppermute | solution.py:104
  66.0 20.2 %collective-permute-start.6 = (bf16[128,1152]{1,0:T(8,128)(2,1)}, bf16[128,1152]{1,0:T(8,128)(2,1)}, u32[]{:S(2)}, u32[]{:S(2)}) collective-permute-start(bf16[128,1152]{1,0:T(8,128)(2,1)} %concatenate.40), channel_id=1, source_target_pairs={{0,1},{1,2},{2,3},{3,0},{4,5},{5,6},{6,7},{7,4},{8,9},{9,10},{10,1... | collective-permute-start | bytes 884744 | tf_op jit(solution)/shard_map/ppermute | solution.py:104
  74.9 18.4 %copy-start.13 = (s32[384]{0:T(512)S(1)}, s32[384]{0:T(512)}, u32[]{:S(2)}) copy-start(s32[384]{0:T(512)} %get-tuple-element.45) | copy-start | bytes 4612
  95.6 1.7 %copy-start.3 = (bf16[8,192,1024]{2,1,0:T(8,128)(2,1)}, bf16[8,192,1024]{2,1,0:T(8,128)(2,1)S(1)}, u32[]{:S(2)}) copy-start(bf16[8,192,1024]{2,1,0:T(8,128)(2,1)S(1)} %fusion.7) | copy-start | bytes 9437188
  116.9 3.5 %copy-start.14 = (bf16[8,192,1024]{2,1,0:T(8,128)(2,1)S(1)}, bf16[8,192,1024]{2,1,0:T(8,128)(2,1)}, u32[]{:S(2)}) copy-start(bf16[8,192,1024]{2,1,0:T(8,128)(2,1)} %convolution_convert_fusion) | copy-start | bytes 9437188
  120.4 10.0 %copy-start.1 = (bf16[8,64,1024]{2,1,0:T(8,128)(2,1)S(1)}, bf16[8,64,1024]{2,1,0:T(8,128)(2,1)}, u32[]{:S(2)}) copy-start(bf16[8,64,1024]{2,1,0:T(8,128)(2,1)} %convolution_convert_fusion.1) | copy-start | bytes 3145732
  122.8 8.4 %collective-permute-start.9 = (bf16[128,1024]{1,0:T(8,128)(2,1)}, bf16[128,1024]{1,0:T(8,128)(2,1)S(1)}, u32[]{:S(2)}, u32[]{:S(2)}) collective-permute-start(bf16[128,1024]{1,0:T(8,128)(2,1)} %get-tuple-element.19), channel_id=1, source_target_pairs={{0,3},{1,0},{2,1},{3,2},{4,7},{5,4},{6,5},{7,6},{8,11},{9,8},{10,9... | collective-permute-start | bytes 786440 | tf_op jit(solution)/shard_map/ppermute | solution.py:104
  122.8 19.1 %collective-permute-start.11 = (bf16[128,1024]{1,0:T(8,128)(2,1)}, bf16[128,1024]{1,0:T(8,128)(2,1)}, u32[]{:S(2)}, u32[]{:S(2)}) collective-permute-start(bf16[128,1024]{1,0:T(8,128)(2,1)} %get-tuple-element.20), channel_id=1, source_target_pairs={{0,1},{1,2},{2,3},{3,0},{4,5},{5,6},{6,7},{7,4},{8,9},{9,10},{10,1... | collective-permute-start | bytes 786440 | tf_op jit(solution)/shard_map/ppermute | solution.py:104
  125.3 24.7 %collective-permute-start.10 = (bf16[128,1024]{1,0:T(8,128)(2,1)}, bf16[128,1024]{1,0:T(8,128)(2,1)}, u32[]{:S(2)}, u32[]{:S(2)}) collective-permute-start(bf16[128,1024]{1,0:T(8,128)(2,1)} %get-tuple-element.21), channel_id=1, source_target_pairs={{0,2},{1,3},{2,0},{3,1},{4,6},{5,7},{6,4},{7,5},{8,10},{9,11},{10,... | collective-permute-start | bytes 786440 | tf_op jit(solution)/shard_map/ppermute | solution.py:104

commit v6 on v5

--- a/solution.py
+++ b/solution.py
@@ -31,14 +31,14 @@
     return jnp.concatenate([front * cosine - back * sine, back * cosine + front * sine], axis=-1)
 
 
-def attend(query, keyval, seg, where_at):
+def attend(query, keyval, query_seg, seg, query_at, where_at):
     plen, groups, width = query.shape
     half = width // 2
     queries = query.reshape(plen, groups, 2, half)
     keys = keyval[..., :half]
     values = keyval[..., half:]
     score = jnp.einsum("qkgd,tkd->kgqt", queries, keys, preferred_element_type=jnp.float32) * 0.125
-    allowed = (seg[:, None] == seg[None, :]) & (where_at[None, :] <= where_at[:, None])
+    allowed = (query_seg[:, None] == seg[None, :]) & (where_at[None, :] <= query_at[:, None])
     score = jnp.where(allowed[None, None], score, -1e30)
     top = jnp.max(score, axis=-1, keepdims=True)
     expo = jnp.exp(score - top)
@@ -62,7 +62,7 @@
     return jnp.concatenate([normed2, high, low, named, fill], axis=1)
 
 
-def expert_mix(packed, sources, width, experts, w_gate, w_up, w_down):
+def expert_mix(packed, sources, width, experts, w_gate, w_up, w_down, pieces):
     tokens_all = packed.shape[0]
     local = w_gate.shape[0]
     rows = tokens_all // sources
@@ -89,14 +89,21 @@
     gate = jnp.einsum("esd,edf->esf", received, w_gate, preferred_element_type=jnp.float32)
     upward = jnp.einsum("esd,edf->esf", received, w_up, preferred_element_type=jnp.float32)
     hidden = (jax.nn.silu(gate) * upward).astype(jnp.bfloat16)
-    result = jnp.einsum("esf,efd->esd", hidden, w_down, preferred_element_type=jnp.float32)
-    result = result.astype(jnp.bfloat16)
     zero = jnp.zeros((), jnp.bfloat16)
     high = jnp.where(picks, high.T[:, None, :], zero)
     low = jnp.where(picks, low.T[:, None, :], zero)
-    partial = jnp.einsum("est,esd->td", high, result, preferred_element_type=jnp.float32)
-    partial = partial + jnp.einsum("est,esd->td", low, result, preferred_element_type=jnp.float32)
-    return partial
+    cut = w_down.shape[2] // pieces
+    outs = []
+    for piece in range(pieces):
+        down = lax.slice_in_dim(w_down, piece * cut, (piece + 1) * cut, axis=2)
+        result = jnp.einsum("esf,efd->esd", hidden, down, preferred_element_type=jnp.float32)
+        result = result.astype(jnp.bfloat16)
+        partial = jnp.einsum("est,esd->td", high, result, preferred_element_type=jnp.float32)
+        partial = partial + jnp.einsum(
+            "est,esd->td", low, result, preferred_element_type=jnp.float32
+        )
+        outs.append(partial)
+    return outs
 
 
 def shifted(x, step):
@@ -169,19 +176,32 @@
     kv_cache = jnp.einsum(
         "rs,skd->rkd", placing.astype(jnp.bfloat16), keyval_heads, preferred_element_type=jnp.float32
     ).astype(jnp.bfloat16)
-    heads_out = attend(query_heads, keyval_heads, step_rows(seg, rows), where_at)
-    attention = jnp.dot(heads_out, w_out, preferred_element_type=jnp.float32).astype(jnp.bfloat16)
-    attention = exchange_sum(attention.reshape(owners, rows, width))
+    seg_rows = step_rows(seg, rows)
+    attention = None
+    for step in list(range(1, owners)) + [0]:
+        picked = slice(step * rows, (step + 1) * rows)
+        heads_out = attend(
+            query_heads[picked], keyval_heads, seg_rows[picked], seg_rows, where_at[picked], where_at
+        )
+        block = jnp.dot(heads_out, w_out, preferred_element_type=jnp.float32)
+        if step:
+            block = shifted(block.astype(jnp.bfloat16), -step).astype(jnp.float32)
+        attention = block if attention is None else attention + block
     resid = tokens.astype(jnp.float32) + attention
     normed2 = rms_scale(resid, norm_moe)
     packed = routing(normed2, expert_ids, w_router)
     experts = w_router.shape[1]
-    moe = expert_mix(packed, 1, width, experts, w_gate, w_up, w_down)
+    moe = expert_mix(packed, 1, width, experts, w_gate, w_up, w_down, 1)[0]
     received = jnp.concatenate([shifted(packed, step) for step in range(1, owners)])
-    others = expert_mix(received, owners - 1, width, experts, w_gate, w_up, w_down)
-    others = others.astype(jnp.bfloat16).reshape(owners - 1, rows, width)
-    for step in range(1, owners):
-        moe = moe + shifted(others[step - 1], -step).astype(jnp.float32)
+    pieces = expert_mix(received, owners - 1, width, experts, w_gate, w_up, w_down, 2)
+    backs = []
+    for piece in pieces:
+        piece = piece.astype(jnp.bfloat16).reshape(owners - 1, rows, -1)
+        back = sum(
+            shifted(piece[step - 1], -step).astype(jnp.float32) for step in range(1, owners)
+        )
+        backs.append(back)
+    moe = moe + jnp.concatenate(backs, axis=1)
     mixed = (resid + moe).astype(jnp.bfloat16)
     return (mixed, kv_cache)
 

time: 153 us -> 146 us (0.954)
  waiting for transfers between devices: 51.6 us -> 24.9 us
  matrix products: 59.7 us -> 73.9 us
  other arithmetic: 8.1 us -> 10.3 us
  starting transfers between devices: 19.4 us -> 21.3 us
    ppermute x12 -> x15, waiting for transfers between devices: 51.6 us -> 24.9 us  [shifted(): lax.ppermute(x, 'exp', [(j, (j + step) % count) for j in range(count)])]
    dot_general x1 -> x4, matrix products: 2.73 us -> 9.92 us  [attend(): jnp.einsum('kgqt,tkd->qkgd', probs, values, preferred_element_type=jnp.fl...]
    dot_general x3 -> x12, matrix products: 23.2 us -> 29.4 us  [the longest x3 14.4 us: expert_mix(): jnp.einsum('esf,efd->esd', hidden, down, preferred_element_type=jnp.float32)]
    dot_general x2 -> x3, matrix products: 1.87 us -> 4.75 us  [expert_mix(): jnp.einsum('est,esd->td', low, result, preferred_element_type=jnp.float32)]
    dot_general x2 -> x3, matrix products: 5.82 us -> 2.95 us  [expert_mix(): jnp.einsum('est,esd->td', high, result, preferred_element_type=jnp.float32)]
    ppermute x12 -> x15, starting transfers between devices: 19.4 us -> 21.3 us  [shifted(): lax.ppermute(x, 'exp', [(j, (j + step) % count) for j in range(count)])]
    unnamed x33 -> x67, local copies, waits for them, and re-layouts: 6.13 us -> 5.17 us
    sub x1 -> x4, matrix products: 3.58 us -> 4.52 us  [attend(): expo = jnp.exp(score - top)]
  transfers between devices with their start and end apart: 12 -> 15, of which waited for: 10 -> 8; matrix products, arithmetic and copies ran while one was open for 17% -> 34% of each run, Pallas kernels for 0% -> 0%
where the time goes in v6:
time: 146 us; the launch traced here: 145 us
  matrix products  73.9 us (51%)
  waiting for transfers between devices  24.9 us (17%)
  starting transfers between devices  21.3 us (15%)
  local copies, waits for them, and re-layouts  13.4 us (9%)
  other arithmetic  10.3 us (7%)
    ppermute x15, waiting for transfers between devices, shifted(): lax.ppermute(x, 'exp', [(j, (j + step) % count) for j in range(count)])  24.9 us
    ppermute x15, starting transfers between devices, shifted(): lax.ppermute(x, 'exp', [(j, (j + step) % count) for j in range(count)])  21.3 us
    dot_general x3, matrix products, expert_mix(): jnp.einsum('esf,efd->esd', hidden, down, preferred_element_type=jnp.float32)  14.4 us
    dot_general x2, matrix products, expert_mix(): jnp.einsum('esd,edf->esf', received, w_gate, preferred_element_type=jnp.f...  11.4 us
    dot_general x4, matrix products, attend(): jnp.einsum('kgqt,tkd->qkgd', probs, values, preferred_element_type=jnp.fl...  9.92 us
    dot_general x4, matrix products, shards(): block = jnp.dot(heads_out, w_out, preferred_element_type=jnp.float32)  6.87 us
    dot_general x4, matrix products, attend(): jnp.einsum('qkgd,tkd->kgqt', queries, keys, preferred_element_type=jnp.fl...  6.26 us
    unnamed x67, local copies, waits for them, and re-layouts  5.17 us
  transfers between devices with their start and end apart: 15, of which 8 were waited for; matrix products, arithmetic and copies ran while one was open for 34% of the time, Pallas kernels for 0%

profile of v6, /device:TPU:0, one launch (start us, length us, event | category | flops | bytes accessed | tf_op | source)
XLA Modules:
  0.0 145.1 jit_solution(18366804486700751541)
XLA Ops:
  0.7 0.9 compare_reduce_fusion
  1.7 1.1 fusion.100
  4.1 1.7 %convolution_convert_fusion.6 = bf16[128,512]{1,0:T(8,128)(2,1)S(1)} fusion(bf16[1024,512]{1,0:T(8,128)(2,1)} %param.18, bf16[128,1024]{1,0:T(8,128)(2,1)} %param.14, f32[1024]{0:T(1024)S(1)} %convert_element_type.160, f32[128]{0:T(128)S(1)} %add_rsqrt_fusion.1), kind=kOutput, calls=%fused_computation.70 | convolution fusion | flops 134807552 | bytes 1446400 | tf_op jit(solution)/shard_map/dot_general | solution.py:159
  5.9 1.9 %fusion.173 = f32[128,512]{0,1:T(8,128)S(1)} fusion(bf16[1024,512]{1,0:T(8,128)(2,1)} %param.17, bf16[128,1024]{1,0:T(8,128)(2,1)} %param.14, f32[1024]{0:T(1024)S(1)} %convert_element_type.160, f32[128]{0:T(128)S(1)} %add_rsqrt_fusion.1), kind=kOutput, calls=%fused_computation.242 | convolution fusion | flops 134742016 | bytes 1577472 | tf_op jit(solution)/shard_map/dot_general | solution.py:156
  7.9 1.0 fusion.175
  10.1 5.1 %collective-permute-start.2 = (bf16[128,2,256]{0,2,1:T(8,128)(2,1)}, bf16[128,2,256]{0,2,1:T(8,128)(2,1)S(1)}, u32[]{:S(2)}, u32[]{:S(2)}) collective-permute-start(bf16[128,2,256]{0,2,1:T(8,128)(2,1)} %get-tuple-element.21), channel_id=1, source_target_pairs={{0,3},{1,0},{2,1},{3,2},{4,7},{5,4},{6,5},{7,6},{8,11},{9,8},{10,9... | collective-permute-start | bytes 393224 | tf_op jit(solution)/shard_map/ppermute | solution.py:111
  15.2 1.0 collective-permute-start
  17.7 1.0 compare_and_fusion.3
  22.5 2.3 %collective-permute-done = bf16[128,2,256]{0,2,1:T(8,128)(2,1)S(1)} collective-permute-done((bf16[128,2,256]{0,2,1:T(8,128)(2,1)}, bf16[128,2,256]{0,2,1:T(8,128)(2,1)S(1)}, u32[]{:S(2)}, u32[]{:S(2)}) %collective-permute-start) | collective-permute-done | bytes 131104 | tf_op jit(solution)/shard_map/ppermute | solution.py:111
  24.8 1.7 %collective-permute-done.1 = bf16[128,2,256]{0,2,1:T(8,128)(2,1)S(1)} collective-permute-done((bf16[128,2,256]{0,2,1:T(8,128)(2,1)S(1)}, bf16[128,2,256]{0,2,1:T(8,128)(2,1)S(1)}, u32[]{:S(2)}, u32[]{:S(2)}) %collective-permute-start.1) | collective-permute-done | bytes 131104 | tf_op jit(solution)/shard_map/ppermute | solution.py:111
  27.2 2.0 %fusion.182 = f32[2,2,128]{2,1,0:T(2,128)} fusion(bf16[512,2,64,1]{0,2,3,1:T(8,128)(2,1)S(1)} %get-tuple-element.18, bf16[128,2,2,64]{0,3,2,1:T(8,128)(2,1)S(1)} %bitcast.191, pred[128,512]{0,1:T(8,128)(4,1)} %get-tuple-element.34), kind=kOutput, calls=%fused_computation.249 | convolution fusion | flops 34603520 | bytes 264192 | tf_op jit(solution)/shard_map/sub | solution.py:44
  29.1 1.3 fusion.37
  31.0 1.4 fusion.35
  33.0 1.3 fusion.33
  34.3 2.7 %convolution_convert_fusion.10 = bf16[2,64,2,128]{3,1,2,0:T(8,128)(2,1)} fusion(bf16[512,2,64,1]{0,2,3,1:T(8,128)(2,1)} %get-tuple-element.19, f32[2,2,128]{2,1,0:T(2,128)} %fusion.182, f32[2,2,128,512]{2,3,1,0:T(8,128)} %fusion.37), kind=kOutput, calls=%fused_computation.74 | convolution fusion | flops 34374656 | bytes 1247232 | tf_op jit(solution)/shard_map/kgqt,tkd->qkgd/dot_general | solution.py:46
  37.0 1.8 %convolution_convert_fusion.5 = bf16[128,1024]{1,0:T(8,128)(2,1)} fusion(bf16[128,256]{0,1:T(8,128)(2,1)} %bitcast.198, bf16[256,1024]{1,0:T(8,128)(2,1)S(1)} %copy-done.2), kind=kOutput, calls=%fused_computation.59 | convolution fusion | flops 67239936 | bytes 851968 | tf_op jit(solution)/shard_map/dot_general | solution.py:186
  38.8 1.6 %collective-permute-start.3 = (bf16[128,1024]{1,0:T(8,128)(2,1)}, bf16[128,1024]{1,0:T(8,128)(2,1)}, u32[]{:S(2)}, u32[]{:S(2)}) collective-permute-start(bf16[128,1024]{1,0:T(8,128)(2,1)} %convolution_convert_fusion.5), channel_id=1, source_target_pairs={{0,3},{1,0},{2,1},{3,2},{4,7},{5,4},{6,5},{7,6},{8,11},{9,8},{10,9... | collective-permute-start | bytes 786440 | tf_op jit(solution)/shard_map/ppermute | solution.py:111
  40.4 2.7 %convolution_convert_fusion.9 = bf16[2,64,2,128]{3,1,2,0:T(8,128)(2,1)} fusion(bf16[512,2,64,1]{0,2,3,1:T(8,128)(2,1)} %get-tuple-element.19, f32[2,2,128]{2,1,0:T(2,128)S(1)} %fusion.181, f32[2,2,128,512]{2,3,1,0:T(8,128)} %fusion.35), kind=kOutput, calls=%fused_computation.73 | convolution fusion | flops 34374656 | bytes 1247232 | tf_op jit(solution)/shard_map/kgqt,tkd->qkgd/dot_general | solution.py:46
  43.1 1.8 %convolution_convert_fusion.4 = bf16[128,1024]{1,0:T(8,128)(2,1)} fusion(bf16[128,256]{0,1:T(8,128)(2,1)} %bitcast.199, bf16[256,1024]{1,0:T(8,128)(2,1)S(1)} %copy-done.2), kind=kOutput, calls=%fused_computation.58 | convolution fusion | flops 67239936 | bytes 851968 | tf_op jit(solution)/shard_map/dot_general | solution.py:186
  44.9 0.9 collective-permute-start.4
  45.8 2.6 %convolution_convert_fusion.8 = bf16[2,64,2,128]{3,1,2,0:T(8,128)(2,1)} fusion(bf16[512,2,64,1]{0,2,3,1:T(8,128)(2,1)} %get-tuple-element.19, f32[2,2,128]{2,1,0:T(2,128)S(1)} %fusion.180, f32[2,2,128,512]{2,3,1,0:T(8,128)} %fusion.33), kind=kOutput, calls=%fused_computation.72 | convolution fusion | flops 34374656 | bytes 1247232 | tf_op jit(solution)/shard_map/kgqt,tkd->qkgd/dot_general | solution.py:46
  48.4 1.8 %convolution_convert_fusion.3 = bf16[128,1024]{1,0:T(8,128)(2,1)} fusion(bf16[128,256]{0,1:T(8,128)(2,1)} %bitcast.200, bf16[256,1024]{1,0:T(8,128)(2,1)S(1)} %copy-done.2), kind=kOutput, calls=%fused_computation.57 | convolution fusion | flops 67239936 | bytes 851968 | tf_op jit(solution)/shard_map/dot_general | solution.py:186
  50.2 2.0 %collective-permute-start.5 = (bf16[128,1024]{1,0:T(8,128)(2,1)}, bf16[128,1024]{1,0:T(8,128)(2,1)}, u32[]{:S(2)}, u32[]{:S(2)}) collective-permute-start(bf16[128,1024]{1,0:T(8,128)(2,1)} %convolution_convert_fusion.3), channel_id=1, source_target_pairs={{0,1},{1,2},{2,3},{3,0},{4,5},{5,6},{6,7},{7,4},{8,9},{9,10},{10,1... | collective-permute-start | bytes 786440 | tf_op jit(solution)/shard_map/ppermute | solution.py:111
  52.3 2.2 %fusion.31 = f32[2,2,128,512]{2,3,1,0:T(8,128)} fusion(bf16[512,2,64,1]{0,2,3,1:T(8,128)(2,1)S(1)} %get-tuple-element.18, bf16[128,2,2,64]{0,3,2,1:T(8,128)(2,1)} %bitcast.189, pred[128,512]{0,1:T(8,128)(4,1)} %get-tuple-element.37), kind=kOutput, calls=%fused_computation.29 | convolution fusion | flops 34078720 | bytes 1310720 | tf_op jit(solution)/shard_map/qkgd,tkd->kgqt/dot_general | solution.py:40
  54.5 1.1 convolution_convert_fusion.2
  55.5 1.5 %fusion.179 = f32[2,2,128]{2,1,0:T(2,128)S(1)} fusion(bf16[512,2,64,1]{0,2,3,1:T(8,128)(2,1)S(1)} %get-tuple-element.18, bf16[128,2,2,64]{0,3,2,1:T(8,128)(2,1)} %bitcast.190, pred[128,512]{0,1:T(8,128)(4,1)} %get-tuple-element.37), kind=kOutput, calls=%fused_computation.246 | convolution fusion | flops 34603520 | bytes 264192 | tf_op jit(solution)/shard_map/sub | solution.py:44
  57.0 1.9 %copy.88 = bf16[512,2,128]{2,1,0:T(2,128)(2,1)} copy(bf16[512,2,128]{2,0,1:T(8,128)(2,1)} %convolution_convert_fusion.2) | data formatting | bytes 524288
  58.9 1.9 %convolution_convert_fusion.7 = bf16[2,64,2,128]{3,1,2,0:T(8,128)(2,1)S(1)} fusion(bf16[512,2,64,1]{0,2,3,1:T(8,128)(2,1)S(1)} %copy-done.11, f32[2,2,128]{2,1,0:T(2,128)S(1)} %fusion.179, f32[2,2,128,512]{2,3,1,0:T(8,128)} %fusion.31), kind=kOutput, calls=%fused_computation.71 | convolution fusion | flops 34374656 | bytes 1247232 | tf_op jit(solution)/shard_map/kgqt,tkd->qkgd/dot_general | solution.py:46
  60.9 3.1 %collective-permute-done.4 = bf16[128,1024]{1,0:T(8,128)(2,1)} collective-permute-done((bf16[128,1024]{1,0:T(8,128)(2,1)}, bf16[128,1024]{1,0:T(8,128)(2,1)}, u32[]{:S(2)}, u32[]{:S(2)}) %collective-permute-start.4) | collective-permute-done | bytes 262176 | tf_op jit(solution)/shard_map/ppermute | solution.py:111
  64.0 1.5 %multiply_reduce_fusion = (f32[128]{0:T(128)S(1)}, f32[128,1024]{1,0:T(8,128)S(1)}) fusion(bf16[128,1024]{1,0:T(8,128)(2,1)} %collective-permute-done.5, bf16[128,1024]{1,0:T(8,128)(2,1)} %collective-permute-done.4, bf16[128,1024]{1,0:T(8,128)(2,1)} %collective-permute-done.3, bf16[128,1024]{1,0:T(8,128)(2,1)S(1)} %copy-done.3, ...), kind=kOutput, calls=%fused_computation.113 | convolution fusion | flops 68419456 | bytes 2163200 | tf_op jit(solution)/shard_map/dot_general | solution.py:186
  67.0 0.9 concatenate.43
  67.9 0.9 collective-permute-start.8
  69.5 2.0 %collective-permute-start.6 = (bf16[128,1152]{1,0:T(8,128)(2,1)}, bf16[128,1152]{1,0:T(8,128)(2,1)}, u32[]{:S(2)}, u32[]{:S(2)}) collective-permute-start(bf16[128,1152]{1,0:T(8,128)(2,1)} %concatenate.43), channel_id=1, source_target_pairs={{0,1},{1,2},{2,3},{3,0},{4,5},{5,6},{6,7},{7,4},{8,9},{9,10},{10,1... | collective-permute-start | bytes 884744 | tf_op jit(solution)/shard_map/ppermute | solution.py:111
  71.5 0.9 compare_bitcast_fusion.1
  72.5 1.0 fusion.83
  73.9 6.0 %fusion.184 = f32[8,64,512]{2,1,0:T(8,128)} fusion(bf16[8,64,1024]{2,1,0:T(8,128)(2,1)S(1)} %convolution_convert_fusion.1, bf16[8,1024,512]{2,1,0:T(8,128)(2,1)} %param.22), kind=kOutput, calls=%fused_computation.251 | convolution fusion | flops 536870912 | bytes 10485760 | tf_op jit(solution)/shard_map/esd,edf->esf/dot_general | solution.py:89
  79.9 10.1 %convolution_convert_fusion = bf16[8,64,1024]{2,1,0:T(8,128)(2,1)} fusion(bf16[8,512,1024]{2,1,0:T(8,128)(2,1)} %param.24, bf16[8,64,1024]{2,1,0:T(8,128)(2,1)S(1)} %convolution_convert_fusion.1, bf16[8,1024,512]{2,1,0:T(8,128)(2,1)} %param.23, f32[8,64,512]{2,1,0:T(8,128)} %fusion.184), kind=kOutput, calls=%fused_computation.21 | convolution fusion | flops 1075838976 | bytes 19922944 | tf_op jit(solution)/shard_map/esf,efd->esd/dot_general | solution.py:99
  90.0 0.9 dynamic-slice_bitcast_fusion.3
  91.0 1.6 %convolution_bitcast_fusion = f32[128,1024]{1,0:T(8,128)S(1)} fusion(bf16[8,64,1024]{2,1,0:T(8,128)(2,1)} %convolution_convert_fusion, s32[8,128]{1,0:T(8,128)S(1)} %fusion.83, pred[8,128]{1,0:T(8,128)(4,1)S(1)} %copy.81, bf16[8,128]{1,0:T(8,128)(2,1)S(1)} %copy.83), kind=kOutput, calls=%fused_computation.53 | convolution fusion | flops 134414336 | bytes 1580032 | tf_op jit(solution)/shard_map/est,esd->td/dot_general | solution.py:102
  93.2 1.0 constant_dynamic-update-slice_fusion.2
  94.2 1.7 %collective-permute-done.7 = bf16[128,1152]{1,0:T(8,128)(2,1)} collective-permute-done((bf16[128,1152]{1,0:T(8,128)(2,1)}, bf16[128,1152]{1,0:T(8,128)(2,1)}, u32[]{:S(2)}, u32[]{:S(2)}) %collective-permute-start.7) | collective-permute-done | bytes 294944 | tf_op jit(solution)/shard_map/ppermute | solution.py:111
  95.9 1.0 constant_dynamic-update-slice_fusion.1
  96.9 1.0 constant_dynamic-update-slice_fusion
  98.1 0.8 dynamic-slice_bitcast_fusion.1
  99.6 1.1 fusion.82
  100.7 2.6 %fusion.13 = bf16[8,192,1024]{2,1,0:T(8,128)(2,1)S(1)} fusion(s32[8,384]{1,0:T(8,128)S(1)} %fusion.82, pred[8,384]{1,0:T(8,128)(4,1)} %copy.84, bf16[384,1152]{1,0:T(8,128)(2,1)S(1)} %constant_dynamic-update-slice_fusion), kind=kOutput, calls=%fused_computation.14 | convolution fusion | flops 1210712064 | bytes 3947520 | tf_op jit(solution)/shard_map/est,td->esd/dot_general | solution.py:86
  103.3 5.4 %fusion.185 = f32[8,192,512]{2,1,0:T(8,128)S(1)} fusion(bf16[8,192,1024]{2,1,0:T(8,128)(2,1)S(1)} %fusion.13, bf16[8,1024,512]{2,1,0:T(8,128)(2,1)} %param.22), kind=kOutput, calls=%fused_computation.252 | convolution fusion | flops 1610612736 | bytes 14680064 | tf_op jit(solution)/shard_map/esd,edf->esf/dot_general | solution.py:89
  108.8 2.0 %multiply_convert_fusion = bf16[8,192,512]{2,1,0:T(8,128)(2,1)S(1)} fusion(f32[8,192,512]{2,1,0:T(8,128)S(1)} %fusion.185, bf16[8,192,1024]{2,1,0:T(8,128)(2,1)S(1)} %fusion.13, bf16[8,1024,512]{2,1,0:T(8,128)(2,1)S(1)} %bitcast.182), kind=kOutput, calls=%fused_computation.8 | convolution fusion | flops 1615331328 | bytes 16252928 | tf_op jit(solution)/shard_map/esd,edf->esf/dot_general | solution.py:90
  111.1 2.1 %fusion.19 = bf16[8,192,512]{2,1,0:T(8,128)(2,1)} fusion(bf16[8,192,512]{2,1,0:T(8,128)(2,1)S(1)} %multiply_convert_fusion, bf16[8,512,1024]{2,1,0:T(8,128)(2,1)S(1)} %bitcast.184), kind=kOutput, calls=%fused_computation.16 | convolution fusion | flops 806092800 | bytes 7340032 | tf_op jit(solution)/shard_map/esf,efd->esd/dot_general | solution.py:99
  113.2 2.1 %fusion.16 = bf16[8,192,512]{2,1,0:T(8,128)(2,1)} fusion(bf16[8,192,512]{2,1,0:T(8,128)(2,1)S(1)} %multiply_convert_fusion, bf16[8,512,1024]{2,1,0:T(8,128)(2,1)S(1)} %bitcast.184), kind=kOutput, calls=%fused_computation.15 | convolution fusion | flops 806092800 | bytes 7340032 | tf_op jit(solution)/shard_map/esf,efd->esd/dot_general | solution.py:99
  115.5 2.4 %fusion.47 = f32[384,512]{1,0:T(8,128)S(1)} fusion(bf16[8,192,512]{2,1,0:T(8,128)(2,1)} %fusion.16, s32[8,384]{1,0:T(8,128)S(1)} %fusion.82, pred[8,384]{1,0:T(8,128)(4,1)S(1)} %copy-done.21, bf16[8,384]{1,0:T(8,128)(2,1)S(1)} %copy.86), kind=kOutput, calls=%fused_computation.45 | convolution fusion | flops 605749248 | bytes 2380800 | tf_op jit(solution)/shard_map/est,esd->td/dot_general | solution.py:102
  117.9 1.1 fusion.65
  119.2 1.9 %collective-permute-start.11 = (bf16[128,512]{1,0:T(8,128)(2,1)S(1)}, bf16[128,512]{1,0:T(8,128)(2,1)S(1)}, u32[]{:S(2)}, u32[]{:S(2)}) collective-permute-start(bf16[128,512]{1,0:T(8,128)(2,1)S(1)} %get-tuple-element.25), channel_id=1, source_target_pairs={{0,1},{1,2},{2,3},{3,0},{4,5},{5,6},{6,7},{7,4},{8,9},{9,10},{10,1... | collective-permute-start | bytes 393224 | tf_op jit(solution)/shard_map/ppermute | solution.py:111
  121.1 1.5 %collective-permute-start.10 = (bf16[128,512]{1,0:T(8,128)(2,1)S(1)}, bf16[128,512]{1,0:T(8,128)(2,1)S(1)}, u32[]{:S(2)}, u32[]{:S(2)}) collective-permute-start(bf16[128,512]{1,0:T(8,128)(2,1)S(1)} %get-tuple-element.26), channel_id=1, source_target_pairs={{0,2},{1,3},{2,0},{3,1},{4,6},{5,7},{6,4},{7,5},{8,10},{9,11},{10,... | collective-permute-start | bytes 393224 | tf_op jit(solution)/shard_map/ppermute | solution.py:111
  122.6 0.8 fusion.50
  123.4 0.8 fusion.68
  124.3 1.0 collective-permute-start.12
  125.3 1.1 collective-permute-start.14
  126.4 1.4 collective-permute-start.13
  127.9 1.4 collective-permute-done.11
  129.3 4.7 %collective-permute-done.10 = bf16[128,512]{1,0:T(8,128)(2,1)S(1)} collective-permute-done((bf16[128,512]{1,0:T(8,128)(2,1)S(1)}, bf16[128,512]{1,0:T(8,128)(2,1)S(1)}, u32[]{:S(2)}, u32[]{:S(2)}) %collective-permute-start.10) | collective-permute-done | bytes 131104 | tf_op jit(solution)/shard_map/ppermute | solution.py:111
  134.0 3.7 %collective-permute-done.14 = bf16[128,512]{1,0:T(8,128)(2,1)S(1)} collective-permute-done((bf16[128,512]{1,0:T(8,128)(2,1)S(1)}, bf16[128,512]{1,0:T(8,128)(2,1)S(1)}, u32[]{:S(2)}, u32[]{:S(2)}) %collective-permute-start.14) | collective-permute-done | bytes 131104 | tf_op jit(solution)/shard_map/ppermute | solution.py:111
  137.8 6.2 %collective-permute-done.13 = bf16[128,512]{1,0:T(8,128)(2,1)S(1)} collective-permute-done((bf16[128,512]{1,0:T(8,128)(2,1)S(1)}, bf16[128,512]{1,0:T(8,128)(2,1)S(1)}, u32[]{:S(2)}, u32[]{:S(2)}) %collective-permute-start.13) | collective-permute-done | bytes 131104 | tf_op jit(solution)/shard_map/ppermute | solution.py:111
  144.0 1.1 fusion.104
  (142 shorter events, 14.9 us)
Async XLA Ops:
  0.6 7.2 %copy-start = (bf16[1024,1024]{1,0:T(8,128)(2,1)S(1)}, bf16[1024,1024]{1,0:T(8,128)(2,1)}, u32[]{:S(2)}) copy-start(bf16[1024,1024]{1,0:T(8,128)(2,1)} %param.16) | copy-start | bytes 6291460
  0.6 7.2 %copy-start.3 = (bf16[128,1024]{1,0:T(8,128)(2,1)S(1)}, bf16[128,1024]{1,0:T(8,128)(2,1)}, u32[]{:S(2)}) copy-start(bf16[128,1024]{1,0:T(8,128)(2,1)} %param.14) | copy-start | bytes 786436
  8.8 8.2 %copy-start.17 = (s32[1,512]{1,0:T(1,128)S(1)}, s32[1,512]{1,0:T(1,128)}, u32[]{:S(2)}) copy-start(s32[1,512]{1,0:T(1,128)} %param.25) | copy-start | bytes 6148
  8.9 8.2 %copy-start.22 = (s32[1,512]{1,0:T(1,128)S(1)}, s32[1,512]{1,0:T(1,128)}, u32[]{:S(2)}) copy-start(s32[1,512]{1,0:T(1,128)} %param.26) | copy-start | bytes 6148
  8.9 8.2 %copy-start.16 = (s32[128,8]{0,1:T(8,128)S(1)}, s32[128,8]{0,1:T(8,128)}, u32[]{:S(2)}) copy-start(s32[128,8]{0,1:T(8,128)} %param.27) | copy-start | bytes 12292
  10.1 14.7 %collective-permute-start.2 = (bf16[128,2,256]{0,2,1:T(8,128)(2,1)}, bf16[128,2,256]{0,2,1:T(8,128)(2,1)S(1)}, u32[]{:S(2)}, u32[]{:S(2)}) collective-permute-start(bf16[128,2,256]{0,2,1:T(8,128)(2,1)} %get-tuple-element.21), channel_id=1, source_target_pairs={{0,3},{1,0},{2,1},{3,2},{4,7},{5,4},{6,5},{7,6},{8,11},{9,8},{10,9... | collective-permute-start | bytes 393224 | tf_op jit(solution)/shard_map/ppermute | solution.py:111
  15.2 11.3 %collective-permute-start.1 = (bf16[128,2,256]{0,2,1:T(8,128)(2,1)S(1)}, bf16[128,2,256]{0,2,1:T(8,128)(2,1)S(1)}, u32[]{:S(2)}, u32[]{:S(2)}) collective-permute-start(bf16[128,2,256]{0,2,1:T(8,128)(2,1)S(1)} %get-tuple-element.22), channel_id=1, source_target_pairs={{0,2},{1,3},{2,0},{3,1},{4,6},{5,7},{6,4},{7,5},{8,10},{9,11},{10,... | collective-permute-start | bytes 393224 | tf_op jit(solution)/shard_map/ppermute | solution.py:111
  15.2 9.6 %collective-permute-start = (bf16[128,2,256]{0,2,1:T(8,128)(2,1)}, bf16[128,2,256]{0,2,1:T(8,128)(2,1)S(1)}, u32[]{:S(2)}, u32[]{:S(2)}) collective-permute-start(bf16[128,2,256]{0,2,1:T(8,128)(2,1)} %get-tuple-element.23), channel_id=1, source_target_pairs={{0,1},{1,2},{2,3},{3,0},{4,5},{5,6},{6,7},{7,4},{8,9},{9,10},{10,1... | collective-permute-start | bytes 393224 | tf_op jit(solution)/shard_map/ppermute | solution.py:111
  22.5 6.6 %copy-start.10 = (pred[128,512]{0,1:T(8,128)(4,1)S(1)}, pred[128,512]{0,1:T(8,128)(4,1)}, u32[]{:S(2)}) copy-start(pred[128,512]{0,1:T(8,128)(4,1)} %get-tuple-element.34) | copy-start | bytes 196612
  22.5 8.0 %copy-start.9 = (pred[128,512]{0,1:T(8,128)(4,1)S(1)}, pred[128,512]{0,1:T(8,128)(4,1)}, u32[]{:S(2)}) copy-start(pred[128,512]{0,1:T(8,128)(4,1)} %get-tuple-element.35) | copy-start | bytes 196612
  29.1 3.3 %copy-start.8 = (pred[128,512]{0,1:T(8,128)(4,1)S(1)}, pred[128,512]{0,1:T(8,128)(4,1)}, u32[]{:S(2)}) copy-start(pred[128,512]{0,1:T(8,128)(4,1)} %get-tuple-element.36) | copy-start | bytes 196612
  34.3 2.7 %copy-start.2 = (bf16[256,1024]{1,0:T(8,128)(2,1)S(1)}, bf16[256,1024]{1,0:T(8,128)(2,1)}, u32[]{:S(2)}) copy-start(bf16[256,1024]{1,0:T(8,128)(2,1)} %param.19) | copy-start | bytes 1572868
  38.8 22.1 %collective-permute-start.3 = (bf16[128,1024]{1,0:T(8,128)(2,1)}, bf16[128,1024]{1,0:T(8,128)(2,1)}, u32[]{:S(2)}, u32[]{:S(2)}) collective-permute-start(bf16[128,1024]{1,0:T(8,128)(2,1)} %convolution_convert_fusion.5), channel_id=1, source_target_pairs={{0,3},{1,0},{2,1},{3,2},{4,7},{5,4},{6,5},{7,6},{8,11},{9,8},{10,9... | collective-permute-start | bytes 786440 | tf_op jit(solution)/shard_map/ppermute | solution.py:111
  44.9 9.6 %copy-start.23 = (s32[512]{0:T(512)S(1)}, s32[512]{0:T(512)}, u32[]{:S(2)}) copy-start(s32[512]{0:T(512)} %pad_add_fusion.2) | copy-start | bytes 6148
  44.9 19.1 %collective-permute-start.4 = (bf16[128,1024]{1,0:T(8,128)(2,1)}, bf16[128,1024]{1,0:T(8,128)(2,1)}, u32[]{:S(2)}, u32[]{:S(2)}) collective-permute-start(bf16[128,1024]{1,0:T(8,128)(2,1)} %convolution_convert_fusion.4), channel_id=1, source_target_pairs={{0,2},{1,3},{2,0},{3,1},{4,6},{5,7},{6,4},{7,5},{8,10},{9,11},{10,... | collective-permute-start | bytes 786440 | tf_op jit(solution)/shard_map/ppermute | solution.py:111
  50.2 13.8 %collective-permute-start.5 = (bf16[128,1024]{1,0:T(8,128)(2,1)}, bf16[128,1024]{1,0:T(8,128)(2,1)}, u32[]{:S(2)}, u32[]{:S(2)}) collective-permute-start(bf16[128,1024]{1,0:T(8,128)(2,1)} %convolution_convert_fusion.3), channel_id=1, source_target_pairs={{0,1},{1,2},{2,3},{3,0},{4,5},{5,6},{6,7},{7,4},{8,9},{9,10},{10,1... | collective-permute-start | bytes 786440 | tf_op jit(solution)/shard_map/ppermute | solution.py:111
  55.5 3.4 %copy-start.11 = (bf16[512,2,64,1]{0,2,3,1:T(8,128)(2,1)S(1)}, bf16[512,2,64,1]{0,2,3,1:T(8,128)(2,1)}, u32[]{:S(2)}) copy-start(bf16[512,2,64,1]{0,2,3,1:T(8,128)(2,1)} %get-tuple-element.19) | copy-start | bytes 393220
  60.8 5.6 %copy-start.13 = (bf16[1024,32]{0,1:T(8,128)(2,1)S(1)}, bf16[1024,32]{0,1:T(8,128)(2,1)}, u32[]{:S(2)}) copy-start(bf16[1024,32]{0,1:T(8,128)(2,1)} %param.21) | copy-start | bytes 196612
  60.9 6.2 %copy-start.12 = (bf16[128,32]{1,0:T(8,128)(2,1)S(1)}, bf16[128,32]{1,0:T(8,128)(2,1)}, u32[]{:S(2)}) copy-start(bf16[128,32]{1,0:T(8,128)(2,1)} %copy.80) | copy-start | bytes 24580
  60.9 11.6 %copy-start.24 = (s32[128]{0:T(128)S(1)}, s32[128]{0:T(128)}, u32[]{:S(2)}) copy-start(s32[128]{0:T(128)} %get-tuple-element.52) | copy-start | bytes 1540
  60.9 11.6 %copy-start.25 = (s32[128]{0:T(128)S(1)}, s32[128]{0:T(128)}, u32[]{:S(2)}) copy-start(s32[128]{0:T(128)} %get-tuple-element.53) | copy-start | bytes 1540
  65.5 0.8 copy-start.4
  67.9 29.0 %collective-permute-start.8 = (bf16[128,1152]{1,0:T(8,128)(2,1)}, bf16[128,1152]{1,0:T(8,128)(2,1)}, u32[]{:S(2)}, u32[]{:S(2)}) collective-permute-start(bf16[128,1152]{1,0:T(8,128)(2,1)} %concatenate.43), channel_id=1, source_target_pairs={{0,3},{1,0},{2,1},{3,2},{4,7},{5,4},{6,5},{7,6},{8,11},{9,8},{10,9... | collective-permute-start | bytes 884744 | tf_op jit(solution)/shard_map/ppermute | solution.py:111
  68.8 27.1 %collective-permute-start.7 = (bf16[128,1152]{1,0:T(8,128)(2,1)}, bf16[128,1152]{1,0:T(8,128)(2,1)}, u32[]{:S(2)}, u32[]{:S(2)}) collective-permute-start(bf16[128,1152]{1,0:T(8,128)(2,1)} %concatenate.43), channel_id=1, source_target_pairs={{0,2},{1,3},{2,0},{3,1},{4,6},{5,7},{6,4},{7,5},{8,10},{9,11},{10,... | collective-permute-start | bytes 884744 | tf_op jit(solution)/shard_map/ppermute | solution.py:111
  69.5 23.7 %collective-permute-start.6 = (bf16[128,1152]{1,0:T(8,128)(2,1)}, bf16[128,1152]{1,0:T(8,128)(2,1)}, u32[]{:S(2)}, u32[]{:S(2)}) collective-permute-start(bf16[128,1152]{1,0:T(8,128)(2,1)} %concatenate.43), channel_id=1, source_target_pairs={{0,1},{1,2},{2,3},{3,0},{4,5},{5,6},{6,7},{7,4},{8,9},{9,10},{10,1... | collective-permute-start | bytes 884744 | tf_op jit(solution)/shard_map/ppermute | solution.py:111
  72.4 18.5 %copy-start.18 = (pred[8,128]{1,0:T(8,128)(4,1)}, pred[8,128]{1,0:T(8,128)(4,1)S(1)}, u32[]{:S(2)}) copy-start(pred[8,128]{1,0:T(8,128)(4,1)S(1)} %copy.81) | copy-start | bytes 3076
  73.5 17.5 %copy-start.14 = (s32[8,128]{1,0:T(8,128)}, s32[8,128]{1,0:T(8,128)S(1)}, u32[]{:S(2)}) copy-start(s32[8,128]{1,0:T(8,128)S(1)} %fusion.83) | copy-start | bytes 12292
  100.6 8.1 %slice-start = ((s8[8388608]{0:T(1024)(128)(4,1)}), s8[4194304]{0:T(1024)(128)(4,1)S(1)}, s32[]{:S(2)}) async-start(s8[8388608]{0:T(1024)(128)(4,1)} %bitcast.181), calls=%async_computation | async-start | bytes 8388608
  103.3 5.5 %slice-start.1 = ((s8[8388608]{0:T(1024)(128)(4,1)}), s8[4194304]{0:T(1024)(128)(4,1)S(1)}, s32[]{:S(2)}) async-start(s8[8388608]{0:T(1024)(128)(4,1)} %bitcast.181), calls=%async_computation.1 | async-start | bytes 8388608
  103.3 7.4 %slice-start.2 = ((s8[8388608]{0:T(1024)(128)(4,1)}), s8[4194304]{0:T(1024)(128)(4,1)S(1)}, s32[]{:S(2)}) async-start(s8[8388608]{0:T(1024)(128)(4,1)} %bitcast.183), calls=%async_computation.2 | async-start | bytes 8388608
  108.8 2.3 %slice-start.3 = ((s8[8388608]{0:T(1024)(128)(4,1)}), s8[4194304]{0:T(1024)(128)(4,1)S(1)}, s32[]{:S(2)}) async-start(s8[8388608]{0:T(1024)(128)(4,1)} %bitcast.183), calls=%async_computation.3 | async-start | bytes 8388608
  113.2 2.1 %copy-start.7 = (bf16[8,384]{0,1:T(8,128)(2,1)S(1)}, bf16[8,384]{0,1:T(8,128)(2,1)}, u32[]{:S(2)}) copy-start(bf16[8,384]{0,1:T(8,128)(2,1)} %get-tuple-element.14) | copy-start | bytes 18436
  113.2 2.2 %copy-start.6 = (bf16[8,384]{0,1:T(8,128)(2,1)S(1)}, bf16[8,384]{0,1:T(8,128)(2,1)}, u32[]{:S(2)}) copy-start(bf16[8,384]{0,1:T(8,128)(2,1)} %get-tuple-element.15) | copy-start | bytes 18436
  113.2 2.3 %copy-start.21 = (pred[8,384]{1,0:T(8,128)(4,1)S(1)}, pred[8,384]{1,0:T(8,128)(4,1)}, u32[]{:S(2)}) copy-start(pred[8,384]{1,0:T(8,128)(4,1)} %copy.84) | copy-start | bytes 9220
  115.5 2.4 %copy-start.27 = (bf16[8,192,512]{2,1,0:T(8,128)(2,1)S(1)}, bf16[8,192,512]{2,1,0:T(8,128)(2,1)}, u32[]{:S(2)}) copy-start(bf16[8,192,512]{2,1,0:T(8,128)(2,1)} %fusion.16) | copy-start | bytes 4718596
  117.9 4.7 %copy-start.26 = (bf16[8,192,512]{2,1,0:T(8,128)(2,1)S(1)}, bf16[8,192,512]{2,1,0:T(8,128)(2,1)}, u32[]{:S(2)}) copy-start(bf16[8,192,512]{2,1,0:T(8,128)(2,1)} %fusion.19) | copy-start | bytes 4718596
  119.0 7.4 %collective-permute-start.9 = (bf16[128,512]{1,0:T(8,128)(2,1)S(1)}, bf16[128,512]{1,0:T(8,128)(2,1)S(1)}, u32[]{:S(2)}, u32[]{:S(2)}) collective-permute-start(bf16[128,512]{1,0:T(8,128)(2,1)S(1)} %get-tuple-element.24), channel_id=1, source_target_pairs={{0,3},{1,0},{2,1},{3,2},{4,7},{5,4},{6,5},{7,6},{8,11},{9,8},{10,9... | collective-permute-start | bytes 393224 | tf_op jit(solution)/shard_map/ppermute | solution.py:111
  119.2 10.1 %collective-permute-start.11 = (bf16[128,512]{1,0:T(8,128)(2,1)S(1)}, bf16[128,512]{1,0:T(8,128)(2,1)S(1)}, u32[]{:S(2)}, u32[]{:S(2)}) collective-permute-start(bf16[128,512]{1,0:T(8,128)(2,1)S(1)} %get-tuple-element.25), channel_id=1, source_target_pairs={{0,1},{1,2},{2,3},{3,0},{4,5},{5,6},{6,7},{7,4},{8,9},{9,10},{10,1... | collective-permute-start | bytes 393224 | tf_op jit(solution)/shard_map/ppermute | solution.py:111
  121.1 12.8 %collective-permute-start.10 = (bf16[128,512]{1,0:T(8,128)(2,1)S(1)}, bf16[128,512]{1,0:T(8,128)(2,1)S(1)}, u32[]{:S(2)}, u32[]{:S(2)}) collective-permute-start(bf16[128,512]{1,0:T(8,128)(2,1)S(1)} %get-tuple-element.26), channel_id=1, source_target_pairs={{0,2},{1,3},{2,0},{3,1},{4,6},{5,7},{6,4},{7,5},{8,10},{9,11},{10,... | collective-permute-start | bytes 393224 | tf_op jit(solution)/shard_map/ppermute | solution.py:111
  123.4 20.6 %copy-start.15 = (s32[8,128]{1,0:T(8,128)S(1)}, s32[8,128]{1,0:T(8,128)}, u32[]{:S(2)}) copy-start(s32[8,128]{1,0:T(8,128)} %copy-done.14) | copy-start | bytes 12292
  123.4 20.6 %copy-start.19 = (pred[8,128]{1,0:T(8,128)(4,1)S(1)}, pred[8,128]{1,0:T(8,128)(4,1)}, u32[]{:S(2)}) copy-start(pred[8,128]{1,0:T(8,128)(4,1)} %copy-done.18) | copy-start | bytes 3076
  123.4 20.6 %copy-start.20 = (bf16[8,128]{1,0:T(8,128)(2,1)S(1)}, bf16[8,128]{1,0:T(8,128)(2,1)}, u32[]{:S(2)}) copy-start(bf16[8,128]{1,0:T(8,128)(2,1)} %copy.82) | copy-start | bytes 6148
  124.3 19.7 %copy-start.1 = (bf16[8,64,1024]{2,1,0:T(8,128)(2,1)S(1)}, bf16[8,64,1024]{2,1,0:T(8,128)(2,1)}, u32[]{:S(2)}) copy-start(bf16[8,64,1024]{2,1,0:T(8,128)(2,1)} %convolution_convert_fusion) | copy-start | bytes 3145732
  124.3 19.7 %copy-start.5 = (f32[128,1024]{1,0:T(8,128)S(1)}, f32[128,1024]{1,0:T(8,128)}, u32[]{:S(2)}) copy-start(f32[128,1024]{1,0:T(8,128)} %copy-done.4) | copy-start | bytes 1572868
  124.3 9.7 %collective-permute-start.12 = (bf16[128,512]{1,0:T(8,128)(2,1)S(1)}, bf16[128,512]{1,0:T(8,128)(2,1)S(1)}, u32[]{:S(2)}, u32[]{:S(2)}) collective-permute-start(bf16[128,512]{1,0:T(8,128)(2,1)S(1)} %get-tuple-element.27), channel_id=1, source_target_pairs={{0,3},{1,0},{2,1},{3,2},{4,7},{5,4},{6,5},{7,6},{8,11},{9,8},{10,9... | collective-permute-start | bytes 393224 | tf_op jit(solution)/shard_map/ppermute | solution.py:111
  125.3 12.4 %collective-permute-start.14 = (bf16[128,512]{1,0:T(8,128)(2,1)S(1)}, bf16[128,512]{1,0:T(8,128)(2,1)S(1)}, u32[]{:S(2)}, u32[]{:S(2)}) collective-permute-start(bf16[128,512]{1,0:T(8,128)(2,1)S(1)} %get-tuple-element.28), channel_id=1, source_target_pairs={{0,1},{1,2},{2,3},{3,0},{4,5},{5,6},{6,7},{7,4},{8,9},{9,10},{10,1... | collective-permute-start | bytes 393224 | tf_op jit(solution)/shard_map/ppermute | solution.py:111
  126.4 17.5 %collective-permute-start.13 = (bf16[128,512]{1,0:T(8,128)(2,1)S(1)}, bf16[128,512]{1,0:T(8,128)(2,1)S(1)}, u32[]{:S(2)}, u32[]{:S(2)}) collective-permute-start(bf16[128,512]{1,0:T(8,128)(2,1)S(1)} %get-tuple-element.29), channel_id=1, source_target_pairs={{0,2},{1,3},{2,0},{3,1},{4,6},{5,7},{6,4},{7,5},{8,10},{9,11},{10,... | collective-permute-start | bytes 393224 | tf_op jit(solution)/shard_map/ppermute | solution.py:111

commit v7 on v6

--- a/solution.py
+++ b/solution.py
@@ -62,7 +62,7 @@
     return jnp.concatenate([normed2, high, low, named, fill], axis=1)
 
 
-def expert_mix(packed, sources, width, experts, w_gate, w_up, w_down, pieces):
+def expert_front(packed, sources, width, experts, w_gate, w_up):
     tokens_all = packed.shape[0]
     local = w_gate.shape[0]
     rows = tokens_all // sources
@@ -92,6 +92,10 @@
     zero = jnp.zeros((), jnp.bfloat16)
     high = jnp.where(picks, high.T[:, None, :], zero)
     low = jnp.where(picks, low.T[:, None, :], zero)
+    return hidden, high, low
+
+
+def expert_back(hidden, high, low, w_down, pieces):
     cut = w_down.shape[2] // pieces
     outs = []
     for piece in range(pieces):
@@ -177,23 +181,18 @@
         "rs,skd->rkd", placing.astype(jnp.bfloat16), keyval_heads, preferred_element_type=jnp.float32
     ).astype(jnp.bfloat16)
     seg_rows = step_rows(seg, rows)
-    attention = None
-    for step in list(range(1, owners)) + [0]:
-        picked = slice(step * rows, (step + 1) * rows)
-        heads_out = attend(
-            query_heads[picked], keyval_heads, seg_rows[picked], seg_rows, where_at[picked], where_at
-        )
-        block = jnp.dot(heads_out, w_out, preferred_element_type=jnp.float32)
-        if step:
-            block = shifted(block.astype(jnp.bfloat16), -step).astype(jnp.float32)
-        attention = block if attention is None else attention + block
+    heads_out = attend(query_heads, keyval_heads, seg_rows, seg_rows, where_at, where_at)
+    attention = jnp.dot(heads_out, w_out, preferred_element_type=jnp.float32).astype(jnp.bfloat16)
+    attention = exchange_sum(attention.reshape(owners, rows, width))
     resid = tokens.astype(jnp.float32) + attention
     normed2 = rms_scale(resid, norm_moe)
     packed = routing(normed2, expert_ids, w_router)
     experts = w_router.shape[1]
-    moe = expert_mix(packed, 1, width, experts, w_gate, w_up, w_down, 1)[0]
+    own = expert_front(packed, 1, width, experts, w_gate, w_up)
     received = jnp.concatenate([shifted(packed, step) for step in range(1, owners)])
-    pieces = expert_mix(received, owners - 1, width, experts, w_gate, w_up, w_down, 2)
+    others = expert_front(received, owners - 1, width, experts, w_gate, w_up)
+    pieces = expert_back(*others, w_down, 2)
+    own, pieces = lax.optimization_barrier((own, pieces))
     backs = []
     for piece in pieces:
         piece = piece.astype(jnp.bfloat16).reshape(owners - 1, rows, -1)
@@ -201,7 +200,7 @@
             shifted(piece[step - 1], -step).astype(jnp.float32) for step in range(1, owners)
         )
         backs.append(back)
-    moe = moe + jnp.concatenate(backs, axis=1)
+    moe = expert_back(*own, w_down, 1)[0] + jnp.concatenate(backs, axis=1)
     mixed = (resid + moe).astype(jnp.bfloat16)
     return (mixed, kv_cache)
 

time: 146 us -> 148 us (1.014)
  matrix products: 73.9 us -> 48 us
  waiting for transfers between devices: 24.9 us -> 50.2 us
  starting transfers between devices: 21.3 us -> 24.5 us
    ppermute x15, waiting for transfers between devices: 24.9 us -> 50.2 us  [shifted(): lax.ppermute(x, 'exp', [(j, (j + step) % count) for j in range(count)])]
    dot_general x24 -> x18, matrix products: 53.6 us -> 35.8 us  [the longest x2 10.4 us: expert_front(): jnp.einsum('esd,edf->esf', received, w_gate, preferred_element_type=jnp.f...]
    dot_general x4 -> x1, matrix products: 9.92 us -> 2.73 us  [attend(): jnp.einsum('kgqt,tkd->qkgd', probs, values, preferred_element_type=jnp.fl...]
    ppermute x15, starting transfers between devices: 21.3 us -> 24.5 us  [shifted(): lax.ppermute(x, 'exp', [(j, (j + step) % count) for j in range(count)])]
    unnamed x67 -> x47, local copies, waits for them, and re-layouts: 5.17 us -> 6.39 us
    sub x4 -> x1, matrix products: 4.52 us -> 3.58 us  [attend(): expo = jnp.exp(score - top)]
  transfers between devices with their start and end apart: 15 -> 15, of which waited for: 8 -> 9; matrix products, arithmetic and copies ran while one was open for 34% -> 15% of each run, Pallas kernels for 0% -> 0%
where the time goes in v7:
time: 148 us; the launch traced here: 147 us
  waiting for transfers between devices  50.2 us (34%)
  matrix products  48 us (32%)
  starting transfers between devices  24.5 us (17%)
  local copies, waits for them, and re-layouts  14.5 us (10%)
  other arithmetic  8.83 us (6%)
    ppermute x15, waiting for transfers between devices, shifted(): lax.ppermute(x, 'exp', [(j, (j + step) % count) for j in range(count)])  50.2 us
    ppermute x15, starting transfers between devices, shifted(): lax.ppermute(x, 'exp', [(j, (j + step) % count) for j in range(count)])  24.5 us
    dot_general x2, matrix products, expert_front(): jnp.einsum('esd,edf->esf', received, w_gate, preferred_element_type=jnp.f...  10.4 us
    dot_general x2, matrix products, expert_front(): jnp.einsum('esd,edf->esf', received, w_up, preferred_element_type=jnp.flo...  6.93 us
    unnamed x47, local copies, waits for them, and re-layouts  6.39 us
    dot_general x3, matrix products, expert_back(): jnp.einsum('esf,efd->esd', hidden, down, preferred_element_type=jnp.float32)  5.9 us
    sub x1, matrix products, attend(): expo = jnp.exp(score - top)  3.58 us
    dot_general x2, matrix products, expert_front(): jnp.einsum('est,td->esd', picks.astype(jnp.bfloat16), rows_all, preferred...  3.52 us
  transfers between devices with their start and end apart: 15, of which 9 were waited for; matrix products, arithmetic and copies ran while one was open for 15% of the time, Pallas kernels for 0%

profile of v7, /device:TPU:0, one launch (start us, length us, event | category | flops | bytes accessed | tf_op | source)
XLA Modules:
  0.0 147.4 jit_solution(6216923466673376617)
XLA Ops:
  0.7 0.9 compare_reduce_fusion
  1.7 1.1 fusion.78
  3.4 0.7 convert_element_type.130
  4.1 1.7 %convolution_convert_fusion.4 = bf16[128,512]{1,0:T(8,128)(2,1)S(1)} fusion(bf16[1024,512]{1,0:T(8,128)(2,1)} %param.18, bf16[128,1024]{1,0:T(8,128)(2,1)} %param.14, f32[1024]{0:T(1024)S(1)} %convert_element_type.130, f32[128]{0:T(128)S(1)} %add_rsqrt_fusion.1), kind=kOutput, calls=%fused_computation.52 | convolution fusion | flops 134807552 | bytes 1446400 | tf_op jit(solution)/shard_map/dot_general | solution.py:163
  5.9 1.9 %fusion.127 = f32[128,512]{0,1:T(8,128)S(1)} fusion(bf16[1024,512]{1,0:T(8,128)(2,1)} %param.17, bf16[128,1024]{1,0:T(8,128)(2,1)} %param.14, f32[1024]{0:T(1024)S(1)} %convert_element_type.130, f32[128]{0:T(128)S(1)} %add_rsqrt_fusion.1), kind=kOutput, calls=%fused_computation.186 | convolution fusion | flops 134742016 | bytes 1577472 | tf_op jit(solution)/shard_map/dot_general | solution.py:160
  7.9 1.0 fusion.129
  9.4 5.1 %collective-permute-start.2 = (bf16[128,2,256]{0,2,1:T(8,128)(2,1)S(1)}, bf16[128,2,256]{0,2,1:T(8,128)(2,1)S(1)}, u32[]{:S(2)}, u32[]{:S(2)}) collective-permute-start(bf16[128,2,256]{0,2,1:T(8,128)(2,1)S(1)} %get-tuple-element.32), channel_id=1, source_target_pairs={{0,3},{1,0},{2,1},{3,2},{4,7},{5,4},{6,5},{7,6},{8,11},{9,8},{10,9... | collective-permute-start | bytes 393224 | tf_op jit(solution)/shard_map/ppermute | solution.py:115
  14.5 1.0 collective-permute-start
  15.5 0.6 add_select_fusion
  16.8 1.6 %collective-permute-done.2 = bf16[128,2,256]{0,2,1:T(8,128)(2,1)S(1)} collective-permute-done((bf16[128,2,256]{0,2,1:T(8,128)(2,1)S(1)}, bf16[128,2,256]{0,2,1:T(8,128)(2,1)S(1)}, u32[]{:S(2)}, u32[]{:S(2)}) %collective-permute-start.2) | collective-permute-done | bytes 131104 | tf_op jit(solution)/shard_map/ppermute | solution.py:115
  18.4 7.3 %collective-permute-done.1 = bf16[128,2,256]{0,2,1:T(8,128)(2,1)S(1)} collective-permute-done((bf16[128,2,256]{0,2,1:T(8,128)(2,1)S(1)}, bf16[128,2,256]{0,2,1:T(8,128)(2,1)S(1)}, u32[]{:S(2)}, u32[]{:S(2)}) %collective-permute-start.1) | collective-permute-done | bytes 131104 | tf_op jit(solution)/shard_map/ppermute | solution.py:115
  25.7 0.7 copy-done.5
  26.4 1.0 pad_maximum_fusion.1
  27.4 3.6 %fusion.134 = (f32[2,2,512]{2,1,0:T(2,128)S(1)}, f32[2,2,512,512]{2,3,1,0:T(8,128)}) fusion(pred[512,512]{0,1:T(8,128)(4,1)S(1)} %compare_and_fusion, bf16[512,2,2,64]{0,3,2,1:T(8,128)(2,1)S(1)} %bitcast.137, bf16[512,2,256]{0,2,1:T(8,128)(2,1)S(1)} %pad_maximum_fusion.1), kind=kOutput, calls=%fused_computation.191 | convolution fusion | flops 138412544 | bytes 4857856 | tf_op jit(solution)/shard_map/sub | solution.py:44
  31.0 2.7 %fusion.52 = bf16[2,64,2,512]{3,1,2,0:T(8,128)(2,1)S(1)} fusion(f32[2,2,512,512]{2,3,1,0:T(8,128)} %get-tuple-element.58, f32[2,2,512]{2,1,0:T(2,128)S(1)} %get-tuple-element.57, bf16[512,2,256]{0,2,1:T(8,128)(2,1)S(1)} %pad_maximum_fusion.1), kind=kOutput, calls=%fused_computation.41 | convolution fusion | flops 136445952 | bytes 4595712 | tf_op jit(solution)/shard_map/kgqt,tkd->qkgd/dot_general | solution.py:46
  34.2 1.0 copy-done.2
  35.2 0.9 fusion.131
  36.1 1.5 %collective-permute-start.3 = (bf16[128,1024]{1,0:T(8,128)(2,1)}, bf16[128,1024]{1,0:T(8,128)(2,1)S(1)}, u32[]{:S(2)}, u32[]{:S(2)}) collective-permute-start(bf16[128,1024]{1,0:T(8,128)(2,1)} %get-tuple-element.24), channel_id=1, source_target_pairs={{0,3},{1,0},{2,1},{3,2},{4,7},{5,4},{6,5},{7,6},{8,11},{9,8},{10,9... | collective-permute-start | bytes 786440 | tf_op jit(solution)/shard_map/ppermute | solution.py:115
  37.6 0.5 collective-permute-start.5
  38.1 2.6 %collective-permute-start.4 = (bf16[128,1024]{1,0:T(8,128)(2,1)}, bf16[128,1024]{1,0:T(8,128)(2,1)}, u32[]{:S(2)}, u32[]{:S(2)}) collective-permute-start(bf16[128,1024]{1,0:T(8,128)(2,1)} %get-tuple-element.26), channel_id=1, source_target_pairs={{0,2},{1,3},{2,0},{3,1},{4,6},{5,7},{6,4},{7,5},{8,10},{9,11},{10,... | collective-permute-start | bytes 786440 | tf_op jit(solution)/shard_map/ppermute | solution.py:115
  40.7 0.6 and_select_fusion
  41.3 0.7 copy.68
  42.4 1.0 copy.76
  43.4 1.4 collective-permute-done.3
  44.9 8.4 %collective-permute-done.5 = bf16[128,1024]{1,0:T(8,128)(2,1)S(1)} collective-permute-done((bf16[128,1024]{1,0:T(8,128)(2,1)}, bf16[128,1024]{1,0:T(8,128)(2,1)S(1)}, u32[]{:S(2)}, u32[]{:S(2)}) %collective-permute-start.5) | collective-permute-done | bytes 262176 | tf_op jit(solution)/shard_map/ppermute | solution.py:115
  53.2 8.4 %collective-permute-done.4 = bf16[128,1024]{1,0:T(8,128)(2,1)} collective-permute-done((bf16[128,1024]{1,0:T(8,128)(2,1)}, bf16[128,1024]{1,0:T(8,128)(2,1)}, u32[]{:S(2)}, u32[]{:S(2)}) %collective-permute-start.4) | collective-permute-done | bytes 262176 | tf_op jit(solution)/shard_map/ppermute | solution.py:115
  61.6 1.3 multiply_reduce_fusion
  63.1 1.0 fusion.135
  64.5 0.8 concatenate.43
  65.4 1.6 %collective-permute-start.8 = (bf16[128,1152]{1,0:T(8,128)(2,1)}, bf16[128,1152]{1,0:T(8,128)(2,1)}, u32[]{:S(2)}, u32[]{:S(2)}) collective-permute-start(bf16[128,1152]{1,0:T(8,128)(2,1)} %concatenate.43), channel_id=1, source_target_pairs={{0,3},{1,0},{2,1},{3,2},{4,7},{5,4},{6,5},{7,6},{8,11},{9,8},{10,9... | collective-permute-start | bytes 884744 | tf_op jit(solution)/shard_map/ppermute | solution.py:115
  67.0 0.6 collective-permute-start.6
  67.6 0.9 compare_bitcast_fusion.1
  68.5 1.0 fusion.64
  70.0 5.0 %fusion.136 = f32[8,64,512]{2,1,0:T(8,128)S(1)} fusion(bf16[8,64,1024]{2,1,0:T(8,128)(2,1)S(1)} %convolution_convert_fusion.1, bf16[8,1024,512]{2,1,0:T(8,128)(2,1)} %param.22), kind=kOutput, calls=%fused_computation.193 | convolution fusion | flops 536870912 | bytes 10485760 | tf_op jit(solution)/shard_map/esd,edf->esf/dot_general | solution.py:89
  75.0 5.0 %fusion.32 = bf16[8,64,512]{2,1,0:T(8,128)(2,1)S(1)} fusion(bf16[8,64,1024]{2,1,0:T(8,128)(2,1)S(1)} %convolution_convert_fusion.1, bf16[8,1024,512]{2,1,0:T(8,128)(2,1)} %param.23, f32[8,64,512]{2,1,0:T(8,128)S(1)} %fusion.136), kind=kOutput, calls=%fused_computation.30 | convolution fusion | flops 538443776 | bytes 11010048 | tf_op jit(solution)/shard_map/esd,edf->esf/dot_general | solution.py:90
  80.0 0.9 dynamic-slice_bitcast_fusion.2
  81.2 6.1 %collective-permute-done.6 = bf16[128,1152]{1,0:T(8,128)(2,1)} collective-permute-done((bf16[128,1152]{1,0:T(8,128)(2,1)}, bf16[128,1152]{1,0:T(8,128)(2,1)}, u32[]{:S(2)}, u32[]{:S(2)}) %collective-permute-start.6) | collective-permute-done | bytes 294944 | tf_op jit(solution)/shard_map/ppermute | solution.py:115
  87.2 1.0 constant_dynamic-update-slice_fusion.2
  88.2 3.6 %collective-permute-done.7 = bf16[128,1152]{1,0:T(8,128)(2,1)} collective-permute-done((bf16[128,1152]{1,0:T(8,128)(2,1)}, bf16[128,1152]{1,0:T(8,128)(2,1)}, u32[]{:S(2)}, u32[]{:S(2)}) %collective-permute-start.7) | collective-permute-done | bytes 294944 | tf_op jit(solution)/shard_map/ppermute | solution.py:115
  91.8 1.0 constant_dynamic-update-slice_fusion.1
  92.8 1.0 constant_dynamic-update-slice_fusion
  93.9 0.8 copy-done.4
  94.7 0.8 dynamic-slice_bitcast_fusion.1
  95.5 0.7 copy.72
  96.2 1.2 fusion.63
  97.4 3.1 %fusion.11 = bf16[8,192,1024]{2,1,0:T(8,128)(2,1)S(1)} fusion(s32[8,384]{1,0:T(8,128)S(1)} %fusion.63, pred[8,384]{1,0:T(8,128)(4,1)} %copy.72, bf16[384,1152]{1,0:T(8,128)(2,1)} %copy-done.4), kind=kOutput, calls=%fused_computation.15 | convolution fusion | flops 1210712064 | bytes 3947520 | tf_op jit(solution)/shard_map/est,td->esd/dot_general | solution.py:86
  100.6 5.4 %fusion.137 = f32[8,192,512]{2,1,0:T(8,128)S(1)} fusion(bf16[8,192,1024]{2,1,0:T(8,128)(2,1)S(1)} %fusion.11, bf16[8,1024,512]{2,1,0:T(8,128)(2,1)} %param.22), kind=kOutput, calls=%fused_computation.194 | convolution fusion | flops 1610612736 | bytes 14680064 | tf_op jit(solution)/shard_map/esd,edf->esf/dot_general | solution.py:89
  106.0 2.0 %multiply_convert_fusion = bf16[8,192,512]{2,1,0:T(8,128)(2,1)S(1)} fusion(f32[8,192,512]{2,1,0:T(8,128)S(1)} %fusion.137, bf16[8,192,1024]{2,1,0:T(8,128)(2,1)S(1)} %fusion.11, bf16[8,1024,512]{2,1,0:T(8,128)(2,1)S(1)} %bitcast.139), kind=kOutput, calls=%fused_computation.9 | convolution fusion | flops 1615331328 | bytes 16252928 | tf_op jit(solution)/shard_map/esd,edf->esf/dot_general | solution.py:90
  108.3 2.2 %fusion.21 = bf16[8,192,512]{2,1,0:T(8,128)(2,1)} fusion(bf16[8,192,512]{2,1,0:T(8,128)(2,1)S(1)} %multiply_convert_fusion, bf16[8,512,1024]{2,1,0:T(8,128)(2,1)S(1)} %bitcast.129), kind=kOutput, calls=%fused_computation.21 | convolution fusion | flops 806092800 | bytes 7340032 | tf_op jit(solution)/shard_map/esf,efd->esd/dot_general | solution.py:103
  110.4 2.1 %fusion.18 = bf16[8,192,512]{2,1,0:T(8,128)(2,1)} fusion(bf16[8,192,512]{2,1,0:T(8,128)(2,1)S(1)} %multiply_convert_fusion, bf16[8,512,1024]{2,1,0:T(8,128)(2,1)S(1)} %bitcast.129), kind=kOutput, calls=%fused_computation.20 | convolution fusion | flops 806092800 | bytes 7340032 | tf_op jit(solution)/shard_map/esf,efd->esd/dot_general | solution.py:103
  112.6 1.0 copy.73
  113.6 2.4 %fusion.33 = f32[384,512]{1,0:T(8,128)S(1)} fusion(bf16[8,192,512]{2,1,0:T(8,128)(2,1)} %fusion.18, s32[8,384]{1,0:T(8,128)S(1)} %fusion.63, pred[8,384]{1,0:T(8,128)(4,1)S(1)} %copy-done.9, bf16[8,384]{1,0:T(8,128)(2,1)S(1)} %copy.74), kind=kOutput, calls=%fused_computation.31 | convolution fusion | flops 605749248 | bytes 2380800 | tf_op jit(solution)/shard_map/est,esd->td/dot_general | solution.py:106
  116.0 0.8 fusion.36
  116.8 0.6 copy-done.15
  117.4 0.8 fusion.48
  118.2 1.1 fusion.45
  119.4 4.5 %collective-permute-start.10 = (bf16[128,512]{1,0:T(8,128)(2,1)S(1)}, bf16[128,512]{1,0:T(8,128)(2,1)S(1)}, u32[]{:S(2)}, u32[]{:S(2)}) collective-permute-start(bf16[128,512]{1,0:T(8,128)(2,1)S(1)} %get-tuple-element.36), channel_id=1, source_target_pairs={{0,2},{1,3},{2,0},{3,1},{4,6},{5,7},{6,4},{7,5},{8,10},{9,11},{10,... | collective-permute-start | bytes 393224 | tf_op jit(solution)/shard_map/ppermute | solution.py:115
  123.9 1.9 %collective-permute-start.11 = (bf16[128,512]{1,0:T(8,128)(2,1)S(1)}, bf16[128,512]{1,0:T(8,128)(2,1)S(1)}, u32[]{:S(2)}, u32[]{:S(2)}) collective-permute-start(bf16[128,512]{1,0:T(8,128)(2,1)S(1)} %get-tuple-element.37), channel_id=1, source_target_pairs={{0,1},{1,2},{2,3},{3,0},{4,5},{5,6},{6,7},{7,4},{8,9},{9,10},{10,1... | collective-permute-start | bytes 393224 | tf_op jit(solution)/shard_map/ppermute | solution.py:115
  125.9 1.9 %collective-permute-start.12 = (bf16[128,512]{1,0:T(8,128)(2,1)S(1)}, bf16[128,512]{1,0:T(8,128)(2,1)S(1)}, u32[]{:S(2)}, u32[]{:S(2)}) collective-permute-start(bf16[128,512]{1,0:T(8,128)(2,1)S(1)} %get-tuple-element.38), channel_id=1, source_target_pairs={{0,3},{1,0},{2,1},{3,2},{4,7},{5,4},{6,5},{7,6},{8,11},{9,8},{10,9... | collective-permute-start | bytes 393224 | tf_op jit(solution)/shard_map/ppermute | solution.py:115
  127.8 1.6 %convolution_convert_fusion = bf16[8,64,1024]{2,1,0:T(8,128)(2,1)S(1)} fusion(bf16[8,64,512]{2,1,0:T(8,128)(2,1)S(1)} %fusion.32, bf16[8,512,1024]{2,1,0:T(8,128)(2,1)S(1)} %bitcast.131), kind=kOutput, calls=%fused_computation.22 | convolution fusion | flops 537395200 | bytes 9961472 | tf_op jit(solution)/shard_map/esf,efd->esd/dot_general | solution.py:103
  129.8 3.1 %collective-permute-start.14 = (bf16[128,512]{1,0:T(8,128)(2,1)S(1)}, bf16[128,512]{1,0:T(8,128)(2,1)S(1)}, u32[]{:S(2)}, u32[]{:S(2)}) collective-permute-start(bf16[128,512]{1,0:T(8,128)(2,1)S(1)} %get-tuple-element.40), channel_id=1, source_target_pairs={{0,1},{1,2},{2,3},{3,0},{4,5},{5,6},{6,7},{7,4},{8,9},{9,10},{10,1... | collective-permute-start | bytes 393224 | tf_op jit(solution)/shard_map/ppermute | solution.py:115
  132.9 9.3 %collective-permute-done.10 = bf16[128,512]{1,0:T(8,128)(2,1)S(1)} collective-permute-done((bf16[128,512]{1,0:T(8,128)(2,1)S(1)}, bf16[128,512]{1,0:T(8,128)(2,1)S(1)}, u32[]{:S(2)}, u32[]{:S(2)}) %collective-permute-start.10) | collective-permute-done | bytes 131104 | tf_op jit(solution)/shard_map/ppermute | solution.py:115
  142.3 4.0 %collective-permute-done.13 = bf16[128,512]{1,0:T(8,128)(2,1)S(1)} collective-permute-done((bf16[128,512]{1,0:T(8,128)(2,1)S(1)}, bf16[128,512]{1,0:T(8,128)(2,1)S(1)}, u32[]{:S(2)}, u32[]{:S(2)}) %collective-permute-start.13) | collective-permute-done | bytes 131104 | tf_op jit(solution)/shard_map/ppermute | solution.py:115
  146.4 1.0 fusion.82
  (111 shorter events, 5.2 us)
Async XLA Ops:
  0.6 7.2 %copy-start = (bf16[1024,1024]{1,0:T(8,128)(2,1)S(1)}, bf16[1024,1024]{1,0:T(8,128)(2,1)}, u32[]{:S(2)}) copy-start(bf16[1024,1024]{1,0:T(8,128)(2,1)} %param.16) | copy-start | bytes 6291460
  0.6 7.2 %copy-start.1 = (bf16[128,1024]{1,0:T(8,128)(2,1)S(1)}, bf16[128,1024]{1,0:T(8,128)(2,1)}, u32[]{:S(2)}) copy-start(bf16[128,1024]{1,0:T(8,128)(2,1)} %param.14) | copy-start | bytes 786436
  7.9 8.5 %copy-start.8 = (s32[1,512]{1,0:T(1,128)S(1)}, s32[1,512]{1,0:T(1,128)}, u32[]{:S(2)}) copy-start(s32[1,512]{1,0:T(1,128)} %param.25) | copy-start | bytes 6148
  7.9 8.6 %copy-start.10 = (s32[1,512]{1,0:T(1,128)S(1)}, s32[1,512]{1,0:T(1,128)}, u32[]{:S(2)}) copy-start(s32[1,512]{1,0:T(1,128)} %param.26) | copy-start | bytes 6148
  7.9 8.9 %copy-start.7 = (s32[128,8]{0,1:T(8,128)S(1)}, s32[128,8]{0,1:T(8,128)}, u32[]{:S(2)}) copy-start(s32[128,8]{0,1:T(8,128)} %param.27) | copy-start | bytes 12292
  9.4 9.0 %collective-permute-start.2 = (bf16[128,2,256]{0,2,1:T(8,128)(2,1)S(1)}, bf16[128,2,256]{0,2,1:T(8,128)(2,1)S(1)}, u32[]{:S(2)}, u32[]{:S(2)}) collective-permute-start(bf16[128,2,256]{0,2,1:T(8,128)(2,1)S(1)} %get-tuple-element.32), channel_id=1, source_target_pairs={{0,3},{1,0},{2,1},{3,2},{4,7},{5,4},{6,5},{7,6},{8,11},{9,8},{10,9... | collective-permute-start | bytes 393224 | tf_op jit(solution)/shard_map/ppermute | solution.py:115
  14.5 11.2 %collective-permute-start.1 = (bf16[128,2,256]{0,2,1:T(8,128)(2,1)S(1)}, bf16[128,2,256]{0,2,1:T(8,128)(2,1)S(1)}, u32[]{:S(2)}, u32[]{:S(2)}) collective-permute-start(bf16[128,2,256]{0,2,1:T(8,128)(2,1)S(1)} %get-tuple-element.33), channel_id=1, source_target_pairs={{0,2},{1,3},{2,0},{3,1},{4,6},{5,7},{6,4},{7,5},{8,10},{9,11},{10,... | collective-permute-start | bytes 393224 | tf_op jit(solution)/shard_map/ppermute | solution.py:115
  14.5 11.2 %collective-permute-start = (bf16[128,2,256]{0,2,1:T(8,128)(2,1)S(1)}, bf16[128,2,256]{0,2,1:T(8,128)(2,1)S(1)}, u32[]{:S(2)}, u32[]{:S(2)}) collective-permute-start(bf16[128,2,256]{0,2,1:T(8,128)(2,1)S(1)} %get-tuple-element.34), channel_id=1, source_target_pairs={{0,1},{1,2},{2,3},{3,0},{4,5},{5,6},{6,7},{7,4},{8,9},{9,10},{10,1... | collective-permute-start | bytes 393224 | tf_op jit(solution)/shard_map/ppermute | solution.py:115
  25.7 0.7 copy-start.5
  31.0 2.8 %copy-start.3 = (bf16[256,1024]{1,0:T(8,128)(2,1)S(1)}, bf16[256,1024]{1,0:T(8,128)(2,1)}, u32[]{:S(2)}) copy-start(bf16[256,1024]{1,0:T(8,128)(2,1)} %param.19) | copy-start | bytes 1572868
  33.7 7.6 %copy-start.11 = (bf16[1024]{0:T(1024)(128)(2,1)S(1)}, bf16[1024]{0:T(1024)(128)(2,1)}, u32[]{:S(2)}) copy-start(bf16[1024]{0:T(1024)(128)(2,1)} %param.20) | copy-start | bytes 6148
  34.2 1.0 copy-start.2
  36.1 8.8 %collective-permute-start.3 = (bf16[128,1024]{1,0:T(8,128)(2,1)}, bf16[128,1024]{1,0:T(8,128)(2,1)S(1)}, u32[]{:S(2)}, u32[]{:S(2)}) collective-permute-start(bf16[128,1024]{1,0:T(8,128)(2,1)} %get-tuple-element.24), channel_id=1, source_target_pairs={{0,3},{1,0},{2,1},{3,2},{4,7},{5,4},{6,5},{7,6},{8,11},{9,8},{10,9... | collective-permute-start | bytes 786440 | tf_op jit(solution)/shard_map/ppermute | solution.py:115
  37.6 15.6 %collective-permute-start.5 = (bf16[128,1024]{1,0:T(8,128)(2,1)}, bf16[128,1024]{1,0:T(8,128)(2,1)S(1)}, u32[]{:S(2)}, u32[]{:S(2)}) collective-permute-start(bf16[128,1024]{1,0:T(8,128)(2,1)} %get-tuple-element.25), channel_id=1, source_target_pairs={{0,1},{1,2},{2,3},{3,0},{4,5},{5,6},{6,7},{7,4},{8,9},{9,10},{10,1... | collective-permute-start | bytes 786440 | tf_op jit(solution)/shard_map/ppermute | solution.py:115
  38.1 23.5 %collective-permute-start.4 = (bf16[128,1024]{1,0:T(8,128)(2,1)}, bf16[128,1024]{1,0:T(8,128)(2,1)}, u32[]{:S(2)}, u32[]{:S(2)}) collective-permute-start(bf16[128,1024]{1,0:T(8,128)(2,1)} %get-tuple-element.26), channel_id=1, source_target_pairs={{0,2},{1,3},{2,0},{3,1},{4,6},{5,7},{6,4},{7,5},{8,10},{9,11},{10,... | collective-permute-start | bytes 786440 | tf_op jit(solution)/shard_map/ppermute | solution.py:115
  41.3 27.2 %copy-start.12 = (s32[128]{0:T(128)S(1)}, s32[128]{0:T(128)}, u32[]{:S(2)}) copy-start(s32[128]{0:T(128)} %get-tuple-element.63) | copy-start | bytes 1540
  42.4 22.1 %copy-start.6 = (bf16[128,32]{1,0:T(8,128)(2,1)S(1)}, bf16[128,32]{1,0:T(8,128)(2,1)}, u32[]{:S(2)}) copy-start(bf16[128,32]{1,0:T(8,128)(2,1)} %copy.68) | copy-start | bytes 24580
  42.4 26.1 %copy-start.13 = (s32[128]{0:T(128)S(1)}, s32[128]{0:T(128)}, u32[]{:S(2)}) copy-start(s32[128]{0:T(128)} %get-tuple-element.64) | copy-start | bytes 1540
  65.4 27.5 %collective-permute-start.8 = (bf16[128,1152]{1,0:T(8,128)(2,1)}, bf16[128,1152]{1,0:T(8,128)(2,1)}, u32[]{:S(2)}, u32[]{:S(2)}) collective-permute-start(bf16[128,1152]{1,0:T(8,128)(2,1)} %concatenate.43), channel_id=1, source_target_pairs={{0,3},{1,0},{2,1},{3,2},{4,7},{5,4},{6,5},{7,6},{8,11},{9,8},{10,9... | collective-permute-start | bytes 884744 | tf_op jit(solution)/shard_map/ppermute | solution.py:115
  67.0 24.8 %collective-permute-start.7 = (bf16[128,1152]{1,0:T(8,128)(2,1)}, bf16[128,1152]{1,0:T(8,128)(2,1)}, u32[]{:S(2)}, u32[]{:S(2)}) collective-permute-start(bf16[128,1152]{1,0:T(8,128)(2,1)} %concatenate.43), channel_id=1, source_target_pairs={{0,2},{1,3},{2,0},{3,1},{4,6},{5,7},{6,4},{7,5},{8,10},{9,11},{10,... | collective-permute-start | bytes 884744 | tf_op jit(solution)/shard_map/ppermute | solution.py:115
  67.0 20.2 %collective-permute-start.6 = (bf16[128,1152]{1,0:T(8,128)(2,1)}, bf16[128,1152]{1,0:T(8,128)(2,1)}, u32[]{:S(2)}, u32[]{:S(2)}) collective-permute-start(bf16[128,1152]{1,0:T(8,128)(2,1)} %concatenate.43), channel_id=1, source_target_pairs={{0,1},{1,2},{2,3},{3,0},{4,5},{5,6},{6,7},{7,4},{8,9},{9,10},{10,1... | collective-permute-start | bytes 884744 | tf_op jit(solution)/shard_map/ppermute | solution.py:115
  93.8 0.9 copy-start.4
  97.4 8.5 %slice-start.4 = ((s8[8388608]{0:T(1024)(128)(4,1)}), s8[4194304]{0:T(1024)(128)(4,1)S(1)}, s32[]{:S(2)}) async-start(s8[8388608]{0:T(1024)(128)(4,1)} %bitcast.138), calls=%async_computation.4 | async-start | bytes 8388608
  100.5 5.4 %slice-start.5 = ((s8[8388608]{0:T(1024)(128)(4,1)}), s8[4194304]{0:T(1024)(128)(4,1)S(1)}, s32[]{:S(2)}) async-start(s8[8388608]{0:T(1024)(128)(4,1)} %bitcast.138), calls=%async_computation.5 | async-start | bytes 8388608
  100.5 7.4 %slice-start = ((s8[8388608]{0:T(1024)(128)(4,1)}), s8[4194304]{0:T(1024)(128)(4,1)S(1)}, s32[]{:S(2)}) async-start(s8[8388608]{0:T(1024)(128)(4,1)} %bitcast.128), calls=%async_computation | async-start | bytes 8388608
  106.0 2.3 %slice-start.1 = ((s8[8388608]{0:T(1024)(128)(4,1)}), s8[4194304]{0:T(1024)(128)(4,1)S(1)}, s32[]{:S(2)}) async-start(s8[8388608]{0:T(1024)(128)(4,1)} %bitcast.128), calls=%async_computation.1 | async-start | bytes 8388608
  110.4 3.2 %copy-start.9 = (pred[8,384]{1,0:T(8,128)(4,1)S(1)}, pred[8,384]{1,0:T(8,128)(4,1)}, u32[]{:S(2)}) copy-start(pred[8,384]{1,0:T(8,128)(4,1)} %copy.72) | copy-start | bytes 9220
  113.6 2.4 %copy-start.14 = (bf16[8,192,512]{2,1,0:T(8,128)(2,1)S(1)}, bf16[8,192,512]{2,1,0:T(8,128)(2,1)}, u32[]{:S(2)}) copy-start(bf16[8,192,512]{2,1,0:T(8,128)(2,1)} %fusion.21) | copy-start | bytes 4718596
  116.0 1.4 copy-start.15
  117.4 10.4 %slice-start.2 = ((s8[8388608]{0:T(1024)(128)(4,1)}), s8[4194304]{0:T(1024)(128)(4,1)S(1)}, s32[]{:S(2)}) async-start(s8[8388608]{0:T(1024)(128)(4,1)} %bitcast.130), calls=%async_computation.2 | async-start | bytes 8388608
  118.2 9.6 %slice-start.3 = ((s8[8388608]{0:T(1024)(128)(4,1)}), s8[4194304]{0:T(1024)(128)(4,1)S(1)}, s32[]{:S(2)}) async-start(s8[8388608]{0:T(1024)(128)(4,1)} %bitcast.130), calls=%async_computation.3 | async-start | bytes 8388608
  119.3 10.4 %collective-permute-start.9 = (bf16[128,512]{1,0:T(8,128)(2,1)S(1)}, bf16[128,512]{1,0:T(8,128)(2,1)S(1)}, u32[]{:S(2)}, u32[]{:S(2)}) collective-permute-start(bf16[128,512]{1,0:T(8,128)(2,1)S(1)} %get-tuple-element.35), channel_id=1, source_target_pairs={{0,3},{1,0},{2,1},{3,2},{4,7},{5,4},{6,5},{7,6},{8,11},{9,8},{10,9... | collective-permute-start | bytes 393224 | tf_op jit(solution)/shard_map/ppermute | solution.py:115
  119.4 22.8 %collective-permute-start.10 = (bf16[128,512]{1,0:T(8,128)(2,1)S(1)}, bf16[128,512]{1,0:T(8,128)(2,1)S(1)}, u32[]{:S(2)}, u32[]{:S(2)}) collective-permute-start(bf16[128,512]{1,0:T(8,128)(2,1)S(1)} %get-tuple-element.36), channel_id=1, source_target_pairs={{0,2},{1,3},{2,0},{3,1},{4,6},{5,7},{6,4},{7,5},{8,10},{9,11},{10,... | collective-permute-start | bytes 393224 | tf_op jit(solution)/shard_map/ppermute | solution.py:115
  123.9 18.3 %collective-permute-start.11 = (bf16[128,512]{1,0:T(8,128)(2,1)S(1)}, bf16[128,512]{1,0:T(8,128)(2,1)S(1)}, u32[]{:S(2)}, u32[]{:S(2)}) collective-permute-start(bf16[128,512]{1,0:T(8,128)(2,1)S(1)} %get-tuple-element.37), channel_id=1, source_target_pairs={{0,1},{1,2},{2,3},{3,0},{4,5},{5,6},{6,7},{7,4},{8,9},{9,10},{10,1... | collective-permute-start | bytes 393224 | tf_op jit(solution)/shard_map/ppermute | solution.py:115
  125.9 16.4 %collective-permute-start.12 = (bf16[128,512]{1,0:T(8,128)(2,1)S(1)}, bf16[128,512]{1,0:T(8,128)(2,1)S(1)}, u32[]{:S(2)}, u32[]{:S(2)}) collective-permute-start(bf16[128,512]{1,0:T(8,128)(2,1)S(1)} %get-tuple-element.38), channel_id=1, source_target_pairs={{0,3},{1,0},{2,1},{3,2},{4,7},{5,4},{6,5},{7,6},{8,11},{9,8},{10,9... | collective-permute-start | bytes 393224 | tf_op jit(solution)/shard_map/ppermute | solution.py:115
  127.8 18.5 %collective-permute-start.13 = (bf16[128,512]{1,0:T(8,128)(2,1)S(1)}, bf16[128,512]{1,0:T(8,128)(2,1)S(1)}, u32[]{:S(2)}, u32[]{:S(2)}) collective-permute-start(bf16[128,512]{1,0:T(8,128)(2,1)S(1)} %get-tuple-element.39), channel_id=1, source_target_pairs={{0,2},{1,3},{2,0},{3,1},{4,6},{5,7},{6,4},{7,5},{8,10},{9,11},{10,... | collective-permute-start | bytes 393224 | tf_op jit(solution)/shard_map/ppermute | solution.py:115
  129.8 16.5 %collective-permute-start.14 = (bf16[128,512]{1,0:T(8,128)(2,1)S(1)}, bf16[128,512]{1,0:T(8,128)(2,1)S(1)}, u32[]{:S(2)}, u32[]{:S(2)}) collective-permute-start(bf16[128,512]{1,0:T(8,128)(2,1)S(1)} %get-tuple-element.40), channel_id=1, source_target_pairs={{0,1},{1,2},{2,3},{3,0},{4,5},{5,6},{6,7},{7,4},{8,9},{9,10},{10,1... | collective-permute-start | bytes 393224 | tf_op jit(solution)/shard_map/ppermute | solution.py:115

commit v8 on v6

--- a/solution.py
+++ b/solution.py
@@ -125,6 +125,19 @@
         lax.dynamic_slice_in_dim(x, (here - step) % count * rows, rows) for step in range(count)
     ]
     return jnp.concatenate(parts)
+
+
+def gather_w_out(w_out):
+    count = lax.axis_size("exp")
+    mates = lax.axis_size("req")
+    part = lax.axis_index("req") % 2
+    cut = w_out.shape[0] // 2
+    mine = lax.dynamic_slice_in_dim(w_out, part * cut, cut, 0)
+    got = jnp.stack([shifted(mine, step) for step in range(1, count)])
+    other = lax.ppermute(got, "req", [(j, j ^ 1) for j in range(mates)])
+    lower = jnp.where(part == 0, got, other)
+    upper = jnp.where(part == 0, other, got)
+    return jnp.concatenate([lower, upper], axis=1)
 
 
 def shards(
@@ -177,16 +190,15 @@
         "rs,skd->rkd", placing.astype(jnp.bfloat16), keyval_heads, preferred_element_type=jnp.float32
     ).astype(jnp.bfloat16)
     seg_rows = step_rows(seg, rows)
-    attention = None
-    for step in list(range(1, owners)) + [0]:
-        picked = slice(step * rows, (step + 1) * rows)
-        heads_out = attend(
-            query_heads[picked], keyval_heads, seg_rows[picked], seg_rows, where_at[picked], where_at
+    heads_out = attend(query_heads, keyval_heads, seg_rows, seg_rows, where_at, where_at)
+    blocks = heads_out.reshape(owners, rows, -1)
+    remote = gather_w_out(w_out)
+    attention = jnp.dot(blocks[0], w_out, preferred_element_type=jnp.float32)
+    for step in range(1, owners):
+        got = shifted(blocks[step], -step)
+        attention = attention + jnp.dot(
+            got, remote[owners - step - 1], preferred_element_type=jnp.float32
         )
-        block = jnp.dot(heads_out, w_out, preferred_element_type=jnp.float32)
-        if step:
-            block = shifted(block.astype(jnp.bfloat16), -step).astype(jnp.float32)
-        attention = block if attention is None else attention + block
     resid = tokens.astype(jnp.float32) + attention
     normed2 = rms_scale(resid, norm_moe)
     packed = routing(normed2, expert_ids, w_router)

time: 146 us -> 136 us (0.932)
  matrix products: 73.9 us -> 48 us
  starting transfers between devices: 21.3 us -> 37 us
  waiting for transfers between devices: 24.9 us -> 32.4 us
  local copies, waits for them, and re-layouts: 13.4 us -> 8.15 us
    ppermute x15 -> x18, starting transfers between devices: 21.3 us -> 37 us  [shifted(): lax.ppermute(x, 'exp', [(j, (j + step) % count) for j in range(count)])]
    dot_general x8 -> x4, matrix products: 13.1 us -> 1.1 us  [the longest x3 0.86 us: shards(): jnp.dot(got, remote[owners - step - 1], preferred_element_type=jnp.float32)]
    ppermute x15 -> x18, waiting for transfers between devices: 24.9 us -> 32.4 us  [shifted(): lax.ppermute(x, 'exp', [(j, (j + step) % count) for j in range(count)])]
    dot_general x4 -> x1, matrix products: 9.92 us -> 2.73 us  [attend(): jnp.einsum('kgqt,tkd->qkgd', probs, values, preferred_element_type=jnp.fl...]
    transpose x4, local copies, waits for them, and re-layouts: 2.46 us -> 0.35 us  [expert_mix(): high = jnp.where(picks, high.T[:, None, :], zero)]
    dynamic_slice x0 -> x1, local copies, waits for them, and re-layouts: none -> 1.82 us  [gather_w_out(): mine = lax.dynamic_slice_in_dim(w_out, part * cut, cut, 0)]
    unnamed x67 -> x39, local copies, waits for them, and re-layouts: 5.17 us -> 3.39 us
    dot_general x2, matrix products: 2.07 us -> 0.6 us  [expert_mix(): jnp.dot(before.astype(jnp.bfloat16), named, preferred_element_type=jnp.fl...]
  transfers between devices with their start and end apart: 15 -> 19, of which waited for: 8 -> 9; matrix products, arithmetic and copies ran while one was open for 34% -> 30% of each run, Pallas kernels for 0% -> 0%
where the time goes in v8:
time: 136 us
  matrix products  48 us (35%)
  starting transfers between devices  37 us (27%)
  waiting for transfers between devices  32.4 us (24%)
  other arithmetic  8.97 us (7%)
  local copies, waits for them, and re-layouts  8.15 us (6%)
  between operations  1.37 us (1%)
    ppermute x18, starting transfers between devices, shifted(): lax.ppermute(x, 'exp', [(j, (j + step) % count) for j in range(count)])  37 us
    ppermute x18, waiting for transfers between devices, shifted(): lax.ppermute(x, 'exp', [(j, (j + step) % count) for j in range(count)])  32.4 us
    dot_general x3, matrix products, expert_mix(): jnp.einsum('esf,efd->esd', hidden, down, preferred_element_type=jnp.float32)  13.1 us
    dot_general x2, matrix products, expert_mix(): jnp.einsum('esd,edf->esf', received, w_gate, preferred_element_type=jnp.f...  10.4 us
    dot_general x3, matrix products, expert_mix(): jnp.einsum('est,esd->td', low, result, preferred_element_type=jnp.float32)  4.32 us
    sub x1, matrix products, attend(): expo = jnp.exp(score - top)  3.59 us
    unnamed x39, local copies, waits for them, and re-layouts  3.39 us
    dot_general x3, matrix products, expert_mix(): jnp.einsum('est,esd->td', high, result, preferred_element_type=jnp.float32)  2.94 us
  transfers between devices with their start and end apart: 19, of which 9 were waited for; matrix products, arithmetic and copies ran while one was open for 30% of the time, Pallas kernels for 0%

profile of v8, /device:TPU:0, one launch (start us, length us, event | category | flops | bytes accessed | tf_op | source)
XLA Modules:
  0.0 135.9 jit_solution(5087978173503601415)
XLA Ops:
  0.7 1.8 %constant_dynamic-slice_fusion.4 = bf16[128,1024]{1,0:T(8,128)(2,1)} fusion(bf16[256,1024]{1,0:T(8,128)(2,1)} %param.19, s32[]{:T(128)S(6)} %select_n.200), kind=kLoop, calls=%fused_computation.169 | loop fusion | bytes 524292 | tf_op jit(solution)/shard_map/dynamic_slice | solution.py:135
  2.5 5.1 %collective-permute-start.6 = (bf16[128,1024]{1,0:T(8,128)(2,1)}, bf16[128,1024]{1,0:T(8,128)(2,1)S(1)}, u32[]{:S(2)}, u32[]{:S(2)}) collective-permute-start(bf16[128,1024]{1,0:T(8,128)(2,1)} %constant_dynamic-slice_fusion.4), channel_id=1, source_target_pairs={{0,3},{1,0},{2,1},{3,2},{4,7},{5,4},{6,5},{7,6},{8,11},{9,8},{10,9... | collective-permute-start | bytes 786440 | tf_op jit(solution)/shard_map/ppermute | solution.py:111
  7.6 0.5 multiply_power_fusion
  8.1 0.8 compare_reduce_fusion
  9.0 1.1 fusion.90
  10.1 0.3 reduce-window.9
  10.7 0.7 bitcast_subtract_fusion
  11.3 0.7 convert_element_type.115
  12.0 1.7 %convolution_convert_fusion.3 = bf16[128,512]{1,0:T(8,128)(2,1)S(1)} fusion(bf16[1024,512]{1,0:T(8,128)(2,1)} %param.18, bf16[128,1024]{1,0:T(8,128)(2,1)} %param.14, f32[1024]{0:T(1024)S(1)} %convert_element_type.115, f32[128]{0:T(128)S(1)} %add_rsqrt_fusion.1), kind=kOutput, calls=%fused_computation.62 | convolution fusion | flops 134807552 | bytes 1446400 | tf_op jit(solution)/shard_map/dot_general | solution.py:172
  13.8 1.9 %fusion.168 = f32[128,512]{0,1:T(8,128)S(1)} fusion(bf16[1024,512]{1,0:T(8,128)(2,1)} %param.17, bf16[128,1024]{1,0:T(8,128)(2,1)} %param.14, f32[1024]{0:T(1024)S(1)} %convert_element_type.115, f32[128]{0:T(128)S(1)} %add_rsqrt_fusion.1), kind=kOutput, calls=%fused_computation.225 | convolution fusion | flops 134742016 | bytes 1577472 | tf_op jit(solution)/shard_map/dot_general | solution.py:169
  15.8 1.0 fusion.170
  16.8 0.8 dynamic-slice_convert_fusion
  17.5 0.7 multiply_cosine_fusion
  18.5 0.5 collective-permute-start.2
  19.1 2.6 %collective-permute-start.1 = (bf16[128,2,256]{0,2,1:T(8,128)(2,1)S(1)}, bf16[128,2,256]{0,2,1:T(8,128)(2,1)S(1)}, u32[]{:S(2)}, u32[]{:S(2)}) collective-permute-start(bf16[128,2,256]{0,2,1:T(8,128)(2,1)S(1)} %get-tuple-element.20), channel_id=1, source_target_pairs={{0,2},{1,3},{2,0},{3,1},{4,6},{5,7},{6,4},{7,5},{8,10},{9,11},{10,... | collective-permute-start | bytes 393224 | tf_op jit(solution)/shard_map/ppermute | solution.py:111
  21.6 1.9 %collective-permute-start = (bf16[128,2,256]{0,2,1:T(8,128)(2,1)S(1)}, bf16[128,2,256]{0,2,1:T(8,128)(2,1)S(1)}, u32[]{:S(2)}, u32[]{:S(2)}) collective-permute-start(bf16[128,2,256]{0,2,1:T(8,128)(2,1)S(1)} %get-tuple-element.21), channel_id=1, source_target_pairs={{0,1},{1,2},{2,3},{3,0},{4,5},{5,6},{6,7},{7,4},{8,9},{9,10},{10,1... | collective-permute-start | bytes 393224 | tf_op jit(solution)/shard_map/ppermute | solution.py:111
  24.0 0.3 compare_and_fusion
  24.4 3.4 %collective-permute-done.2 = bf16[128,2,256]{0,2,1:T(8,128)(2,1)S(1)} collective-permute-done((bf16[128,2,256]{0,2,1:T(8,128)(2,1)S(1)}, bf16[128,2,256]{0,2,1:T(8,128)(2,1)S(1)}, u32[]{:S(2)}, u32[]{:S(2)}) %collective-permute-start.2) | collective-permute-done | bytes 131104 | tf_op jit(solution)/shard_map/ppermute | solution.py:111
  27.8 12.4 %collective-permute-start.4 = (bf16[128,1024]{1,0:T(8,128)(2,1)}, bf16[128,1024]{1,0:T(8,128)(2,1)S(1)}, u32[]{:S(2)}, u32[]{:S(2)}) collective-permute-start(bf16[128,1024]{1,0:T(8,128)(2,1)} %constant_dynamic-slice_fusion.4), channel_id=1, source_target_pairs={{0,1},{1,2},{2,3},{3,0},{4,5},{5,6},{6,7},{7,4},{8,9},{9,10},{10,1... | collective-permute-start | bytes 786440 | tf_op jit(solution)/shard_map/ppermute | solution.py:111
  40.3 1.1 collective-permute-done.1
  41.5 0.3 convolution_convert_fusion.2
  41.8 1.0 copy.76
  42.8 3.6 %fusion.175 = (f32[2,2,512]{2,1,0:T(2,128)S(1)}, f32[2,2,512,512]{2,3,1,0:T(8,128)}) fusion(pred[512,512]{0,1:T(8,128)(4,1)S(1)} %compare_and_fusion, bf16[512,2,2,64]{0,3,2,1:T(8,128)(2,1)S(1)} %bitcast.163, bf16[512,2,256]{0,2,1:T(8,128)(2,1)S(1)} %pad_maximum_fusion.3), kind=kOutput, calls=%fused_computation.230 | convolution fusion | flops 138412544 | bytes 4857856 | tf_op jit(solution)/shard_map/sub | solution.py:44
  46.4 1.0 pad_maximum_fusion
  47.5 2.7 %fusion.71 = bf16[512,2,2,64]{0,3,2,1:T(8,128)(2,1)S(1)} fusion(f32[2,2,512,512]{2,3,1,0:T(8,128)} %get-tuple-element.47, f32[2,2,512]{2,1,0:T(2,128)S(1)} %get-tuple-element.46, bf16[512,2,256]{0,2,1:T(8,128)(2,1)S(1)} %pad_maximum_fusion.3), kind=kOutput, calls=%fused_computation.61 | convolution fusion | flops 136445952 | bytes 4595712 | tf_op jit(solution)/shard_map/kgqt,tkd->qkgd/dot_general | solution.py:46
  50.3 0.5 collective-permute-start.9
  50.8 3.4 %collective-permute-start.3 = (bf16[128,256]{0,1:T(8,128)(2,1)S(1)}, bf16[128,256]{0,1:T(8,128)(2,1)S(1)}, u32[]{:S(2)}, u32[]{:S(2)}) collective-permute-start(bf16[128,256]{0,1:T(8,128)(2,1)S(1)} %bitcast.167), channel_id=1, source_target_pairs={{0,3},{1,0},{2,1},{3,2},{4,7},{5,4},{6,5},{7,6},{8,11},{9,8},{10,9... | collective-permute-start | bytes 196616 | tf_op jit(solution)/shard_map/ppermute | solution.py:111
  54.5 1.1 broadcast_select_fusion.1
  55.6 2.8 %collective-permute-done.3 = bf16[128,256]{0,1:T(8,128)(2,1)S(1)} collective-permute-done((bf16[128,256]{0,1:T(8,128)(2,1)S(1)}, bf16[128,256]{0,1:T(8,128)(2,1)S(1)}, u32[]{:S(2)}, u32[]{:S(2)}) %collective-permute-start.3) | collective-permute-done | bytes 65568 | tf_op jit(solution)/shard_map/ppermute | solution.py:111
  58.3 0.3 convolution_add_fusion.1
  58.8 0.5 collective-permute-done.8
  59.4 0.4 multiply_reduce_fusion
  60.6 2.0 %collective-permute-start.12 = (bf16[128,1152]{1,0:T(8,128)(2,1)S(1)}, bf16[128,1152]{1,0:T(8,128)(2,1)}, u32[]{:S(2)}, u32[]{:S(2)}) collective-permute-start(bf16[128,1152]{1,0:T(8,128)(2,1)S(1)} %concatenate.47), channel_id=1, source_target_pairs={{0,3},{1,0},{2,1},{3,2},{4,7},{5,4},{6,5},{7,6},{8,11},{9,8},{10,9... | collective-permute-start | bytes 884744 | tf_op jit(solution)/shard_map/ppermute | solution.py:111
  62.6 1.5 %collective-permute-start.11 = (bf16[128,1152]{1,0:T(8,128)(2,1)S(1)}, bf16[128,1152]{1,0:T(8,128)(2,1)}, u32[]{:S(2)}, u32[]{:S(2)}) collective-permute-start(bf16[128,1152]{1,0:T(8,128)(2,1)S(1)} %concatenate.47), channel_id=1, source_target_pairs={{0,2},{1,3},{2,0},{3,1},{4,6},{5,7},{6,4},{7,5},{8,10},{9,11},{10,... | collective-permute-start | bytes 884744 | tf_op jit(solution)/shard_map/ppermute | solution.py:111
  64.2 0.3 fusion.73
  64.5 0.4 convolution_convert_fusion.1
  64.9 5.0 %fusion.178 = f32[8,64,512]{2,1,0:T(8,128)S(1)} fusion(bf16[8,64,1024]{2,1,0:T(8,128)(2,1)S(1)} %convolution_convert_fusion.1, bf16[8,1024,512]{2,1,0:T(8,128)(2,1)} %param.22), kind=kOutput, calls=%fused_computation.233 | convolution fusion | flops 536870912 | bytes 10485760 | tf_op jit(solution)/shard_map/esd,edf->esf/dot_general | solution.py:89
  69.9 8.8 %convolution_convert_fusion = bf16[8,64,1024]{2,1,0:T(8,128)(2,1)S(1)} fusion(bf16[8,512,1024]{2,1,0:T(8,128)(2,1)} %param.24, bf16[8,64,1024]{2,1,0:T(8,128)(2,1)S(1)} %convolution_convert_fusion.1, bf16[8,1024,512]{2,1,0:T(8,128)(2,1)} %param.23, f32[8,64,512]{2,1,0:T(8,128)S(1)} %fusion.178), kind=kOutput, calls=%fused_computation.26 | convolution fusion | flops 1075838976 | bytes 19922944 | tf_op jit(solution)/shard_map/esf,efd->esd/dot_general | solution.py:99
  78.8 1.2 convolution_bitcast_fusion
  80.1 2.7 %collective-permute-done.10 = bf16[128,1152]{1,0:T(8,128)(2,1)} collective-permute-done((bf16[128,1152]{1,0:T(8,128)(2,1)S(1)}, bf16[128,1152]{1,0:T(8,128)(2,1)}, u32[]{:S(2)}, u32[]{:S(2)}) %collective-permute-start.10) | collective-permute-done | bytes 294944 | tf_op jit(solution)/shard_map/ppermute | solution.py:111
  82.8 1.0 constant_dynamic-update-slice_fusion.2
  83.8 5.8 %collective-permute-done.11 = bf16[128,1152]{1,0:T(8,128)(2,1)} collective-permute-done((bf16[128,1152]{1,0:T(8,128)(2,1)S(1)}, bf16[128,1152]{1,0:T(8,128)(2,1)}, u32[]{:S(2)}, u32[]{:S(2)}) %collective-permute-start.11) | collective-permute-done | bytes 294944 | tf_op jit(solution)/shard_map/ppermute | solution.py:111
  89.5 1.0 constant_dynamic-update-slice_fusion.1
  90.5 1.0 constant_dynamic-update-slice_fusion
  91.9 0.3 fusion.72
  92.2 1.8 %fusion.11 = bf16[8,192,1024]{2,1,0:T(8,128)(2,1)S(1)} fusion(s32[8,384]{1,0:T(8,128)S(1)} %fusion.72, pred[8,384]{1,0:T(8,128)(4,1)S(1)} %copy.72, bf16[384,1152]{1,0:T(8,128)(2,1)S(1)} %constant_dynamic-update-slice_fusion), kind=kOutput, calls=%fused_computation.15 | convolution fusion | flops 1210712064 | bytes 3947520 | tf_op jit(solution)/shard_map/est,td->esd/dot_general | solution.py:86
  94.1 5.4 %fusion.179 = f32[8,192,512]{2,1,0:T(8,128)S(1)} fusion(bf16[8,192,1024]{2,1,0:T(8,128)(2,1)S(1)} %fusion.11, bf16[8,1024,512]{2,1,0:T(8,128)(2,1)} %param.22), kind=kOutput, calls=%fused_computation.234 | convolution fusion | flops 1610612736 | bytes 14680064 | tf_op jit(solution)/shard_map/esd,edf->esf/dot_general | solution.py:89
  99.5 2.0 %multiply_convert_fusion = bf16[8,192,512]{2,1,0:T(8,128)(2,1)S(1)} fusion(f32[8,192,512]{2,1,0:T(8,128)S(1)} %fusion.179, bf16[8,192,1024]{2,1,0:T(8,128)(2,1)S(1)} %fusion.11, bf16[8,1024,512]{2,1,0:T(8,128)(2,1)S(1)} %bitcast.152), kind=kOutput, calls=%fused_computation.9 | convolution fusion | flops 1615331328 | bytes 16252928 | tf_op jit(solution)/shard_map/esd,edf->esf/dot_general | solution.py:90
  101.5 0.3 slice-done.3
  101.8 2.2 %fusion.21 = bf16[8,192,512]{2,1,0:T(8,128)(2,1)} fusion(bf16[8,192,512]{2,1,0:T(8,128)(2,1)S(1)} %multiply_convert_fusion, bf16[8,512,1024]{2,1,0:T(8,128)(2,1)S(1)} %bitcast.154), kind=kOutput, calls=%fused_computation.25 | convolution fusion | flops 806092800 | bytes 7340032 | tf_op jit(solution)/shard_map/esf,efd->esd/dot_general | solution.py:99
  104.0 2.1 %fusion.18 = bf16[8,192,512]{2,1,0:T(8,128)(2,1)} fusion(bf16[8,192,512]{2,1,0:T(8,128)(2,1)S(1)} %multiply_convert_fusion, bf16[8,512,1024]{2,1,0:T(8,128)(2,1)S(1)} %bitcast.154), kind=kOutput, calls=%fused_computation.24 | convolution fusion | flops 806092800 | bytes 7340032 | tf_op jit(solution)/shard_map/esf,efd->esd/dot_general | solution.py:99
  106.3 2.4 %fusion.33 = f32[384,512]{1,0:T(8,128)S(1)} fusion(bf16[8,192,512]{2,1,0:T(8,128)(2,1)} %fusion.18, s32[8,384]{1,0:T(8,128)S(1)} %fusion.72, pred[8,384]{1,0:T(8,128)(4,1)S(1)} %copy.72, bf16[8,384]{1,0:T(8,128)(2,1)S(1)} %copy.74), kind=kOutput, calls=%fused_computation.34 | convolution fusion | flops 605749248 | bytes 2380800 | tf_op jit(solution)/shard_map/est,esd->td/dot_general | solution.py:102
  108.7 1.1 fusion.51
  109.8 2.0 %collective-permute-start.15 = (bf16[128,512]{1,0:T(8,128)(2,1)S(1)}, bf16[128,512]{1,0:T(8,128)(2,1)S(1)}, u32[]{:S(2)}, u32[]{:S(2)}) collective-permute-start(bf16[128,512]{1,0:T(8,128)(2,1)S(1)} %get-tuple-element.23), channel_id=1, source_target_pairs={{0,1},{1,2},{2,3},{3,0},{4,5},{5,6},{6,7},{7,4},{8,9},{9,10},{10,1... | collective-permute-start | bytes 393224 | tf_op jit(solution)/shard_map/ppermute | solution.py:111
  111.9 2.3 %collective-permute-start.14 = (bf16[128,512]{1,0:T(8,128)(2,1)S(1)}, bf16[128,512]{1,0:T(8,128)(2,1)S(1)}, u32[]{:S(2)}, u32[]{:S(2)}) collective-permute-start(bf16[128,512]{1,0:T(8,128)(2,1)S(1)} %get-tuple-element.24), channel_id=1, source_target_pairs={{0,2},{1,3},{2,0},{3,1},{4,6},{5,7},{6,4},{7,5},{8,10},{9,11},{10,... | collective-permute-start | bytes 393224 | tf_op jit(solution)/shard_map/ppermute | solution.py:111
  114.1 0.8 fusion.36
  115.0 0.8 fusion.54
  115.8 1.0 collective-permute-start.16
  116.8 1.1 collective-permute-start.18
  117.9 0.7 collective-permute-start.17
  118.6 2.1 %collective-permute-done.15 = bf16[128,512]{1,0:T(8,128)(2,1)S(1)} collective-permute-done((bf16[128,512]{1,0:T(8,128)(2,1)S(1)}, bf16[128,512]{1,0:T(8,128)(2,1)S(1)}, u32[]{:S(2)}, u32[]{:S(2)}) %collective-permute-start.15) | collective-permute-done | bytes 131104 | tf_op jit(solution)/shard_map/ppermute | solution.py:111
  120.7 9.8 %collective-permute-done.14 = bf16[128,512]{1,0:T(8,128)(2,1)S(1)} collective-permute-done((bf16[128,512]{1,0:T(8,128)(2,1)S(1)}, bf16[128,512]{1,0:T(8,128)(2,1)S(1)}, u32[]{:S(2)}, u32[]{:S(2)}) %collective-permute-start.14) | collective-permute-done | bytes 131104 | tf_op jit(solution)/shard_map/ppermute | solution.py:111
  130.5 4.2 %collective-permute-done.17 = bf16[128,512]{1,0:T(8,128)(2,1)S(1)} collective-permute-done((bf16[128,512]{1,0:T(8,128)(2,1)S(1)}, bf16[128,512]{1,0:T(8,128)(2,1)S(1)}, u32[]{:S(2)}, u32[]{:S(2)}) %collective-permute-start.17) | collective-permute-done | bytes 131104 | tf_op jit(solution)/shard_map/ppermute | solution.py:111
  134.8 1.1 fusion.104
  (113 shorter events, 3.9 us)
Async XLA Ops:
  0.6 15.1 %copy-start = (bf16[1024,1024]{1,0:T(8,128)(2,1)S(1)}, bf16[1024,1024]{1,0:T(8,128)(2,1)}, u32[]{:S(2)}) copy-start(bf16[1024,1024]{1,0:T(8,128)(2,1)} %param.16) | copy-start | bytes 6291460
  0.6 15.1 %copy-start.2 = (bf16[128,1024]{1,0:T(8,128)(2,1)S(1)}, bf16[128,1024]{1,0:T(8,128)(2,1)}, u32[]{:S(2)}) copy-start(bf16[128,1024]{1,0:T(8,128)(2,1)} %param.14) | copy-start | bytes 786436
  2.5 43.9 %collective-permute-start.6 = (bf16[128,1024]{1,0:T(8,128)(2,1)}, bf16[128,1024]{1,0:T(8,128)(2,1)S(1)}, u32[]{:S(2)}, u32[]{:S(2)}) collective-permute-start(bf16[128,1024]{1,0:T(8,128)(2,1)} %constant_dynamic-slice_fusion.4), channel_id=1, source_target_pairs={{0,3},{1,0},{2,1},{3,2},{4,7},{5,4},{6,5},{7,6},{8,11},{9,8},{10,9... | collective-permute-start | bytes 786440 | tf_op jit(solution)/shard_map/ppermute | solution.py:111
  7.6 38.8 %collective-permute-start.5 = (bf16[128,1024]{1,0:T(8,128)(2,1)}, bf16[128,1024]{1,0:T(8,128)(2,1)}, u32[]{:S(2)}, u32[]{:S(2)}) collective-permute-start(bf16[128,1024]{1,0:T(8,128)(2,1)} %constant_dynamic-slice_fusion.4), channel_id=1, source_target_pairs={{0,2},{1,3},{2,0},{3,1},{4,6},{5,7},{6,4},{7,5},{8,10},{9,11},{10,... | collective-permute-start | bytes 786440 | tf_op jit(solution)/shard_map/ppermute | solution.py:111
  15.7 8.1 %copy-start.9 = (s32[1,512]{1,0:T(1,128)S(1)}, s32[1,512]{1,0:T(1,128)}, u32[]{:S(2)}) copy-start(s32[1,512]{1,0:T(1,128)} %param.25) | copy-start | bytes 6148
  15.7 8.2 %copy-start.8 = (s32[128,8]{0,1:T(8,128)S(1)}, s32[128,8]{0,1:T(8,128)}, u32[]{:S(2)}) copy-start(s32[128,8]{0,1:T(8,128)} %param.27) | copy-start | bytes 12292
  16.7 7.2 %copy-start.10 = (s32[1,512]{1,0:T(1,128)S(1)}, s32[1,512]{1,0:T(1,128)}, u32[]{:S(2)}) copy-start(s32[1,512]{1,0:T(1,128)} %param.26) | copy-start | bytes 6148
  16.7 7.5 %copy-start.11 = (bf16[1024]{0:T(1024)(128)(2,1)S(1)}, bf16[1024]{0:T(1024)(128)(2,1)}, u32[]{:S(2)}) copy-start(bf16[1024]{0:T(1024)(128)(2,1)} %param.20) | copy-start | bytes 6148
  18.5 9.3 %collective-permute-start.2 = (bf16[128,2,256]{0,2,1:T(8,128)(2,1)S(1)}, bf16[128,2,256]{0,2,1:T(8,128)(2,1)S(1)}, u32[]{:S(2)}, u32[]{:S(2)}) collective-permute-start(bf16[128,2,256]{0,2,1:T(8,128)(2,1)S(1)} %get-tuple-element.19), channel_id=1, source_target_pairs={{0,3},{1,0},{2,1},{3,2},{4,7},{5,4},{6,5},{7,6},{8,11},{9,8},{10,9... | collective-permute-start | bytes 393224 | tf_op jit(solution)/shard_map/ppermute | solution.py:111
  19.1 22.3 %collective-permute-start.1 = (bf16[128,2,256]{0,2,1:T(8,128)(2,1)S(1)}, bf16[128,2,256]{0,2,1:T(8,128)(2,1)S(1)}, u32[]{:S(2)}, u32[]{:S(2)}) collective-permute-start(bf16[128,2,256]{0,2,1:T(8,128)(2,1)S(1)} %get-tuple-element.20), channel_id=1, source_target_pairs={{0,2},{1,3},{2,0},{3,1},{4,6},{5,7},{6,4},{7,5},{8,10},{9,11},{10,... | collective-permute-start | bytes 393224 | tf_op jit(solution)/shard_map/ppermute | solution.py:111
  21.6 19.8 %collective-permute-start = (bf16[128,2,256]{0,2,1:T(8,128)(2,1)S(1)}, bf16[128,2,256]{0,2,1:T(8,128)(2,1)S(1)}, u32[]{:S(2)}, u32[]{:S(2)}) collective-permute-start(bf16[128,2,256]{0,2,1:T(8,128)(2,1)S(1)} %get-tuple-element.21), channel_id=1, source_target_pairs={{0,1},{1,2},{2,3},{3,0},{4,5},{5,6},{6,7},{7,4},{8,9},{9,10},{10,1... | collective-permute-start | bytes 393224 | tf_op jit(solution)/shard_map/ppermute | solution.py:111
  27.8 18.6 %collective-permute-start.4 = (bf16[128,1024]{1,0:T(8,128)(2,1)}, bf16[128,1024]{1,0:T(8,128)(2,1)S(1)}, u32[]{:S(2)}, u32[]{:S(2)}) collective-permute-start(bf16[128,1024]{1,0:T(8,128)(2,1)} %constant_dynamic-slice_fusion.4), channel_id=1, source_target_pairs={{0,1},{1,2},{2,3},{3,0},{4,5},{5,6},{6,7},{7,4},{8,9},{9,10},{10,1... | collective-permute-start | bytes 786440 | tf_op jit(solution)/shard_map/ppermute | solution.py:111
  47.5 7.0 %collective-permute-start.7 = (bf16[3,128,1024]{2,1,0:T(8,128)(2,1)S(1)}, bf16[3,128,1024]{2,1,0:T(8,128)(2,1)S(1)}, u32[]{:S(2)}, u32[]{:S(2)}) collective-permute-start(bf16[3,128,1024]{2,1,0:T(8,128)(2,1)S(1)} %pad_maximum_fusion), channel_id=1, source_target_pairs={{0,4},{4,0},{8,12},{12,8},{16,20},{20,16},{24,28},{28,24},{1,5},{5... | collective-permute-start | bytes 2359304 | tf_op jit(solution)/shard_map/ppermute | solution.py:137
  47.5 6.7 %copy-start.6 = (bf16[256,1024]{1,0:T(8,128)(2,1)S(1)}, bf16[256,1024]{1,0:T(8,128)(2,1)}, u32[]{:S(2)}) copy-start(bf16[256,1024]{1,0:T(8,128)(2,1)} %param.19) | copy-start | bytes 1572868
  50.3 8.3 %collective-permute-start.9 = (bf16[128,256]{0,1:T(8,128)(2,1)S(1)}, bf16[128,256]{0,1:T(8,128)(2,1)S(1)}, u32[]{:S(2)}, u32[]{:S(2)}) collective-permute-start(bf16[128,256]{0,1:T(8,128)(2,1)S(1)} %bitcast.166), channel_id=1, source_target_pairs={{0,1},{1,2},{2,3},{3,0},{4,5},{5,6},{6,7},{7,4},{8,9},{9,10},{10,1... | collective-permute-start | bytes 196616 | tf_op jit(solution)/shard_map/ppermute | solution.py:111
  50.8 8.6 %collective-permute-start.8 = (bf16[128,256]{0,1:T(8,128)(2,1)S(1)}, bf16[128,256]{0,1:T(8,128)(2,1)S(1)}, u32[]{:S(2)}, u32[]{:S(2)}) collective-permute-start(bf16[128,256]{0,1:T(8,128)(2,1)S(1)} %bitcast.165), channel_id=1, source_target_pairs={{0,2},{1,3},{2,0},{3,1},{4,6},{5,7},{6,4},{7,5},{8,10},{9,11},{10,... | collective-permute-start | bytes 196616 | tf_op jit(solution)/shard_map/ppermute | solution.py:111
  50.8 7.5 %collective-permute-start.3 = (bf16[128,256]{0,1:T(8,128)(2,1)S(1)}, bf16[128,256]{0,1:T(8,128)(2,1)S(1)}, u32[]{:S(2)}, u32[]{:S(2)}) collective-permute-start(bf16[128,256]{0,1:T(8,128)(2,1)S(1)} %bitcast.167), channel_id=1, source_target_pairs={{0,3},{1,0},{2,1},{3,2},{4,7},{5,4},{6,5},{7,6},{8,11},{9,8},{10,9... | collective-permute-start | bytes 196616 | tf_op jit(solution)/shard_map/ppermute | solution.py:111
  58.6 1.3 copy-start.7
  59.7 4.8 %copy-start.3 = (f32[128,1024]{1,0:T(8,128)}, f32[128,1024]{1,0:T(8,128)S(1)}, u32[]{:S(2)}) copy-start(f32[128,1024]{1,0:T(8,128)S(1)} %get-tuple-element.49) | copy-start | bytes 1572868
  60.6 29.9 %collective-permute-start.12 = (bf16[128,1152]{1,0:T(8,128)(2,1)S(1)}, bf16[128,1152]{1,0:T(8,128)(2,1)}, u32[]{:S(2)}, u32[]{:S(2)}) collective-permute-start(bf16[128,1152]{1,0:T(8,128)(2,1)S(1)} %concatenate.47), channel_id=1, source_target_pairs={{0,3},{1,0},{2,1},{3,2},{4,7},{5,4},{6,5},{7,6},{8,11},{9,8},{10,9... | collective-permute-start | bytes 884744 | tf_op jit(solution)/shard_map/ppermute | solution.py:111
  62.6 26.9 %collective-permute-start.11 = (bf16[128,1152]{1,0:T(8,128)(2,1)S(1)}, bf16[128,1152]{1,0:T(8,128)(2,1)}, u32[]{:S(2)}, u32[]{:S(2)}) collective-permute-start(bf16[128,1152]{1,0:T(8,128)(2,1)S(1)} %concatenate.47), channel_id=1, source_target_pairs={{0,2},{1,3},{2,0},{3,1},{4,6},{5,7},{6,4},{7,5},{8,10},{9,11},{10,... | collective-permute-start | bytes 884744 | tf_op jit(solution)/shard_map/ppermute | solution.py:111
  64.1 18.7 %collective-permute-start.10 = (bf16[128,1152]{1,0:T(8,128)(2,1)S(1)}, bf16[128,1152]{1,0:T(8,128)(2,1)}, u32[]{:S(2)}, u32[]{:S(2)}) collective-permute-start(bf16[128,1152]{1,0:T(8,128)(2,1)S(1)} %concatenate.47), channel_id=1, source_target_pairs={{0,1},{1,2},{2,3},{3,0},{4,5},{5,6},{6,7},{7,4},{8,9},{9,10},{10,1... | collective-permute-start | bytes 884744 | tf_op jit(solution)/shard_map/ppermute | solution.py:111
  92.2 7.3 %slice-start = ((s8[8388608]{0:T(1024)(128)(4,1)}), s8[4194304]{0:T(1024)(128)(4,1)S(1)}, s32[]{:S(2)}) async-start(s8[8388608]{0:T(1024)(128)(4,1)} %bitcast.151), calls=%async_computation | async-start | bytes 8388608
  94.1 5.5 %slice-start.1 = ((s8[8388608]{0:T(1024)(128)(4,1)}), s8[4194304]{0:T(1024)(128)(4,1)S(1)}, s32[]{:S(2)}) async-start(s8[8388608]{0:T(1024)(128)(4,1)} %bitcast.151), calls=%async_computation.1 | async-start | bytes 8388608
  94.1 7.4 %slice-start.2 = ((s8[8388608]{0:T(1024)(128)(4,1)}), s8[4194304]{0:T(1024)(128)(4,1)S(1)}, s32[]{:S(2)}) async-start(s8[8388608]{0:T(1024)(128)(4,1)} %bitcast.153), calls=%async_computation.2 | async-start | bytes 8388608
  99.5 2.3 %slice-start.3 = ((s8[8388608]{0:T(1024)(128)(4,1)}), s8[4194304]{0:T(1024)(128)(4,1)S(1)}, s32[]{:S(2)}) async-start(s8[8388608]{0:T(1024)(128)(4,1)} %bitcast.153), calls=%async_computation.3 | async-start | bytes 8388608
  106.3 2.4 %copy-start.13 = (bf16[8,192,512]{2,1,0:T(8,128)(2,1)S(1)}, bf16[8,192,512]{2,1,0:T(8,128)(2,1)}, u32[]{:S(2)}) copy-start(bf16[8,192,512]{2,1,0:T(8,128)(2,1)} %fusion.18) | copy-start | bytes 4718596
  108.7 5.5 %copy-start.12 = (bf16[8,192,512]{2,1,0:T(8,128)(2,1)S(1)}, bf16[8,192,512]{2,1,0:T(8,128)(2,1)}, u32[]{:S(2)}) copy-start(bf16[8,192,512]{2,1,0:T(8,128)(2,1)} %fusion.21) | copy-start | bytes 4718596
  109.8 8.1 %collective-permute-start.13 = (bf16[128,512]{1,0:T(8,128)(2,1)S(1)}, bf16[128,512]{1,0:T(8,128)(2,1)S(1)}, u32[]{:S(2)}, u32[]{:S(2)}) collective-permute-start(bf16[128,512]{1,0:T(8,128)(2,1)S(1)} %get-tuple-element.22), channel_id=1, source_target_pairs={{0,3},{1,0},{2,1},{3,2},{4,7},{5,4},{6,5},{7,6},{8,11},{9,8},{10,9... | collective-permute-start | bytes 393224 | tf_op jit(solution)/shard_map/ppermute | solution.py:111
  109.8 10.9 %collective-permute-start.15 = (bf16[128,512]{1,0:T(8,128)(2,1)S(1)}, bf16[128,512]{1,0:T(8,128)(2,1)S(1)}, u32[]{:S(2)}, u32[]{:S(2)}) collective-permute-start(bf16[128,512]{1,0:T(8,128)(2,1)S(1)} %get-tuple-element.23), channel_id=1, source_target_pairs={{0,1},{1,2},{2,3},{3,0},{4,5},{5,6},{6,7},{7,4},{8,9},{9,10},{10,1... | collective-permute-start | bytes 393224 | tf_op jit(solution)/shard_map/ppermute | solution.py:111
  111.9 18.6 %collective-permute-start.14 = (bf16[128,512]{1,0:T(8,128)(2,1)S(1)}, bf16[128,512]{1,0:T(8,128)(2,1)S(1)}, u32[]{:S(2)}, u32[]{:S(2)}) collective-permute-start(bf16[128,512]{1,0:T(8,128)(2,1)S(1)} %get-tuple-element.24), channel_id=1, source_target_pairs={{0,2},{1,3},{2,0},{3,1},{4,6},{5,7},{6,4},{7,5},{8,10},{9,11},{10,... | collective-permute-start | bytes 393224 | tf_op jit(solution)/shard_map/ppermute | solution.py:111
  114.9 19.9 %copy-start.4 = (f32[128,1024]{1,0:T(8,128)S(1)}, f32[128,1024]{1,0:T(8,128)}, u32[]{:S(2)}) copy-start(f32[128,1024]{1,0:T(8,128)} %copy-done.3) | copy-start | bytes 1572868
  114.9 19.9 %copy-start.5 = (f32[128,1024]{1,0:T(8,128)S(1)}, f32[128,1024]{1,0:T(8,128)}, u32[]{:S(2)}) copy-start(f32[128,1024]{1,0:T(8,128)} %convolution_bitcast_fusion) | copy-start | bytes 1572868
  115.0 20.9 %copy-start.1 = (bf16[1024,1024]{1,0:T(8,128)(2,1)S(1)}, bf16[1024,1024]{1,0:T(8,128)(2,1)}, u32[]{:S(2)}) copy-start(bf16[1024,1024]{1,0:T(8,128)(2,1)} %param.16) | copy-start | bytes 6291460
  115.8 14.7 %collective-permute-start.16 = (bf16[128,512]{1,0:T(8,128)(2,1)S(1)}, bf16[128,512]{1,0:T(8,128)(2,1)S(1)}, u32[]{:S(2)}, u32[]{:S(2)}) collective-permute-start(bf16[128,512]{1,0:T(8,128)(2,1)S(1)} %get-tuple-element.25), channel_id=1, source_target_pairs={{0,3},{1,0},{2,1},{3,2},{4,7},{5,4},{6,5},{7,6},{8,11},{9,8},{10,9... | collective-permute-start | bytes 393224 | tf_op jit(solution)/shard_map/ppermute | solution.py:111
  116.8 13.7 %collective-permute-start.18 = (bf16[128,512]{1,0:T(8,128)(2,1)S(1)}, bf16[128,512]{1,0:T(8,128)(2,1)S(1)}, u32[]{:S(2)}, u32[]{:S(2)}) collective-permute-start(bf16[128,512]{1,0:T(8,128)(2,1)S(1)} %get-tuple-element.26), channel_id=1, source_target_pairs={{0,1},{1,2},{2,3},{3,0},{4,5},{5,6},{6,7},{7,4},{8,9},{9,10},{10,1... | collective-permute-start | bytes 393224 | tf_op jit(solution)/shard_map/ppermute | solution.py:111
  117.9 16.8 %collective-permute-start.17 = (bf16[128,512]{1,0:T(8,128)(2,1)S(1)}, bf16[128,512]{1,0:T(8,128)(2,1)S(1)}, u32[]{:S(2)}, u32[]{:S(2)}) collective-permute-start(bf16[128,512]{1,0:T(8,128)(2,1)S(1)} %get-tuple-element.27), channel_id=1, source_target_pairs={{0,2},{1,3},{2,0},{3,1},{4,6},{5,7},{6,4},{7,5},{8,10},{9,11},{10,... | collective-permute-start | bytes 393224 | tf_op jit(solution)/shard_map/ppermute | solution.py:111

commit v9 on v8

--- a/solution.py
+++ b/solution.py
@@ -177,6 +177,7 @@
     owners = lax.axis_size("exp")
     share = groups // owners
     both = jnp.concatenate([query, keyval], axis=-1)
+    remote = gather_w_out(lax.optimization_barrier((w_out, both))[0])
     parts = [lax.dynamic_slice_in_dim(both, here * share, share, 1)]
     for step in range(1, owners):
         send = lax.dynamic_slice_in_dim(both, (here + step) % owners * share, share, 1)
@@ -192,7 +193,6 @@
     seg_rows = step_rows(seg, rows)
     heads_out = attend(query_heads, keyval_heads, seg_rows, seg_rows, where_at, where_at)
     blocks = heads_out.reshape(owners, rows, -1)
-    remote = gather_w_out(w_out)
     attention = jnp.dot(blocks[0], w_out, preferred_element_type=jnp.float32)
     for step in range(1, owners):
         got = shifted(blocks[step], -step)

time: 136 us -> 146 us (1.074)
  waiting for transfers between devices: 32.4 us -> 38.1 us
  starting transfers between devices: 37 us -> 42 us
  local copies, waits for them, and re-layouts: 8.15 us -> 6.37 us
    ppermute x18, waiting for transfers between devices: 32.4 us -> 38.1 us  [shifted(): lax.ppermute(x, 'exp', [(j, (j + step) % count) for j in range(count)])]
    ppermute x18, starting transfers between devices: 37 us -> 42 us  [shifted(): lax.ppermute(x, 'exp', [(j, (j + step) % count) for j in range(count)])]
    dynamic_slice x1, local copies, waits for them, and re-layouts: 1.82 us -> 0.02 us  [gather_w_out(): mine = lax.dynamic_slice_in_dim(w_out, part * cut, cut, 0)]
    unnamed x39 -> x45, local copies, waits for them, and re-layouts: 3.39 us -> 3.4 us
  transfers between devices with their start and end apart: 19 -> 19, of which waited for: 9 -> 10; matrix products, arithmetic and copies ran while one was open for 30% -> 21% of each run, Pallas kernels for 0% -> 0%
where the time goes in v9:
time: 146 us
  matrix products  48.7 us (33%)
  starting transfers between devices  42 us (29%)
  waiting for transfers between devices  38.1 us (26%)
  other arithmetic  9.31 us (6%)
  local copies, waits for them, and re-layouts  6.37 us (4%)
    ppermute x18, starting transfers between devices, shifted(): lax.ppermute(x, 'exp', [(j, (j + step) % count) for j in range(count)])  42 us
    ppermute x18, waiting for transfers between devices, shifted(): lax.ppermute(x, 'exp', [(j, (j + step) % count) for j in range(count)])  38.1 us
    dot_general x3, matrix products, expert_mix(): jnp.einsum('esf,efd->esd', hidden, down, preferred_element_type=jnp.float32)  13 us
    dot_general x2, matrix products, expert_mix(): jnp.einsum('esd,edf->esf', received, w_gate, preferred_element_type=jnp.f...  10.4 us
    dot_general x3, matrix products, expert_mix(): jnp.einsum('est,esd->td', low, result, preferred_element_type=jnp.float32)  4.33 us
    sub x1, matrix products, attend(): expo = jnp.exp(score - top)  3.56 us
    unnamed x45, local copies, waits for them, and re-layouts  3.4 us
    dot_general x3, matrix products, expert_mix(): jnp.einsum('est,esd->td', high, result, preferred_element_type=jnp.float32)  2.93 us
  transfers between devices with their start and end apart: 19, of which 10 were waited for; matrix products, arithmetic and copies ran while one was open for 21% of the time, Pallas kernels for 0%

profile of v9, /device:TPU:0, one launch (start us, length us, event | category | flops | bytes accessed | tf_op | source)
XLA Modules:
  0.0 145.9 jit_solution(2964726634988159616)
XLA Ops:
  0.7 0.6 multiply_power_fusion
  1.3 0.9 compare_reduce_fusion
  2.1 1.1 fusion.90
  3.3 0.3 reduce-window.9
  3.8 0.7 bitcast_subtract_fusion
  4.5 0.7 convert_element_type.115
  5.2 1.7 %convolution_convert_fusion.3 = bf16[128,512]{1,0:T(8,128)(2,1)S(1)} fusion(bf16[1024,512]{1,0:T(8,128)(2,1)} %param.18, bf16[128,1024]{1,0:T(8,128)(2,1)} %param.14, f32[1024]{0:T(1024)S(1)} %convert_element_type.115, f32[128]{0:T(128)S(1)} %add_rsqrt_fusion.1), kind=kOutput, calls=%fused_computation.62 | convolution fusion | flops 134807552 | bytes 1446400 | tf_op jit(solution)/shard_map/dot_general | solution.py:172
  7.0 2.6 %fusion.168 = f32[128,512]{0,1:T(8,128)} fusion(bf16[1024,512]{1,0:T(8,128)(2,1)} %param.17, bf16[128,1024]{1,0:T(8,128)(2,1)} %param.14, f32[1024]{0:T(1024)S(1)} %convert_element_type.115, f32[128]{0:T(128)S(1)} %add_rsqrt_fusion.1), kind=kOutput, calls=%fused_computation.225 | convolution fusion | flops 134742016 | bytes 1577472 | tf_op jit(solution)/shard_map/dot_general | solution.py:169
  9.6 1.0 fusion.170
  10.6 0.8 dynamic-slice_convert_fusion
  11.4 0.8 multiply_cosine_fusion
  12.2 1.0 subtract_convert_fusion.1
  13.4 5.1 %collective-permute-start.6 = (bf16[128,1024]{1,0:T(8,128)(2,1)S(1)}, bf16[128,1024]{1,0:T(8,128)(2,1)S(1)}, u32[]{:S(2)}, u32[]{:S(2)}) collective-permute-start(bf16[128,1024]{1,0:T(8,128)(2,1)S(1)} %constant_dynamic-slice_fusion.4), channel_id=1, source_target_pairs={{0,3},{1,0},{2,1},{3,2},{4,7},{5,4},{6,5},{7,6},{8,11},{9,8},{10,9... | collective-permute-start | bytes 786440 | tf_op jit(solution)/shard_map/ppermute | solution.py:111
  18.6 0.5 collective-permute-start.2
  19.1 2.6 %collective-permute-start.1 = (bf16[128,2,256]{0,2,1:T(8,128)(2,1)S(1)}, bf16[128,2,256]{0,2,1:T(8,128)(2,1)S(1)}, u32[]{:S(2)}, u32[]{:S(2)}) collective-permute-start(bf16[128,2,256]{0,2,1:T(8,128)(2,1)S(1)} %get-tuple-element.22), channel_id=1, source_target_pairs={{0,2},{1,3},{2,0},{3,1},{4,6},{5,7},{6,4},{7,5},{8,10},{9,11},{10,... | collective-permute-start | bytes 393224 | tf_op jit(solution)/shard_map/ppermute | solution.py:111
  21.7 1.9 %collective-permute-start = (bf16[128,2,256]{0,2,1:T(8,128)(2,1)S(1)}, bf16[128,2,256]{0,2,1:T(8,128)(2,1)S(1)}, u32[]{:S(2)}, u32[]{:S(2)}) collective-permute-start(bf16[128,2,256]{0,2,1:T(8,128)(2,1)S(1)} %get-tuple-element.23), channel_id=1, source_target_pairs={{0,1},{1,2},{2,3},{3,0},{4,5},{5,6},{6,7},{7,4},{8,9},{9,10},{10,1... | collective-permute-start | bytes 393224 | tf_op jit(solution)/shard_map/ppermute | solution.py:111
  24.0 0.3 compare_and_fusion
  24.5 9.2 %collective-permute-done.2 = bf16[128,2,256]{0,2,1:T(8,128)(2,1)S(1)} collective-permute-done((bf16[128,2,256]{0,2,1:T(8,128)(2,1)S(1)}, bf16[128,2,256]{0,2,1:T(8,128)(2,1)S(1)}, u32[]{:S(2)}, u32[]{:S(2)}) %collective-permute-start.2) | collective-permute-done | bytes 131104 | tf_op jit(solution)/shard_map/ppermute | solution.py:111
  33.7 17.3 %collective-permute-start.4 = (bf16[128,1024]{1,0:T(8,128)(2,1)S(1)}, bf16[128,1024]{1,0:T(8,128)(2,1)S(1)}, u32[]{:S(2)}, u32[]{:S(2)}) collective-permute-start(bf16[128,1024]{1,0:T(8,128)(2,1)S(1)} %constant_dynamic-slice_fusion.4), channel_id=1, source_target_pairs={{0,1},{1,2},{2,3},{3,0},{4,5},{5,6},{6,7},{7,4},{8,9},{9,10},{10,1... | collective-permute-start | bytes 786440 | tf_op jit(solution)/shard_map/ppermute | solution.py:111
  51.0 1.1 collective-permute-done.1
  52.2 0.3 convolution_convert_fusion.2
  52.6 1.0 copy.76
  53.5 3.6 %fusion.175 = (f32[2,2,512]{2,1,0:T(2,128)S(1)}, f32[2,2,512,512]{2,3,1,0:T(8,128)}) fusion(pred[512,512]{0,1:T(8,128)(4,1)S(1)} %compare_and_fusion, bf16[512,2,2,64]{0,3,2,1:T(8,128)(2,1)S(1)} %bitcast.165, bf16[512,2,256]{0,2,1:T(8,128)(2,1)S(1)} %pad_maximum_fusion.3), kind=kOutput, calls=%fused_computation.230 | convolution fusion | flops 138412544 | bytes 4857856 | tf_op jit(solution)/shard_map/sub | solution.py:44
  57.3 2.7 %fusion.71 = bf16[512,2,2,64]{0,3,2,1:T(8,128)(2,1)S(1)} fusion(f32[2,2,512,512]{2,3,1,0:T(8,128)} %get-tuple-element.49, f32[2,2,512]{2,1,0:T(2,128)S(1)} %get-tuple-element.48, bf16[512,2,256]{0,2,1:T(8,128)(2,1)S(1)} %pad_maximum_fusion.3), kind=kOutput, calls=%fused_computation.61 | convolution fusion | flops 136445952 | bytes 4595712 | tf_op jit(solution)/shard_map/kgqt,tkd->qkgd/dot_general | solution.py:46
  60.4 3.7 %collective-permute-start.3 = (bf16[128,256]{0,1:T(8,128)(2,1)S(1)}, bf16[128,256]{0,1:T(8,128)(2,1)S(1)}, u32[]{:S(2)}, u32[]{:S(2)}) collective-permute-start(bf16[128,256]{0,1:T(8,128)(2,1)S(1)} %bitcast.169), channel_id=1, source_target_pairs={{0,3},{1,0},{2,1},{3,2},{4,7},{5,4},{6,5},{7,6},{8,11},{9,8},{10,9... | collective-permute-start | bytes 196616 | tf_op jit(solution)/shard_map/ppermute | solution.py:111
  64.3 1.2 broadcast_select_fusion.1
  65.6 2.6 %collective-permute-done.3 = bf16[128,256]{0,1:T(8,128)(2,1)S(1)} collective-permute-done((bf16[128,256]{0,1:T(8,128)(2,1)S(1)}, bf16[128,256]{0,1:T(8,128)(2,1)S(1)}, u32[]{:S(2)}, u32[]{:S(2)}) %collective-permute-start.3) | collective-permute-done | bytes 65568 | tf_op jit(solution)/shard_map/ppermute | solution.py:111
  68.1 0.3 convolution_add_fusion.1
  68.4 0.2 fusion.100
  68.6 0.3 collective-permute-done.8
  68.9 0.4 multiply_reduce_fusion
  70.1 2.1 %collective-permute-start.12 = (bf16[128,1152]{1,0:T(8,128)(2,1)S(1)}, bf16[128,1152]{1,0:T(8,128)(2,1)}, u32[]{:S(2)}, u32[]{:S(2)}) collective-permute-start(bf16[128,1152]{1,0:T(8,128)(2,1)S(1)} %concatenate.47), channel_id=1, source_target_pairs={{0,3},{1,0},{2,1},{3,2},{4,7},{5,4},{6,5},{7,6},{8,11},{9,8},{10,9... | collective-permute-start | bytes 884744 | tf_op jit(solution)/shard_map/ppermute | solution.py:111
  72.2 1.5 %collective-permute-start.11 = (bf16[128,1152]{1,0:T(8,128)(2,1)S(1)}, bf16[128,1152]{1,0:T(8,128)(2,1)}, u32[]{:S(2)}, u32[]{:S(2)}) collective-permute-start(bf16[128,1152]{1,0:T(8,128)(2,1)S(1)} %concatenate.47), channel_id=1, source_target_pairs={{0,2},{1,3},{2,0},{3,1},{4,6},{5,7},{6,4},{7,5},{8,10},{9,11},{10,... | collective-permute-start | bytes 884744 | tf_op jit(solution)/shard_map/ppermute | solution.py:111
  73.9 0.3 fusion.73
  74.2 0.4 convolution_convert_fusion.1
  74.6 5.0 %fusion.178 = f32[8,64,512]{2,1,0:T(8,128)S(1)} fusion(bf16[8,64,1024]{2,1,0:T(8,128)(2,1)S(1)} %convolution_convert_fusion.1, bf16[8,1024,512]{2,1,0:T(8,128)(2,1)} %param.22), kind=kOutput, calls=%fused_computation.233 | convolution fusion | flops 536870912 | bytes 10485760 | tf_op jit(solution)/shard_map/esd,edf->esf/dot_general | solution.py:89
  79.6 8.8 %convolution_convert_fusion = bf16[8,64,1024]{2,1,0:T(8,128)(2,1)S(1)} fusion(bf16[8,512,1024]{2,1,0:T(8,128)(2,1)} %param.24, bf16[8,64,1024]{2,1,0:T(8,128)(2,1)S(1)} %convolution_convert_fusion.1, bf16[8,1024,512]{2,1,0:T(8,128)(2,1)} %param.23, f32[8,64,512]{2,1,0:T(8,128)S(1)} %fusion.178), kind=kOutput, calls=%fused_computation.26 | convolution fusion | flops 1075838976 | bytes 19922944 | tf_op jit(solution)/shard_map/esf,efd->esd/dot_general | solution.py:99
  88.5 1.2 convolution_bitcast_fusion
  89.7 2.7 %collective-permute-done.10 = bf16[128,1152]{1,0:T(8,128)(2,1)} collective-permute-done((bf16[128,1152]{1,0:T(8,128)(2,1)S(1)}, bf16[128,1152]{1,0:T(8,128)(2,1)}, u32[]{:S(2)}, u32[]{:S(2)}) %collective-permute-start.10) | collective-permute-done | bytes 294944 | tf_op jit(solution)/shard_map/ppermute | solution.py:111
  92.5 1.0 constant_dynamic-update-slice_fusion.2
  93.5 5.8 %collective-permute-done.11 = bf16[128,1152]{1,0:T(8,128)(2,1)} collective-permute-done((bf16[128,1152]{1,0:T(8,128)(2,1)S(1)}, bf16[128,1152]{1,0:T(8,128)(2,1)}, u32[]{:S(2)}, u32[]{:S(2)}) %collective-permute-start.11) | collective-permute-done | bytes 294944 | tf_op jit(solution)/shard_map/ppermute | solution.py:111
  99.3 1.0 constant_dynamic-update-slice_fusion.1
  100.3 1.0 constant_dynamic-update-slice_fusion
  101.7 0.3 fusion.72
  102.0 1.8 %fusion.11 = bf16[8,192,1024]{2,1,0:T(8,128)(2,1)S(1)} fusion(s32[8,384]{1,0:T(8,128)S(1)} %fusion.72, pred[8,384]{1,0:T(8,128)(4,1)S(1)} %copy.72, bf16[384,1152]{1,0:T(8,128)(2,1)S(1)} %constant_dynamic-update-slice_fusion), kind=kOutput, calls=%fused_computation.15 | convolution fusion | flops 1210712064 | bytes 3947520 | tf_op jit(solution)/shard_map/est,td->esd/dot_general | solution.py:86
  103.9 5.4 %fusion.179 = f32[8,192,512]{2,1,0:T(8,128)S(1)} fusion(bf16[8,192,1024]{2,1,0:T(8,128)(2,1)S(1)} %fusion.11, bf16[8,1024,512]{2,1,0:T(8,128)(2,1)} %param.22), kind=kOutput, calls=%fused_computation.234 | convolution fusion | flops 1610612736 | bytes 14680064 | tf_op jit(solution)/shard_map/esd,edf->esf/dot_general | solution.py:89
  109.3 2.0 %multiply_convert_fusion = bf16[8,192,512]{2,1,0:T(8,128)(2,1)S(1)} fusion(f32[8,192,512]{2,1,0:T(8,128)S(1)} %fusion.179, bf16[8,192,1024]{2,1,0:T(8,128)(2,1)S(1)} %fusion.11, bf16[8,1024,512]{2,1,0:T(8,128)(2,1)S(1)} %bitcast.152), kind=kOutput, calls=%fused_computation.9 | convolution fusion | flops 1615331328 | bytes 16252928 | tf_op jit(solution)/shard_map/esd,edf->esf/dot_general | solution.py:90
  111.3 0.3 slice-done.3
  111.6 2.2 %fusion.21 = bf16[8,192,512]{2,1,0:T(8,128)(2,1)} fusion(bf16[8,192,512]{2,1,0:T(8,128)(2,1)S(1)} %multiply_convert_fusion, bf16[8,512,1024]{2,1,0:T(8,128)(2,1)S(1)} %bitcast.154), kind=kOutput, calls=%fused_computation.25 | convolution fusion | flops 806092800 | bytes 7340032 | tf_op jit(solution)/shard_map/esf,efd->esd/dot_general | solution.py:99
  113.7 2.1 %fusion.18 = bf16[8,192,512]{2,1,0:T(8,128)(2,1)} fusion(bf16[8,192,512]{2,1,0:T(8,128)(2,1)S(1)} %multiply_convert_fusion, bf16[8,512,1024]{2,1,0:T(8,128)(2,1)S(1)} %bitcast.154), kind=kOutput, calls=%fused_computation.24 | convolution fusion | flops 806092800 | bytes 7340032 | tf_op jit(solution)/shard_map/esf,efd->esd/dot_general | solution.py:99
  116.0 2.4 %fusion.33 = f32[384,512]{1,0:T(8,128)S(1)} fusion(bf16[8,192,512]{2,1,0:T(8,128)(2,1)} %fusion.18, s32[8,384]{1,0:T(8,128)S(1)} %fusion.72, pred[8,384]{1,0:T(8,128)(4,1)S(1)} %copy.72, bf16[8,384]{1,0:T(8,128)(2,1)S(1)} %copy.74), kind=kOutput, calls=%fused_computation.34 | convolution fusion | flops 605749248 | bytes 2380800 | tf_op jit(solution)/shard_map/est,esd->td/dot_general | solution.py:102
  118.4 1.1 fusion.51
  119.6 2.0 %collective-permute-start.15 = (bf16[128,512]{1,0:T(8,128)(2,1)S(1)}, bf16[128,512]{1,0:T(8,128)(2,1)S(1)}, u32[]{:S(2)}, u32[]{:S(2)}) collective-permute-start(bf16[128,512]{1,0:T(8,128)(2,1)S(1)} %get-tuple-element.25), channel_id=1, source_target_pairs={{0,1},{1,2},{2,3},{3,0},{4,5},{5,6},{6,7},{7,4},{8,9},{9,10},{10,1... | collective-permute-start | bytes 393224 | tf_op jit(solution)/shard_map/ppermute | solution.py:111
  121.6 2.2 %collective-permute-start.14 = (bf16[128,512]{1,0:T(8,128)(2,1)S(1)}, bf16[128,512]{1,0:T(8,128)(2,1)S(1)}, u32[]{:S(2)}, u32[]{:S(2)}) collective-permute-start(bf16[128,512]{1,0:T(8,128)(2,1)S(1)} %get-tuple-element.26), channel_id=1, source_target_pairs={{0,2},{1,3},{2,0},{3,1},{4,6},{5,7},{6,4},{7,5},{8,10},{9,11},{10,... | collective-permute-start | bytes 393224 | tf_op jit(solution)/shard_map/ppermute | solution.py:111
  123.8 0.8 fusion.36
  124.6 0.8 fusion.54
  125.5 1.0 collective-permute-start.16
  126.5 1.1 collective-permute-start.18
  127.6 0.7 collective-permute-start.17
  128.3 2.2 %collective-permute-done.15 = bf16[128,512]{1,0:T(8,128)(2,1)S(1)} collective-permute-done((bf16[128,512]{1,0:T(8,128)(2,1)S(1)}, bf16[128,512]{1,0:T(8,128)(2,1)S(1)}, u32[]{:S(2)}, u32[]{:S(2)}) %collective-permute-start.15) | collective-permute-done | bytes 131104 | tf_op jit(solution)/shard_map/ppermute | solution.py:111
  130.5 5.2 %collective-permute-done.14 = bf16[128,512]{1,0:T(8,128)(2,1)S(1)} collective-permute-done((bf16[128,512]{1,0:T(8,128)(2,1)S(1)}, bf16[128,512]{1,0:T(8,128)(2,1)S(1)}, u32[]{:S(2)}, u32[]{:S(2)}) %collective-permute-start.14) | collective-permute-done | bytes 131104 | tf_op jit(solution)/shard_map/ppermute | solution.py:111
  135.8 3.1 %collective-permute-done.18 = bf16[128,512]{1,0:T(8,128)(2,1)S(1)} collective-permute-done((bf16[128,512]{1,0:T(8,128)(2,1)S(1)}, bf16[128,512]{1,0:T(8,128)(2,1)S(1)}, u32[]{:S(2)}, u32[]{:S(2)}) %collective-permute-start.18) | collective-permute-done | bytes 131104 | tf_op jit(solution)/shard_map/ppermute | solution.py:111
  138.9 5.9 %collective-permute-done.17 = bf16[128,512]{1,0:T(8,128)(2,1)S(1)} collective-permute-done((bf16[128,512]{1,0:T(8,128)(2,1)S(1)}, bf16[128,512]{1,0:T(8,128)(2,1)S(1)}, u32[]{:S(2)}, u32[]{:S(2)}) %collective-permute-start.17) | collective-permute-done | bytes 131104 | tf_op jit(solution)/shard_map/ppermute | solution.py:111
  144.8 1.1 fusion.104
  (119 shorter events, 3.9 us)
Async XLA Ops:
  0.6 9.0 %copy-start = (bf16[1024,1024]{1,0:T(8,128)(2,1)S(1)}, bf16[1024,1024]{1,0:T(8,128)(2,1)}, u32[]{:S(2)}) copy-start(bf16[1024,1024]{1,0:T(8,128)(2,1)} %param.16) | copy-start | bytes 6291460
  0.6 9.0 %copy-start.2 = (bf16[128,1024]{1,0:T(8,128)(2,1)S(1)}, bf16[128,1024]{1,0:T(8,128)(2,1)}, u32[]{:S(2)}) copy-start(bf16[128,1024]{1,0:T(8,128)(2,1)} %param.14) | copy-start | bytes 786436
  9.6 3.8 %copy-start.6 = (bf16[256,1024]{1,0:T(8,128)(2,1)S(1)}, bf16[256,1024]{1,0:T(8,128)(2,1)}, u32[]{:S(2)}) copy-start(bf16[256,1024]{1,0:T(8,128)(2,1)} %param.19) | copy-start | bytes 1572868
  9.6 14.2 %copy-start.12 = (s32[1,512]{1,0:T(1,128)S(1)}, s32[1,512]{1,0:T(1,128)}, u32[]{:S(2)}) copy-start(s32[1,512]{1,0:T(1,128)} %param.25) | copy-start | bytes 6148
  9.6 14.3 %copy-start.11 = (s32[128,8]{0,1:T(8,128)S(1)}, s32[128,8]{0,1:T(8,128)}, u32[]{:S(2)}) copy-start(s32[128,8]{0,1:T(8,128)} %param.27) | copy-start | bytes 12292
  10.6 13.3 %copy-start.13 = (s32[1,512]{1,0:T(1,128)S(1)}, s32[1,512]{1,0:T(1,128)}, u32[]{:S(2)}) copy-start(s32[1,512]{1,0:T(1,128)} %param.26) | copy-start | bytes 6148
  10.6 13.7 %copy-start.14 = (bf16[1024]{0:T(1024)(128)(2,1)S(1)}, bf16[1024]{0:T(1024)(128)(2,1)}, u32[]{:S(2)}) copy-start(bf16[1024]{0:T(1024)(128)(2,1)} %param.20) | copy-start | bytes 6148
  13.4 43.7 %collective-permute-start.6 = (bf16[128,1024]{1,0:T(8,128)(2,1)S(1)}, bf16[128,1024]{1,0:T(8,128)(2,1)S(1)}, u32[]{:S(2)}, u32[]{:S(2)}) collective-permute-start(bf16[128,1024]{1,0:T(8,128)(2,1)S(1)} %constant_dynamic-slice_fusion.4), channel_id=1, source_target_pairs={{0,3},{1,0},{2,1},{3,2},{4,7},{5,4},{6,5},{7,6},{8,11},{9,8},{10,9... | collective-permute-start | bytes 786440 | tf_op jit(solution)/shard_map/ppermute | solution.py:111
  18.6 38.5 %collective-permute-start.5 = (bf16[128,1024]{1,0:T(8,128)(2,1)S(1)}, bf16[128,1024]{1,0:T(8,128)(2,1)S(1)}, u32[]{:S(2)}, u32[]{:S(2)}) collective-permute-start(bf16[128,1024]{1,0:T(8,128)(2,1)S(1)} %constant_dynamic-slice_fusion.4), channel_id=1, source_target_pairs={{0,2},{1,3},{2,0},{3,1},{4,6},{5,7},{6,4},{7,5},{8,10},{9,11},{10,... | collective-permute-start | bytes 786440 | tf_op jit(solution)/shard_map/ppermute | solution.py:111
  18.6 15.1 %collective-permute-start.2 = (bf16[128,2,256]{0,2,1:T(8,128)(2,1)S(1)}, bf16[128,2,256]{0,2,1:T(8,128)(2,1)S(1)}, u32[]{:S(2)}, u32[]{:S(2)}) collective-permute-start(bf16[128,2,256]{0,2,1:T(8,128)(2,1)S(1)} %get-tuple-element.21), channel_id=1, source_target_pairs={{0,3},{1,0},{2,1},{3,2},{4,7},{5,4},{6,5},{7,6},{8,11},{9,8},{10,9... | collective-permute-start | bytes 393224 | tf_op jit(solution)/shard_map/ppermute | solution.py:111
  19.1 33.0 %collective-permute-start.1 = (bf16[128,2,256]{0,2,1:T(8,128)(2,1)S(1)}, bf16[128,2,256]{0,2,1:T(8,128)(2,1)S(1)}, u32[]{:S(2)}, u32[]{:S(2)}) collective-permute-start(bf16[128,2,256]{0,2,1:T(8,128)(2,1)S(1)} %get-tuple-element.22), channel_id=1, source_target_pairs={{0,2},{1,3},{2,0},{3,1},{4,6},{5,7},{6,4},{7,5},{8,10},{9,11},{10,... | collective-permute-start | bytes 393224 | tf_op jit(solution)/shard_map/ppermute | solution.py:111
  21.7 30.4 %collective-permute-start = (bf16[128,2,256]{0,2,1:T(8,128)(2,1)S(1)}, bf16[128,2,256]{0,2,1:T(8,128)(2,1)S(1)}, u32[]{:S(2)}, u32[]{:S(2)}) collective-permute-start(bf16[128,2,256]{0,2,1:T(8,128)(2,1)S(1)} %get-tuple-element.23), channel_id=1, source_target_pairs={{0,1},{1,2},{2,3},{3,0},{4,5},{5,6},{6,7},{7,4},{8,9},{9,10},{10,1... | collective-permute-start | bytes 393224 | tf_op jit(solution)/shard_map/ppermute | solution.py:111
  33.7 23.4 %collective-permute-start.4 = (bf16[128,1024]{1,0:T(8,128)(2,1)S(1)}, bf16[128,1024]{1,0:T(8,128)(2,1)S(1)}, u32[]{:S(2)}, u32[]{:S(2)}) collective-permute-start(bf16[128,1024]{1,0:T(8,128)(2,1)S(1)} %constant_dynamic-slice_fusion.4), channel_id=1, source_target_pairs={{0,1},{1,2},{2,3},{3,0},{4,5},{5,6},{6,7},{7,4},{8,9},{9,10},{10,1... | collective-permute-start | bytes 786440 | tf_op jit(solution)/shard_map/ppermute | solution.py:111
  57.1 3.0 %copy-start.7 = (bf16[128,1024]{1,0:T(8,128)(2,1)}, bf16[128,1024]{1,0:T(8,128)(2,1)S(1)}, u32[]{:S(2)}) copy-start(bf16[128,1024]{1,0:T(8,128)(2,1)S(1)} %collective-permute-done.6) | copy-start | bytes 786436
  57.1 3.0 %copy-start.8 = (bf16[128,1024]{1,0:T(8,128)(2,1)}, bf16[128,1024]{1,0:T(8,128)(2,1)S(1)}, u32[]{:S(2)}) copy-start(bf16[128,1024]{1,0:T(8,128)(2,1)S(1)} %collective-permute-done.5) | copy-start | bytes 786436
  57.1 3.0 %copy-start.9 = (bf16[128,1024]{1,0:T(8,128)(2,1)}, bf16[128,1024]{1,0:T(8,128)(2,1)S(1)}, u32[]{:S(2)}) copy-start(bf16[128,1024]{1,0:T(8,128)(2,1)S(1)} %collective-permute-done.4) | copy-start | bytes 786436
  57.2 7.1 %collective-permute-start.7 = (bf16[3,128,1024]{2,1,0:T(8,128)(2,1)S(1)}, bf16[3,128,1024]{2,1,0:T(8,128)(2,1)S(1)}, u32[]{:S(2)}, u32[]{:S(2)}) collective-permute-start(bf16[3,128,1024]{2,1,0:T(8,128)(2,1)S(1)} %pad_maximum_fusion), channel_id=1, source_target_pairs={{0,4},{4,0},{8,12},{12,8},{16,20},{20,16},{24,28},{28,24},{1,5},{5... | collective-permute-start | bytes 2359304 | tf_op jit(solution)/shard_map/ppermute | solution.py:137
  60.2 8.2 %collective-permute-start.9 = (bf16[128,256]{0,1:T(8,128)(2,1)S(1)}, bf16[128,256]{0,1:T(8,128)(2,1)S(1)}, u32[]{:S(2)}, u32[]{:S(2)}) collective-permute-start(bf16[128,256]{0,1:T(8,128)(2,1)S(1)} %bitcast.168), channel_id=1, source_target_pairs={{0,1},{1,2},{2,3},{3,0},{4,5},{5,6},{6,7},{7,4},{8,9},{9,10},{10,1... | collective-permute-start | bytes 196616 | tf_op jit(solution)/shard_map/ppermute | solution.py:111
  60.4 8.5 %collective-permute-start.8 = (bf16[128,256]{0,1:T(8,128)(2,1)S(1)}, bf16[128,256]{0,1:T(8,128)(2,1)S(1)}, u32[]{:S(2)}, u32[]{:S(2)}) collective-permute-start(bf16[128,256]{0,1:T(8,128)(2,1)S(1)} %bitcast.167), channel_id=1, source_target_pairs={{0,2},{1,3},{2,0},{3,1},{4,6},{5,7},{6,4},{7,5},{8,10},{9,11},{10,... | collective-permute-start | bytes 196616 | tf_op jit(solution)/shard_map/ppermute | solution.py:111
  60.4 7.7 %collective-permute-start.3 = (bf16[128,256]{0,1:T(8,128)(2,1)S(1)}, bf16[128,256]{0,1:T(8,128)(2,1)S(1)}, u32[]{:S(2)}, u32[]{:S(2)}) collective-permute-start(bf16[128,256]{0,1:T(8,128)(2,1)S(1)} %bitcast.169), channel_id=1, source_target_pairs={{0,3},{1,0},{2,1},{3,2},{4,7},{5,4},{6,5},{7,6},{8,11},{9,8},{10,9... | collective-permute-start | bytes 196616 | tf_op jit(solution)/shard_map/ppermute | solution.py:111
  68.4 1.1 copy-start.10
  69.3 4.9 %copy-start.3 = (f32[128,1024]{1,0:T(8,128)}, f32[128,1024]{1,0:T(8,128)S(1)}, u32[]{:S(2)}) copy-start(f32[128,1024]{1,0:T(8,128)S(1)} %get-tuple-element.51) | copy-start | bytes 1572868
  70.1 30.2 %collective-permute-start.12 = (bf16[128,1152]{1,0:T(8,128)(2,1)S(1)}, bf16[128,1152]{1,0:T(8,128)(2,1)}, u32[]{:S(2)}, u32[]{:S(2)}) collective-permute-start(bf16[128,1152]{1,0:T(8,128)(2,1)S(1)} %concatenate.47), channel_id=1, source_target_pairs={{0,3},{1,0},{2,1},{3,2},{4,7},{5,4},{6,5},{7,6},{8,11},{9,8},{10,9... | collective-permute-start | bytes 884744 | tf_op jit(solution)/shard_map/ppermute | solution.py:111
  72.2 27.1 %collective-permute-start.11 = (bf16[128,1152]{1,0:T(8,128)(2,1)S(1)}, bf16[128,1152]{1,0:T(8,128)(2,1)}, u32[]{:S(2)}, u32[]{:S(2)}) collective-permute-start(bf16[128,1152]{1,0:T(8,128)(2,1)S(1)} %concatenate.47), channel_id=1, source_target_pairs={{0,2},{1,3},{2,0},{3,1},{4,6},{5,7},{6,4},{7,5},{8,10},{9,11},{10,... | collective-permute-start | bytes 884744 | tf_op jit(solution)/shard_map/ppermute | solution.py:111
  73.7 18.8 %collective-permute-start.10 = (bf16[128,1152]{1,0:T(8,128)(2,1)S(1)}, bf16[128,1152]{1,0:T(8,128)(2,1)}, u32[]{:S(2)}, u32[]{:S(2)}) collective-permute-start(bf16[128,1152]{1,0:T(8,128)(2,1)S(1)} %concatenate.47), channel_id=1, source_target_pairs={{0,1},{1,2},{2,3},{3,0},{4,5},{5,6},{6,7},{7,4},{8,9},{9,10},{10,1... | collective-permute-start | bytes 884744 | tf_op jit(solution)/shard_map/ppermute | solution.py:111
  102.0 7.3 %slice-start = ((s8[8388608]{0:T(1024)(128)(4,1)}), s8[4194304]{0:T(1024)(128)(4,1)S(1)}, s32[]{:S(2)}) async-start(s8[8388608]{0:T(1024)(128)(4,1)} %bitcast.151), calls=%async_computation | async-start | bytes 8388608
  103.8 5.4 %slice-start.1 = ((s8[8388608]{0:T(1024)(128)(4,1)}), s8[4194304]{0:T(1024)(128)(4,1)S(1)}, s32[]{:S(2)}) async-start(s8[8388608]{0:T(1024)(128)(4,1)} %bitcast.151), calls=%async_computation.1 | async-start | bytes 8388608
  103.8 7.4 %slice-start.2 = ((s8[8388608]{0:T(1024)(128)(4,1)}), s8[4194304]{0:T(1024)(128)(4,1)S(1)}, s32[]{:S(2)}) async-start(s8[8388608]{0:T(1024)(128)(4,1)} %bitcast.153), calls=%async_computation.2 | async-start | bytes 8388608
  109.3 2.3 %slice-start.3 = ((s8[8388608]{0:T(1024)(128)(4,1)}), s8[4194304]{0:T(1024)(128)(4,1)S(1)}, s32[]{:S(2)}) async-start(s8[8388608]{0:T(1024)(128)(4,1)} %bitcast.153), calls=%async_computation.3 | async-start | bytes 8388608
  116.0 2.4 %copy-start.16 = (bf16[8,192,512]{2,1,0:T(8,128)(2,1)S(1)}, bf16[8,192,512]{2,1,0:T(8,128)(2,1)}, u32[]{:S(2)}) copy-start(bf16[8,192,512]{2,1,0:T(8,128)(2,1)} %fusion.18) | copy-start | bytes 4718596
  118.4 5.4 %copy-start.15 = (bf16[8,192,512]{2,1,0:T(8,128)(2,1)S(1)}, bf16[8,192,512]{2,1,0:T(8,128)(2,1)}, u32[]{:S(2)}) copy-start(bf16[8,192,512]{2,1,0:T(8,128)(2,1)} %fusion.21) | copy-start | bytes 4718596
  119.5 8.1 %collective-permute-start.13 = (bf16[128,512]{1,0:T(8,128)(2,1)S(1)}, bf16[128,512]{1,0:T(8,128)(2,1)S(1)}, u32[]{:S(2)}, u32[]{:S(2)}) collective-permute-start(bf16[128,512]{1,0:T(8,128)(2,1)S(1)} %get-tuple-element.24), channel_id=1, source_target_pairs={{0,3},{1,0},{2,1},{3,2},{4,7},{5,4},{6,5},{7,6},{8,11},{9,8},{10,9... | collective-permute-start | bytes 393224 | tf_op jit(solution)/shard_map/ppermute | solution.py:111
  119.6 10.9 %collective-permute-start.15 = (bf16[128,512]{1,0:T(8,128)(2,1)S(1)}, bf16[128,512]{1,0:T(8,128)(2,1)S(1)}, u32[]{:S(2)}, u32[]{:S(2)}) collective-permute-start(bf16[128,512]{1,0:T(8,128)(2,1)S(1)} %get-tuple-element.25), channel_id=1, source_target_pairs={{0,1},{1,2},{2,3},{3,0},{4,5},{5,6},{6,7},{7,4},{8,9},{9,10},{10,1... | collective-permute-start | bytes 393224 | tf_op jit(solution)/shard_map/ppermute | solution.py:111
  121.6 14.1 %collective-permute-start.14 = (bf16[128,512]{1,0:T(8,128)(2,1)S(1)}, bf16[128,512]{1,0:T(8,128)(2,1)S(1)}, u32[]{:S(2)}, u32[]{:S(2)}) collective-permute-start(bf16[128,512]{1,0:T(8,128)(2,1)S(1)} %get-tuple-element.26), channel_id=1, source_target_pairs={{0,2},{1,3},{2,0},{3,1},{4,6},{5,7},{6,4},{7,5},{8,10},{9,11},{10,... | collective-permute-start | bytes 393224 | tf_op jit(solution)/shard_map/ppermute | solution.py:111
  124.6 20.2 %copy-start.4 = (f32[128,1024]{1,0:T(8,128)S(1)}, f32[128,1024]{1,0:T(8,128)}, u32[]{:S(2)}) copy-start(f32[128,1024]{1,0:T(8,128)} %copy-done.3) | copy-start | bytes 1572868
  124.6 20.2 %copy-start.5 = (f32[128,1024]{1,0:T(8,128)S(1)}, f32[128,1024]{1,0:T(8,128)}, u32[]{:S(2)}) copy-start(f32[128,1024]{1,0:T(8,128)} %convolution_bitcast_fusion) | copy-start | bytes 1572868
  124.6 21.2 %copy-start.1 = (bf16[1024,1024]{1,0:T(8,128)(2,1)S(1)}, bf16[1024,1024]{1,0:T(8,128)(2,1)}, u32[]{:S(2)}) copy-start(bf16[1024,1024]{1,0:T(8,128)(2,1)} %param.16) | copy-start | bytes 6291460
  125.5 10.3 %collective-permute-start.16 = (bf16[128,512]{1,0:T(8,128)(2,1)S(1)}, bf16[128,512]{1,0:T(8,128)(2,1)S(1)}, u32[]{:S(2)}, u32[]{:S(2)}) collective-permute-start(bf16[128,512]{1,0:T(8,128)(2,1)S(1)} %get-tuple-element.27), channel_id=1, source_target_pairs={{0,3},{1,0},{2,1},{3,2},{4,7},{5,4},{6,5},{7,6},{8,11},{9,8},{10,9... | collective-permute-start | bytes 393224 | tf_op jit(solution)/shard_map/ppermute | solution.py:111
  126.5 12.3 %collective-permute-start.18 = (bf16[128,512]{1,0:T(8,128)(2,1)S(1)}, bf16[128,512]{1,0:T(8,128)(2,1)S(1)}, u32[]{:S(2)}, u32[]{:S(2)}) collective-permute-start(bf16[128,512]{1,0:T(8,128)(2,1)S(1)} %get-tuple-element.28), channel_id=1, source_target_pairs={{0,1},{1,2},{2,3},{3,0},{4,5},{5,6},{6,7},{7,4},{8,9},{9,10},{10,1... | collective-permute-start | bytes 393224 | tf_op jit(solution)/shard_map/ppermute | solution.py:111
  127.6 17.1 %collective-permute-start.17 = (bf16[128,512]{1,0:T(8,128)(2,1)S(1)}, bf16[128,512]{1,0:T(8,128)(2,1)S(1)}, u32[]{:S(2)}, u32[]{:S(2)}) collective-permute-start(bf16[128,512]{1,0:T(8,128)(2,1)S(1)} %get-tuple-element.29), channel_id=1, source_target_pairs={{0,2},{1,3},{2,0},{3,1},{4,6},{5,7},{6,4},{7,5},{8,10},{9,11},{10,... | collective-permute-start | bytes 393224 | tf_op jit(solution)/shard_map/ppermute | solution.py:111

commit v10 on v8

--- a/solution.py
+++ b/solution.py
@@ -93,17 +93,15 @@
     high = jnp.where(picks, high.T[:, None, :], zero)
     low = jnp.where(picks, low.T[:, None, :], zero)
     cut = w_down.shape[2] // pieces
-    outs = []
+    results = []
     for piece in range(pieces):
         down = lax.slice_in_dim(w_down, piece * cut, (piece + 1) * cut, axis=2)
         result = jnp.einsum("esf,efd->esd", hidden, down, preferred_element_type=jnp.float32)
-        result = result.astype(jnp.bfloat16)
-        partial = jnp.einsum("est,esd->td", high, result, preferred_element_type=jnp.float32)
-        partial = partial + jnp.einsum(
-            "est,esd->td", low, result, preferred_element_type=jnp.float32
-        )
-        outs.append(partial)
-    return outs
+        results.append(result.astype(jnp.bfloat16))
+    result = jnp.concatenate(results, axis=2)
+    partial = jnp.einsum("est,esd->td", high, result, preferred_element_type=jnp.float32)
+    partial = partial + jnp.einsum("est,esd->td", low, result, preferred_element_type=jnp.float32)
+    return [partial]
 
 
 def shifted(x, step):

time: 136 us -> 141 us (1.037)
  waiting for transfers between devices: 32.4 us -> 35.7 us
  starting transfers between devices: 37 us -> 34.2 us
  local copies, waits for them, and re-layouts: 8.15 us -> 10.6 us
    ppermute x18 -> x15, waiting for transfers between devices: 32.4 us -> 35.7 us  [shifted(): lax.ppermute(x, 'exp', [(j, (j + step) % count) for j in range(count)])]
    ppermute x18 -> x15, starting transfers between devices: 37 us -> 34.2 us  [shifted(): lax.ppermute(x, 'exp', [(j, (j + step) % count) for j in range(count)])]
    dot_general x3 -> x2, matrix products: 2.94 us -> 3.68 us  [expert_mix(): jnp.einsum('est,esd->td', high, result, preferred_element_type=jnp.float32)]
    dot_general x3 -> x2, matrix products: 4.32 us -> 3.83 us  [expert_mix(): jnp.einsum('est,esd->td', low, result, preferred_element_type=jnp.float32)]
    unnamed x39 -> x35, local copies, waits for them, and re-layouts: 3.39 us -> 3.39 us
  transfers between devices with their start and end apart: 19 -> 16, of which waited for: 9 -> 9; matrix products, arithmetic and copies ran while one was open for 30% -> 29% of each run, Pallas kernels for 0% -> 0%
where the time goes in v10:
time: 141 us; the launch traced here: 140 us
  matrix products  49 us (35%)
  waiting for transfers between devices  35.7 us (25%)
  starting transfers between devices  34.2 us (24%)
  local copies, waits for them, and re-layouts  10.6 us (8%)
  other arithmetic  9.76 us (7%)
    ppermute x15, waiting for transfers between devices, shifted(): lax.ppermute(x, 'exp', [(j, (j + step) % count) for j in range(count)])  35.7 us
    ppermute x15, starting transfers between devices, shifted(): lax.ppermute(x, 'exp', [(j, (j + step) % count) for j in range(count)])  34.2 us
    dot_general x3, matrix products, expert_mix(): jnp.einsum('esf,efd->esd', hidden, down, preferred_element_type=jnp.float32)  13.1 us
    dot_general x2, matrix products, expert_mix(): jnp.einsum('esd,edf->esf', received, w_gate, preferred_element_type=jnp.f...  10.4 us
    dot_general x2, matrix products, expert_mix(): jnp.einsum('est,esd->td', low, result, preferred_element_type=jnp.float32)  3.83 us
    dot_general x2, matrix products, expert_mix(): jnp.einsum('est,esd->td', high, result, preferred_element_type=jnp.float32)  3.68 us
    sub x1, matrix products, attend(): expo = jnp.exp(score - top)  3.58 us
    unnamed x35, local copies, waits for them, and re-layouts  3.39 us
  transfers between devices with their start and end apart: 16, of which 9 were waited for; matrix products, arithmetic and copies ran while one was open for 29% of the time, Pallas kernels for 0%

profile of v10, /device:TPU:0, one launch (start us, length us, event | category | flops | bytes accessed | tf_op | source)
XLA Modules:
  0.0 140.5 jit_solution(10981832828236799749)
XLA Ops:
  0.7 1.8 %constant_dynamic-slice_fusion.4 = bf16[128,1024]{1,0:T(8,128)(2,1)} fusion(bf16[256,1024]{1,0:T(8,128)(2,1)} %param.19, s32[]{:T(128)S(6)} %select_n.200), kind=kLoop, calls=%fused_computation.150 | loop fusion | bytes 524292 | tf_op jit(solution)/shard_map/dynamic_slice | solution.py:133
  2.5 5.1 %collective-permute-start.6 = (bf16[128,1024]{1,0:T(8,128)(2,1)}, bf16[128,1024]{1,0:T(8,128)(2,1)S(1)}, u32[]{:S(2)}, u32[]{:S(2)}) collective-permute-start(bf16[128,1024]{1,0:T(8,128)(2,1)} %constant_dynamic-slice_fusion.4), channel_id=1, source_target_pairs={{0,3},{1,0},{2,1},{3,2},{4,7},{5,4},{6,5},{7,6},{8,11},{9,8},{10,9... | collective-permute-start | bytes 786440 | tf_op jit(solution)/shard_map/ppermute | solution.py:109
  7.6 0.6 multiply_power_fusion
  8.1 0.8 compare_reduce_fusion
  9.0 1.1 fusion.55
  10.2 0.3 reduce-window.9
  10.7 0.7 bitcast_subtract_fusion
  11.4 0.7 convert_element_type.103
  12.0 1.7 %convolution_convert_fusion.3 = bf16[128,512]{1,0:T(8,128)(2,1)S(1)} fusion(bf16[1024,512]{1,0:T(8,128)(2,1)} %param.18, bf16[128,1024]{1,0:T(8,128)(2,1)} %param.14, f32[1024]{0:T(1024)S(1)} %convert_element_type.103, f32[128]{0:T(128)S(1)} %add_rsqrt_fusion.1), kind=kOutput, calls=%fused_computation.51 | convolution fusion | flops 134807552 | bytes 1446400 | tf_op jit(solution)/shard_map/dot_general | solution.py:170
  13.8 1.9 %fusion.131 = f32[128,512]{0,1:T(8,128)S(1)} fusion(bf16[1024,512]{1,0:T(8,128)(2,1)} %param.17, bf16[128,1024]{1,0:T(8,128)(2,1)} %param.14, f32[1024]{0:T(1024)S(1)} %convert_element_type.103, f32[128]{0:T(128)S(1)} %add_rsqrt_fusion.1), kind=kOutput, calls=%fused_computation.206 | convolution fusion | flops 134742016 | bytes 1577472 | tf_op jit(solution)/shard_map/dot_general | solution.py:167
  15.8 1.0 fusion.133
  16.8 0.8 dynamic-slice_convert_fusion
  17.6 0.8 multiply_cosine_fusion
  18.6 0.5 collective-permute-start.2
  19.1 2.6 %collective-permute-start.1 = (bf16[128,2,256]{0,2,1:T(8,128)(2,1)S(1)}, bf16[128,2,256]{0,2,1:T(8,128)(2,1)S(1)}, u32[]{:S(2)}, u32[]{:S(2)}) collective-permute-start(bf16[128,2,256]{0,2,1:T(8,128)(2,1)S(1)} %get-tuple-element.23), channel_id=1, source_target_pairs={{0,2},{1,3},{2,0},{3,1},{4,6},{5,7},{6,4},{7,5},{8,10},{9,11},{10,... | collective-permute-start | bytes 393224 | tf_op jit(solution)/shard_map/ppermute | solution.py:109
  21.7 1.9 %collective-permute-start = (bf16[128,2,256]{0,2,1:T(8,128)(2,1)S(1)}, bf16[128,2,256]{0,2,1:T(8,128)(2,1)S(1)}, u32[]{:S(2)}, u32[]{:S(2)}) collective-permute-start(bf16[128,2,256]{0,2,1:T(8,128)(2,1)S(1)} %get-tuple-element.24), channel_id=1, source_target_pairs={{0,1},{1,2},{2,3},{3,0},{4,5},{5,6},{6,7},{7,4},{8,9},{9,10},{10,1... | collective-permute-start | bytes 393224 | tf_op jit(solution)/shard_map/ppermute | solution.py:109
  24.0 0.3 compare_and_fusion
  24.5 3.3 %collective-permute-done.2 = bf16[128,2,256]{0,2,1:T(8,128)(2,1)S(1)} collective-permute-done((bf16[128,2,256]{0,2,1:T(8,128)(2,1)S(1)}, bf16[128,2,256]{0,2,1:T(8,128)(2,1)S(1)}, u32[]{:S(2)}, u32[]{:S(2)}) %collective-permute-start.2) | collective-permute-done | bytes 131104 | tf_op jit(solution)/shard_map/ppermute | solution.py:109
  27.8 12.5 %collective-permute-start.4 = (bf16[128,1024]{1,0:T(8,128)(2,1)}, bf16[128,1024]{1,0:T(8,128)(2,1)S(1)}, u32[]{:S(2)}, u32[]{:S(2)}) collective-permute-start(bf16[128,1024]{1,0:T(8,128)(2,1)} %constant_dynamic-slice_fusion.4), channel_id=1, source_target_pairs={{0,1},{1,2},{2,3},{3,0},{4,5},{5,6},{6,7},{7,4},{8,9},{9,10},{10,1... | collective-permute-start | bytes 786440 | tf_op jit(solution)/shard_map/ppermute | solution.py:109
  40.3 1.1 collective-permute-done.1
  41.5 0.3 convolution_convert_fusion.2
  41.8 1.0 copy.76
  42.8 3.6 %fusion.137 = (f32[2,2,512]{2,1,0:T(2,128)S(1)}, f32[2,2,512,512]{2,3,1,0:T(8,128)}) fusion(pred[512,512]{0,1:T(8,128)(4,1)S(1)} %compare_and_fusion, bf16[512,2,2,64]{0,3,2,1:T(8,128)(2,1)S(1)} %bitcast.149, bf16[512,2,256]{0,2,1:T(8,128)(2,1)S(1)} %pad_maximum_fusion.8), kind=kOutput, calls=%fused_computation.210 | convolution fusion | flops 138412544 | bytes 4857856 | tf_op jit(solution)/shard_map/sub | solution.py:44
  46.4 1.0 pad_maximum_fusion.5
  47.5 2.7 %fusion.40 = bf16[512,2,2,64]{0,3,2,1:T(8,128)(2,1)S(1)} fusion(f32[2,2,512,512]{2,3,1,0:T(8,128)} %get-tuple-element.44, f32[2,2,512]{2,1,0:T(2,128)S(1)} %get-tuple-element.43, bf16[512,2,256]{0,2,1:T(8,128)(2,1)S(1)} %pad_maximum_fusion.8), kind=kOutput, calls=%fused_computation.50 | convolution fusion | flops 136445952 | bytes 4595712 | tf_op jit(solution)/shard_map/kgqt,tkd->qkgd/dot_general | solution.py:46
  50.3 0.5 collective-permute-start.9
  50.8 3.4 %collective-permute-start.3 = (bf16[128,256]{0,1:T(8,128)(2,1)S(1)}, bf16[128,256]{0,1:T(8,128)(2,1)S(1)}, u32[]{:S(2)}, u32[]{:S(2)}) collective-permute-start(bf16[128,256]{0,1:T(8,128)(2,1)S(1)} %bitcast.153), channel_id=1, source_target_pairs={{0,3},{1,0},{2,1},{3,2},{4,7},{5,4},{6,5},{7,6},{8,11},{9,8},{10,9... | collective-permute-start | bytes 196616 | tf_op jit(solution)/shard_map/ppermute | solution.py:109
  54.5 1.1 broadcast_select_fusion.1
  55.6 2.8 %collective-permute-done.3 = bf16[128,256]{0,1:T(8,128)(2,1)S(1)} collective-permute-done((bf16[128,256]{0,1:T(8,128)(2,1)S(1)}, bf16[128,256]{0,1:T(8,128)(2,1)S(1)}, u32[]{:S(2)}, u32[]{:S(2)}) %collective-permute-start.3) | collective-permute-done | bytes 65568 | tf_op jit(solution)/shard_map/ppermute | solution.py:109
  58.3 0.3 convolution_add_fusion.1
  58.6 0.2 fusion.65
  58.8 0.5 collective-permute-done.8
  59.4 0.4 multiply_reduce_fusion
  60.5 0.8 concatenate.47
  61.3 1.9 %collective-permute-start.12 = (bf16[128,1152]{1,0:T(8,128)(2,1)}, bf16[128,1152]{1,0:T(8,128)(2,1)}, u32[]{:S(2)}, u32[]{:S(2)}) collective-permute-start(bf16[128,1152]{1,0:T(8,128)(2,1)} %concatenate.47), channel_id=1, source_target_pairs={{0,3},{1,0},{2,1},{3,2},{4,7},{5,4},{6,5},{7,6},{8,11},{9,8},{10,9... | collective-permute-start | bytes 884744 | tf_op jit(solution)/shard_map/ppermute | solution.py:109
  63.3 1.5 %collective-permute-start.11 = (bf16[128,1152]{1,0:T(8,128)(2,1)}, bf16[128,1152]{1,0:T(8,128)(2,1)}, u32[]{:S(2)}, u32[]{:S(2)}) collective-permute-start(bf16[128,1152]{1,0:T(8,128)(2,1)} %concatenate.47), channel_id=1, source_target_pairs={{0,2},{1,3},{2,0},{3,1},{4,6},{5,7},{6,4},{7,5},{8,10},{9,11},{10,... | collective-permute-start | bytes 884744 | tf_op jit(solution)/shard_map/ppermute | solution.py:109
  64.7 0.9 compare_bitcast_fusion.1
  65.7 1.0 fusion.42
  66.7 0.4 convolution_convert_fusion.1
  67.2 5.0 %fusion.140 = f32[8,64,512]{2,1,0:T(8,128)S(1)} fusion(bf16[8,64,1024]{2,1,0:T(8,128)(2,1)S(1)} %convolution_convert_fusion.1, bf16[8,1024,512]{2,1,0:T(8,128)(2,1)} %param.22), kind=kOutput, calls=%fused_computation.213 | convolution fusion | flops 536870912 | bytes 10485760 | tf_op jit(solution)/shard_map/esd,edf->esf/dot_general | solution.py:89
  72.2 8.8 %convolution_convert_fusion = bf16[8,64,1024]{2,1,0:T(8,128)(2,1)S(1)} fusion(bf16[8,512,1024]{2,1,0:T(8,128)(2,1)} %param.24, bf16[8,64,1024]{2,1,0:T(8,128)(2,1)S(1)} %convolution_convert_fusion.1, bf16[8,1024,512]{2,1,0:T(8,128)(2,1)} %param.23, f32[8,64,512]{2,1,0:T(8,128)S(1)} %fusion.140), kind=kOutput, calls=%fused_computation.31 | convolution fusion | flops 1075838976 | bytes 19922944 | tf_op jit(solution)/shard_map/esf,efd->esd/dot_general | solution.py:99
  80.9 2.7 %collective-permute-done.10 = bf16[128,1152]{1,0:T(8,128)(2,1)} collective-permute-done((bf16[128,1152]{1,0:T(8,128)(2,1)}, bf16[128,1152]{1,0:T(8,128)(2,1)}, u32[]{:S(2)}, u32[]{:S(2)}) %collective-permute-start.10) | collective-permute-done | bytes 294944 | tf_op jit(solution)/shard_map/ppermute | solution.py:109
  83.7 1.0 constant_dynamic-update-slice_fusion.2
  84.6 5.8 %collective-permute-done.11 = bf16[128,1152]{1,0:T(8,128)(2,1)} collective-permute-done((bf16[128,1152]{1,0:T(8,128)(2,1)}, bf16[128,1152]{1,0:T(8,128)(2,1)}, u32[]{:S(2)}, u32[]{:S(2)}) %collective-permute-start.11) | collective-permute-done | bytes 294944 | tf_op jit(solution)/shard_map/ppermute | solution.py:109
  90.4 1.0 constant_dynamic-update-slice_fusion.1
  91.4 1.0 constant_dynamic-update-slice_fusion
  92.6 0.3 fusion.41
  93.0 1.8 %fusion.11 = bf16[8,192,1024]{2,1,0:T(8,128)(2,1)S(1)} fusion(s32[8,384]{1,0:T(8,128)S(1)} %fusion.41, pred[8,384]{1,0:T(8,128)(4,1)S(1)} %copy.72, bf16[384,1152]{1,0:T(8,128)(2,1)S(1)} %constant_dynamic-update-slice_fusion), kind=kOutput, calls=%fused_computation.16 | convolution fusion | flops 1210712064 | bytes 3947520 | tf_op jit(solution)/shard_map/est,td->esd/dot_general | solution.py:86
  94.8 5.4 %fusion.141 = f32[8,192,512]{2,1,0:T(8,128)S(1)} fusion(bf16[8,192,1024]{2,1,0:T(8,128)(2,1)S(1)} %fusion.11, bf16[8,1024,512]{2,1,0:T(8,128)(2,1)} %param.22), kind=kOutput, calls=%fused_computation.214 | convolution fusion | flops 1610612736 | bytes 14680064 | tf_op jit(solution)/shard_map/esd,edf->esf/dot_general | solution.py:89
  100.3 2.0 %multiply_convert_fusion = bf16[8,192,512]{2,1,0:T(8,128)(2,1)S(1)} fusion(f32[8,192,512]{2,1,0:T(8,128)S(1)} %fusion.141, bf16[8,192,1024]{2,1,0:T(8,128)(2,1)S(1)} %fusion.11, bf16[8,1024,512]{2,1,0:T(8,128)(2,1)S(1)} %bitcast.138), kind=kOutput, calls=%fused_computation.10 | convolution fusion | flops 1615331328 | bytes 16252928 | tf_op jit(solution)/shard_map/esd,edf->esf/dot_general | solution.py:90
  102.3 0.3 slice-done.3
  102.6 2.2 %fusion.23 = bf16[8,192,512]{2,1,0:T(8,128)(2,1)} fusion(bf16[8,192,512]{2,1,0:T(8,128)(2,1)S(1)} %multiply_convert_fusion, bf16[8,512,1024]{2,1,0:T(8,128)(2,1)S(1)} %bitcast.140), kind=kOutput, calls=%fused_computation.28 | convolution fusion | flops 806092800 | bytes 7340032 | tf_op jit(solution)/shard_map/esf,efd->esd/dot_general | solution.py:99
  104.7 2.1 %fusion.20 = bf16[8,192,512]{2,1,0:T(8,128)(2,1)} fusion(bf16[8,192,512]{2,1,0:T(8,128)(2,1)S(1)} %multiply_convert_fusion, bf16[8,512,1024]{2,1,0:T(8,128)(2,1)S(1)} %bitcast.140), kind=kOutput, calls=%fused_computation.27 | convolution fusion | flops 806092800 | bytes 7340032 | tf_op jit(solution)/shard_map/esf,efd->esd/dot_general | solution.py:99
  107.1 3.5 %fusion.18 = f32[384,1024,1]{1,0,2:T(8,128)S(1)} fusion(bf16[8,192,512]{2,1,0:T(8,128)(2,1)} %fusion.23, bf16[8,192,512]{2,1,0:T(8,128)(2,1)} %fusion.20, s32[8,384]{1,0:T(8,128)S(1)} %fusion.41, pred[8,384]{1,0:T(8,128)(4,1)S(1)} %copy.72, bf16[8,384]{1,0:T(8,128)(2,1)S(1)} %copy.74), kind=kOutput, calls=%fused_computation.21 | convolution fusion | flops 1216020480 | bytes 4740096 | tf_op jit(solution)/shard_map/est,esd->td/dot_general | solution.py:103
  110.6 1.4 %fusion.26 = bf16[384,1024]{1,0:T(8,128)(2,1)S(1)} fusion(f32[384,1024,1]{1,0,2:T(8,128)S(1)} %fusion.18, bf16[8,192,512]{2,1,0:T(8,128)(2,1)S(1)} %copy-done.10, bf16[8,192,512]{2,1,0:T(8,128)(2,1)S(1)} %copy-done.11, s32[8,384]{1,0:T(8,128)S(1)} %fusion.41, pred[8,384]{1,0:T(8,128)(4,1)S(1)} %copy.72, bf16[8,384]{1,0:T(8,128)(2,1)S(1)} %copy.73), kind=kOutput, calls=%fused_computation.30 | convolution fusion | flops 1216806912 | bytes 5526528 | tf_op jit(solution)/shard_map/est,esd->td/dot_general | solution.py:102
  112.1 0.9 fusion.135
  113.0 2.0 %collective-permute-start.15 = (bf16[128,1024]{1,0:T(8,128)(2,1)}, bf16[128,1024]{1,0:T(8,128)(2,1)}, u32[]{:S(2)}, u32[]{:S(2)}) collective-permute-start(bf16[128,1024]{1,0:T(8,128)(2,1)} %get-tuple-element.17), channel_id=1, source_target_pairs={{0,1},{1,2},{2,3},{3,0},{4,5},{5,6},{6,7},{7,4},{8,9},{9,10},{10,1... | collective-permute-start | bytes 786440 | tf_op jit(solution)/shard_map/ppermute | solution.py:109
  115.0 2.3 %collective-permute-start.14 = (bf16[128,1024]{1,0:T(8,128)(2,1)}, bf16[128,1024]{1,0:T(8,128)(2,1)}, u32[]{:S(2)}, u32[]{:S(2)}) collective-permute-start(bf16[128,1024]{1,0:T(8,128)(2,1)} %get-tuple-element.18), channel_id=1, source_target_pairs={{0,2},{1,3},{2,0},{3,1},{4,6},{5,7},{6,4},{7,5},{8,10},{9,11},{10,... | collective-permute-start | bytes 786440 | tf_op jit(solution)/shard_map/ppermute | solution.py:109
  117.3 0.9 dynamic-slice_bitcast_fusion.3
  118.3 0.4 convolution_bitcast_fusion
  118.7 1.5 %collective-permute-done.13 = bf16[128,1024]{1,0:T(8,128)(2,1)S(1)} collective-permute-done((bf16[128,1024]{1,0:T(8,128)(2,1)}, bf16[128,1024]{1,0:T(8,128)(2,1)S(1)}, u32[]{:S(2)}, u32[]{:S(2)}) %collective-permute-start.13) | collective-permute-done | bytes 262176 | tf_op jit(solution)/shard_map/ppermute | solution.py:109
  120.2 9.7 %collective-permute-done.15 = bf16[128,1024]{1,0:T(8,128)(2,1)} collective-permute-done((bf16[128,1024]{1,0:T(8,128)(2,1)}, bf16[128,1024]{1,0:T(8,128)(2,1)}, u32[]{:S(2)}, u32[]{:S(2)}) %collective-permute-start.15) | collective-permute-done | bytes 262176 | tf_op jit(solution)/shard_map/ppermute | solution.py:109
  129.9 8.3 %collective-permute-done.14 = bf16[128,1024]{1,0:T(8,128)(2,1)} collective-permute-done((bf16[128,1024]{1,0:T(8,128)(2,1)}, bf16[128,1024]{1,0:T(8,128)(2,1)}, u32[]{:S(2)}, u32[]{:S(2)}) %collective-permute-start.14) | collective-permute-done | bytes 262176 | tf_op jit(solution)/shard_map/ppermute | solution.py:109
  138.2 2.3 %add_convert_fusion = bf16[128,1024]{1,0:T(8,128)(2,1)} fusion(f32[128,1024]{1,0:T(8,128)} %copy-done.3, bf16[128,1024]{1,0:T(8,128)(2,1)} %collective-permute-done.15, bf16[128,1024]{1,0:T(8,128)(2,1)} %collective-permute-done.14, bf16[128,1024]{1,0:T(8,128)(2,1)S(1)} %collective-permute-done.13, f32[128,1024]{1,0:T(8,128)S(1)} %convolution_bitcast_fusion, ...), kind=kOutput, calls=%fused_computation.89 | convolution fusion | flops 135593984 | bytes 3152896 | tf_op jit(solution)/shard_map/est,esd->td/dot_general | solution.py:102
  (98 shorter events, 3.1 us)
Async XLA Ops:
  0.6 15.1 %copy-start = (bf16[1024,1024]{1,0:T(8,128)(2,1)S(1)}, bf16[1024,1024]{1,0:T(8,128)(2,1)}, u32[]{:S(2)}) copy-start(bf16[1024,1024]{1,0:T(8,128)(2,1)} %param.16) | copy-start | bytes 6291460
  0.6 15.1 %copy-start.2 = (bf16[128,1024]{1,0:T(8,128)(2,1)S(1)}, bf16[128,1024]{1,0:T(8,128)(2,1)}, u32[]{:S(2)}) copy-start(bf16[128,1024]{1,0:T(8,128)(2,1)} %param.14) | copy-start | bytes 786436
  2.5 43.9 %collective-permute-start.6 = (bf16[128,1024]{1,0:T(8,128)(2,1)}, bf16[128,1024]{1,0:T(8,128)(2,1)S(1)}, u32[]{:S(2)}, u32[]{:S(2)}) collective-permute-start(bf16[128,1024]{1,0:T(8,128)(2,1)} %constant_dynamic-slice_fusion.4), channel_id=1, source_target_pairs={{0,3},{1,0},{2,1},{3,2},{4,7},{5,4},{6,5},{7,6},{8,11},{9,8},{10,9... | collective-permute-start | bytes 786440 | tf_op jit(solution)/shard_map/ppermute | solution.py:109
  7.6 38.8 %collective-permute-start.5 = (bf16[128,1024]{1,0:T(8,128)(2,1)}, bf16[128,1024]{1,0:T(8,128)(2,1)}, u32[]{:S(2)}, u32[]{:S(2)}) collective-permute-start(bf16[128,1024]{1,0:T(8,128)(2,1)} %constant_dynamic-slice_fusion.4), channel_id=1, source_target_pairs={{0,2},{1,3},{2,0},{3,1},{4,6},{5,7},{6,4},{7,5},{8,10},{9,11},{10,... | collective-permute-start | bytes 786440 | tf_op jit(solution)/shard_map/ppermute | solution.py:109
  15.8 8.1 %copy-start.7 = (s32[1,512]{1,0:T(1,128)S(1)}, s32[1,512]{1,0:T(1,128)}, u32[]{:S(2)}) copy-start(s32[1,512]{1,0:T(1,128)} %param.25) | copy-start | bytes 6148
  15.8 8.2 %copy-start.6 = (s32[128,8]{0,1:T(8,128)S(1)}, s32[128,8]{0,1:T(8,128)}, u32[]{:S(2)}) copy-start(s32[128,8]{0,1:T(8,128)} %param.27) | copy-start | bytes 12292
  16.8 7.2 %copy-start.8 = (s32[1,512]{1,0:T(1,128)S(1)}, s32[1,512]{1,0:T(1,128)}, u32[]{:S(2)}) copy-start(s32[1,512]{1,0:T(1,128)} %param.26) | copy-start | bytes 6148
  16.8 7.6 %copy-start.9 = (bf16[1024]{0:T(1024)(128)(2,1)S(1)}, bf16[1024]{0:T(1024)(128)(2,1)}, u32[]{:S(2)}) copy-start(bf16[1024]{0:T(1024)(128)(2,1)} %param.20) | copy-start | bytes 6148
  18.6 9.1 %collective-permute-start.2 = (bf16[128,2,256]{0,2,1:T(8,128)(2,1)S(1)}, bf16[128,2,256]{0,2,1:T(8,128)(2,1)S(1)}, u32[]{:S(2)}, u32[]{:S(2)}) collective-permute-start(bf16[128,2,256]{0,2,1:T(8,128)(2,1)S(1)} %get-tuple-element.22), channel_id=1, source_target_pairs={{0,3},{1,0},{2,1},{3,2},{4,7},{5,4},{6,5},{7,6},{8,11},{9,8},{10,9... | collective-permute-start | bytes 393224 | tf_op jit(solution)/shard_map/ppermute | solution.py:109
  19.1 22.3 %collective-permute-start.1 = (bf16[128,2,256]{0,2,1:T(8,128)(2,1)S(1)}, bf16[128,2,256]{0,2,1:T(8,128)(2,1)S(1)}, u32[]{:S(2)}, u32[]{:S(2)}) collective-permute-start(bf16[128,2,256]{0,2,1:T(8,128)(2,1)S(1)} %get-tuple-element.23), channel_id=1, source_target_pairs={{0,2},{1,3},{2,0},{3,1},{4,6},{5,7},{6,4},{7,5},{8,10},{9,11},{10,... | collective-permute-start | bytes 393224 | tf_op jit(solution)/shard_map/ppermute | solution.py:109
  21.7 19.7 %collective-permute-start = (bf16[128,2,256]{0,2,1:T(8,128)(2,1)S(1)}, bf16[128,2,256]{0,2,1:T(8,128)(2,1)S(1)}, u32[]{:S(2)}, u32[]{:S(2)}) collective-permute-start(bf16[128,2,256]{0,2,1:T(8,128)(2,1)S(1)} %get-tuple-element.24), channel_id=1, source_target_pairs={{0,1},{1,2},{2,3},{3,0},{4,5},{5,6},{6,7},{7,4},{8,9},{9,10},{10,1... | collective-permute-start | bytes 393224 | tf_op jit(solution)/shard_map/ppermute | solution.py:109
  27.8 18.6 %collective-permute-start.4 = (bf16[128,1024]{1,0:T(8,128)(2,1)}, bf16[128,1024]{1,0:T(8,128)(2,1)S(1)}, u32[]{:S(2)}, u32[]{:S(2)}) collective-permute-start(bf16[128,1024]{1,0:T(8,128)(2,1)} %constant_dynamic-slice_fusion.4), channel_id=1, source_target_pairs={{0,1},{1,2},{2,3},{3,0},{4,5},{5,6},{6,7},{7,4},{8,9},{9,10},{10,1... | collective-permute-start | bytes 786440 | tf_op jit(solution)/shard_map/ppermute | solution.py:109
  47.5 7.0 %collective-permute-start.7 = (bf16[3,128,1024]{2,1,0:T(8,128)(2,1)S(1)}, bf16[3,128,1024]{2,1,0:T(8,128)(2,1)S(1)}, u32[]{:S(2)}, u32[]{:S(2)}) collective-permute-start(bf16[3,128,1024]{2,1,0:T(8,128)(2,1)S(1)} %pad_maximum_fusion.5), channel_id=1, source_target_pairs={{0,4},{4,0},{8,12},{12,8},{16,20},{20,16},{24,28},{28,24},{1,5},{5... | collective-permute-start | bytes 2359304 | tf_op jit(solution)/shard_map/ppermute | solution.py:135
  47.5 6.7 %copy-start.4 = (bf16[256,1024]{1,0:T(8,128)(2,1)S(1)}, bf16[256,1024]{1,0:T(8,128)(2,1)}, u32[]{:S(2)}) copy-start(bf16[256,1024]{1,0:T(8,128)(2,1)} %param.19) | copy-start | bytes 1572868
  50.3 8.3 %collective-permute-start.9 = (bf16[128,256]{0,1:T(8,128)(2,1)S(1)}, bf16[128,256]{0,1:T(8,128)(2,1)S(1)}, u32[]{:S(2)}, u32[]{:S(2)}) collective-permute-start(bf16[128,256]{0,1:T(8,128)(2,1)S(1)} %bitcast.152), channel_id=1, source_target_pairs={{0,1},{1,2},{2,3},{3,0},{4,5},{5,6},{6,7},{7,4},{8,9},{9,10},{10,1... | collective-permute-start | bytes 196616 | tf_op jit(solution)/shard_map/ppermute | solution.py:109
  50.8 8.6 %collective-permute-start.8 = (bf16[128,256]{0,1:T(8,128)(2,1)S(1)}, bf16[128,256]{0,1:T(8,128)(2,1)S(1)}, u32[]{:S(2)}, u32[]{:S(2)}) collective-permute-start(bf16[128,256]{0,1:T(8,128)(2,1)S(1)} %bitcast.151), channel_id=1, source_target_pairs={{0,2},{1,3},{2,0},{3,1},{4,6},{5,7},{6,4},{7,5},{8,10},{9,11},{10,... | collective-permute-start | bytes 196616 | tf_op jit(solution)/shard_map/ppermute | solution.py:109
  50.8 7.5 %collective-permute-start.3 = (bf16[128,256]{0,1:T(8,128)(2,1)S(1)}, bf16[128,256]{0,1:T(8,128)(2,1)S(1)}, u32[]{:S(2)}, u32[]{:S(2)}) collective-permute-start(bf16[128,256]{0,1:T(8,128)(2,1)S(1)} %bitcast.153), channel_id=1, source_target_pairs={{0,3},{1,0},{2,1},{3,2},{4,7},{5,4},{6,5},{7,6},{8,11},{9,8},{10,9... | collective-permute-start | bytes 196616 | tf_op jit(solution)/shard_map/ppermute | solution.py:109
  58.6 1.3 copy-start.5
  59.7 7.0 %copy-start.3 = (f32[128,1024]{1,0:T(8,128)}, f32[128,1024]{1,0:T(8,128)S(1)}, u32[]{:S(2)}) copy-start(f32[128,1024]{1,0:T(8,128)S(1)} %get-tuple-element.46) | copy-start | bytes 1572868
  61.3 30.1 %collective-permute-start.12 = (bf16[128,1152]{1,0:T(8,128)(2,1)}, bf16[128,1152]{1,0:T(8,128)(2,1)}, u32[]{:S(2)}, u32[]{:S(2)}) collective-permute-start(bf16[128,1152]{1,0:T(8,128)(2,1)} %concatenate.47), channel_id=1, source_target_pairs={{0,3},{1,0},{2,1},{3,2},{4,7},{5,4},{6,5},{7,6},{8,11},{9,8},{10,9... | collective-permute-start | bytes 884744 | tf_op jit(solution)/shard_map/ppermute | solution.py:109
  63.3 27.1 %collective-permute-start.11 = (bf16[128,1152]{1,0:T(8,128)(2,1)}, bf16[128,1152]{1,0:T(8,128)(2,1)}, u32[]{:S(2)}, u32[]{:S(2)}) collective-permute-start(bf16[128,1152]{1,0:T(8,128)(2,1)} %concatenate.47), channel_id=1, source_target_pairs={{0,2},{1,3},{2,0},{3,1},{4,6},{5,7},{6,4},{7,5},{8,10},{9,11},{10,... | collective-permute-start | bytes 884744 | tf_op jit(solution)/shard_map/ppermute | solution.py:109
  64.7 18.9 %collective-permute-start.10 = (bf16[128,1152]{1,0:T(8,128)(2,1)}, bf16[128,1152]{1,0:T(8,128)(2,1)}, u32[]{:S(2)}, u32[]{:S(2)}) collective-permute-start(bf16[128,1152]{1,0:T(8,128)(2,1)} %concatenate.47), channel_id=1, source_target_pairs={{0,1},{1,2},{2,3},{3,0},{4,5},{5,6},{6,7},{7,4},{8,9},{9,10},{10,1... | collective-permute-start | bytes 884744 | tf_op jit(solution)/shard_map/ppermute | solution.py:109
  92.9 7.3 %slice-start = ((s8[8388608]{0:T(1024)(128)(4,1)}), s8[4194304]{0:T(1024)(128)(4,1)S(1)}, s32[]{:S(2)}) async-start(s8[8388608]{0:T(1024)(128)(4,1)} %bitcast.137), calls=%async_computation | async-start | bytes 8388608
  94.8 5.4 %slice-start.1 = ((s8[8388608]{0:T(1024)(128)(4,1)}), s8[4194304]{0:T(1024)(128)(4,1)S(1)}, s32[]{:S(2)}) async-start(s8[8388608]{0:T(1024)(128)(4,1)} %bitcast.137), calls=%async_computation.1 | async-start | bytes 8388608
  94.8 7.4 %slice-start.2 = ((s8[8388608]{0:T(1024)(128)(4,1)}), s8[4194304]{0:T(1024)(128)(4,1)S(1)}, s32[]{:S(2)}) async-start(s8[8388608]{0:T(1024)(128)(4,1)} %bitcast.139), calls=%async_computation.2 | async-start | bytes 8388608
  100.3 2.3 %slice-start.3 = ((s8[8388608]{0:T(1024)(128)(4,1)}), s8[4194304]{0:T(1024)(128)(4,1)S(1)}, s32[]{:S(2)}) async-start(s8[8388608]{0:T(1024)(128)(4,1)} %bitcast.139), calls=%async_computation.3 | async-start | bytes 8388608
  107.1 3.5 %copy-start.10 = (bf16[8,192,512]{2,1,0:T(8,128)(2,1)S(1)}, bf16[8,192,512]{2,1,0:T(8,128)(2,1)}, u32[]{:S(2)}) copy-start(bf16[8,192,512]{2,1,0:T(8,128)(2,1)} %fusion.23) | copy-start | bytes 4718596
  107.1 3.5 %copy-start.11 = (bf16[8,192,512]{2,1,0:T(8,128)(2,1)S(1)}, bf16[8,192,512]{2,1,0:T(8,128)(2,1)}, u32[]{:S(2)}) copy-start(bf16[8,192,512]{2,1,0:T(8,128)(2,1)} %fusion.20) | copy-start | bytes 4718596
  110.6 29.8 %copy-start.1 = (bf16[1024,1024]{1,0:T(8,128)(2,1)S(1)}, bf16[1024,1024]{1,0:T(8,128)(2,1)}, u32[]{:S(2)}) copy-start(bf16[1024,1024]{1,0:T(8,128)(2,1)} %param.16) | copy-start | bytes 6291460
  113.0 7.2 %collective-permute-start.13 = (bf16[128,1024]{1,0:T(8,128)(2,1)}, bf16[128,1024]{1,0:T(8,128)(2,1)S(1)}, u32[]{:S(2)}, u32[]{:S(2)}) collective-permute-start(bf16[128,1024]{1,0:T(8,128)(2,1)} %get-tuple-element.16), channel_id=1, source_target_pairs={{0,3},{1,0},{2,1},{3,2},{4,7},{5,4},{6,5},{7,6},{8,11},{9,8},{10,9... | collective-permute-start | bytes 786440 | tf_op jit(solution)/shard_map/ppermute | solution.py:109
  113.0 16.9 %collective-permute-start.15 = (bf16[128,1024]{1,0:T(8,128)(2,1)}, bf16[128,1024]{1,0:T(8,128)(2,1)}, u32[]{:S(2)}, u32[]{:S(2)}) collective-permute-start(bf16[128,1024]{1,0:T(8,128)(2,1)} %get-tuple-element.17), channel_id=1, source_target_pairs={{0,1},{1,2},{2,3},{3,0},{4,5},{5,6},{6,7},{7,4},{8,9},{9,10},{10,1... | collective-permute-start | bytes 786440 | tf_op jit(solution)/shard_map/ppermute | solution.py:109
  115.0 23.2 %collective-permute-start.14 = (bf16[128,1024]{1,0:T(8,128)(2,1)}, bf16[128,1024]{1,0:T(8,128)(2,1)}, u32[]{:S(2)}, u32[]{:S(2)}) collective-permute-start(bf16[128,1024]{1,0:T(8,128)(2,1)} %get-tuple-element.18), channel_id=1, source_target_pairs={{0,2},{1,3},{2,0},{3,1},{4,6},{5,7},{6,4},{7,5},{8,10},{9,11},{10,... | collective-permute-start | bytes 786440 | tf_op jit(solution)/shard_map/ppermute | solution.py:109

commit v11 on v8

--- a/solution.py
+++ b/solution.py
@@ -63,44 +63,41 @@
 
 
 def expert_mix(packed, sources, width, experts, w_gate, w_up, w_down, pieces):
-    tokens_all = packed.shape[0]
     local = w_gate.shape[0]
-    rows = tokens_all // sources
-    cap = CAP * sources
+    rows = packed.shape[0] // sources
     here = lax.axis_index("exp")
-    rows_all = packed[:, :width]
+    rows_all = packed[:, :width].reshape(sources, rows, width)
 
     def columns(block):
-        return lax.dynamic_slice_in_dim(packed, width + block * experts + here * local, local, 1)
+        start = width + block * experts + here * local
+        return lax.dynamic_slice_in_dim(packed, start, local, 1).reshape(sources, rows, local)
 
     high, low, named = columns(0), columns(1), columns(2)
-    hits = named > 0
-    order = jnp.arange(tokens_all, dtype=jnp.int32)
-    block = order // rows
-    before = (order[None, :] < order[:, None]) & (block[None, :] == block[:, None])
-    slot = jnp.dot(before.astype(jnp.bfloat16), named, preferred_element_type=jnp.float32)
-    slot = slot.astype(jnp.int32) + (block * CAP)[:, None]
-    picks = hits.T[:, None, :] & (
-        slot.T[:, None, :] == jnp.arange(cap, dtype=jnp.int32)[None, :, None]
+    order = jnp.arange(rows, dtype=jnp.int32)
+    before = (order[None, :] < order[:, None]).astype(jnp.bfloat16)
+    slot = jnp.einsum("tu,bue->bet", before, named, preferred_element_type=jnp.float32)
+    hits = jnp.transpose(named, (0, 2, 1)) > 0
+    picks = hits[:, :, None, :] & (
+        slot.astype(jnp.int32)[:, :, None, :] == jnp.arange(CAP, dtype=jnp.int32)[None, None, :, None]
     )
     received = jnp.einsum(
-        "est,td->esd", picks.astype(jnp.bfloat16), rows_all, preferred_element_type=jnp.float32
+        "becr,brd->becd", picks.astype(jnp.bfloat16), rows_all, preferred_element_type=jnp.float32
     ).astype(jnp.bfloat16)
-    gate = jnp.einsum("esd,edf->esf", received, w_gate, preferred_element_type=jnp.float32)
-    upward = jnp.einsum("esd,edf->esf", received, w_up, preferred_element_type=jnp.float32)
+    gate = jnp.einsum("becd,edf->becf", received, w_gate, preferred_element_type=jnp.float32)
+    upward = jnp.einsum("becd,edf->becf", received, w_up, preferred_element_type=jnp.float32)
     hidden = (jax.nn.silu(gate) * upward).astype(jnp.bfloat16)
     zero = jnp.zeros((), jnp.bfloat16)
-    high = jnp.where(picks, high.T[:, None, :], zero)
-    low = jnp.where(picks, low.T[:, None, :], zero)
+    high = jnp.where(picks, jnp.transpose(high, (0, 2, 1))[:, :, None, :], zero)
+    low = jnp.where(picks, jnp.transpose(low, (0, 2, 1))[:, :, None, :], zero)
     cut = w_down.shape[2] // pieces
     outs = []
     for piece in range(pieces):
         down = lax.slice_in_dim(w_down, piece * cut, (piece + 1) * cut, axis=2)
-        result = jnp.einsum("esf,efd->esd", hidden, down, preferred_element_type=jnp.float32)
+        result = jnp.einsum("becf,efd->becd", hidden, down, preferred_element_type=jnp.float32)
         result = result.astype(jnp.bfloat16)
-        partial = jnp.einsum("est,esd->td", high, result, preferred_element_type=jnp.float32)
+        partial = jnp.einsum("becr,becd->brd", high, result, preferred_element_type=jnp.float32)
         partial = partial + jnp.einsum(
-            "est,esd->td", low, result, preferred_element_type=jnp.float32
+            "becr,becd->brd", low, result, preferred_element_type=jnp.float32
         )
         outs.append(partial)
     return outs
@@ -203,12 +200,12 @@
     normed2 = rms_scale(resid, norm_moe)
     packed = routing(normed2, expert_ids, w_router)
     experts = w_router.shape[1]
-    moe = expert_mix(packed, 1, width, experts, w_gate, w_up, w_down, 1)[0]
+    moe = expert_mix(packed, 1, width, experts, w_gate, w_up, w_down, 1)[0][0]
     received = jnp.concatenate([shifted(packed, step) for step in range(1, owners)])
     pieces = expert_mix(received, owners - 1, width, experts, w_gate, w_up, w_down, 2)
     backs = []
     for piece in pieces:
-        piece = piece.astype(jnp.bfloat16).reshape(owners - 1, rows, -1)
+        piece = piece.astype(jnp.bfloat16)
         back = sum(
             shifted(piece[step - 1], -step).astype(jnp.float32) for step in range(1, owners)
         )

time: 136 us -> 128 us (0.941)
  waiting for transfers between devices: 32.4 us -> 22.2 us
  starting transfers between devices: 37 us -> 41.7 us
  matrix products: 48 us -> 45.5 us
    ppermute x18, waiting for transfers between devices: 32.4 us -> 22.2 us  [shifted(): lax.ppermute(x, 'exp', [(j, (j + step) % count) for j in range(count)])]
    ppermute x18, starting transfers between devices: 37 us -> 41.6 us  [shifted(): lax.ppermute(x, 'exp', [(j, (j + step) % count) for j in range(count)])]
    dot_general x16, matrix products: 35.5 us -> 33 us  [the longest x3 12.2 us: expert_mix(): jnp.einsum('becf,efd->becd', hidden, down, preferred_element_type=jnp.flo...]
  transfers between devices with their start and end apart: 19 -> 19, of which waited for: 9 -> 7; matrix products, arithmetic and copies ran while one was open for 30% -> 32% of each run, Pallas kernels for 0% -> 0%
where the time goes in v11:
time: 128 us; the launch traced here: 127 us
  matrix products  45.5 us (36%)
  starting transfers between devices  41.7 us (33%)
  waiting for transfers between devices  22.2 us (17%)
  other arithmetic  8.27 us (6%)
  local copies, waits for them, and re-layouts  8.24 us (6%)
  between operations  1.33 us (1%)
    ppermute x18, starting transfers between devices, shifted(): lax.ppermute(x, 'exp', [(j, (j + step) % count) for j in range(count)])  41.6 us
    ppermute x18, waiting for transfers between devices, shifted(): lax.ppermute(x, 'exp', [(j, (j + step) % count) for j in range(count)])  22.2 us
    dot_general x3, matrix products, expert_mix(): jnp.einsum('becf,efd->becd', hidden, down, preferred_element_type=jnp.flo...  12.2 us
    dot_general x2, matrix products, expert_mix(): jnp.einsum('becd,edf->becf', received, w_gate, preferred_element_type=jnp...  8 us
    dot_general x1, matrix products, expert_mix(): jnp.einsum('becd,edf->becf', received, w_up, preferred_element_type=jnp.f...  5.54 us
    sub x1, matrix products, attend(): expo = jnp.exp(score - top)  3.59 us
    dot_general x3, matrix products, expert_mix(): jnp.einsum('becr,becd->brd', low, result, preferred_element_type=jnp.floa...  3.47 us
    unnamed x39, local copies, waits for them, and re-layouts  3.35 us
  transfers between devices with their start and end apart: 19, of which 7 were waited for; matrix products, arithmetic and copies ran while one was open for 32% of the time, Pallas kernels for 0%

profile of v11, /device:TPU:0, one launch (start us, length us, event | category | flops | bytes accessed | tf_op | source)
XLA Modules:
  0.0 127.2 jit_solution(6687288325198361952)
XLA Ops:
  0.7 1.8 %constant_dynamic-slice_fusion.9 = bf16[128,1024]{1,0:T(8,128)(2,1)} fusion(bf16[256,1024]{1,0:T(8,128)(2,1)} %param.19, s32[]{:T(128)S(6)} %select_n.170), kind=kLoop, calls=%fused_computation.185 | loop fusion | bytes 524292 | tf_op jit(solution)/shard_map/dynamic_slice | solution.py:132
  2.5 5.1 %collective-permute-start.6 = (bf16[128,1024]{1,0:T(8,128)(2,1)}, bf16[128,1024]{1,0:T(8,128)(2,1)S(1)}, u32[]{:S(2)}, u32[]{:S(2)}) collective-permute-start(bf16[128,1024]{1,0:T(8,128)(2,1)} %constant_dynamic-slice_fusion.9), channel_id=1, source_target_pairs={{0,3},{1,0},{2,1},{3,2},{4,7},{5,4},{6,5},{7,6},{8,11},{9,8},{10,9... | collective-permute-start | bytes 786440 | tf_op jit(solution)/shard_map/ppermute | solution.py:108
  7.6 0.6 multiply_power_fusion
  8.2 0.7 convert_element_type.124
  8.9 1.1 fusion.87
  10.0 1.7 %convolution_convert_fusion.4 = bf16[128,512]{1,0:T(8,128)(2,1)S(1)} fusion(bf16[1024,512]{1,0:T(8,128)(2,1)} %param.18, bf16[128,1024]{1,0:T(8,128)(2,1)} %param.14, f32[1024]{0:T(1024)S(1)} %convert_element_type.124, f32[128]{0:T(128)S(1)} %add_rsqrt_fusion.1), kind=kOutput, calls=%fused_computation.70 | convolution fusion | flops 134807552 | bytes 1446400 | tf_op jit(solution)/shard_map/dot_general | solution.py:169
  11.8 1.9 %fusion.177 = f32[128,512]{0,1:T(8,128)S(1)} fusion(bf16[1024,512]{1,0:T(8,128)(2,1)} %param.17, bf16[128,1024]{1,0:T(8,128)(2,1)} %param.14, f32[1024]{0:T(1024)S(1)} %convert_element_type.124, f32[128]{0:T(128)S(1)} %add_rsqrt_fusion.1), kind=kOutput, calls=%fused_computation.228 | convolution fusion | flops 134742016 | bytes 1577472 | tf_op jit(solution)/shard_map/dot_general | solution.py:166
  13.9 0.3 reduce-window.9
  14.4 0.7 bitcast_subtract_fusion
  15.1 1.0 fusion.179
  16.1 0.8 dynamic-slice_convert_fusion
  16.8 0.8 multiply_cosine_fusion
  17.9 0.5 collective-permute-start.2
  18.4 2.5 %collective-permute-start.1 = (bf16[128,2,256]{0,2,1:T(8,128)(2,1)S(1)}, bf16[128,2,256]{0,2,1:T(8,128)(2,1)S(1)}, u32[]{:S(2)}, u32[]{:S(2)}) collective-permute-start(bf16[128,2,256]{0,2,1:T(8,128)(2,1)S(1)} %get-tuple-element.23), channel_id=1, source_target_pairs={{0,2},{1,3},{2,0},{3,1},{4,6},{5,7},{6,4},{7,5},{8,10},{9,11},{10,... | collective-permute-start | bytes 393224 | tf_op jit(solution)/shard_map/ppermute | solution.py:108
  21.0 1.9 %collective-permute-start = (bf16[128,2,256]{0,2,1:T(8,128)(2,1)S(1)}, bf16[128,2,256]{0,2,1:T(8,128)(2,1)S(1)}, u32[]{:S(2)}, u32[]{:S(2)}) collective-permute-start(bf16[128,2,256]{0,2,1:T(8,128)(2,1)S(1)} %get-tuple-element.24), channel_id=1, source_target_pairs={{0,1},{1,2},{2,3},{3,0},{4,5},{5,6},{6,7},{7,4},{8,9},{9,10},{10,1... | collective-permute-start | bytes 393224 | tf_op jit(solution)/shard_map/ppermute | solution.py:108
  23.3 0.3 compare_and_fusion
  23.8 4.0 %collective-permute-done.2 = bf16[128,2,256]{0,2,1:T(8,128)(2,1)S(1)} collective-permute-done((bf16[128,2,256]{0,2,1:T(8,128)(2,1)S(1)}, bf16[128,2,256]{0,2,1:T(8,128)(2,1)S(1)}, u32[]{:S(2)}, u32[]{:S(2)}) %collective-permute-start.2) | collective-permute-done | bytes 131104 | tf_op jit(solution)/shard_map/ppermute | solution.py:108
  27.8 12.5 %collective-permute-start.4 = (bf16[128,1024]{1,0:T(8,128)(2,1)}, bf16[128,1024]{1,0:T(8,128)(2,1)S(1)}, u32[]{:S(2)}, u32[]{:S(2)}) collective-permute-start(bf16[128,1024]{1,0:T(8,128)(2,1)} %constant_dynamic-slice_fusion.9), channel_id=1, source_target_pairs={{0,1},{1,2},{2,3},{3,0},{4,5},{5,6},{6,7},{7,4},{8,9},{9,10},{10,1... | collective-permute-start | bytes 786440 | tf_op jit(solution)/shard_map/ppermute | solution.py:108
  40.3 1.1 collective-permute-done.1
  41.5 3.6 %fusion.182 = (f32[2,2,512]{2,1,0:T(2,128)S(1)}, f32[2,2,512,512]{2,3,1,0:T(8,128)}) fusion(pred[512,512]{0,1:T(8,128)(4,1)S(1)} %compare_and_fusion, bf16[512,2,2,64]{0,3,2,1:T(8,128)(2,1)S(1)} %bitcast.270, bf16[512,2,256]{0,2,1:T(8,128)(2,1)S(1)} %pad_maximum_fusion.3), kind=kOutput, calls=%fused_computation.231 | convolution fusion | flops 138412544 | bytes 4857856 | tf_op jit(solution)/shard_map/sub | solution.py:44
  45.1 1.0 pad_maximum_fusion
  46.2 2.7 %fusion.73 = bf16[512,2,2,64]{0,3,2,1:T(8,128)(2,1)S(1)} fusion(f32[2,2,512,512]{2,3,1,0:T(8,128)} %get-tuple-element.50, f32[2,2,512]{2,1,0:T(2,128)S(1)} %get-tuple-element.49, bf16[512,2,256]{0,2,1:T(8,128)(2,1)S(1)} %pad_maximum_fusion.3), kind=kOutput, calls=%fused_computation.69 | convolution fusion | flops 136445952 | bytes 4595712 | tf_op jit(solution)/shard_map/kgqt,tkd->qkgd/dot_general | solution.py:46
  49.0 1.8 %collective-permute-start.9 = (bf16[128,256]{0,1:T(8,128)(2,1)S(1)}, bf16[128,256]{0,1:T(8,128)(2,1)S(1)}, u32[]{:S(2)}, u32[]{:S(2)}) collective-permute-start(bf16[128,256]{0,1:T(8,128)(2,1)S(1)} %bitcast.273), channel_id=1, source_target_pairs={{0,1},{1,2},{2,3},{3,0},{4,5},{5,6},{6,7},{7,4},{8,9},{9,10},{10,1... | collective-permute-start | bytes 196616 | tf_op jit(solution)/shard_map/ppermute | solution.py:108
  50.8 2.1 %collective-permute-start.3 = (bf16[128,256]{0,1:T(8,128)(2,1)S(1)}, bf16[128,256]{0,1:T(8,128)(2,1)S(1)}, u32[]{:S(2)}, u32[]{:S(2)}) collective-permute-start(bf16[128,256]{0,1:T(8,128)(2,1)S(1)} %bitcast.274), channel_id=1, source_target_pairs={{0,3},{1,0},{2,1},{3,2},{4,7},{5,4},{6,5},{7,6},{8,11},{9,8},{10,9... | collective-permute-start | bytes 196616 | tf_op jit(solution)/shard_map/ppermute | solution.py:108
  52.9 0.3 convolution_convert_fusion.3
  53.3 1.0 copy.113
  54.2 0.2 fusion.183
  54.5 1.1 broadcast_select_fusion.1
  55.6 1.0 collective-permute-done.3
  56.6 0.3 convolution_add_fusion.1
  56.9 0.2 fusion.97
  57.1 2.0 %collective-permute-done.8 = bf16[128,256]{0,1:T(8,128)(2,1)S(1)} collective-permute-done((bf16[128,256]{0,1:T(8,128)(2,1)S(1)}, bf16[128,256]{0,1:T(8,128)(2,1)S(1)}, u32[]{:S(2)}, u32[]{:S(2)}) %collective-permute-start.8) | collective-permute-done | bytes 65568 | tf_op jit(solution)/shard_map/ppermute | solution.py:108
  59.1 0.4 multiply_reduce_fusion
  60.4 2.3 %collective-permute-start.11 = (bf16[128,1152]{1,0:T(8,128)(2,1)S(1)}, bf16[128,1152]{1,0:T(8,128)(2,1)}, u32[]{:S(2)}, u32[]{:S(2)}) collective-permute-start(bf16[128,1152]{1,0:T(8,128)(2,1)S(1)} %concatenate.47), channel_id=1, source_target_pairs={{0,2},{1,3},{2,0},{3,1},{4,6},{5,7},{6,4},{7,5},{8,10},{9,11},{10,... | collective-permute-start | bytes 884744 | tf_op jit(solution)/shard_map/ppermute | solution.py:108
  62.7 1.5 %collective-permute-start.12 = (bf16[128,1152]{1,0:T(8,128)(2,1)S(1)}, bf16[128,1152]{1,0:T(8,128)(2,1)}, u32[]{:S(2)}, u32[]{:S(2)}) collective-permute-start(bf16[128,1152]{1,0:T(8,128)(2,1)S(1)} %concatenate.47), channel_id=1, source_target_pairs={{0,3},{1,0},{2,1},{3,2},{4,7},{5,4},{6,5},{7,6},{8,11},{9,8},{10,9... | collective-permute-start | bytes 884744 | tf_op jit(solution)/shard_map/ppermute | solution.py:108
  64.2 0.2 convolution_convert_fusion.6
  64.7 0.5 convolution_convert_fusion.2
  65.1 5.9 %convolution_bitcast_fusion.1 = f32[1,8,64,512]{3,2,1,0:T(8,128)} fusion(bf16[8,64,1024]{2,1,0:T(8,128)(2,1)S(1)} %convolution_convert_fusion.2, bf16[8,1024,512]{2,1,0:T(8,128)(2,1)} %param.22), kind=kOutput, calls=%fused_computation.49 | convolution fusion | flops 536870912 | bytes 10485760 | tf_op jit(solution)/shard_map/becd,edf->becf/dot_general | solution.py:86
  71.1 9.1 %convolution_convert_fusion.1 = bf16[8,64,1024]{2,1,0:T(8,128)(2,1)S(1)} fusion(bf16[8,512,1024]{2,1,0:T(8,128)(2,1)} %param.24, bf16[8,64,1024]{2,1,0:T(8,128)(2,1)S(1)} %convolution_convert_fusion.2, bf16[8,1024,512]{2,1,0:T(8,128)(2,1)} %param.23, f32[1,8,64,512]{3,2,1,0:T(8,128)} %convolution_bitcast_fusion.1), kind=kOutput, calls=%fused_computation.37 | convolution fusion | flops 1075838976 | bytes 19922944 | tf_op jit(solution)/shard_map/becf,efd->becd/dot_general | solution.py:96
  80.3 1.2 convolution_bitcast_fusion.2
  81.5 1.0 constant_dynamic-update-slice_fusion.2
  82.6 1.0 collective-permute-done.11
  83.6 1.0 constant_dynamic-update-slice_fusion.1
  84.6 1.0 constant_dynamic-update-slice_fusion
  85.9 0.2 convolution_convert_fusion.5
  86.1 1.0 convolution_convert_fusion
  87.1 5.5 %fusion.1 = f32[8,3,64,512]{3,2,1,0:T(8,128)S(1)} fusion(bf16[8,1024,512]{2,1,0:T(8,128)(2,1)} %param.23, bf16[3,8,64,1024]{3,2,1,0:T(8,128)(2,1)S(1)} %convolution_convert_fusion), kind=kOutput, calls=%fused_computation.1 | convolution fusion | flops 1610612736 | bytes 14680064 | tf_op jit(solution)/shard_map/becd,edf->becf/dot_general | solution.py:87
  92.7 2.1 %fusion.12 = bf16[3,8,64,512]{3,2,0,1:T(8,128)(2,1)S(1)} fusion(f32[8,3,64,512]{3,2,1,0:T(8,128)S(1)} %fusion.1, bf16[8,1024,512]{2,1,0:T(8,128)(2,1)S(1)} %bitcast.257, bf16[3,8,64,1024]{3,2,1,0:T(8,128)(2,1)S(1)} %convolution_convert_fusion), kind=kOutput, calls=%fused_computation.16 | convolution fusion | flops 1615331328 | bytes 16252928 | tf_op jit(solution)/shard_map/becd,edf->becf/dot_general | solution.py:86
  94.8 0.3 slice-done.3
  95.1 1.0 fusion.28
  96.1 2.1 %fusion.31 = bf16[3,8,64,512]{3,2,0,1:T(8,128)(2,1)} fusion(bf16[3,8,64,512]{3,2,0,1:T(8,128)(2,1)S(1)} %fusion.12, bf16[8,512,1024]{2,1,0:T(8,128)(2,1)S(1)} %bitcast.259), kind=kOutput, calls=%fused_computation.36 | convolution fusion | flops 806092800 | bytes 7340032 | tf_op jit(solution)/shard_map/becf,efd->becd/dot_general | solution.py:96
  98.4 0.4 fusion.50
  98.8 1.9 %fusion.65 = bf16[3,128,512]{2,1,0:T(8,128)(2,1)S(1)} fusion(f32[3,128,512]{2,1,0:T(8,128)S(1)} %fusion.50, bf16[3,8,64,512]{3,2,0,1:T(8,128)(2,1)} %copy-done.13, s32[3,8,128]{2,1,0:T(8,128)S(1)} %convolution_convert_fusion.5, pred[3,8,128]{2,1,0:T(8,128)(4,1)S(1)} %compare_bitcast_fusion.1, bf16[3,8,128]{2,1,0:T(8,128)(2,1)S(1)} %bitcast.277), kind=kOutput, calls=%fused_computation.58 | convolution fusion | flops 202309632 | bytes 2774016 | tf_op jit(solution)/shard_map/becr,becd->brd/dot_general | solution.py:99
  100.7 5.0 %collective-permute-start.18 = (bf16[128,512]{1,0:T(8,128)(2,1)S(1)}, bf16[128,512]{1,0:T(8,128)(2,1)S(1)}, u32[]{:S(2)}, u32[]{:S(2)}) collective-permute-start(bf16[128,512]{1,0:T(8,128)(2,1)S(1)} %get-tuple-element.29), channel_id=1, source_target_pairs={{0,1},{1,2},{2,3},{3,0},{4,5},{5,6},{6,7},{7,4},{8,9},{9,10},{10,1... | collective-permute-start | bytes 393224 | tf_op jit(solution)/shard_map/ppermute | solution.py:108
  105.7 1.0 collective-permute-start.17
  106.7 1.5 %collective-permute-start.16 = (bf16[128,512]{1,0:T(8,128)(2,1)S(1)}, bf16[128,512]{1,0:T(8,128)(2,1)S(1)}, u32[]{:S(2)}, u32[]{:S(2)}) collective-permute-start(bf16[128,512]{1,0:T(8,128)(2,1)S(1)} %get-tuple-element.28), channel_id=1, source_target_pairs={{0,3},{1,0},{2,1},{3,2},{4,7},{5,4},{6,5},{7,6},{8,11},{9,8},{10,9... | collective-permute-start | bytes 393224 | tf_op jit(solution)/shard_map/ppermute | solution.py:108
  108.2 0.4 fusion.44
  108.6 0.4 fusion.62
  109.1 0.6 collective-permute-start.15
  109.7 2.0 %collective-permute-start.14 = (bf16[128,512]{1,0:T(8,128)(2,1)S(1)}, bf16[128,512]{1,0:T(8,128)(2,1)S(1)}, u32[]{:S(2)}, u32[]{:S(2)}) collective-permute-start(bf16[128,512]{1,0:T(8,128)(2,1)S(1)} %get-tuple-element.27), channel_id=1, source_target_pairs={{0,2},{1,3},{2,0},{3,1},{4,6},{5,7},{6,4},{7,5},{8,10},{9,11},{10,... | collective-permute-start | bytes 393224 | tf_op jit(solution)/shard_map/ppermute | solution.py:108
  111.7 1.3 %collective-permute-start.13 = (bf16[128,512]{1,0:T(8,128)(2,1)S(1)}, bf16[128,512]{1,0:T(8,128)(2,1)S(1)}, u32[]{:S(2)}, u32[]{:S(2)}) collective-permute-start(bf16[128,512]{1,0:T(8,128)(2,1)S(1)} %get-tuple-element.25), channel_id=1, source_target_pairs={{0,3},{1,0},{2,1},{3,2},{4,7},{5,4},{6,5},{7,6},{8,11},{9,8},{10,9... | collective-permute-start | bytes 393224 | tf_op jit(solution)/shard_map/ppermute | solution.py:108
  113.0 6.4 %collective-permute-done.17 = bf16[128,512]{1,0:T(8,128)(2,1)S(1)} collective-permute-done((bf16[128,512]{1,0:T(8,128)(2,1)S(1)}, bf16[128,512]{1,0:T(8,128)(2,1)S(1)}, u32[]{:S(2)}, u32[]{:S(2)}) %collective-permute-start.17) | collective-permute-done | bytes 131104 | tf_op jit(solution)/shard_map/ppermute | solution.py:108
  119.5 6.6 %collective-permute-done.14 = bf16[128,512]{1,0:T(8,128)(2,1)S(1)} collective-permute-done((bf16[128,512]{1,0:T(8,128)(2,1)S(1)}, bf16[128,512]{1,0:T(8,128)(2,1)S(1)}, u32[]{:S(2)}, u32[]{:S(2)}) %collective-permute-start.14) | collective-permute-done | bytes 131104 | tf_op jit(solution)/shard_map/ppermute | solution.py:108
  126.1 1.1 fusion.101
  (112 shorter events, 3.5 us)
Async XLA Ops:
  0.6 14.4 %copy-start = (bf16[1024,1024]{1,0:T(8,128)(2,1)S(1)}, bf16[1024,1024]{1,0:T(8,128)(2,1)}, u32[]{:S(2)}) copy-start(bf16[1024,1024]{1,0:T(8,128)(2,1)} %param.16) | copy-start | bytes 6291460
  0.6 14.4 %copy-start.2 = (bf16[128,1024]{1,0:T(8,128)(2,1)S(1)}, bf16[128,1024]{1,0:T(8,128)(2,1)}, u32[]{:S(2)}) copy-start(bf16[128,1024]{1,0:T(8,128)(2,1)} %param.14) | copy-start | bytes 786436
  0.7 13.0 %copy-start.9 = (s32[1,512]{1,0:T(1,128)S(1)}, s32[1,512]{1,0:T(1,128)}, u32[]{:S(2)}) copy-start(s32[1,512]{1,0:T(1,128)} %param.25) | copy-start | bytes 6148
  2.5 42.6 %collective-permute-start.6 = (bf16[128,1024]{1,0:T(8,128)(2,1)}, bf16[128,1024]{1,0:T(8,128)(2,1)S(1)}, u32[]{:S(2)}, u32[]{:S(2)}) collective-permute-start(bf16[128,1024]{1,0:T(8,128)(2,1)} %constant_dynamic-slice_fusion.9), channel_id=1, source_target_pairs={{0,3},{1,0},{2,1},{3,2},{4,7},{5,4},{6,5},{7,6},{8,11},{9,8},{10,9... | collective-permute-start | bytes 786440 | tf_op jit(solution)/shard_map/ppermute | solution.py:108
  7.6 37.5 %collective-permute-start.5 = (bf16[128,1024]{1,0:T(8,128)(2,1)}, bf16[128,1024]{1,0:T(8,128)(2,1)}, u32[]{:S(2)}, u32[]{:S(2)}) collective-permute-start(bf16[128,1024]{1,0:T(8,128)(2,1)} %constant_dynamic-slice_fusion.9), channel_id=1, source_target_pairs={{0,2},{1,3},{2,0},{3,1},{4,6},{5,7},{6,4},{7,5},{8,10},{9,11},{10,... | collective-permute-start | bytes 786440 | tf_op jit(solution)/shard_map/ppermute | solution.py:108
  15.1 8.2 %copy-start.8 = (s32[128,8]{0,1:T(8,128)S(1)}, s32[128,8]{0,1:T(8,128)}, u32[]{:S(2)}) copy-start(s32[128,8]{0,1:T(8,128)} %param.27) | copy-start | bytes 12292
  16.1 7.5 %copy-start.10 = (s32[1,512]{1,0:T(1,128)S(1)}, s32[1,512]{1,0:T(1,128)}, u32[]{:S(2)}) copy-start(s32[1,512]{1,0:T(1,128)} %param.26) | copy-start | bytes 6148
  16.1 7.6 %copy-start.11 = (bf16[1024]{0:T(1024)(128)(2,1)S(1)}, bf16[1024]{0:T(1024)(128)(2,1)}, u32[]{:S(2)}) copy-start(bf16[1024]{0:T(1024)(128)(2,1)} %param.20) | copy-start | bytes 6148
  17.9 9.9 %collective-permute-start.2 = (bf16[128,2,256]{0,2,1:T(8,128)(2,1)S(1)}, bf16[128,2,256]{0,2,1:T(8,128)(2,1)S(1)}, u32[]{:S(2)}, u32[]{:S(2)}) collective-permute-start(bf16[128,2,256]{0,2,1:T(8,128)(2,1)S(1)} %get-tuple-element.22), channel_id=1, source_target_pairs={{0,3},{1,0},{2,1},{3,2},{4,7},{5,4},{6,5},{7,6},{8,11},{9,8},{10,9... | collective-permute-start | bytes 393224 | tf_op jit(solution)/shard_map/ppermute | solution.py:108
  18.4 22.9 %collective-permute-start.1 = (bf16[128,2,256]{0,2,1:T(8,128)(2,1)S(1)}, bf16[128,2,256]{0,2,1:T(8,128)(2,1)S(1)}, u32[]{:S(2)}, u32[]{:S(2)}) collective-permute-start(bf16[128,2,256]{0,2,1:T(8,128)(2,1)S(1)} %get-tuple-element.23), channel_id=1, source_target_pairs={{0,2},{1,3},{2,0},{3,1},{4,6},{5,7},{6,4},{7,5},{8,10},{9,11},{10,... | collective-permute-start | bytes 393224 | tf_op jit(solution)/shard_map/ppermute | solution.py:108
  21.0 20.4 %collective-permute-start = (bf16[128,2,256]{0,2,1:T(8,128)(2,1)S(1)}, bf16[128,2,256]{0,2,1:T(8,128)(2,1)S(1)}, u32[]{:S(2)}, u32[]{:S(2)}) collective-permute-start(bf16[128,2,256]{0,2,1:T(8,128)(2,1)S(1)} %get-tuple-element.24), channel_id=1, source_target_pairs={{0,1},{1,2},{2,3},{3,0},{4,5},{5,6},{6,7},{7,4},{8,9},{9,10},{10,1... | collective-permute-start | bytes 393224 | tf_op jit(solution)/shard_map/ppermute | solution.py:108
  27.8 17.3 %collective-permute-start.4 = (bf16[128,1024]{1,0:T(8,128)(2,1)}, bf16[128,1024]{1,0:T(8,128)(2,1)S(1)}, u32[]{:S(2)}, u32[]{:S(2)}) collective-permute-start(bf16[128,1024]{1,0:T(8,128)(2,1)} %constant_dynamic-slice_fusion.9), channel_id=1, source_target_pairs={{0,1},{1,2},{2,3},{3,0},{4,5},{5,6},{6,7},{7,4},{8,9},{9,10},{10,1... | collective-permute-start | bytes 786440 | tf_op jit(solution)/shard_map/ppermute | solution.py:108
  46.1 8.4 %collective-permute-start.7 = (bf16[3,128,1024]{2,1,0:T(8,128)(2,1)S(1)}, bf16[3,128,1024]{2,1,0:T(8,128)(2,1)S(1)}, u32[]{:S(2)}, u32[]{:S(2)}) collective-permute-start(bf16[3,128,1024]{2,1,0:T(8,128)(2,1)S(1)} %pad_maximum_fusion), channel_id=1, source_target_pairs={{0,4},{4,0},{8,12},{12,8},{16,20},{20,16},{24,28},{28,24},{1,5},{5... | collective-permute-start | bytes 2359304 | tf_op jit(solution)/shard_map/ppermute | solution.py:134
  46.2 8.0 %copy-start.6 = (bf16[256,1024]{1,0:T(8,128)(2,1)S(1)}, bf16[256,1024]{1,0:T(8,128)(2,1)}, u32[]{:S(2)}) copy-start(bf16[256,1024]{1,0:T(8,128)(2,1)} %param.19) | copy-start | bytes 1572868
  49.0 7.8 %collective-permute-start.9 = (bf16[128,256]{0,1:T(8,128)(2,1)S(1)}, bf16[128,256]{0,1:T(8,128)(2,1)S(1)}, u32[]{:S(2)}, u32[]{:S(2)}) collective-permute-start(bf16[128,256]{0,1:T(8,128)(2,1)S(1)} %bitcast.273), channel_id=1, source_target_pairs={{0,1},{1,2},{2,3},{3,0},{4,5},{5,6},{6,7},{7,4},{8,9},{9,10},{10,1... | collective-permute-start | bytes 196616 | tf_op jit(solution)/shard_map/ppermute | solution.py:108
  50.8 5.7 %collective-permute-start.3 = (bf16[128,256]{0,1:T(8,128)(2,1)S(1)}, bf16[128,256]{0,1:T(8,128)(2,1)S(1)}, u32[]{:S(2)}, u32[]{:S(2)}) collective-permute-start(bf16[128,256]{0,1:T(8,128)(2,1)S(1)} %bitcast.274), channel_id=1, source_target_pairs={{0,3},{1,0},{2,1},{3,2},{4,7},{5,4},{6,5},{7,6},{8,11},{9,8},{10,9... | collective-permute-start | bytes 196616 | tf_op jit(solution)/shard_map/ppermute | solution.py:108
  52.9 6.2 %collective-permute-start.8 = (bf16[128,256]{0,1:T(8,128)(2,1)S(1)}, bf16[128,256]{0,1:T(8,128)(2,1)S(1)}, u32[]{:S(2)}, u32[]{:S(2)}) collective-permute-start(bf16[128,256]{0,1:T(8,128)(2,1)S(1)} %bitcast.272), channel_id=1, source_target_pairs={{0,2},{1,3},{2,0},{3,1},{4,6},{5,7},{6,4},{7,5},{8,10},{9,11},{10,... | collective-permute-start | bytes 196616 | tf_op jit(solution)/shard_map/ppermute | solution.py:108
  56.8 2.8 %copy-start.7 = (bf16[1024,32]{0,1:T(8,128)(2,1)S(1)}, bf16[1024,32]{0,1:T(8,128)(2,1)}, u32[]{:S(2)}) copy-start(bf16[1024,32]{0,1:T(8,128)(2,1)} %param.21) | copy-start | bytes 196612
  59.5 11.6 %copy-start.3 = (f32[128,1024]{1,0:T(8,128)}, f32[128,1024]{1,0:T(8,128)S(1)}, u32[]{:S(2)}) copy-start(f32[128,1024]{1,0:T(8,128)S(1)} %get-tuple-element.52) | copy-start | bytes 1572868
  60.4 21.2 %collective-permute-start.10 = (bf16[128,1152]{1,0:T(8,128)(2,1)S(1)}, bf16[128,1152]{1,0:T(8,128)(2,1)}, u32[]{:S(2)}, u32[]{:S(2)}) collective-permute-start(bf16[128,1152]{1,0:T(8,128)(2,1)S(1)} %concatenate.47), channel_id=1, source_target_pairs={{0,1},{1,2},{2,3},{3,0},{4,5},{5,6},{6,7},{7,4},{8,9},{9,10},{10,1... | collective-permute-start | bytes 884744 | tf_op jit(solution)/shard_map/ppermute | solution.py:108
  60.4 23.1 %collective-permute-start.11 = (bf16[128,1152]{1,0:T(8,128)(2,1)S(1)}, bf16[128,1152]{1,0:T(8,128)(2,1)}, u32[]{:S(2)}, u32[]{:S(2)}) collective-permute-start(bf16[128,1152]{1,0:T(8,128)(2,1)S(1)} %concatenate.47), channel_id=1, source_target_pairs={{0,2},{1,3},{2,0},{3,1},{4,6},{5,7},{6,4},{7,5},{8,10},{9,11},{10,... | collective-permute-start | bytes 884744 | tf_op jit(solution)/shard_map/ppermute | solution.py:108
  62.7 21.8 %collective-permute-start.12 = (bf16[128,1152]{1,0:T(8,128)(2,1)S(1)}, bf16[128,1152]{1,0:T(8,128)(2,1)}, u32[]{:S(2)}, u32[]{:S(2)}) collective-permute-start(bf16[128,1152]{1,0:T(8,128)(2,1)S(1)} %concatenate.47), channel_id=1, source_target_pairs={{0,3},{1,0},{2,1},{3,2},{4,7},{5,4},{6,5},{7,6},{8,11},{9,8},{10,9... | collective-permute-start | bytes 884744 | tf_op jit(solution)/shard_map/ppermute | solution.py:108
  86.1 6.6 %slice-start = ((s8[8388608]{0:T(1024)(128)(4,1)}), s8[4194304]{0:T(1024)(128)(4,1)S(1)}, s32[]{:S(2)}) async-start(s8[8388608]{0:T(1024)(128)(4,1)} %bitcast.256), calls=%async_computation | async-start | bytes 8388608
  87.1 5.6 %slice-start.1 = ((s8[8388608]{0:T(1024)(128)(4,1)}), s8[4194304]{0:T(1024)(128)(4,1)S(1)}, s32[]{:S(2)}) async-start(s8[8388608]{0:T(1024)(128)(4,1)} %bitcast.256), calls=%async_computation.1 | async-start | bytes 8388608
  87.1 7.7 %slice-start.2 = ((s8[8388608]{0:T(1024)(128)(4,1)}), s8[4194304]{0:T(1024)(128)(4,1)S(1)}, s32[]{:S(2)}) async-start(s8[8388608]{0:T(1024)(128)(4,1)} %bitcast.258), calls=%async_computation.2 | async-start | bytes 8388608
  92.7 2.4 %slice-start.3 = ((s8[8388608]{0:T(1024)(128)(4,1)}), s8[4194304]{0:T(1024)(128)(4,1)S(1)}, s32[]{:S(2)}) async-start(s8[8388608]{0:T(1024)(128)(4,1)} %bitcast.258), calls=%async_computation.3 | async-start | bytes 8388608
  96.1 2.3 %copy-start.13 = (bf16[3,8,64,512]{3,2,0,1:T(8,128)(2,1)}, bf16[3,8,64,512]{3,2,0,1:T(8,128)(2,1)S(1)}, u32[]{:S(2)}) copy-start(bf16[3,8,64,512]{3,2,0,1:T(8,128)(2,1)S(1)} %fusion.28) | copy-start | bytes 4718596
  98.4 9.8 %copy-start.12 = (bf16[3,8,64,512]{3,2,0,1:T(8,128)(2,1)S(1)}, bf16[3,8,64,512]{3,2,0,1:T(8,128)(2,1)}, u32[]{:S(2)}) copy-start(bf16[3,8,64,512]{3,2,0,1:T(8,128)(2,1)} %fusion.31) | copy-start | bytes 4718596
  100.7 11.0 %collective-permute-start.18 = (bf16[128,512]{1,0:T(8,128)(2,1)S(1)}, bf16[128,512]{1,0:T(8,128)(2,1)S(1)}, u32[]{:S(2)}, u32[]{:S(2)}) collective-permute-start(bf16[128,512]{1,0:T(8,128)(2,1)S(1)} %get-tuple-element.29), channel_id=1, source_target_pairs={{0,1},{1,2},{2,3},{3,0},{4,5},{5,6},{6,7},{7,4},{8,9},{9,10},{10,1... | collective-permute-start | bytes 393224 | tf_op jit(solution)/shard_map/ppermute | solution.py:108
  105.7 13.7 %collective-permute-start.17 = (bf16[128,512]{1,0:T(8,128)(2,1)S(1)}, bf16[128,512]{1,0:T(8,128)(2,1)S(1)}, u32[]{:S(2)}, u32[]{:S(2)}) collective-permute-start(bf16[128,512]{1,0:T(8,128)(2,1)S(1)} %get-tuple-element.30), channel_id=1, source_target_pairs={{0,2},{1,3},{2,0},{3,1},{4,6},{5,7},{6,4},{7,5},{8,10},{9,11},{10,... | collective-permute-start | bytes 393224 | tf_op jit(solution)/shard_map/ppermute | solution.py:108
  106.7 12.7 %collective-permute-start.16 = (bf16[128,512]{1,0:T(8,128)(2,1)S(1)}, bf16[128,512]{1,0:T(8,128)(2,1)S(1)}, u32[]{:S(2)}, u32[]{:S(2)}) collective-permute-start(bf16[128,512]{1,0:T(8,128)(2,1)S(1)} %get-tuple-element.28), channel_id=1, source_target_pairs={{0,3},{1,0},{2,1},{3,2},{4,7},{5,4},{6,5},{7,6},{8,11},{9,8},{10,9... | collective-permute-start | bytes 393224 | tf_op jit(solution)/shard_map/ppermute | solution.py:108
  108.6 17.5 %copy-start.4 = (f32[128,1024]{1,0:T(8,128)S(1)}, f32[128,1024]{1,0:T(8,128)}, u32[]{:S(2)}) copy-start(f32[128,1024]{1,0:T(8,128)} %copy-done.3) | copy-start | bytes 1572868
  108.6 17.5 %copy-start.5 = (f32[128,1024]{1,0:T(8,128)S(1)}, f32[128,1024]{1,0:T(8,128)}, u32[]{:S(2)}) copy-start(f32[128,1024]{1,0:T(8,128)} %convolution_bitcast_fusion.2) | copy-start | bytes 1572868
  108.6 18.6 %copy-start.1 = (bf16[1024,1024]{1,0:T(8,128)(2,1)S(1)}, bf16[1024,1024]{1,0:T(8,128)(2,1)}, u32[]{:S(2)}) copy-start(bf16[1024,1024]{1,0:T(8,128)(2,1)} %param.16) | copy-start | bytes 6291460
  109.1 10.3 %collective-permute-start.15 = (bf16[128,512]{1,0:T(8,128)(2,1)S(1)}, bf16[128,512]{1,0:T(8,128)(2,1)S(1)}, u32[]{:S(2)}, u32[]{:S(2)}) collective-permute-start(bf16[128,512]{1,0:T(8,128)(2,1)S(1)} %get-tuple-element.26), channel_id=1, source_target_pairs={{0,1},{1,2},{2,3},{3,0},{4,5},{5,6},{6,7},{7,4},{8,9},{9,10},{10,1... | collective-permute-start | bytes 393224 | tf_op jit(solution)/shard_map/ppermute | solution.py:108
  109.7 16.4 %collective-permute-start.14 = (bf16[128,512]{1,0:T(8,128)(2,1)S(1)}, bf16[128,512]{1,0:T(8,128)(2,1)S(1)}, u32[]{:S(2)}, u32[]{:S(2)}) collective-permute-start(bf16[128,512]{1,0:T(8,128)(2,1)S(1)} %get-tuple-element.27), channel_id=1, source_target_pairs={{0,2},{1,3},{2,0},{3,1},{4,6},{5,7},{6,4},{7,5},{8,10},{9,11},{10,... | collective-permute-start | bytes 393224 | tf_op jit(solution)/shard_map/ppermute | solution.py:108
  111.7 14.4 %collective-permute-start.13 = (bf16[128,512]{1,0:T(8,128)(2,1)S(1)}, bf16[128,512]{1,0:T(8,128)(2,1)S(1)}, u32[]{:S(2)}, u32[]{:S(2)}) collective-permute-start(bf16[128,512]{1,0:T(8,128)(2,1)S(1)} %get-tuple-element.25), channel_id=1, source_target_pairs={{0,3},{1,0},{2,1},{3,2},{4,7},{5,4},{6,5},{7,6},{8,11},{9,8},{10,9... | collective-permute-start | bytes 393224 | tf_op jit(solution)/shard_map/ppermute | solution.py:108

commit v12 on v11

--- a/solution.py
+++ b/solution.py
@@ -92,6 +92,8 @@
     cut = w_down.shape[2] // pieces
     outs = []
     for piece in range(pieces):
+        if outs:
+            outs, hidden = lax.optimization_barrier((outs, hidden))
         down = lax.slice_in_dim(w_down, piece * cut, (piece + 1) * cut, axis=2)
         result = jnp.einsum("becf,efd->becd", hidden, down, preferred_element_type=jnp.float32)
         result = result.astype(jnp.bfloat16)

time: 128 us -> 129 us (level)
    dot_general x3, matrix products: 3.47 us -> 2.03 us  [expert_mix(): jnp.einsum('becr,becd->brd', low, result, preferred_element_type=jnp.floa...]
  transfers between devices with their start and end apart: 19 -> 19, of which waited for: 7 -> 7; matrix products, arithmetic and copies ran while one was open for 32% -> 31% of each run, Pallas kernels for 0% -> 0%
where the time goes in v12:
time: 129 us; the launch traced here: 128 us
  matrix products  45.1 us (35%)
  starting transfers between devices  42.1 us (33%)
  waiting for transfers between devices  22.7 us (18%)
  local copies, waits for them, and re-layouts  8.95 us (7%)
  other arithmetic  8.27 us (6%)
  between operations  1.32 us (1%)
    ppermute x18, starting transfers between devices, shifted(): lax.ppermute(x, 'exp', [(j, (j + step) % count) for j in range(count)])  42 us
    ppermute x18, waiting for transfers between devices, shifted(): lax.ppermute(x, 'exp', [(j, (j + step) % count) for j in range(count)])  22.7 us
    dot_general x3, matrix products, expert_mix(): jnp.einsum('becf,efd->becd', hidden, down, preferred_element_type=jnp.flo...  13.3 us
    dot_general x2, matrix products, expert_mix(): jnp.einsum('becd,edf->becf', received, w_gate, preferred_element_type=jnp...  8 us
    dot_general x1, matrix products, expert_mix(): jnp.einsum('becd,edf->becf', received, w_up, preferred_element_type=jnp.f...  5.54 us
    unnamed x39, local copies, waits for them, and re-layouts  4.06 us
    sub x1, matrix products, attend(): expo = jnp.exp(score - top)  3.59 us
    dot_general x1, matrix products, attend(): jnp.einsum('kgqt,tkd->qkgd', probs, values, preferred_element_type=jnp.fl...  2.73 us
  transfers between devices with their start and end apart: 19, of which 7 were waited for; matrix products, arithmetic and copies ran while one was open for 31% of the time, Pallas kernels for 0%

profile of v12, /device:TPU:0, one launch (start us, length us, event | category | flops | bytes accessed | tf_op | source)
XLA Modules:
  0.0 128.4 jit_solution(12494562123686938572)
XLA Ops:
  0.7 1.8 %constant_dynamic-slice_fusion.9 = bf16[128,1024]{1,0:T(8,128)(2,1)} fusion(bf16[256,1024]{1,0:T(8,128)(2,1)} %param.19, s32[]{:T(128)S(6)} %select_n.170), kind=kLoop, calls=%fused_computation.184 | loop fusion | bytes 524292 | tf_op jit(solution)/shard_map/dynamic_slice | solution.py:134
  2.5 5.1 %collective-permute-start.6 = (bf16[128,1024]{1,0:T(8,128)(2,1)}, bf16[128,1024]{1,0:T(8,128)(2,1)S(1)}, u32[]{:S(2)}, u32[]{:S(2)}) collective-permute-start(bf16[128,1024]{1,0:T(8,128)(2,1)} %constant_dynamic-slice_fusion.9), channel_id=1, source_target_pairs={{0,3},{1,0},{2,1},{3,2},{4,7},{5,4},{6,5},{7,6},{8,11},{9,8},{10,9... | collective-permute-start | bytes 786440 | tf_op jit(solution)/shard_map/ppermute | solution.py:110
  7.6 0.6 multiply_power_fusion
  8.2 0.7 convert_element_type.124
  8.9 1.1 fusion.84
  10.0 1.7 %convolution_convert_fusion.4 = bf16[128,512]{1,0:T(8,128)(2,1)S(1)} fusion(bf16[1024,512]{1,0:T(8,128)(2,1)} %param.18, bf16[128,1024]{1,0:T(8,128)(2,1)} %param.14, f32[1024]{0:T(1024)S(1)} %convert_element_type.124, f32[128]{0:T(128)S(1)} %add_rsqrt_fusion.1), kind=kOutput, calls=%fused_computation.69 | convolution fusion | flops 134807552 | bytes 1446400 | tf_op jit(solution)/shard_map/dot_general | solution.py:171
  11.8 1.9 %fusion.174 = f32[128,512]{0,1:T(8,128)S(1)} fusion(bf16[1024,512]{1,0:T(8,128)(2,1)} %param.17, bf16[128,1024]{1,0:T(8,128)(2,1)} %param.14, f32[1024]{0:T(1024)S(1)} %convert_element_type.124, f32[128]{0:T(128)S(1)} %add_rsqrt_fusion.1), kind=kOutput, calls=%fused_computation.227 | convolution fusion | flops 134742016 | bytes 1577472 | tf_op jit(solution)/shard_map/dot_general | solution.py:168
  13.9 0.3 reduce-window.9
  14.4 0.7 bitcast_subtract_fusion
  15.1 1.0 fusion.176
  16.1 0.8 dynamic-slice_convert_fusion
  16.8 0.8 multiply_cosine_fusion
  17.9 0.5 collective-permute-start.2
  18.4 2.5 %collective-permute-start.1 = (bf16[128,2,256]{0,2,1:T(8,128)(2,1)S(1)}, bf16[128,2,256]{0,2,1:T(8,128)(2,1)S(1)}, u32[]{:S(2)}, u32[]{:S(2)}) collective-permute-start(bf16[128,2,256]{0,2,1:T(8,128)(2,1)S(1)} %get-tuple-element.27), channel_id=1, source_target_pairs={{0,2},{1,3},{2,0},{3,1},{4,6},{5,7},{6,4},{7,5},{8,10},{9,11},{10,... | collective-permute-start | bytes 393224 | tf_op jit(solution)/shard_map/ppermute | solution.py:110
  21.0 1.9 %collective-permute-start = (bf16[128,2,256]{0,2,1:T(8,128)(2,1)S(1)}, bf16[128,2,256]{0,2,1:T(8,128)(2,1)S(1)}, u32[]{:S(2)}, u32[]{:S(2)}) collective-permute-start(bf16[128,2,256]{0,2,1:T(8,128)(2,1)S(1)} %get-tuple-element.28), channel_id=1, source_target_pairs={{0,1},{1,2},{2,3},{3,0},{4,5},{5,6},{6,7},{7,4},{8,9},{9,10},{10,1... | collective-permute-start | bytes 393224 | tf_op jit(solution)/shard_map/ppermute | solution.py:110
  23.3 0.3 compare_and_fusion
  23.8 4.0 %collective-permute-done.2 = bf16[128,2,256]{0,2,1:T(8,128)(2,1)S(1)} collective-permute-done((bf16[128,2,256]{0,2,1:T(8,128)(2,1)S(1)}, bf16[128,2,256]{0,2,1:T(8,128)(2,1)S(1)}, u32[]{:S(2)}, u32[]{:S(2)}) %collective-permute-start.2) | collective-permute-done | bytes 131104 | tf_op jit(solution)/shard_map/ppermute | solution.py:110
  27.8 12.5 %collective-permute-start.4 = (bf16[128,1024]{1,0:T(8,128)(2,1)}, bf16[128,1024]{1,0:T(8,128)(2,1)S(1)}, u32[]{:S(2)}, u32[]{:S(2)}) collective-permute-start(bf16[128,1024]{1,0:T(8,128)(2,1)} %constant_dynamic-slice_fusion.9), channel_id=1, source_target_pairs={{0,1},{1,2},{2,3},{3,0},{4,5},{5,6},{6,7},{7,4},{8,9},{9,10},{10,1... | collective-permute-start | bytes 786440 | tf_op jit(solution)/shard_map/ppermute | solution.py:110
  40.3 1.1 collective-permute-done.1
  41.5 3.6 %fusion.179 = (f32[2,2,512]{2,1,0:T(2,128)S(1)}, f32[2,2,512,512]{2,3,1,0:T(8,128)}) fusion(pred[512,512]{0,1:T(8,128)(4,1)S(1)} %compare_and_fusion, bf16[512,2,2,64]{0,3,2,1:T(8,128)(2,1)S(1)} %bitcast.268, bf16[512,2,256]{0,2,1:T(8,128)(2,1)S(1)} %pad_maximum_fusion.3), kind=kOutput, calls=%fused_computation.230 | convolution fusion | flops 138412544 | bytes 4857856 | tf_op jit(solution)/shard_map/sub | solution.py:44
  45.1 1.0 pad_maximum_fusion
  46.2 2.7 %fusion.70 = bf16[512,2,2,64]{0,3,2,1:T(8,128)(2,1)S(1)} fusion(f32[2,2,512,512]{2,3,1,0:T(8,128)} %get-tuple-element.54, f32[2,2,512]{2,1,0:T(2,128)S(1)} %get-tuple-element.53, bf16[512,2,256]{0,2,1:T(8,128)(2,1)S(1)} %pad_maximum_fusion.3), kind=kOutput, calls=%fused_computation.68 | convolution fusion | flops 136445952 | bytes 4595712 | tf_op jit(solution)/shard_map/kgqt,tkd->qkgd/dot_general | solution.py:46
  49.0 1.8 %collective-permute-start.9 = (bf16[128,256]{0,1:T(8,128)(2,1)S(1)}, bf16[128,256]{0,1:T(8,128)(2,1)S(1)}, u32[]{:S(2)}, u32[]{:S(2)}) collective-permute-start(bf16[128,256]{0,1:T(8,128)(2,1)S(1)} %bitcast.271), channel_id=1, source_target_pairs={{0,1},{1,2},{2,3},{3,0},{4,5},{5,6},{6,7},{7,4},{8,9},{9,10},{10,1... | collective-permute-start | bytes 196616 | tf_op jit(solution)/shard_map/ppermute | solution.py:110
  50.8 2.1 %collective-permute-start.3 = (bf16[128,256]{0,1:T(8,128)(2,1)S(1)}, bf16[128,256]{0,1:T(8,128)(2,1)S(1)}, u32[]{:S(2)}, u32[]{:S(2)}) collective-permute-start(bf16[128,256]{0,1:T(8,128)(2,1)S(1)} %bitcast.272), channel_id=1, source_target_pairs={{0,3},{1,0},{2,1},{3,2},{4,7},{5,4},{6,5},{7,6},{8,11},{9,8},{10,9... | collective-permute-start | bytes 196616 | tf_op jit(solution)/shard_map/ppermute | solution.py:110
  52.9 0.3 convolution_convert_fusion.3
  53.3 1.0 copy.113
  54.2 0.2 fusion.180
  54.5 1.1 broadcast_select_fusion.1
  55.6 1.0 collective-permute-done.3
  56.6 0.3 convolution_add_fusion.1
  56.9 0.2 fusion.94
  57.1 2.0 %collective-permute-done.8 = bf16[128,256]{0,1:T(8,128)(2,1)S(1)} collective-permute-done((bf16[128,256]{0,1:T(8,128)(2,1)S(1)}, bf16[128,256]{0,1:T(8,128)(2,1)S(1)}, u32[]{:S(2)}, u32[]{:S(2)}) %collective-permute-start.8) | collective-permute-done | bytes 65568 | tf_op jit(solution)/shard_map/ppermute | solution.py:110
  59.1 0.4 multiply_reduce_fusion
  60.4 2.3 %collective-permute-start.11 = (bf16[128,1152]{1,0:T(8,128)(2,1)S(1)}, bf16[128,1152]{1,0:T(8,128)(2,1)}, u32[]{:S(2)}, u32[]{:S(2)}) collective-permute-start(bf16[128,1152]{1,0:T(8,128)(2,1)S(1)} %concatenate.47), channel_id=1, source_target_pairs={{0,2},{1,3},{2,0},{3,1},{4,6},{5,7},{6,4},{7,5},{8,10},{9,11},{10,... | collective-permute-start | bytes 884744 | tf_op jit(solution)/shard_map/ppermute | solution.py:110
  62.7 1.5 %collective-permute-start.12 = (bf16[128,1152]{1,0:T(8,128)(2,1)S(1)}, bf16[128,1152]{1,0:T(8,128)(2,1)}, u32[]{:S(2)}, u32[]{:S(2)}) collective-permute-start(bf16[128,1152]{1,0:T(8,128)(2,1)S(1)} %concatenate.47), channel_id=1, source_target_pairs={{0,3},{1,0},{2,1},{3,2},{4,7},{5,4},{6,5},{7,6},{8,11},{9,8},{10,9... | collective-permute-start | bytes 884744 | tf_op jit(solution)/shard_map/ppermute | solution.py:110
  64.2 0.2 convolution_convert_fusion.6
  64.7 0.5 convolution_convert_fusion.2
  65.1 5.9 %convolution_bitcast_fusion.1 = f32[1,8,64,512]{3,2,1,0:T(8,128)} fusion(bf16[8,64,1024]{2,1,0:T(8,128)(2,1)S(1)} %convolution_convert_fusion.2, bf16[8,1024,512]{2,1,0:T(8,128)(2,1)} %param.22), kind=kOutput, calls=%fused_computation.49 | convolution fusion | flops 536870912 | bytes 10485760 | tf_op jit(solution)/shard_map/becd,edf->becf/dot_general | solution.py:86
  71.1 9.1 %convolution_convert_fusion.1 = bf16[8,64,1024]{2,1,0:T(8,128)(2,1)S(1)} fusion(bf16[8,512,1024]{2,1,0:T(8,128)(2,1)} %param.24, bf16[8,64,1024]{2,1,0:T(8,128)(2,1)S(1)} %convolution_convert_fusion.2, bf16[8,1024,512]{2,1,0:T(8,128)(2,1)} %param.23, f32[1,8,64,512]{3,2,1,0:T(8,128)} %convolution_bitcast_fusion.1), kind=kOutput, calls=%fused_computation.37 | convolution fusion | flops 1075838976 | bytes 19922944 | tf_op jit(solution)/shard_map/becf,efd->becd/dot_general | solution.py:98
  80.3 1.2 convolution_bitcast_fusion.2
  81.6 1.0 constant_dynamic-update-slice_fusion.2
  82.6 1.0 collective-permute-done.11
  83.6 1.0 constant_dynamic-update-slice_fusion.1
  84.6 1.0 constant_dynamic-update-slice_fusion
  86.1 1.0 convolution_convert_fusion
  87.1 5.5 %fusion.1 = f32[8,3,64,512]{3,2,1,0:T(8,128)S(1)} fusion(bf16[8,1024,512]{2,1,0:T(8,128)(2,1)} %param.23, bf16[3,8,64,1024]{3,2,1,0:T(8,128)(2,1)S(1)} %convolution_convert_fusion), kind=kOutput, calls=%fused_computation.1 | convolution fusion | flops 1610612736 | bytes 14680064 | tf_op jit(solution)/shard_map/becd,edf->becf/dot_general | solution.py:87
  92.7 2.1 %fusion.12 = bf16[3,8,64,512]{3,2,0,1:T(8,128)(2,1)S(1)} fusion(f32[8,3,64,512]{3,2,1,0:T(8,128)S(1)} %fusion.1, bf16[8,1024,512]{2,1,0:T(8,128)(2,1)S(1)} %bitcast.255, bf16[3,8,64,1024]{3,2,1,0:T(8,128)(2,1)S(1)} %convolution_convert_fusion), kind=kOutput, calls=%fused_computation.16 | convolution fusion | flops 1615331328 | bytes 16252928 | tf_op jit(solution)/shard_map/becd,edf->becf/dot_general | solution.py:86
  94.8 0.3 slice-done.3
  95.1 1.0 fusion.31
  96.4 0.4 fusion.44
  96.8 0.4 fusion.59
  97.3 0.5 copy-done.13
  97.8 3.2 %fusion.28 = bf16[3,8,64,512]{3,2,0,1:T(8,128)(2,1)S(1)} fusion(bf16[3,8,64,512]{3,2,0,1:T(8,128)(2,1)S(1)} %copy-done.13, bf16[8,512,1024]{2,1,0:T(8,128)(2,1)} %param.24), kind=kOutput, calls=%fused_computation.35 | convolution fusion | flops 806092800 | bytes 7340032 | tf_op jit(solution)/shard_map/becf,efd->becd/dot_general | solution.py:98
  101.0 0.4 fusion.50
  101.5 0.4 fusion.62
  101.9 5.0 %collective-permute-start.18 = (bf16[128,512]{1,0:T(8,128)(2,1)S(1)}, bf16[128,512]{1,0:T(8,128)(2,1)S(1)}, u32[]{:S(2)}, u32[]{:S(2)}) collective-permute-start(bf16[128,512]{1,0:T(8,128)(2,1)S(1)} %get-tuple-element.33), channel_id=1, source_target_pairs={{0,1},{1,2},{2,3},{3,0},{4,5},{5,6},{6,7},{7,4},{8,9},{9,10},{10,1... | collective-permute-start | bytes 393224 | tf_op jit(solution)/shard_map/ppermute | solution.py:110
  106.9 1.0 collective-permute-start.17
  107.9 1.5 %collective-permute-start.16 = (bf16[128,512]{1,0:T(8,128)(2,1)S(1)}, bf16[128,512]{1,0:T(8,128)(2,1)S(1)}, u32[]{:S(2)}, u32[]{:S(2)}) collective-permute-start(bf16[128,512]{1,0:T(8,128)(2,1)S(1)} %get-tuple-element.32), channel_id=1, source_target_pairs={{0,3},{1,0},{2,1},{3,2},{4,7},{5,4},{6,5},{7,6},{8,11},{9,8},{10,9... | collective-permute-start | bytes 393224 | tf_op jit(solution)/shard_map/ppermute | solution.py:110
  109.4 0.6 collective-permute-start.15
  110.0 2.0 %collective-permute-start.14 = (bf16[128,512]{1,0:T(8,128)(2,1)S(1)}, bf16[128,512]{1,0:T(8,128)(2,1)S(1)}, u32[]{:S(2)}, u32[]{:S(2)}) collective-permute-start(bf16[128,512]{1,0:T(8,128)(2,1)S(1)} %get-tuple-element.30), channel_id=1, source_target_pairs={{0,2},{1,3},{2,0},{3,1},{4,6},{5,7},{6,4},{7,5},{8,10},{9,11},{10,... | collective-permute-start | bytes 393224 | tf_op jit(solution)/shard_map/ppermute | solution.py:110
  112.0 1.7 %collective-permute-start.13 = (bf16[128,512]{1,0:T(8,128)(2,1)S(1)}, bf16[128,512]{1,0:T(8,128)(2,1)S(1)}, u32[]{:S(2)}, u32[]{:S(2)}) collective-permute-start(bf16[128,512]{1,0:T(8,128)(2,1)S(1)} %get-tuple-element.29), channel_id=1, source_target_pairs={{0,3},{1,0},{2,1},{3,2},{4,7},{5,4},{6,5},{7,6},{8,11},{9,8},{10,9... | collective-permute-start | bytes 393224 | tf_op jit(solution)/shard_map/ppermute | solution.py:110
  113.7 6.9 %collective-permute-done.17 = bf16[128,512]{1,0:T(8,128)(2,1)S(1)} collective-permute-done((bf16[128,512]{1,0:T(8,128)(2,1)S(1)}, bf16[128,512]{1,0:T(8,128)(2,1)S(1)}, u32[]{:S(2)}, u32[]{:S(2)}) %collective-permute-start.17) | collective-permute-done | bytes 131104 | tf_op jit(solution)/shard_map/ppermute | solution.py:110
  120.7 6.6 %collective-permute-done.14 = bf16[128,512]{1,0:T(8,128)(2,1)S(1)} collective-permute-done((bf16[128,512]{1,0:T(8,128)(2,1)S(1)}, bf16[128,512]{1,0:T(8,128)(2,1)S(1)}, u32[]{:S(2)}, u32[]{:S(2)}) %collective-permute-start.14) | collective-permute-done | bytes 131104 | tf_op jit(solution)/shard_map/ppermute | solution.py:110
  127.3 1.1 fusion.98
  (112 shorter events, 3.8 us)
Async XLA Ops:
  0.6 14.4 %copy-start = (bf16[1024,1024]{1,0:T(8,128)(2,1)S(1)}, bf16[1024,1024]{1,0:T(8,128)(2,1)}, u32[]{:S(2)}) copy-start(bf16[1024,1024]{1,0:T(8,128)(2,1)} %param.16) | copy-start | bytes 6291460
  0.6 14.4 %copy-start.2 = (bf16[128,1024]{1,0:T(8,128)(2,1)S(1)}, bf16[128,1024]{1,0:T(8,128)(2,1)}, u32[]{:S(2)}) copy-start(bf16[128,1024]{1,0:T(8,128)(2,1)} %param.14) | copy-start | bytes 786436
  0.7 13.0 %copy-start.9 = (s32[1,512]{1,0:T(1,128)S(1)}, s32[1,512]{1,0:T(1,128)}, u32[]{:S(2)}) copy-start(s32[1,512]{1,0:T(1,128)} %param.25) | copy-start | bytes 6148
  2.5 42.6 %collective-permute-start.6 = (bf16[128,1024]{1,0:T(8,128)(2,1)}, bf16[128,1024]{1,0:T(8,128)(2,1)S(1)}, u32[]{:S(2)}, u32[]{:S(2)}) collective-permute-start(bf16[128,1024]{1,0:T(8,128)(2,1)} %constant_dynamic-slice_fusion.9), channel_id=1, source_target_pairs={{0,3},{1,0},{2,1},{3,2},{4,7},{5,4},{6,5},{7,6},{8,11},{9,8},{10,9... | collective-permute-start | bytes 786440 | tf_op jit(solution)/shard_map/ppermute | solution.py:110
  7.6 37.5 %collective-permute-start.5 = (bf16[128,1024]{1,0:T(8,128)(2,1)}, bf16[128,1024]{1,0:T(8,128)(2,1)}, u32[]{:S(2)}, u32[]{:S(2)}) collective-permute-start(bf16[128,1024]{1,0:T(8,128)(2,1)} %constant_dynamic-slice_fusion.9), channel_id=1, source_target_pairs={{0,2},{1,3},{2,0},{3,1},{4,6},{5,7},{6,4},{7,5},{8,10},{9,11},{10,... | collective-permute-start | bytes 786440 | tf_op jit(solution)/shard_map/ppermute | solution.py:110
  15.1 8.2 %copy-start.8 = (s32[128,8]{0,1:T(8,128)S(1)}, s32[128,8]{0,1:T(8,128)}, u32[]{:S(2)}) copy-start(s32[128,8]{0,1:T(8,128)} %param.27) | copy-start | bytes 12292
  16.1 7.5 %copy-start.10 = (s32[1,512]{1,0:T(1,128)S(1)}, s32[1,512]{1,0:T(1,128)}, u32[]{:S(2)}) copy-start(s32[1,512]{1,0:T(1,128)} %param.26) | copy-start | bytes 6148
  16.1 7.6 %copy-start.11 = (bf16[1024]{0:T(1024)(128)(2,1)S(1)}, bf16[1024]{0:T(1024)(128)(2,1)}, u32[]{:S(2)}) copy-start(bf16[1024]{0:T(1024)(128)(2,1)} %param.20) | copy-start | bytes 6148
  17.9 9.9 %collective-permute-start.2 = (bf16[128,2,256]{0,2,1:T(8,128)(2,1)S(1)}, bf16[128,2,256]{0,2,1:T(8,128)(2,1)S(1)}, u32[]{:S(2)}, u32[]{:S(2)}) collective-permute-start(bf16[128,2,256]{0,2,1:T(8,128)(2,1)S(1)} %get-tuple-element.26), channel_id=1, source_target_pairs={{0,3},{1,0},{2,1},{3,2},{4,7},{5,4},{6,5},{7,6},{8,11},{9,8},{10,9... | collective-permute-start | bytes 393224 | tf_op jit(solution)/shard_map/ppermute | solution.py:110
  18.4 22.9 %collective-permute-start.1 = (bf16[128,2,256]{0,2,1:T(8,128)(2,1)S(1)}, bf16[128,2,256]{0,2,1:T(8,128)(2,1)S(1)}, u32[]{:S(2)}, u32[]{:S(2)}) collective-permute-start(bf16[128,2,256]{0,2,1:T(8,128)(2,1)S(1)} %get-tuple-element.27), channel_id=1, source_target_pairs={{0,2},{1,3},{2,0},{3,1},{4,6},{5,7},{6,4},{7,5},{8,10},{9,11},{10,... | collective-permute-start | bytes 393224 | tf_op jit(solution)/shard_map/ppermute | solution.py:110
  21.0 20.4 %collective-permute-start = (bf16[128,2,256]{0,2,1:T(8,128)(2,1)S(1)}, bf16[128,2,256]{0,2,1:T(8,128)(2,1)S(1)}, u32[]{:S(2)}, u32[]{:S(2)}) collective-permute-start(bf16[128,2,256]{0,2,1:T(8,128)(2,1)S(1)} %get-tuple-element.28), channel_id=1, source_target_pairs={{0,1},{1,2},{2,3},{3,0},{4,5},{5,6},{6,7},{7,4},{8,9},{9,10},{10,1... | collective-permute-start | bytes 393224 | tf_op jit(solution)/shard_map/ppermute | solution.py:110
  27.8 17.3 %collective-permute-start.4 = (bf16[128,1024]{1,0:T(8,128)(2,1)}, bf16[128,1024]{1,0:T(8,128)(2,1)S(1)}, u32[]{:S(2)}, u32[]{:S(2)}) collective-permute-start(bf16[128,1024]{1,0:T(8,128)(2,1)} %constant_dynamic-slice_fusion.9), channel_id=1, source_target_pairs={{0,1},{1,2},{2,3},{3,0},{4,5},{5,6},{6,7},{7,4},{8,9},{9,10},{10,1... | collective-permute-start | bytes 786440 | tf_op jit(solution)/shard_map/ppermute | solution.py:110
  46.1 8.4 %collective-permute-start.7 = (bf16[3,128,1024]{2,1,0:T(8,128)(2,1)S(1)}, bf16[3,128,1024]{2,1,0:T(8,128)(2,1)S(1)}, u32[]{:S(2)}, u32[]{:S(2)}) collective-permute-start(bf16[3,128,1024]{2,1,0:T(8,128)(2,1)S(1)} %pad_maximum_fusion), channel_id=1, source_target_pairs={{0,4},{4,0},{8,12},{12,8},{16,20},{20,16},{24,28},{28,24},{1,5},{5... | collective-permute-start | bytes 2359304 | tf_op jit(solution)/shard_map/ppermute | solution.py:136
  46.2 8.0 %copy-start.6 = (bf16[256,1024]{1,0:T(8,128)(2,1)S(1)}, bf16[256,1024]{1,0:T(8,128)(2,1)}, u32[]{:S(2)}) copy-start(bf16[256,1024]{1,0:T(8,128)(2,1)} %param.19) | copy-start | bytes 1572868
  49.0 7.8 %collective-permute-start.9 = (bf16[128,256]{0,1:T(8,128)(2,1)S(1)}, bf16[128,256]{0,1:T(8,128)(2,1)S(1)}, u32[]{:S(2)}, u32[]{:S(2)}) collective-permute-start(bf16[128,256]{0,1:T(8,128)(2,1)S(1)} %bitcast.271), channel_id=1, source_target_pairs={{0,1},{1,2},{2,3},{3,0},{4,5},{5,6},{6,7},{7,4},{8,9},{9,10},{10,1... | collective-permute-start | bytes 196616 | tf_op jit(solution)/shard_map/ppermute | solution.py:110
  50.8 5.7 %collective-permute-start.3 = (bf16[128,256]{0,1:T(8,128)(2,1)S(1)}, bf16[128,256]{0,1:T(8,128)(2,1)S(1)}, u32[]{:S(2)}, u32[]{:S(2)}) collective-permute-start(bf16[128,256]{0,1:T(8,128)(2,1)S(1)} %bitcast.272), channel_id=1, source_target_pairs={{0,3},{1,0},{2,1},{3,2},{4,7},{5,4},{6,5},{7,6},{8,11},{9,8},{10,9... | collective-permute-start | bytes 196616 | tf_op jit(solution)/shard_map/ppermute | solution.py:110
  52.9 6.2 %collective-permute-start.8 = (bf16[128,256]{0,1:T(8,128)(2,1)S(1)}, bf16[128,256]{0,1:T(8,128)(2,1)S(1)}, u32[]{:S(2)}, u32[]{:S(2)}) collective-permute-start(bf16[128,256]{0,1:T(8,128)(2,1)S(1)} %bitcast.270), channel_id=1, source_target_pairs={{0,2},{1,3},{2,0},{3,1},{4,6},{5,7},{6,4},{7,5},{8,10},{9,11},{10,... | collective-permute-start | bytes 196616 | tf_op jit(solution)/shard_map/ppermute | solution.py:110
  56.8 2.8 %copy-start.7 = (bf16[1024,32]{0,1:T(8,128)(2,1)S(1)}, bf16[1024,32]{0,1:T(8,128)(2,1)}, u32[]{:S(2)}) copy-start(bf16[1024,32]{0,1:T(8,128)(2,1)} %param.21) | copy-start | bytes 196612
  59.5 11.6 %copy-start.3 = (f32[128,1024]{1,0:T(8,128)}, f32[128,1024]{1,0:T(8,128)S(1)}, u32[]{:S(2)}) copy-start(f32[128,1024]{1,0:T(8,128)S(1)} %get-tuple-element.56) | copy-start | bytes 1572868
  60.4 21.2 %collective-permute-start.10 = (bf16[128,1152]{1,0:T(8,128)(2,1)S(1)}, bf16[128,1152]{1,0:T(8,128)(2,1)}, u32[]{:S(2)}, u32[]{:S(2)}) collective-permute-start(bf16[128,1152]{1,0:T(8,128)(2,1)S(1)} %concatenate.47), channel_id=1, source_target_pairs={{0,1},{1,2},{2,3},{3,0},{4,5},{5,6},{6,7},{7,4},{8,9},{9,10},{10,1... | collective-permute-start | bytes 884744 | tf_op jit(solution)/shard_map/ppermute | solution.py:110
  60.4 23.1 %collective-permute-start.11 = (bf16[128,1152]{1,0:T(8,128)(2,1)S(1)}, bf16[128,1152]{1,0:T(8,128)(2,1)}, u32[]{:S(2)}, u32[]{:S(2)}) collective-permute-start(bf16[128,1152]{1,0:T(8,128)(2,1)S(1)} %concatenate.47), channel_id=1, source_target_pairs={{0,2},{1,3},{2,0},{3,1},{4,6},{5,7},{6,4},{7,5},{8,10},{9,11},{10,... | collective-permute-start | bytes 884744 | tf_op jit(solution)/shard_map/ppermute | solution.py:110
  62.7 21.8 %collective-permute-start.12 = (bf16[128,1152]{1,0:T(8,128)(2,1)S(1)}, bf16[128,1152]{1,0:T(8,128)(2,1)}, u32[]{:S(2)}, u32[]{:S(2)}) collective-permute-start(bf16[128,1152]{1,0:T(8,128)(2,1)S(1)} %concatenate.47), channel_id=1, source_target_pairs={{0,3},{1,0},{2,1},{3,2},{4,7},{5,4},{6,5},{7,6},{8,11},{9,8},{10,9... | collective-permute-start | bytes 884744 | tf_op jit(solution)/shard_map/ppermute | solution.py:110
  86.1 6.6 %slice-start = ((s8[8388608]{0:T(1024)(128)(4,1)}), s8[4194304]{0:T(1024)(128)(4,1)S(1)}, s32[]{:S(2)}) async-start(s8[8388608]{0:T(1024)(128)(4,1)} %bitcast.254), calls=%async_computation | async-start | bytes 8388608
  87.1 5.6 %slice-start.1 = ((s8[8388608]{0:T(1024)(128)(4,1)}), s8[4194304]{0:T(1024)(128)(4,1)S(1)}, s32[]{:S(2)}) async-start(s8[8388608]{0:T(1024)(128)(4,1)} %bitcast.254), calls=%async_computation.1 | async-start | bytes 8388608
  87.1 7.7 %slice-start.2 = ((s8[8388608]{0:T(1024)(128)(4,1)}), s8[4194304]{0:T(1024)(128)(4,1)S(1)}, s32[]{:S(2)}) async-start(s8[8388608]{0:T(1024)(128)(4,1)} %bitcast.256), calls=%async_computation.2 | async-start | bytes 8388608
  92.7 2.4 %slice-start.3 = ((s8[8388608]{0:T(1024)(128)(4,1)}), s8[4194304]{0:T(1024)(128)(4,1)S(1)}, s32[]{:S(2)}) async-start(s8[8388608]{0:T(1024)(128)(4,1)} %bitcast.256), calls=%async_computation.3 | async-start | bytes 8388608
  95.1 1.2 copy-start.12
  96.4 1.4 %copy-start.13 = (bf16[3,8,64,512]{3,2,0,1:T(8,128)(2,1)S(1)}, bf16[3,8,64,512]{3,2,0,1:T(8,128)(2,1)}, u32[]{:S(2)}) copy-start(bf16[3,8,64,512]{3,2,0,1:T(8,128)(2,1)} %copy-done.12) | copy-start | bytes 4718596
  101.4 25.9 %copy-start.4 = (f32[128,1024]{1,0:T(8,128)S(1)}, f32[128,1024]{1,0:T(8,128)}, u32[]{:S(2)}) copy-start(f32[128,1024]{1,0:T(8,128)} %copy-done.3) | copy-start | bytes 1572868
  101.4 25.9 %copy-start.5 = (f32[128,1024]{1,0:T(8,128)S(1)}, f32[128,1024]{1,0:T(8,128)}, u32[]{:S(2)}) copy-start(f32[128,1024]{1,0:T(8,128)} %convolution_bitcast_fusion.2) | copy-start | bytes 1572868
  101.4 27.0 %copy-start.1 = (bf16[1024,1024]{1,0:T(8,128)(2,1)S(1)}, bf16[1024,1024]{1,0:T(8,128)(2,1)}, u32[]{:S(2)}) copy-start(bf16[1024,1024]{1,0:T(8,128)(2,1)} %param.16) | copy-start | bytes 6291460
  101.9 10.0 %collective-permute-start.18 = (bf16[128,512]{1,0:T(8,128)(2,1)S(1)}, bf16[128,512]{1,0:T(8,128)(2,1)S(1)}, u32[]{:S(2)}, u32[]{:S(2)}) collective-permute-start(bf16[128,512]{1,0:T(8,128)(2,1)S(1)} %get-tuple-element.33), channel_id=1, source_target_pairs={{0,1},{1,2},{2,3},{3,0},{4,5},{5,6},{6,7},{7,4},{8,9},{9,10},{10,1... | collective-permute-start | bytes 393224 | tf_op jit(solution)/shard_map/ppermute | solution.py:110
  106.9 13.7 %collective-permute-start.17 = (bf16[128,512]{1,0:T(8,128)(2,1)S(1)}, bf16[128,512]{1,0:T(8,128)(2,1)S(1)}, u32[]{:S(2)}, u32[]{:S(2)}) collective-permute-start(bf16[128,512]{1,0:T(8,128)(2,1)S(1)} %get-tuple-element.34), channel_id=1, source_target_pairs={{0,2},{1,3},{2,0},{3,1},{4,6},{5,7},{6,4},{7,5},{8,10},{9,11},{10,... | collective-permute-start | bytes 393224 | tf_op jit(solution)/shard_map/ppermute | solution.py:110
  107.9 12.7 %collective-permute-start.16 = (bf16[128,512]{1,0:T(8,128)(2,1)S(1)}, bf16[128,512]{1,0:T(8,128)(2,1)S(1)}, u32[]{:S(2)}, u32[]{:S(2)}) collective-permute-start(bf16[128,512]{1,0:T(8,128)(2,1)S(1)} %get-tuple-element.32), channel_id=1, source_target_pairs={{0,3},{1,0},{2,1},{3,2},{4,7},{5,4},{6,5},{7,6},{8,11},{9,8},{10,9... | collective-permute-start | bytes 393224 | tf_op jit(solution)/shard_map/ppermute | solution.py:110
  109.4 11.3 %collective-permute-start.15 = (bf16[128,512]{1,0:T(8,128)(2,1)S(1)}, bf16[128,512]{1,0:T(8,128)(2,1)S(1)}, u32[]{:S(2)}, u32[]{:S(2)}) collective-permute-start(bf16[128,512]{1,0:T(8,128)(2,1)S(1)} %get-tuple-element.31), channel_id=1, source_target_pairs={{0,1},{1,2},{2,3},{3,0},{4,5},{5,6},{6,7},{7,4},{8,9},{9,10},{10,1... | collective-permute-start | bytes 393224 | tf_op jit(solution)/shard_map/ppermute | solution.py:110
  110.0 17.3 %collective-permute-start.14 = (bf16[128,512]{1,0:T(8,128)(2,1)S(1)}, bf16[128,512]{1,0:T(8,128)(2,1)S(1)}, u32[]{:S(2)}, u32[]{:S(2)}) collective-permute-start(bf16[128,512]{1,0:T(8,128)(2,1)S(1)} %get-tuple-element.30), channel_id=1, source_target_pairs={{0,2},{1,3},{2,0},{3,1},{4,6},{5,7},{6,4},{7,5},{8,10},{9,11},{10,... | collective-permute-start | bytes 393224 | tf_op jit(solution)/shard_map/ppermute | solution.py:110
  112.0 15.3 %collective-permute-start.13 = (bf16[128,512]{1,0:T(8,128)(2,1)S(1)}, bf16[128,512]{1,0:T(8,128)(2,1)S(1)}, u32[]{:S(2)}, u32[]{:S(2)}) collective-permute-start(bf16[128,512]{1,0:T(8,128)(2,1)S(1)} %get-tuple-element.29), channel_id=1, source_target_pairs={{0,3},{1,0},{2,1},{3,2},{4,7},{5,4},{6,5},{7,6},{8,11},{9,8},{10,9... | collective-permute-start | bytes 393224 | tf_op jit(solution)/shard_map/ppermute | solution.py:110

commit v13 on v11

--- a/solution.py
+++ b/solution.py
@@ -173,29 +173,43 @@
     keyval = jnp.concatenate([keys, values], axis=-1)
     owners = lax.axis_size("exp")
     share = groups // owners
-    both = jnp.concatenate([query, keyval], axis=-1)
-    parts = [lax.dynamic_slice_in_dim(both, here * share, share, 1)]
+    plen = seg.shape[0]
+    reach = min(owners - 1, -(-(plen // 2 - 1) // rows))
+    remote = gather_w_out(w_out)
+    parts = [lax.dynamic_slice_in_dim(keyval, here * share, share, 1)]
     for step in range(1, owners):
-        send = lax.dynamic_slice_in_dim(both, (here + step) % owners * share, share, 1)
+        send = lax.dynamic_slice_in_dim(keyval, (here + step) % owners * share, share, 1)
         parts.append(shifted(send, step))
-    both = jnp.concatenate(parts)
-    query_heads, keyval_heads = both[..., : 2 * HD], both[..., 2 * HD :]
-    plen = keyval_heads.shape[0]
-    where_at = step_rows(jnp.arange(plen, dtype=jnp.int32), rows)
+    cache_rows = jnp.concatenate(parts)
     placing = step_rows(page_order[0], rows)[None, :] == jnp.arange(plen, dtype=jnp.int32)[:, None]
     kv_cache = jnp.einsum(
-        "rs,skd->rkd", placing.astype(jnp.bfloat16), keyval_heads, preferred_element_type=jnp.float32
+        "rs,skd->rkd", placing.astype(jnp.bfloat16), cache_rows, preferred_element_type=jnp.float32
     ).astype(jnp.bfloat16)
-    seg_rows = step_rows(seg, rows)
-    heads_out = attend(query_heads, keyval_heads, seg_rows, seg_rows, where_at, where_at)
-    blocks = heads_out.reshape(owners, rows, -1)
-    remote = gather_w_out(w_out)
-    attention = jnp.dot(blocks[0], w_out, preferred_element_type=jnp.float32)
+    index = jnp.arange(rows, dtype=jnp.int32)
+    windows, key_at, key_seg = [keyval], [here * rows + index], [lax.dynamic_slice_in_dim(seg, here * rows, rows)]
+    for back in range(1, reach + 1):
+        pairs = [(j, j + back) for j in range(owners - back)]
+        windows.append(lax.ppermute(keyval, "exp", pairs))
+        start = (here - back) * rows
+        key_at.append(jnp.where(here >= back, start + index, 4 * plen))
+        key_seg.append(lax.dynamic_slice_in_dim(seg, jnp.maximum(start, 0), rows))
+    heads_out = attend(
+        query,
+        jnp.concatenate(windows),
+        key_seg[0],
+        jnp.concatenate(key_seg),
+        key_at[0],
+        jnp.concatenate(key_at),
+    )
+    cols = heads_out.shape[1] // owners
+    attention = jnp.dot(
+        lax.dynamic_slice_in_dim(heads_out, here * cols, cols, 1),
+        w_out,
+        preferred_element_type=jnp.float32,
+    )
     for step in range(1, owners):
-        got = shifted(blocks[step], -step)
-        attention = attention + jnp.dot(
-            got, remote[owners - step - 1], preferred_element_type=jnp.float32
-        )
+        block = lax.dynamic_slice_in_dim(heads_out, (here - step) % owners * cols, cols, 1)
+        attention = attention + jnp.dot(block, remote[step - 1], preferred_element_type=jnp.float32)
     resid = tokens.astype(jnp.float32) + attention
     normed2 = rms_scale(resid, norm_moe)
     packed = routing(normed2, expert_ids, w_router)

time: 128 us -> 130 us (1.016)
  waiting for transfers between devices: 22.2 us -> 13.7 us
  starting transfers between devices: 41.7 us -> 48.7 us
  matrix products: 45.5 us -> 41.8 us
  local copies, waits for them, and re-layouts: 8.24 us -> 11.9 us
  other arithmetic: 8.27 us -> 11.2 us
    ppermute x18 -> x15, waiting for transfers between devices: 22.2 us -> 11.9 us  [shifted(): lax.ppermute(x, 'exp', [(j, (j + step) % count) for j in range(count)])]
    ppermute x0 -> x2, starting transfers between devices: none -> 6.71 us  [shards(): windows.append(lax.ppermute(keyval, 'exp', pairs))]
    sub x1 -> x0, matrix products: 3.59 us -> none  [attend(): expo = jnp.exp(score - top)]
    dot_general x1, matrix products: 2.73 us -> 0.43 us  [attend(): jnp.einsum('kgqt,tkd->qkgd', probs, values, preferred_element_type=jnp.fl...]
    ppermute x0 -> x2, waiting for transfers between devices: none -> 1.78 us  [shards(): windows.append(lax.ppermute(keyval, 'exp', pairs))]
    dot_general x5 -> x6, matrix products: 1.45 us -> 3 us  [the longest x1 1.24 us: shards(): jnp.einsum('rs,skd->rkd', placing.astype(jnp.bfloat16), cache_rows, prefe...]
    dynamic_slice x1 -> x2, local copies, waits for them, and re-layouts: 0.05 us -> 1.57 us  [the longest x1 0.88 us: shards(): key_seg.append(lax.dynamic_slice_in_dim(seg, jnp.maximum(start, 0), rows))]
    another operation x4, other arithmetic: 0.46 us -> 1.93 us
  transfers between devices with their start and end apart: 19 -> 18, of which waited for: 7 -> 5; matrix products, arithmetic and copies ran while one was open for 32% -> 33% of each run, Pallas kernels for 0% -> 0%
where the time goes in v13:
time: 130 us; the launch traced here: 129 us
  starting transfers between devices  48.7 us (37%)
  matrix products  41.8 us (32%)
  waiting for transfers between devices  13.7 us (11%)
  local copies, waits for them, and re-layouts  11.9 us (9%)
  other arithmetic  11.2 us (9%)
  between operations  1.3 us (1%)
    ppermute x15, starting transfers between devices, shifted(): lax.ppermute(x, 'exp', [(j, (j + step) % count) for j in range(count)])  41.9 us
    dot_general x3, matrix products, expert_mix(): jnp.einsum('becf,efd->becd', hidden, down, preferred_element_type=jnp.flo...  12.2 us
    ppermute x15, waiting for transfers between devices, shifted(): lax.ppermute(x, 'exp', [(j, (j + step) % count) for j in range(count)])  11.9 us
    dot_general x2, matrix products, expert_mix(): jnp.einsum('becd,edf->becf', received, w_gate, preferred_element_type=jnp...  8 us
    ppermute x2, starting transfers between devices, shards(): windows.append(lax.ppermute(keyval, 'exp', pairs))  6.71 us
    dot_general x1, matrix products, expert_mix(): jnp.einsum('becd,edf->becf', received, w_up, preferred_element_type=jnp.f...  5.54 us
    unnamed x49, local copies, waits for them, and re-layouts  4.61 us
    dot_general x3, matrix products, expert_mix(): jnp.einsum('becr,becd->brd', low, result, preferred_element_type=jnp.floa...  3.46 us
  transfers between devices with their start and end apart: 18, of which 5 were waited for; matrix products, arithmetic and copies ran while one was open for 33% of the time, Pallas kernels for 0%

profile of v13, /device:TPU:0, one launch (start us, length us, event | category | flops | bytes accessed | tf_op | source)
XLA Modules:
  0.0 128.7 jit_solution(3520832184773255413)
XLA Ops:
  0.7 1.8 %constant_dynamic-slice_fusion.13 = bf16[128,1024]{1,0:T(8,128)(2,1)} fusion(bf16[256,1024]{1,0:T(8,128)(2,1)} %param.19, s32[]{:T(128)S(6)} %select_n.173), kind=kLoop, calls=%fused_computation.201 | loop fusion | bytes 524292 | tf_op jit(solution)/shard_map/dynamic_slice | solution.py:132
  2.5 5.1 %collective-permute-start.4 = (bf16[128,1024]{1,0:T(8,128)(2,1)}, bf16[128,1024]{1,0:T(8,128)(2,1)S(1)}, u32[]{:S(2)}, u32[]{:S(2)}) collective-permute-start(bf16[128,1024]{1,0:T(8,128)(2,1)} %constant_dynamic-slice_fusion.13), channel_id=1, source_target_pairs={{0,3},{1,0},{2,1},{3,2},{4,7},{5,4},{6,5},{7,6},{8,11},{9,8},{10,9... | collective-permute-start | bytes 786440 | tf_op jit(solution)/shard_map/ppermute | solution.py:108
  7.6 1.0 collective-permute-start.2
  8.6 0.5 multiply_power_fusion
  9.1 0.7 convert_element_type.121
  9.8 1.1 fusion.85
  10.9 1.7 %convolution_convert_fusion.4 = bf16[128,512]{1,0:T(8,128)(2,1)S(1)} fusion(bf16[1024,512]{1,0:T(8,128)(2,1)} %param.18, bf16[128,1024]{1,0:T(8,128)(2,1)} %param.14, f32[1024]{0:T(1024)S(1)} %convert_element_type.121, f32[128]{0:T(128)S(1)} %add_rsqrt_fusion.1), kind=kOutput, calls=%fused_computation.69 | convolution fusion | flops 134807552 | bytes 1446400 | tf_op jit(solution)/shard_map/dot_general | solution.py:169
  12.7 1.9 %fusion.193 = f32[128,512]{0,1:T(8,128)S(1)} fusion(bf16[1024,512]{1,0:T(8,128)(2,1)} %param.17, bf16[128,1024]{1,0:T(8,128)(2,1)} %param.14, f32[1024]{0:T(1024)S(1)} %convert_element_type.121, f32[128]{0:T(128)S(1)} %add_rsqrt_fusion.1), kind=kOutput, calls=%fused_computation.246 | convolution fusion | flops 134742016 | bytes 1577472 | tf_op jit(solution)/shard_map/dot_general | solution.py:166
  14.8 0.3 reduce-window.9
  15.5 1.4 %multiply_cosine_fusion = (f32[128,32]{0,1:T(8,128)S(1)}, f32[128,32]{0,1:T(8,128)}) fusion(f32[32]{0:T(128)} %multiply_power_fusion, f32[128]{0:T(128)S(1)} %dynamic-slice_convert_fusion), kind=kLoop, calls=%fused_computation.178 | loop fusion | flops 4096 | bytes 33408 | tf_op jit(solution)/shard_map/cos | solution.py:27
  16.9 0.8 subtract_convert_fusion.1
  17.7 0.6 copy-done.7
  18.3 0.7 constant_dynamic-slice_fusion.3
  19.0 2.8 %collective-permute-start.17 = (bf16[128,2,128]{0,2,1:T(8,128)(2,1)}, bf16[128,2,128]{0,2,1:T(8,128)(2,1)}, u32[]{:S(2)}, u32[]{:S(2)}) collective-permute-start(bf16[128,2,128]{0,2,1:T(8,128)(2,1)} %get-tuple-element.34), channel_id=1, source_target_pairs={{0,3},{1,0},{2,1},{3,2},{4,7},{5,4},{6,5},{7,6},{8,11},{9,8},{10,9... | collective-permute-start | bytes 196616 | tf_op jit(solution)/shard_map/ppermute | solution.py:108
  21.8 1.1 collective-permute-start.16
  23.0 0.6 iota_add_fusion
  23.5 1.6 %fusion.190 = f32[128,1024]{0,1:T(8,128)S(1)} fusion(bf16[1024,1024]{1,0:T(8,128)(2,1)S(1)} %copy-done, bf16[128,1024]{1,0:T(8,128)(2,1)S(1)} %copy-done.2, f32[1024]{0:T(1024)} %copy-done.12, f32[128]{0:T(128)} %copy-done.16), kind=kOutput, calls=%fused_computation.245 | convolution fusion | flops 268959744 | bytes 2888192 | tf_op jit(solution)/shard_map/dot_general | solution.py:162
  25.2 0.8 subtract_convert_fusion
  26.1 0.7 fusion.146
  26.8 0.9 fusion.170
  27.7 0.7 pad_add_fusion
  28.3 0.8 compare_and_fusion
  29.2 0.7 fusion.172
  29.9 5.1 %collective-permute-start.15 = (bf16[128,2,128]{0,2,1:T(8,128)(2,1)}, bf16[128,2,128]{0,2,1:T(8,128)(2,1)S(1)}, u32[]{:S(2)}, u32[]{:S(2)}) collective-permute-start(bf16[128,2,128]{0,2,1:T(8,128)(2,1)} %get-tuple-element.33), channel_id=1, source_target_pairs={{0,1},{1,2},{2,3},{3,0},{4,5},{5,6},{6,7},{7,4},{8,9},{9,10},{10,1... | collective-permute-start | bytes 196616 | tf_op jit(solution)/shard_map/ppermute | solution.py:108
  35.0 0.7 convert_element_type.128
  35.7 0.7 copy.100
  36.4 1.3 %collective-permute-start.1 = (bf16[128,8,128]{0,2,1:T(8,128)(2,1)S(1)}, bf16[128,8,128]{0,2,1:T(8,128)(2,1)S(1)}, u32[]{:S(2)}, u32[]{:S(2)}) collective-permute-start(bf16[128,8,128]{0,2,1:T(8,128)(2,1)S(1)} %pad_maximum_fusion.3), channel_id=1, source_target_pairs={{0,2},{1,3},{4,6},{5,7},{8,10},{9,11},{12,14},{13,15},{16,18},{17,... | collective-permute-start | bytes 786440 | tf_op jit(solution)/shard_map/ppermute | solution.py:192
  37.8 5.4 %collective-permute-start = (bf16[128,8,128]{0,2,1:T(8,128)(2,1)S(1)}, bf16[128,8,128]{0,2,1:T(8,128)(2,1)S(1)}, u32[]{:S(2)}, u32[]{:S(2)}) collective-permute-start(bf16[128,8,128]{0,2,1:T(8,128)(2,1)S(1)} %pad_maximum_fusion.3), channel_id=1, source_target_pairs={{0,1},{1,2},{2,3},{4,5},{5,6},{6,7},{8,9},{9,10},{10,11},{12,13},{... | collective-permute-start | bytes 786440 | tf_op jit(solution)/shard_map/ppermute | solution.py:192
  43.3 1.2 convolution_convert_fusion.3
  44.5 1.0 copy.114
  45.7 1.8 %collective-permute-done = bf16[128,8,128]{0,2,1:T(8,128)(2,1)S(1)} collective-permute-done((bf16[128,8,128]{0,2,1:T(8,128)(2,1)S(1)}, bf16[128,8,128]{0,2,1:T(8,128)(2,1)S(1)}, u32[]{:S(2)}, u32[]{:S(2)}) %collective-permute-start) | collective-permute-done | bytes 262176 | tf_op jit(solution)/shard_map/ppermute | solution.py:192
  47.6 0.6 fusion.105
  48.2 0.9 fusion.195
  49.1 0.4 fusion.71
  49.6 0.6 copy-done.6
  51.2 0.4 multiply_reduce_fusion
  52.5 7.2 %collective-permute-start.6 = (bf16[128,1152]{1,0:T(8,128)(2,1)S(1)}, bf16[128,1152]{1,0:T(8,128)(2,1)}, u32[]{:S(2)}, u32[]{:S(2)}) collective-permute-start(bf16[128,1152]{1,0:T(8,128)(2,1)S(1)} %concatenate.57), channel_id=1, source_target_pairs={{0,1},{1,2},{2,3},{3,0},{4,5},{5,6},{6,7},{7,4},{8,9},{9,10},{10,1... | collective-permute-start | bytes 884744 | tf_op jit(solution)/shard_map/ppermute | solution.py:108
  59.7 2.0 %collective-permute-start.7 = (bf16[128,1152]{1,0:T(8,128)(2,1)S(1)}, bf16[128,1152]{1,0:T(8,128)(2,1)}, u32[]{:S(2)}, u32[]{:S(2)}) collective-permute-start(bf16[128,1152]{1,0:T(8,128)(2,1)S(1)} %concatenate.57), channel_id=1, source_target_pairs={{0,2},{1,3},{2,0},{3,1},{4,6},{5,7},{6,4},{7,5},{8,10},{9,11},{10,... | collective-permute-start | bytes 884744 | tf_op jit(solution)/shard_map/ppermute | solution.py:108
  61.7 2.8 %collective-permute-start.8 = (bf16[128,1152]{1,0:T(8,128)(2,1)S(1)}, bf16[128,1152]{1,0:T(8,128)(2,1)}, u32[]{:S(2)}, u32[]{:S(2)}) collective-permute-start(bf16[128,1152]{1,0:T(8,128)(2,1)S(1)} %concatenate.57), channel_id=1, source_target_pairs={{0,3},{1,0},{2,1},{3,2},{4,7},{5,4},{6,5},{7,6},{8,11},{9,8},{10,9... | collective-permute-start | bytes 884744 | tf_op jit(solution)/shard_map/ppermute | solution.py:108
  64.9 0.4 convolution_convert_fusion.2
  65.4 5.9 %convolution_bitcast_fusion.1 = f32[1,8,64,512]{3,2,1,0:T(8,128)} fusion(bf16[8,64,1024]{2,1,0:T(8,128)(2,1)S(1)} %convolution_convert_fusion.2, bf16[8,1024,512]{2,1,0:T(8,128)(2,1)} %param.22), kind=kOutput, calls=%fused_computation.49 | convolution fusion | flops 536870912 | bytes 10485760 | tf_op jit(solution)/shard_map/becd,edf->becf/dot_general | solution.py:86
  71.3 9.1 %convolution_convert_fusion.1 = bf16[8,64,1024]{2,1,0:T(8,128)(2,1)S(1)} fusion(bf16[8,512,1024]{2,1,0:T(8,128)(2,1)} %param.24, bf16[8,64,1024]{2,1,0:T(8,128)(2,1)S(1)} %convolution_convert_fusion.2, bf16[8,1024,512]{2,1,0:T(8,128)(2,1)} %param.23, f32[1,8,64,512]{3,2,1,0:T(8,128)} %convolution_bitcast_fusion.1), kind=kOutput, calls=%fused_computation.37 | convolution fusion | flops 1075838976 | bytes 19922944 | tf_op jit(solution)/shard_map/becf,efd->becd/dot_general | solution.py:96
  80.6 1.2 convolution_bitcast_fusion.2
  81.8 1.0 constant_dynamic-update-slice_fusion.2
  82.9 1.0 constant_dynamic-update-slice_fusion.1
  83.9 1.0 constant_dynamic-update-slice_fusion
  85.4 1.0 convolution_convert_fusion
  86.4 5.5 %fusion.1 = f32[8,3,64,512]{3,2,1,0:T(8,128)S(1)} fusion(bf16[8,1024,512]{2,1,0:T(8,128)(2,1)} %param.23, bf16[3,8,64,1024]{3,2,1,0:T(8,128)(2,1)S(1)} %convolution_convert_fusion), kind=kOutput, calls=%fused_computation.1 | convolution fusion | flops 1610612736 | bytes 14680064 | tf_op jit(solution)/shard_map/becd,edf->becf/dot_general | solution.py:87
  92.0 2.1 %fusion.11 = bf16[3,8,64,512]{3,2,0,1:T(8,128)(2,1)S(1)} fusion(f32[8,3,64,512]{3,2,1,0:T(8,128)S(1)} %fusion.1, bf16[8,1024,512]{2,1,0:T(8,128)(2,1)S(1)} %bitcast.237, bf16[3,8,64,1024]{3,2,1,0:T(8,128)(2,1)S(1)} %convolution_convert_fusion), kind=kOutput, calls=%fused_computation.12 | convolution fusion | flops 1615331328 | bytes 16252928 | tf_op jit(solution)/shard_map/becd,edf->becf/dot_general | solution.py:86
  94.1 0.3 slice-done.3
  94.4 1.0 fusion.28
  95.4 2.1 %fusion.31 = bf16[3,8,64,512]{3,2,0,1:T(8,128)(2,1)} fusion(bf16[3,8,64,512]{3,2,0,1:T(8,128)(2,1)S(1)} %fusion.11, bf16[8,512,1024]{2,1,0:T(8,128)(2,1)S(1)} %bitcast.239), kind=kOutput, calls=%fused_computation.36 | convolution fusion | flops 806092800 | bytes 7340032 | tf_op jit(solution)/shard_map/becf,efd->becd/dot_general | solution.py:96
  97.7 0.4 fusion.50
  98.1 1.9 %fusion.65 = bf16[3,128,512]{2,1,0:T(8,128)(2,1)S(1)} fusion(f32[3,128,512]{2,1,0:T(8,128)S(1)} %fusion.50, bf16[3,8,64,512]{3,2,0,1:T(8,128)(2,1)} %copy-done.18, s32[3,8,128]{2,1,0:T(8,128)S(1)} %convolution_convert_fusion.5, pred[3,8,128]{2,1,0:T(8,128)(4,1)S(1)} %compare_bitcast_fusion.1, bf16[3,8,128]{2,1,0:T(8,128)(2,1)S(1)} %bitcast.260), kind=kOutput, calls=%fused_computation.58 | convolution fusion | flops 202309632 | bytes 2774016 | tf_op jit(solution)/shard_map/becr,becd->brd/dot_general | solution.py:99
  100.0 4.8 %collective-permute-start.14 = (bf16[128,512]{1,0:T(8,128)(2,1)S(1)}, bf16[128,512]{1,0:T(8,128)(2,1)S(1)}, u32[]{:S(2)}, u32[]{:S(2)}) collective-permute-start(bf16[128,512]{1,0:T(8,128)(2,1)S(1)} %get-tuple-element.25), channel_id=1, source_target_pairs={{0,1},{1,2},{2,3},{3,0},{4,5},{5,6},{6,7},{7,4},{8,9},{9,10},{10,1... | collective-permute-start | bytes 393224 | tf_op jit(solution)/shard_map/ppermute | solution.py:108
  104.8 3.5 %collective-permute-start.13 = (bf16[128,512]{1,0:T(8,128)(2,1)S(1)}, bf16[128,512]{1,0:T(8,128)(2,1)S(1)}, u32[]{:S(2)}, u32[]{:S(2)}) collective-permute-start(bf16[128,512]{1,0:T(8,128)(2,1)S(1)} %get-tuple-element.26), channel_id=1, source_target_pairs={{0,2},{1,3},{2,0},{3,1},{4,6},{5,7},{6,4},{7,5},{8,10},{9,11},{10,... | collective-permute-start | bytes 393224 | tf_op jit(solution)/shard_map/ppermute | solution.py:108
  108.3 0.4 fusion.44
  108.8 0.4 fusion.62
  109.2 2.1 %collective-permute-start.11 = (bf16[128,512]{1,0:T(8,128)(2,1)S(1)}, bf16[128,512]{1,0:T(8,128)(2,1)S(1)}, u32[]{:S(2)}, u32[]{:S(2)}) collective-permute-start(bf16[128,512]{1,0:T(8,128)(2,1)S(1)} %get-tuple-element.22), channel_id=1, source_target_pairs={{0,1},{1,2},{2,3},{3,0},{4,5},{5,6},{6,7},{7,4},{8,9},{9,10},{10,1... | collective-permute-start | bytes 393224 | tf_op jit(solution)/shard_map/ppermute | solution.py:108
  111.3 0.9 collective-permute-done.14
  112.2 4.3 %collective-permute-start.9 = (bf16[128,512]{1,0:T(8,128)(2,1)S(1)}, bf16[128,512]{1,0:T(8,128)(2,1)S(1)}, u32[]{:S(2)}, u32[]{:S(2)}) collective-permute-start(bf16[128,512]{1,0:T(8,128)(2,1)S(1)} %get-tuple-element.21), channel_id=1, source_target_pairs={{0,3},{1,0},{2,1},{3,2},{4,7},{5,4},{6,5},{7,6},{8,11},{9,8},{10,9... | collective-permute-start | bytes 393224 | tf_op jit(solution)/shard_map/ppermute | solution.py:108
  116.6 3.9 %collective-permute-done.13 = bf16[128,512]{1,0:T(8,128)(2,1)S(1)} collective-permute-done((bf16[128,512]{1,0:T(8,128)(2,1)S(1)}, bf16[128,512]{1,0:T(8,128)(2,1)S(1)}, u32[]{:S(2)}, u32[]{:S(2)}) %collective-permute-start.13) | collective-permute-done | bytes 131104 | tf_op jit(solution)/shard_map/ppermute | solution.py:108
  120.6 7.0 %collective-permute-done.10 = bf16[128,512]{1,0:T(8,128)(2,1)S(1)} collective-permute-done((bf16[128,512]{1,0:T(8,128)(2,1)S(1)}, bf16[128,512]{1,0:T(8,128)(2,1)S(1)}, u32[]{:S(2)}, u32[]{:S(2)}) %collective-permute-start.10) | collective-permute-done | bytes 131104 | tf_op jit(solution)/shard_map/ppermute | solution.py:108
  127.6 1.1 fusion.98
  (113 shorter events, 4.5 us)
Async XLA Ops:
  0.6 22.9 %copy-start = (bf16[1024,1024]{1,0:T(8,128)(2,1)S(1)}, bf16[1024,1024]{1,0:T(8,128)(2,1)}, u32[]{:S(2)}) copy-start(bf16[1024,1024]{1,0:T(8,128)(2,1)} %param.16) | copy-start | bytes 6291460
  0.6 22.9 %copy-start.2 = (bf16[128,1024]{1,0:T(8,128)(2,1)S(1)}, bf16[128,1024]{1,0:T(8,128)(2,1)}, u32[]{:S(2)}) copy-start(bf16[128,1024]{1,0:T(8,128)(2,1)} %param.14) | copy-start | bytes 786436
  0.7 14.0 %copy-start.15 = (s32[1,512]{1,0:T(1,128)S(1)}, s32[1,512]{1,0:T(1,128)}, u32[]{:S(2)}) copy-start(s32[1,512]{1,0:T(1,128)} %param.25) | copy-start | bytes 6148
  2.5 43.0 %collective-permute-start.4 = (bf16[128,1024]{1,0:T(8,128)(2,1)}, bf16[128,1024]{1,0:T(8,128)(2,1)S(1)}, u32[]{:S(2)}, u32[]{:S(2)}) collective-permute-start(bf16[128,1024]{1,0:T(8,128)(2,1)} %constant_dynamic-slice_fusion.13), channel_id=1, source_target_pairs={{0,3},{1,0},{2,1},{3,2},{4,7},{5,4},{6,5},{7,6},{8,11},{9,8},{10,9... | collective-permute-start | bytes 786440 | tf_op jit(solution)/shard_map/ppermute | solution.py:108
  7.6 37.9 %collective-permute-start.3 = (bf16[128,1024]{1,0:T(8,128)(2,1)}, bf16[128,1024]{1,0:T(8,128)(2,1)S(1)}, u32[]{:S(2)}, u32[]{:S(2)}) collective-permute-start(bf16[128,1024]{1,0:T(8,128)(2,1)} %constant_dynamic-slice_fusion.13), channel_id=1, source_target_pairs={{0,2},{1,3},{2,0},{3,1},{4,6},{5,7},{6,4},{7,5},{8,10},{9,11},{10,... | collective-permute-start | bytes 786440 | tf_op jit(solution)/shard_map/ppermute | solution.py:108
  7.6 37.9 %collective-permute-start.2 = (bf16[128,1024]{1,0:T(8,128)(2,1)}, bf16[128,1024]{1,0:T(8,128)(2,1)S(1)}, u32[]{:S(2)}, u32[]{:S(2)}) collective-permute-start(bf16[128,1024]{1,0:T(8,128)(2,1)} %constant_dynamic-slice_fusion.13), channel_id=1, source_target_pairs={{0,1},{1,2},{2,3},{3,0},{4,5},{5,6},{6,7},{7,4},{8,9},{9,10},{10,1... | collective-permute-start | bytes 786440 | tf_op jit(solution)/shard_map/ppermute | solution.py:108
  9.8 5.6 %copy-start.12 = (f32[1024]{0:T(1024)}, f32[1024]{0:T(1024)S(1)}, u32[]{:S(2)}) copy-start(f32[1024]{0:T(1024)S(1)} %convert_element_type.121) | copy-start | bytes 12292
  10.9 3.7 %copy-start.16 = (f32[128]{0:T(128)}, f32[128]{0:T(128)S(1)}, u32[]{:S(2)}) copy-start(f32[128]{0:T(128)S(1)} %add_rsqrt_fusion.1) | copy-start | bytes 1540
  17.7 0.6 copy-start.7
  17.7 0.6 copy-start.9
  19.0 10.9 %collective-permute-start.17 = (bf16[128,2,128]{0,2,1:T(8,128)(2,1)}, bf16[128,2,128]{0,2,1:T(8,128)(2,1)}, u32[]{:S(2)}, u32[]{:S(2)}) collective-permute-start(bf16[128,2,128]{0,2,1:T(8,128)(2,1)} %get-tuple-element.34), channel_id=1, source_target_pairs={{0,3},{1,0},{2,1},{3,2},{4,7},{5,4},{6,5},{7,6},{8,11},{9,8},{10,9... | collective-permute-start | bytes 196616 | tf_op jit(solution)/shard_map/ppermute | solution.py:108
  21.8 14.6 %collective-permute-start.16 = (bf16[128,2,128]{0,2,1:T(8,128)(2,1)}, bf16[128,2,128]{0,2,1:T(8,128)(2,1)}, u32[]{:S(2)}, u32[]{:S(2)}) collective-permute-start(bf16[128,2,128]{0,2,1:T(8,128)(2,1)} %get-tuple-element.32), channel_id=1, source_target_pairs={{0,2},{1,3},{2,0},{3,1},{4,6},{5,7},{6,4},{7,5},{8,10},{9,11},{10,... | collective-permute-start | bytes 196616 | tf_op jit(solution)/shard_map/ppermute | solution.py:108
  25.2 22.3 %copy-start.8 = (bf16[128,8,32]{0,2,1:T(8,128)(2,1)S(1)}, bf16[128,8,32]{0,2,1:T(8,128)(2,1)}, u32[]{:S(2)}) copy-start(bf16[128,8,32]{0,2,1:T(8,128)(2,1)} %copy-done.7) | copy-start | bytes 196612
  25.2 22.3 %copy-start.10 = (bf16[128,8,32]{0,2,1:T(8,128)(2,1)S(1)}, bf16[128,8,32]{0,2,1:T(8,128)(2,1)}, u32[]{:S(2)}) copy-start(bf16[128,8,32]{0,2,1:T(8,128)(2,1)} %copy-done.9) | copy-start | bytes 196612
  29.9 7.9 %collective-permute-start.15 = (bf16[128,2,128]{0,2,1:T(8,128)(2,1)}, bf16[128,2,128]{0,2,1:T(8,128)(2,1)S(1)}, u32[]{:S(2)}, u32[]{:S(2)}) collective-permute-start(bf16[128,2,128]{0,2,1:T(8,128)(2,1)} %get-tuple-element.33), channel_id=1, source_target_pairs={{0,1},{1,2},{2,3},{3,0},{4,5},{5,6},{6,7},{7,4},{8,9},{9,10},{10,1... | collective-permute-start | bytes 196616 | tf_op jit(solution)/shard_map/ppermute | solution.py:108
  36.4 9.2 %collective-permute-start.1 = (bf16[128,8,128]{0,2,1:T(8,128)(2,1)S(1)}, bf16[128,8,128]{0,2,1:T(8,128)(2,1)S(1)}, u32[]{:S(2)}, u32[]{:S(2)}) collective-permute-start(bf16[128,8,128]{0,2,1:T(8,128)(2,1)S(1)} %pad_maximum_fusion.3), channel_id=1, source_target_pairs={{0,2},{1,3},{4,6},{5,7},{8,10},{9,11},{12,14},{13,15},{16,18},{17,... | collective-permute-start | bytes 786440 | tf_op jit(solution)/shard_map/ppermute | solution.py:192
  37.8 9.6 %collective-permute-start = (bf16[128,8,128]{0,2,1:T(8,128)(2,1)S(1)}, bf16[128,8,128]{0,2,1:T(8,128)(2,1)S(1)}, u32[]{:S(2)}, u32[]{:S(2)}) collective-permute-start(bf16[128,8,128]{0,2,1:T(8,128)(2,1)S(1)} %pad_maximum_fusion.3), channel_id=1, source_target_pairs={{0,1},{1,2},{2,3},{4,5},{5,6},{6,7},{8,9},{9,10},{10,11},{12,13},{... | collective-permute-start | bytes 786440 | tf_op jit(solution)/shard_map/ppermute | solution.py:192
  45.6 4.8 %collective-permute-start.5 = (bf16[3,128,1024]{2,1,0:T(8,128)(2,1)S(1)}, bf16[3,128,1024]{2,1,0:T(8,128)(2,1)S(1)}, u32[]{:S(2)}, u32[]{:S(2)}) collective-permute-start(bf16[3,128,1024]{2,1,0:T(8,128)(2,1)S(1)} %pad_maximum_fusion.1), channel_id=1, source_target_pairs={{0,4},{4,0},{8,12},{12,8},{16,20},{20,16},{24,28},{28,24},{1,5},{5... | collective-permute-start | bytes 2359304 | tf_op jit(solution)/shard_map/ppermute | solution.py:134
  49.1 1.0 copy-start.6
  50.9 0.8 copy-start.13
  50.9 1.0 copy-start.14
  51.0 1.4 %copy-start.11 = (bf16[128,32]{1,0:T(8,128)(2,1)S(1)}, bf16[128,32]{1,0:T(8,128)(2,1)}, u32[]{:S(2)}) copy-start(bf16[128,32]{1,0:T(8,128)(2,1)} %copy.100) | copy-start | bytes 24580
  51.6 19.8 %copy-start.3 = (f32[128,1024]{1,0:T(8,128)}, f32[128,1024]{1,0:T(8,128)S(1)}, u32[]{:S(2)}) copy-start(f32[128,1024]{1,0:T(8,128)S(1)} %get-tuple-element.47) | copy-start | bytes 1572868
  52.5 29.3 %collective-permute-start.6 = (bf16[128,1152]{1,0:T(8,128)(2,1)S(1)}, bf16[128,1152]{1,0:T(8,128)(2,1)}, u32[]{:S(2)}, u32[]{:S(2)}) collective-permute-start(bf16[128,1152]{1,0:T(8,128)(2,1)S(1)} %concatenate.57), channel_id=1, source_target_pairs={{0,1},{1,2},{2,3},{3,0},{4,5},{5,6},{6,7},{7,4},{8,9},{9,10},{10,1... | collective-permute-start | bytes 884744 | tf_op jit(solution)/shard_map/ppermute | solution.py:108
  59.7 23.1 %collective-permute-start.7 = (bf16[128,1152]{1,0:T(8,128)(2,1)S(1)}, bf16[128,1152]{1,0:T(8,128)(2,1)}, u32[]{:S(2)}, u32[]{:S(2)}) collective-permute-start(bf16[128,1152]{1,0:T(8,128)(2,1)S(1)} %concatenate.57), channel_id=1, source_target_pairs={{0,2},{1,3},{2,0},{3,1},{4,6},{5,7},{6,4},{7,5},{8,10},{9,11},{10,... | collective-permute-start | bytes 884744 | tf_op jit(solution)/shard_map/ppermute | solution.py:108
  61.7 22.2 %collective-permute-start.8 = (bf16[128,1152]{1,0:T(8,128)(2,1)S(1)}, bf16[128,1152]{1,0:T(8,128)(2,1)}, u32[]{:S(2)}, u32[]{:S(2)}) collective-permute-start(bf16[128,1152]{1,0:T(8,128)(2,1)S(1)} %concatenate.57), channel_id=1, source_target_pairs={{0,3},{1,0},{2,1},{3,2},{4,7},{5,4},{6,5},{7,6},{8,11},{9,8},{10,9... | collective-permute-start | bytes 884744 | tf_op jit(solution)/shard_map/ppermute | solution.py:108
  85.4 6.6 %slice-start = ((s8[8388608]{0:T(1024)(128)(4,1)}), s8[4194304]{0:T(1024)(128)(4,1)S(1)}, s32[]{:S(2)}) async-start(s8[8388608]{0:T(1024)(128)(4,1)} %bitcast.236), calls=%async_computation | async-start | bytes 8388608
  86.4 5.6 %slice-start.1 = ((s8[8388608]{0:T(1024)(128)(4,1)}), s8[4194304]{0:T(1024)(128)(4,1)S(1)}, s32[]{:S(2)}) async-start(s8[8388608]{0:T(1024)(128)(4,1)} %bitcast.236), calls=%async_computation.1 | async-start | bytes 8388608
  86.4 7.7 %slice-start.2 = ((s8[8388608]{0:T(1024)(128)(4,1)}), s8[4194304]{0:T(1024)(128)(4,1)S(1)}, s32[]{:S(2)}) async-start(s8[8388608]{0:T(1024)(128)(4,1)} %bitcast.238), calls=%async_computation.2 | async-start | bytes 8388608
  92.0 2.4 %slice-start.3 = ((s8[8388608]{0:T(1024)(128)(4,1)}), s8[4194304]{0:T(1024)(128)(4,1)S(1)}, s32[]{:S(2)}) async-start(s8[8388608]{0:T(1024)(128)(4,1)} %bitcast.238), calls=%async_computation.3 | async-start | bytes 8388608
  95.3 2.3 %copy-start.18 = (bf16[3,8,64,512]{3,2,0,1:T(8,128)(2,1)}, bf16[3,8,64,512]{3,2,0,1:T(8,128)(2,1)S(1)}, u32[]{:S(2)}) copy-start(bf16[3,8,64,512]{3,2,0,1:T(8,128)(2,1)S(1)} %fusion.28) | copy-start | bytes 4718596
  97.6 10.7 %copy-start.17 = (bf16[3,8,64,512]{3,2,0,1:T(8,128)(2,1)S(1)}, bf16[3,8,64,512]{3,2,0,1:T(8,128)(2,1)}, u32[]{:S(2)}) copy-start(bf16[3,8,64,512]{3,2,0,1:T(8,128)(2,1)} %fusion.31) | copy-start | bytes 4718596
  100.0 12.2 %collective-permute-start.14 = (bf16[128,512]{1,0:T(8,128)(2,1)S(1)}, bf16[128,512]{1,0:T(8,128)(2,1)S(1)}, u32[]{:S(2)}, u32[]{:S(2)}) collective-permute-start(bf16[128,512]{1,0:T(8,128)(2,1)S(1)} %get-tuple-element.25), channel_id=1, source_target_pairs={{0,1},{1,2},{2,3},{3,0},{4,5},{5,6},{6,7},{7,4},{8,9},{9,10},{10,1... | collective-permute-start | bytes 393224 | tf_op jit(solution)/shard_map/ppermute | solution.py:108
  104.8 15.7 %collective-permute-start.13 = (bf16[128,512]{1,0:T(8,128)(2,1)S(1)}, bf16[128,512]{1,0:T(8,128)(2,1)S(1)}, u32[]{:S(2)}, u32[]{:S(2)}) collective-permute-start(bf16[128,512]{1,0:T(8,128)(2,1)S(1)} %get-tuple-element.26), channel_id=1, source_target_pairs={{0,2},{1,3},{2,0},{3,1},{4,6},{5,7},{6,4},{7,5},{8,10},{9,11},{10,... | collective-permute-start | bytes 393224 | tf_op jit(solution)/shard_map/ppermute | solution.py:108
  108.3 12.2 %collective-permute-start.12 = (bf16[128,512]{1,0:T(8,128)(2,1)S(1)}, bf16[128,512]{1,0:T(8,128)(2,1)S(1)}, u32[]{:S(2)}, u32[]{:S(2)}) collective-permute-start(bf16[128,512]{1,0:T(8,128)(2,1)S(1)} %get-tuple-element.24), channel_id=1, source_target_pairs={{0,3},{1,0},{2,1},{3,2},{4,7},{5,4},{6,5},{7,6},{8,11},{9,8},{10,9... | collective-permute-start | bytes 393224 | tf_op jit(solution)/shard_map/ppermute | solution.py:108
  108.8 18.9 %copy-start.4 = (f32[128,1024]{1,0:T(8,128)S(1)}, f32[128,1024]{1,0:T(8,128)}, u32[]{:S(2)}) copy-start(f32[128,1024]{1,0:T(8,128)} %copy-done.3) | copy-start | bytes 1572868
  108.8 18.9 %copy-start.5 = (f32[128,1024]{1,0:T(8,128)S(1)}, f32[128,1024]{1,0:T(8,128)}, u32[]{:S(2)}) copy-start(f32[128,1024]{1,0:T(8,128)} %convolution_bitcast_fusion.2) | copy-start | bytes 1572868
  108.8 19.9 %copy-start.1 = (bf16[1024,1024]{1,0:T(8,128)(2,1)S(1)}, bf16[1024,1024]{1,0:T(8,128)(2,1)}, u32[]{:S(2)}) copy-start(bf16[1024,1024]{1,0:T(8,128)(2,1)} %param.16) | copy-start | bytes 6291460
  109.2 11.3 %collective-permute-start.11 = (bf16[128,512]{1,0:T(8,128)(2,1)S(1)}, bf16[128,512]{1,0:T(8,128)(2,1)S(1)}, u32[]{:S(2)}, u32[]{:S(2)}) collective-permute-start(bf16[128,512]{1,0:T(8,128)(2,1)S(1)} %get-tuple-element.22), channel_id=1, source_target_pairs={{0,1},{1,2},{2,3},{3,0},{4,5},{5,6},{6,7},{7,4},{8,9},{9,10},{10,1... | collective-permute-start | bytes 393224 | tf_op jit(solution)/shard_map/ppermute | solution.py:108
  111.3 16.2 %collective-permute-start.10 = (bf16[128,512]{1,0:T(8,128)(2,1)S(1)}, bf16[128,512]{1,0:T(8,128)(2,1)S(1)}, u32[]{:S(2)}, u32[]{:S(2)}) collective-permute-start(bf16[128,512]{1,0:T(8,128)(2,1)S(1)} %get-tuple-element.23), channel_id=1, source_target_pairs={{0,2},{1,3},{2,0},{3,1},{4,6},{5,7},{6,4},{7,5},{8,10},{9,11},{10,... | collective-permute-start | bytes 393224 | tf_op jit(solution)/shard_map/ppermute | solution.py:108
  112.2 15.3 %collective-permute-start.9 = (bf16[128,512]{1,0:T(8,128)(2,1)S(1)}, bf16[128,512]{1,0:T(8,128)(2,1)S(1)}, u32[]{:S(2)}, u32[]{:S(2)}) collective-permute-start(bf16[128,512]{1,0:T(8,128)(2,1)S(1)} %get-tuple-element.21), channel_id=1, source_target_pairs={{0,3},{1,0},{2,1},{3,2},{4,7},{5,4},{6,5},{7,6},{8,11},{9,8},{10,9... | collective-permute-start | bytes 393224 | tf_op jit(solution)/shard_map/ppermute | solution.py:108

commit v14 on v11

--- a/solution.py
+++ b/solution.py
@@ -200,7 +200,7 @@
     normed2 = rms_scale(resid, norm_moe)
     packed = routing(normed2, expert_ids, w_router)
     experts = w_router.shape[1]
-    moe = expert_mix(packed, 1, width, experts, w_gate, w_up, w_down, 1)[0][0]
+    moe = jnp.concatenate(expert_mix(packed, 1, width, experts, w_gate, w_up, w_down, 2), axis=2)[0]
     received = jnp.concatenate([shifted(packed, step) for step in range(1, owners)])
     pieces = expert_mix(received, owners - 1, width, experts, w_gate, w_up, w_down, 2)
     backs = []

time: 128 us -> 132 us (1.031)
  waiting for transfers between devices: 22.2 us -> 34.8 us
  matrix products: 45.5 us -> 39.9 us
  starting transfers between devices: 41.7 us -> 37.3 us
  other arithmetic: 8.27 us -> 9.89 us
    ppermute x18, waiting for transfers between devices: 22.2 us -> 34.8 us  [shifted(): lax.ppermute(x, 'exp', [(j, (j + step) % count) for j in range(count)])]
    dot_general x3 -> x4, matrix products: 12.2 us -> 4.84 us  [expert_mix(): jnp.einsum('becf,efd->becd', hidden, down, preferred_element_type=jnp.flo...]
    dot_general x1 -> x2, matrix products: 5.54 us -> 10.7 us  [expert_mix(): jnp.einsum('becd,edf->becf', received, w_up, preferred_element_type=jnp.f...]
    ppermute x18, starting transfers between devices: 41.6 us -> 37.2 us  [shifted(): lax.ppermute(x, 'exp', [(j, (j + step) % count) for j in range(count)])]
    dot_general x3 -> x4, matrix products: 3.47 us -> 1.41 us  [expert_mix(): jnp.einsum('becr,becd->brd', low, result, preferred_element_type=jnp.floa...]
    unnamed x39 -> x35, local copies, waits for them, and re-layouts: 3.35 us -> 3.33 us
  transfers between devices with their start and end apart: 19 -> 19, of which waited for: 7 -> 10; matrix products, arithmetic and copies ran while one was open for 32% -> 29% of each run, Pallas kernels for 0% -> 0%
where the time goes in v14:
time: 132 us
  matrix products  39.9 us (30%)
  starting transfers between devices  37.3 us (28%)
  waiting for transfers between devices  34.8 us (26%)
  other arithmetic  9.89 us (7%)
  local copies, waits for them, and re-layouts  8.25 us (6%)
  between operations  1.38 us (1%)
    ppermute x18, starting transfers between devices, shifted(): lax.ppermute(x, 'exp', [(j, (j + step) % count) for j in range(count)])  37.2 us
    ppermute x18, waiting for transfers between devices, shifted(): lax.ppermute(x, 'exp', [(j, (j + step) % count) for j in range(count)])  34.8 us
    dot_general x2, matrix products, expert_mix(): jnp.einsum('becd,edf->becf', received, w_up, preferred_element_type=jnp.f...  10.7 us
    dot_general x2, matrix products, expert_mix(): jnp.einsum('becd,edf->becf', received, w_gate, preferred_element_type=jnp...  7.21 us
    dot_general x4, matrix products, expert_mix(): jnp.einsum('becf,efd->becd', hidden, down, preferred_element_type=jnp.flo...  4.84 us
    sub x1, matrix products, attend(): expo = jnp.exp(score - top)  3.6 us
    unnamed x35, local copies, waits for them, and re-layouts  3.33 us
    dot_general x1, matrix products, attend(): jnp.einsum('kgqt,tkd->qkgd', probs, values, preferred_element_type=jnp.fl...  2.74 us
  transfers between devices with their start and end apart: 19, of which 10 were waited for; matrix products, arithmetic and copies ran while one was open for 29% of the time, Pallas kernels for 0%

profile of v14, /device:TPU:0, one launch (start us, length us, event | category | flops | bytes accessed | tf_op | source)
XLA Modules:
  0.0 131.5 jit_solution(11238553924857088713)
XLA Ops:
  0.7 1.8 %constant_dynamic-slice_fusion.9 = bf16[128,1024]{1,0:T(8,128)(2,1)} fusion(bf16[256,1024]{1,0:T(8,128)(2,1)} %param.19, s32[]{:T(128)S(6)} %select_n.172), kind=kLoop, calls=%fused_computation.200 | loop fusion | bytes 524292 | tf_op jit(solution)/shard_map/dynamic_slice | solution.py:132
  2.5 5.1 %collective-permute-start.6 = (bf16[128,1024]{1,0:T(8,128)(2,1)}, bf16[128,1024]{1,0:T(8,128)(2,1)S(1)}, u32[]{:S(2)}, u32[]{:S(2)}) collective-permute-start(bf16[128,1024]{1,0:T(8,128)(2,1)} %constant_dynamic-slice_fusion.9), channel_id=1, source_target_pairs={{0,3},{1,0},{2,1},{3,2},{4,7},{5,4},{6,5},{7,6},{8,11},{9,8},{10,9... | collective-permute-start | bytes 786440 | tf_op jit(solution)/shard_map/ppermute | solution.py:108
  7.6 0.6 multiply_power_fusion
  8.2 0.8 compare_reduce_fusion
  9.0 1.1 fusion.97
  10.2 0.3 reduce-window.9
  10.7 0.7 bitcast_subtract_fusion
  11.4 0.7 convert_element_type.130
  12.1 1.7 %convolution_convert_fusion.3 = bf16[128,512]{1,0:T(8,128)(2,1)S(1)} fusion(bf16[1024,512]{1,0:T(8,128)(2,1)} %param.18, bf16[128,1024]{1,0:T(8,128)(2,1)} %param.14, f32[1024]{0:T(1024)S(1)} %convert_element_type.130, f32[128]{0:T(128)S(1)} %add_rsqrt_fusion.1), kind=kOutput, calls=%fused_computation.80 | convolution fusion | flops 134807552 | bytes 1446400 | tf_op jit(solution)/shard_map/dot_general | solution.py:169
  13.9 1.9 %fusion.196 = f32[128,512]{0,1:T(8,128)S(1)} fusion(bf16[1024,512]{1,0:T(8,128)(2,1)} %param.17, bf16[128,1024]{1,0:T(8,128)(2,1)} %param.14, f32[1024]{0:T(1024)S(1)} %convert_element_type.130, f32[128]{0:T(128)S(1)} %add_rsqrt_fusion.1), kind=kOutput, calls=%fused_computation.244 | convolution fusion | flops 134742016 | bytes 1577472 | tf_op jit(solution)/shard_map/dot_general | solution.py:166
  15.8 1.0 fusion.198
  16.8 0.8 dynamic-slice_convert_fusion
  17.6 0.8 multiply_cosine_fusion
  18.7 0.5 collective-permute-start.2
  19.2 2.5 %collective-permute-start.1 = (bf16[128,2,256]{0,2,1:T(8,128)(2,1)S(1)}, bf16[128,2,256]{0,2,1:T(8,128)(2,1)S(1)}, u32[]{:S(2)}, u32[]{:S(2)}) collective-permute-start(bf16[128,2,256]{0,2,1:T(8,128)(2,1)S(1)} %get-tuple-element.23), channel_id=1, source_target_pairs={{0,2},{1,3},{2,0},{3,1},{4,6},{5,7},{6,4},{7,5},{8,10},{9,11},{10,... | collective-permute-start | bytes 393224 | tf_op jit(solution)/shard_map/ppermute | solution.py:108
  21.8 1.9 %collective-permute-start = (bf16[128,2,256]{0,2,1:T(8,128)(2,1)S(1)}, bf16[128,2,256]{0,2,1:T(8,128)(2,1)S(1)}, u32[]{:S(2)}, u32[]{:S(2)}) collective-permute-start(bf16[128,2,256]{0,2,1:T(8,128)(2,1)S(1)} %get-tuple-element.24), channel_id=1, source_target_pairs={{0,1},{1,2},{2,3},{3,0},{4,5},{5,6},{6,7},{7,4},{8,9},{9,10},{10,1... | collective-permute-start | bytes 393224 | tf_op jit(solution)/shard_map/ppermute | solution.py:108
  24.1 0.3 compare_and_fusion
  24.6 3.1 %collective-permute-done.2 = bf16[128,2,256]{0,2,1:T(8,128)(2,1)S(1)} collective-permute-done((bf16[128,2,256]{0,2,1:T(8,128)(2,1)S(1)}, bf16[128,2,256]{0,2,1:T(8,128)(2,1)S(1)}, u32[]{:S(2)}, u32[]{:S(2)}) %collective-permute-start.2) | collective-permute-done | bytes 131104 | tf_op jit(solution)/shard_map/ppermute | solution.py:108
  27.6 12.6 %collective-permute-start.4 = (bf16[128,1024]{1,0:T(8,128)(2,1)}, bf16[128,1024]{1,0:T(8,128)(2,1)S(1)}, u32[]{:S(2)}, u32[]{:S(2)}) collective-permute-start(bf16[128,1024]{1,0:T(8,128)(2,1)} %constant_dynamic-slice_fusion.9), channel_id=1, source_target_pairs={{0,1},{1,2},{2,3},{3,0},{4,5},{5,6},{6,7},{7,4},{8,9},{9,10},{10,1... | collective-permute-start | bytes 786440 | tf_op jit(solution)/shard_map/ppermute | solution.py:108
  40.3 1.1 collective-permute-done.1
  41.5 0.3 convolution_convert_fusion.2
  41.8 1.0 copy.113
  42.8 3.6 %fusion.201 = (f32[2,2,512]{2,1,0:T(2,128)S(1)}, f32[2,2,512,512]{2,3,1,0:T(8,128)}) fusion(pred[512,512]{0,1:T(8,128)(4,1)S(1)} %compare_and_fusion, bf16[512,2,2,64]{0,3,2,1:T(8,128)(2,1)S(1)} %bitcast.287, bf16[512,2,256]{0,2,1:T(8,128)(2,1)S(1)} %pad_maximum_fusion.3), kind=kOutput, calls=%fused_computation.247 | convolution fusion | flops 138412544 | bytes 4857856 | tf_op jit(solution)/shard_map/sub | solution.py:44
  46.4 1.0 pad_maximum_fusion
  47.6 2.7 %fusion.82 = bf16[512,2,2,64]{0,3,2,1:T(8,128)(2,1)S(1)} fusion(f32[2,2,512,512]{2,3,1,0:T(8,128)} %get-tuple-element.50, f32[2,2,512]{2,1,0:T(2,128)S(1)} %get-tuple-element.49, bf16[512,2,256]{0,2,1:T(8,128)(2,1)S(1)} %pad_maximum_fusion.3), kind=kOutput, calls=%fused_computation.75 | convolution fusion | flops 136445952 | bytes 4595712 | tf_op jit(solution)/shard_map/kgqt,tkd->qkgd/dot_general | solution.py:46
  50.4 0.5 collective-permute-start.9
  50.8 3.4 %collective-permute-start.3 = (bf16[128,256]{0,1:T(8,128)(2,1)S(1)}, bf16[128,256]{0,1:T(8,128)(2,1)S(1)}, u32[]{:S(2)}, u32[]{:S(2)}) collective-permute-start(bf16[128,256]{0,1:T(8,128)(2,1)S(1)} %bitcast.291), channel_id=1, source_target_pairs={{0,3},{1,0},{2,1},{3,2},{4,7},{5,4},{6,5},{7,6},{8,11},{9,8},{10,9... | collective-permute-start | bytes 196616 | tf_op jit(solution)/shard_map/ppermute | solution.py:108
  54.5 1.1 broadcast_select_fusion.1
  55.6 2.7 %collective-permute-done.3 = bf16[128,256]{0,1:T(8,128)(2,1)S(1)} collective-permute-done((bf16[128,256]{0,1:T(8,128)(2,1)S(1)}, bf16[128,256]{0,1:T(8,128)(2,1)S(1)}, u32[]{:S(2)}, u32[]{:S(2)}) %collective-permute-start.3) | collective-permute-done | bytes 65568 | tf_op jit(solution)/shard_map/ppermute | solution.py:108
  58.9 0.5 collective-permute-done.8
  59.4 0.4 multiply_reduce_fusion
  61.0 2.0 %collective-permute-start.12 = (bf16[128,1152]{1,0:T(8,128)(2,1)S(1)}, bf16[128,1152]{1,0:T(8,128)(2,1)}, u32[]{:S(2)}, u32[]{:S(2)}) collective-permute-start(bf16[128,1152]{1,0:T(8,128)(2,1)S(1)} %concatenate.50), channel_id=1, source_target_pairs={{0,3},{1,0},{2,1},{3,2},{4,7},{5,4},{6,5},{7,6},{8,11},{9,8},{10,9... | collective-permute-start | bytes 884744 | tf_op jit(solution)/shard_map/ppermute | solution.py:108
  63.0 1.5 %collective-permute-start.11 = (bf16[128,1152]{1,0:T(8,128)(2,1)S(1)}, bf16[128,1152]{1,0:T(8,128)(2,1)}, u32[]{:S(2)}, u32[]{:S(2)}) collective-permute-start(bf16[128,1152]{1,0:T(8,128)(2,1)S(1)} %concatenate.50), channel_id=1, source_target_pairs={{0,2},{1,3},{2,0},{3,1},{4,6},{5,7},{6,4},{7,5},{8,10},{9,11},{10,... | collective-permute-start | bytes 884744 | tf_op jit(solution)/shard_map/ppermute | solution.py:108
  64.5 0.4 convolution_convert_fusion.1
  65.0 5.1 %convolution_bitcast_fusion.1 = f32[1,8,64,512]{3,2,1,0:T(8,128)S(1)} fusion(bf16[8,64,1024]{2,1,0:T(8,128)(2,1)S(1)} %convolution_convert_fusion.1, bf16[8,1024,512]{2,1,0:T(8,128)(2,1)} %param.22), kind=kOutput, calls=%fused_computation.52 | convolution fusion | flops 536870912 | bytes 10485760 | tf_op jit(solution)/shard_map/becd,edf->becf/dot_general | solution.py:86
  70.2 5.1 %fusion.78 = bf16[8,64,512]{2,1,0:T(8,128)(2,1)S(1)} fusion(bf16[8,64,1024]{2,1,0:T(8,128)(2,1)S(1)} %convolution_convert_fusion.1, bf16[8,1024,512]{2,1,0:T(8,128)(2,1)} %param.23, f32[1,8,64,512]{3,2,1,0:T(8,128)S(1)} %convolution_bitcast_fusion.1), kind=kOutput, calls=%fused_computation.64 | convolution fusion | flops 538443776 | bytes 11010048 | tf_op jit(solution)/shard_map/becd,edf->becf/dot_general | solution.py:87
  75.3 0.8 fusion.51
  76.2 0.8 fusion.48
  77.3 0.3 convolution_bitcast_fusion.4
  78.4 4.8 %collective-permute-done.10 = bf16[128,1152]{1,0:T(8,128)(2,1)} collective-permute-done((bf16[128,1152]{1,0:T(8,128)(2,1)S(1)}, bf16[128,1152]{1,0:T(8,128)(2,1)}, u32[]{:S(2)}, u32[]{:S(2)}) %collective-permute-start.10) | collective-permute-done | bytes 294944 | tf_op jit(solution)/shard_map/ppermute | solution.py:108
  83.2 1.0 constant_dynamic-update-slice_fusion.2
  84.1 5.8 %collective-permute-done.11 = bf16[128,1152]{1,0:T(8,128)(2,1)} collective-permute-done((bf16[128,1152]{1,0:T(8,128)(2,1)S(1)}, bf16[128,1152]{1,0:T(8,128)(2,1)}, u32[]{:S(2)}, u32[]{:S(2)}) %collective-permute-start.11) | collective-permute-done | bytes 294944 | tf_op jit(solution)/shard_map/ppermute | solution.py:108
  89.9 1.0 constant_dynamic-update-slice_fusion.1
  90.9 1.0 constant_dynamic-update-slice_fusion
  92.5 1.0 convolution_convert_fusion
  93.5 5.5 %fusion.1 = f32[8,3,64,512]{3,2,1,0:T(8,128)S(1)} fusion(bf16[8,1024,512]{2,1,0:T(8,128)(2,1)} %param.23, bf16[3,8,64,1024]{3,2,1,0:T(8,128)(2,1)S(1)} %convolution_convert_fusion), kind=kOutput, calls=%fused_computation.1 | convolution fusion | flops 1610612736 | bytes 14680064 | tf_op jit(solution)/shard_map/becd,edf->becf/dot_general | solution.py:87
  99.1 2.1 %fusion.16 = bf16[3,8,64,512]{3,2,0,1:T(8,128)(2,1)S(1)} fusion(f32[8,3,64,512]{3,2,1,0:T(8,128)S(1)} %fusion.1, bf16[8,1024,512]{2,1,0:T(8,128)(2,1)S(1)} %bitcast.276, bf16[3,8,64,1024]{3,2,1,0:T(8,128)(2,1)S(1)} %convolution_convert_fusion), kind=kOutput, calls=%fused_computation.20 | convolution fusion | flops 1615331328 | bytes 16252928 | tf_op jit(solution)/shard_map/becd,edf->becf/dot_general | solution.py:86
  101.2 0.3 slice-done.5
  101.4 2.2 %fusion.32 = bf16[3,8,64,512]{3,2,0,1:T(8,128)(2,1)} fusion(bf16[3,8,64,512]{3,2,0,1:T(8,128)(2,1)S(1)} %fusion.16, bf16[8,512,1024]{2,1,0:T(8,128)(2,1)S(1)} %bitcast.303), kind=kOutput, calls=%fused_computation.39 | convolution fusion | flops 806092800 | bytes 7340032 | tf_op jit(solution)/shard_map/becf,efd->becd/dot_general | solution.py:96
  103.6 1.0 fusion.35
  104.8 0.4 fusion.54
  105.2 0.4 fusion.72
  105.7 2.0 %collective-permute-start.15 = (bf16[128,512]{1,0:T(8,128)(2,1)S(1)}, bf16[128,512]{1,0:T(8,128)(2,1)S(1)}, u32[]{:S(2)}, u32[]{:S(2)}) collective-permute-start(bf16[128,512]{1,0:T(8,128)(2,1)S(1)} %get-tuple-element.26), channel_id=1, source_target_pairs={{0,1},{1,2},{2,3},{3,0},{4,5},{5,6},{6,7},{7,4},{8,9},{9,10},{10,1... | collective-permute-start | bytes 393224 | tf_op jit(solution)/shard_map/ppermute | solution.py:108
  107.7 2.2 %collective-permute-start.14 = (bf16[128,512]{1,0:T(8,128)(2,1)S(1)}, bf16[128,512]{1,0:T(8,128)(2,1)S(1)}, u32[]{:S(2)}, u32[]{:S(2)}) collective-permute-start(bf16[128,512]{1,0:T(8,128)(2,1)S(1)} %get-tuple-element.27), channel_id=1, source_target_pairs={{0,2},{1,3},{2,0},{3,1},{4,6},{5,7},{6,4},{7,5},{8,10},{9,11},{10,... | collective-permute-start | bytes 393224 | tf_op jit(solution)/shard_map/ppermute | solution.py:108
  110.0 0.4 fusion.60
  110.4 0.4 fusion.75
  110.9 1.0 collective-permute-start.16
  111.9 1.1 collective-permute-start.18
  113.0 0.5 collective-permute-done.13
  113.5 0.8 collective-permute-start.17
  114.3 2.3 %collective-permute-done.15 = bf16[128,512]{1,0:T(8,128)(2,1)S(1)} collective-permute-done((bf16[128,512]{1,0:T(8,128)(2,1)S(1)}, bf16[128,512]{1,0:T(8,128)(2,1)S(1)}, u32[]{:S(2)}, u32[]{:S(2)}) %collective-permute-start.15) | collective-permute-done | bytes 131104 | tf_op jit(solution)/shard_map/ppermute | solution.py:108
  116.6 9.8 %collective-permute-done.14 = bf16[128,512]{1,0:T(8,128)(2,1)S(1)} collective-permute-done((bf16[128,512]{1,0:T(8,128)(2,1)S(1)}, bf16[128,512]{1,0:T(8,128)(2,1)S(1)}, u32[]{:S(2)}, u32[]{:S(2)}) %collective-permute-start.14) | collective-permute-done | bytes 131104 | tf_op jit(solution)/shard_map/ppermute | solution.py:108
  126.4 4.2 %collective-permute-done.17 = bf16[128,512]{1,0:T(8,128)(2,1)S(1)} collective-permute-done((bf16[128,512]{1,0:T(8,128)(2,1)S(1)}, bf16[128,512]{1,0:T(8,128)(2,1)S(1)}, u32[]{:S(2)}, u32[]{:S(2)}) %collective-permute-start.17) | collective-permute-done | bytes 131104 | tf_op jit(solution)/shard_map/ppermute | solution.py:108
  130.7 0.8 fusion.112
  (114 shorter events, 5.4 us)
Async XLA Ops:
  0.6 15.2 %copy-start = (bf16[1024,1024]{1,0:T(8,128)(2,1)S(1)}, bf16[1024,1024]{1,0:T(8,128)(2,1)}, u32[]{:S(2)}) copy-start(bf16[1024,1024]{1,0:T(8,128)(2,1)} %param.16) | copy-start | bytes 6291460
  0.6 15.2 %copy-start.2 = (bf16[128,1024]{1,0:T(8,128)(2,1)S(1)}, bf16[128,1024]{1,0:T(8,128)(2,1)}, u32[]{:S(2)}) copy-start(bf16[128,1024]{1,0:T(8,128)(2,1)} %param.14) | copy-start | bytes 786436
  2.5 43.9 %collective-permute-start.6 = (bf16[128,1024]{1,0:T(8,128)(2,1)}, bf16[128,1024]{1,0:T(8,128)(2,1)S(1)}, u32[]{:S(2)}, u32[]{:S(2)}) collective-permute-start(bf16[128,1024]{1,0:T(8,128)(2,1)} %constant_dynamic-slice_fusion.9), channel_id=1, source_target_pairs={{0,3},{1,0},{2,1},{3,2},{4,7},{5,4},{6,5},{7,6},{8,11},{9,8},{10,9... | collective-permute-start | bytes 786440 | tf_op jit(solution)/shard_map/ppermute | solution.py:108
  7.6 38.8 %collective-permute-start.5 = (bf16[128,1024]{1,0:T(8,128)(2,1)}, bf16[128,1024]{1,0:T(8,128)(2,1)}, u32[]{:S(2)}, u32[]{:S(2)}) collective-permute-start(bf16[128,1024]{1,0:T(8,128)(2,1)} %constant_dynamic-slice_fusion.9), channel_id=1, source_target_pairs={{0,2},{1,3},{2,0},{3,1},{4,6},{5,7},{6,4},{7,5},{8,10},{9,11},{10,... | collective-permute-start | bytes 786440 | tf_op jit(solution)/shard_map/ppermute | solution.py:108
  15.8 8.1 %copy-start.6 = (s32[1,512]{1,0:T(1,128)S(1)}, s32[1,512]{1,0:T(1,128)}, u32[]{:S(2)}) copy-start(s32[1,512]{1,0:T(1,128)} %param.25) | copy-start | bytes 6148
  15.8 8.2 %copy-start.5 = (s32[128,8]{0,1:T(8,128)S(1)}, s32[128,8]{0,1:T(8,128)}, u32[]{:S(2)}) copy-start(s32[128,8]{0,1:T(8,128)} %param.27) | copy-start | bytes 12292
  16.8 7.5 %copy-start.7 = (s32[1,512]{1,0:T(1,128)S(1)}, s32[1,512]{1,0:T(1,128)}, u32[]{:S(2)}) copy-start(s32[1,512]{1,0:T(1,128)} %param.26) | copy-start | bytes 6148
  16.8 7.6 %copy-start.8 = (bf16[1024]{0:T(1024)(128)(2,1)S(1)}, bf16[1024]{0:T(1024)(128)(2,1)}, u32[]{:S(2)}) copy-start(bf16[1024]{0:T(1024)(128)(2,1)} %param.20) | copy-start | bytes 6148
  18.7 8.9 %collective-permute-start.2 = (bf16[128,2,256]{0,2,1:T(8,128)(2,1)S(1)}, bf16[128,2,256]{0,2,1:T(8,128)(2,1)S(1)}, u32[]{:S(2)}, u32[]{:S(2)}) collective-permute-start(bf16[128,2,256]{0,2,1:T(8,128)(2,1)S(1)} %get-tuple-element.22), channel_id=1, source_target_pairs={{0,3},{1,0},{2,1},{3,2},{4,7},{5,4},{6,5},{7,6},{8,11},{9,8},{10,9... | collective-permute-start | bytes 393224 | tf_op jit(solution)/shard_map/ppermute | solution.py:108
  19.2 22.2 %collective-permute-start.1 = (bf16[128,2,256]{0,2,1:T(8,128)(2,1)S(1)}, bf16[128,2,256]{0,2,1:T(8,128)(2,1)S(1)}, u32[]{:S(2)}, u32[]{:S(2)}) collective-permute-start(bf16[128,2,256]{0,2,1:T(8,128)(2,1)S(1)} %get-tuple-element.23), channel_id=1, source_target_pairs={{0,2},{1,3},{2,0},{3,1},{4,6},{5,7},{6,4},{7,5},{8,10},{9,11},{10,... | collective-permute-start | bytes 393224 | tf_op jit(solution)/shard_map/ppermute | solution.py:108
  21.8 19.6 %collective-permute-start = (bf16[128,2,256]{0,2,1:T(8,128)(2,1)S(1)}, bf16[128,2,256]{0,2,1:T(8,128)(2,1)S(1)}, u32[]{:S(2)}, u32[]{:S(2)}) collective-permute-start(bf16[128,2,256]{0,2,1:T(8,128)(2,1)S(1)} %get-tuple-element.24), channel_id=1, source_target_pairs={{0,1},{1,2},{2,3},{3,0},{4,5},{5,6},{6,7},{7,4},{8,9},{9,10},{10,1... | collective-permute-start | bytes 393224 | tf_op jit(solution)/shard_map/ppermute | solution.py:108
  27.6 18.8 %collective-permute-start.4 = (bf16[128,1024]{1,0:T(8,128)(2,1)}, bf16[128,1024]{1,0:T(8,128)(2,1)S(1)}, u32[]{:S(2)}, u32[]{:S(2)}) collective-permute-start(bf16[128,1024]{1,0:T(8,128)(2,1)} %constant_dynamic-slice_fusion.9), channel_id=1, source_target_pairs={{0,1},{1,2},{2,3},{3,0},{4,5},{5,6},{6,7},{7,4},{8,9},{9,10},{10,1... | collective-permute-start | bytes 786440 | tf_op jit(solution)/shard_map/ppermute | solution.py:108
  47.5 7.0 %collective-permute-start.7 = (bf16[3,128,1024]{2,1,0:T(8,128)(2,1)S(1)}, bf16[3,128,1024]{2,1,0:T(8,128)(2,1)S(1)}, u32[]{:S(2)}, u32[]{:S(2)}) collective-permute-start(bf16[3,128,1024]{2,1,0:T(8,128)(2,1)S(1)} %pad_maximum_fusion), channel_id=1, source_target_pairs={{0,4},{4,0},{8,12},{12,8},{16,20},{20,16},{24,28},{28,24},{1,5},{5... | collective-permute-start | bytes 2359304 | tf_op jit(solution)/shard_map/ppermute | solution.py:134
  47.5 6.7 %copy-start.3 = (bf16[256,1024]{1,0:T(8,128)(2,1)S(1)}, bf16[256,1024]{1,0:T(8,128)(2,1)}, u32[]{:S(2)}) copy-start(bf16[256,1024]{1,0:T(8,128)(2,1)} %param.19) | copy-start | bytes 1572868
  50.4 8.2 %collective-permute-start.9 = (bf16[128,256]{0,1:T(8,128)(2,1)S(1)}, bf16[128,256]{0,1:T(8,128)(2,1)S(1)}, u32[]{:S(2)}, u32[]{:S(2)}) collective-permute-start(bf16[128,256]{0,1:T(8,128)(2,1)S(1)} %bitcast.290), channel_id=1, source_target_pairs={{0,1},{1,2},{2,3},{3,0},{4,5},{5,6},{6,7},{7,4},{8,9},{9,10},{10,1... | collective-permute-start | bytes 196616 | tf_op jit(solution)/shard_map/ppermute | solution.py:108
  50.8 8.6 %collective-permute-start.8 = (bf16[128,256]{0,1:T(8,128)(2,1)S(1)}, bf16[128,256]{0,1:T(8,128)(2,1)S(1)}, u32[]{:S(2)}, u32[]{:S(2)}) collective-permute-start(bf16[128,256]{0,1:T(8,128)(2,1)S(1)} %bitcast.289), channel_id=1, source_target_pairs={{0,2},{1,3},{2,0},{3,1},{4,6},{5,7},{6,4},{7,5},{8,10},{9,11},{10,... | collective-permute-start | bytes 196616 | tf_op jit(solution)/shard_map/ppermute | solution.py:108
  50.8 7.5 %collective-permute-start.3 = (bf16[128,256]{0,1:T(8,128)(2,1)S(1)}, bf16[128,256]{0,1:T(8,128)(2,1)S(1)}, u32[]{:S(2)}, u32[]{:S(2)}) collective-permute-start(bf16[128,256]{0,1:T(8,128)(2,1)S(1)} %bitcast.291), channel_id=1, source_target_pairs={{0,3},{1,0},{2,1},{3,2},{4,7},{5,4},{6,5},{7,6},{8,11},{9,8},{10,9... | collective-permute-start | bytes 196616 | tf_op jit(solution)/shard_map/ppermute | solution.py:108
  58.6 1.3 %copy-start.4 = (bf16[1024,32]{0,1:T(8,128)(2,1)S(1)}, bf16[1024,32]{0,1:T(8,128)(2,1)}, u32[]{:S(2)}) copy-start(bf16[1024,32]{0,1:T(8,128)(2,1)} %param.21) | copy-start | bytes 196612
  61.0 29.9 %collective-permute-start.12 = (bf16[128,1152]{1,0:T(8,128)(2,1)S(1)}, bf16[128,1152]{1,0:T(8,128)(2,1)}, u32[]{:S(2)}, u32[]{:S(2)}) collective-permute-start(bf16[128,1152]{1,0:T(8,128)(2,1)S(1)} %concatenate.50), channel_id=1, source_target_pairs={{0,3},{1,0},{2,1},{3,2},{4,7},{5,4},{6,5},{7,6},{8,11},{9,8},{10,9... | collective-permute-start | bytes 884744 | tf_op jit(solution)/shard_map/ppermute | solution.py:108
  63.0 26.9 %collective-permute-start.11 = (bf16[128,1152]{1,0:T(8,128)(2,1)S(1)}, bf16[128,1152]{1,0:T(8,128)(2,1)}, u32[]{:S(2)}, u32[]{:S(2)}) collective-permute-start(bf16[128,1152]{1,0:T(8,128)(2,1)S(1)} %concatenate.50), channel_id=1, source_target_pairs={{0,2},{1,3},{2,0},{3,1},{4,6},{5,7},{6,4},{7,5},{8,10},{9,11},{10,... | collective-permute-start | bytes 884744 | tf_op jit(solution)/shard_map/ppermute | solution.py:108
  64.5 18.7 %collective-permute-start.10 = (bf16[128,1152]{1,0:T(8,128)(2,1)S(1)}, bf16[128,1152]{1,0:T(8,128)(2,1)}, u32[]{:S(2)}, u32[]{:S(2)}) collective-permute-start(bf16[128,1152]{1,0:T(8,128)(2,1)S(1)} %concatenate.50), channel_id=1, source_target_pairs={{0,1},{1,2},{2,3},{3,0},{4,5},{5,6},{6,7},{7,4},{8,9},{9,10},{10,1... | collective-permute-start | bytes 884744 | tf_op jit(solution)/shard_map/ppermute | solution.py:108
  65.0 10.3 %slice-start.2 = ((s8[8388608]{0:T(1024)(128)(4,1)}), s8[4194304]{0:T(1024)(128)(4,1)S(1)}, s32[]{:S(2)}) async-start(s8[8388608]{0:T(1024)(128)(4,1)} %bitcast.300), calls=%async_computation.2 | async-start | bytes 8388608
  70.1 5.2 %slice-start.3 = ((s8[8388608]{0:T(1024)(128)(4,1)}), s8[4194304]{0:T(1024)(128)(4,1)S(1)}, s32[]{:S(2)}) async-start(s8[8388608]{0:T(1024)(128)(4,1)} %bitcast.300), calls=%async_computation.3 | async-start | bytes 8388608
  92.5 6.6 %slice-start = ((s8[8388608]{0:T(1024)(128)(4,1)}), s8[4194304]{0:T(1024)(128)(4,1)S(1)}, s32[]{:S(2)}) async-start(s8[8388608]{0:T(1024)(128)(4,1)} %bitcast.275), calls=%async_computation | async-start | bytes 8388608
  93.5 5.6 %slice-start.1 = ((s8[8388608]{0:T(1024)(128)(4,1)}), s8[4194304]{0:T(1024)(128)(4,1)S(1)}, s32[]{:S(2)}) async-start(s8[8388608]{0:T(1024)(128)(4,1)} %bitcast.275), calls=%async_computation.1 | async-start | bytes 8388608
  93.5 7.7 %slice-start.4 = ((s8[8388608]{0:T(1024)(128)(4,1)}), s8[4194304]{0:T(1024)(128)(4,1)S(1)}, s32[]{:S(2)}) async-start(s8[8388608]{0:T(1024)(128)(4,1)} %bitcast.302), calls=%async_computation.4 | async-start | bytes 8388608
  99.1 2.4 %slice-start.5 = ((s8[8388608]{0:T(1024)(128)(4,1)}), s8[4194304]{0:T(1024)(128)(4,1)S(1)}, s32[]{:S(2)}) async-start(s8[8388608]{0:T(1024)(128)(4,1)} %bitcast.302), calls=%async_computation.5 | async-start | bytes 8388608
  104.8 5.2 %copy-start.9 = (bf16[3,8,64,512]{3,2,0,1:T(8,128)(2,1)S(1)}, bf16[3,8,64,512]{3,2,0,1:T(8,128)(2,1)}, u32[]{:S(2)}) copy-start(bf16[3,8,64,512]{3,2,0,1:T(8,128)(2,1)} %fusion.32) | copy-start | bytes 4718596
  105.7 7.8 %collective-permute-start.13 = (bf16[128,512]{1,0:T(8,128)(2,1)S(1)}, bf16[128,512]{1,0:T(8,128)(2,1)S(1)}, u32[]{:S(2)}, u32[]{:S(2)}) collective-permute-start(bf16[128,512]{1,0:T(8,128)(2,1)S(1)} %get-tuple-element.25), channel_id=1, source_target_pairs={{0,3},{1,0},{2,1},{3,2},{4,7},{5,4},{6,5},{7,6},{8,11},{9,8},{10,9... | collective-permute-start | bytes 393224 | tf_op jit(solution)/shard_map/ppermute | solution.py:108
  105.7 10.9 %collective-permute-start.15 = (bf16[128,512]{1,0:T(8,128)(2,1)S(1)}, bf16[128,512]{1,0:T(8,128)(2,1)S(1)}, u32[]{:S(2)}, u32[]{:S(2)}) collective-permute-start(bf16[128,512]{1,0:T(8,128)(2,1)S(1)} %get-tuple-element.26), channel_id=1, source_target_pairs={{0,1},{1,2},{2,3},{3,0},{4,5},{5,6},{6,7},{7,4},{8,9},{9,10},{10,1... | collective-permute-start | bytes 393224 | tf_op jit(solution)/shard_map/ppermute | solution.py:108
  107.7 18.6 %collective-permute-start.14 = (bf16[128,512]{1,0:T(8,128)(2,1)S(1)}, bf16[128,512]{1,0:T(8,128)(2,1)S(1)}, u32[]{:S(2)}, u32[]{:S(2)}) collective-permute-start(bf16[128,512]{1,0:T(8,128)(2,1)S(1)} %get-tuple-element.27), channel_id=1, source_target_pairs={{0,2},{1,3},{2,0},{3,1},{4,6},{5,7},{6,4},{7,5},{8,10},{9,11},{10,... | collective-permute-start | bytes 393224 | tf_op jit(solution)/shard_map/ppermute | solution.py:108
  110.0 21.5 %copy-start.1 = (bf16[1024,1024]{1,0:T(8,128)(2,1)S(1)}, bf16[1024,1024]{1,0:T(8,128)(2,1)}, u32[]{:S(2)}) copy-start(bf16[1024,1024]{1,0:T(8,128)(2,1)} %param.16) | copy-start | bytes 6291460
  110.9 15.5 %collective-permute-start.16 = (bf16[128,512]{1,0:T(8,128)(2,1)S(1)}, bf16[128,512]{1,0:T(8,128)(2,1)S(1)}, u32[]{:S(2)}, u32[]{:S(2)}) collective-permute-start(bf16[128,512]{1,0:T(8,128)(2,1)S(1)} %get-tuple-element.28), channel_id=1, source_target_pairs={{0,3},{1,0},{2,1},{3,2},{4,7},{5,4},{6,5},{7,6},{8,11},{9,8},{10,9... | collective-permute-start | bytes 393224 | tf_op jit(solution)/shard_map/ppermute | solution.py:108
  111.9 14.5 %collective-permute-start.18 = (bf16[128,512]{1,0:T(8,128)(2,1)S(1)}, bf16[128,512]{1,0:T(8,128)(2,1)S(1)}, u32[]{:S(2)}, u32[]{:S(2)}) collective-permute-start(bf16[128,512]{1,0:T(8,128)(2,1)S(1)} %get-tuple-element.29), channel_id=1, source_target_pairs={{0,1},{1,2},{2,3},{3,0},{4,5},{5,6},{6,7},{7,4},{8,9},{9,10},{10,1... | collective-permute-start | bytes 393224 | tf_op jit(solution)/shard_map/ppermute | solution.py:108
  113.5 17.1 %collective-permute-start.17 = (bf16[128,512]{1,0:T(8,128)(2,1)S(1)}, bf16[128,512]{1,0:T(8,128)(2,1)S(1)}, u32[]{:S(2)}, u32[]{:S(2)}) collective-permute-start(bf16[128,512]{1,0:T(8,128)(2,1)S(1)} %get-tuple-element.30), channel_id=1, source_target_pairs={{0,2},{1,3},{2,0},{3,1},{4,6},{5,7},{6,4},{7,5},{8,10},{9,11},{10,... | collective-permute-start | bytes 393224 | tf_op jit(solution)/shard_map/ppermute | solution.py:108

commit v15 on v14

--- a/solution.py
+++ b/solution.py
@@ -62,15 +62,15 @@
     return jnp.concatenate([normed2, high, low, named, fill], axis=1)
 
 
-def expert_mix(packed, sources, width, experts, w_gate, w_up, w_down, pieces):
+def expert_mix(chunks, width, experts, w_gate, w_up, w_down, pieces):
     local = w_gate.shape[0]
-    rows = packed.shape[0] // sources
+    rows = chunks[0].shape[0]
     here = lax.axis_index("exp")
-    rows_all = packed[:, :width].reshape(sources, rows, width)
+    rows_all = jnp.stack([chunk[:, :width] for chunk in chunks])
 
     def columns(block):
         start = width + block * experts + here * local
-        return lax.dynamic_slice_in_dim(packed, start, local, 1).reshape(sources, rows, local)
+        return jnp.stack([lax.dynamic_slice_in_dim(chunk, start, local, 1) for chunk in chunks])
 
     high, low, named = columns(0), columns(1), columns(2)
     order = jnp.arange(rows, dtype=jnp.int32)
@@ -200,9 +200,9 @@
     normed2 = rms_scale(resid, norm_moe)
     packed = routing(normed2, expert_ids, w_router)
     experts = w_router.shape[1]
-    moe = jnp.concatenate(expert_mix(packed, 1, width, experts, w_gate, w_up, w_down, 2), axis=2)[0]
-    received = jnp.concatenate([shifted(packed, step) for step in range(1, owners)])
-    pieces = expert_mix(received, owners - 1, width, experts, w_gate, w_up, w_down, 2)
+    moe = expert_mix([packed], width, experts, w_gate, w_up, w_down, 1)[0][0]
+    received = [shifted(packed, step) for step in range(1, owners)]
+    pieces = expert_mix(received, width, experts, w_gate, w_up, w_down, 2)
     backs = []
     for piece in pieces:
         piece = piece.astype(jnp.bfloat16)

time: 132 us -> 134 us (1.015)
  waiting for transfers between devices: 34.8 us -> 25.6 us
  matrix products: 39.9 us -> 48.5 us
  local copies, waits for them, and re-layouts: 8.25 us -> 11.4 us
  other arithmetic: 9.89 us -> 8.29 us
    ppermute x18, waiting for transfers between devices: 34.8 us -> 25.6 us  [shifted(): lax.ppermute(x, 'exp', [(j, (j + step) % count) for j in range(count)])]
    dot_general x4 -> x3, matrix products: 4.84 us -> 12.3 us  [expert_mix(): jnp.einsum('becf,efd->becd', hidden, down, preferred_element_type=jnp.flo...]
    dot_general x2 -> x1, matrix products: 10.7 us -> 5.54 us  [expert_mix(): jnp.einsum('becd,edf->becf', received, w_up, preferred_element_type=jnp.f...]
    dot_general x4 -> x3, matrix products: 1.41 us -> 4.99 us  [expert_mix(): jnp.einsum('becr,becd->brd', low, result, preferred_element_type=jnp.floa...]
    dynamic_slice x7 -> x15, local copies, waits for them, and re-layouts: 0.64 us -> 3.89 us  [columns(): lax.dynamic_slice_in_dim(chunk, start, local, 1)]
    another operation x1 -> x4, local copies, waits for them, and re-layouts: 0.12 us -> 3.02 us  [the longest x3 2.91 us: expert_mix(): rows_all = jnp.stack([chunk[:, :width] for chunk in chunks])]
    unnamed x35, local copies, waits for them, and re-layouts: 3.33 us -> 1.35 us
    dot_general x4 -> x3, matrix products: 1.39 us -> 3.36 us  [expert_mix(): jnp.einsum('becr,becd->brd', high, result, preferred_element_type=jnp.flo...]
  transfers between devices with their start and end apart: 19 -> 19, of which waited for: 10 -> 7; matrix products, arithmetic and copies ran while one was open for 29% -> 32% of each run, Pallas kernels for 0% -> 0%
where the time goes in v15:
time: 134 us; the launch traced here: 133 us
  matrix products  48.5 us (36%)
  starting transfers between devices  37.8 us (28%)
  waiting for transfers between devices  25.6 us (19%)
  local copies, waits for them, and re-layouts  11.4 us (9%)
  other arithmetic  8.29 us (6%)
  between operations  1.35 us (1%)
    ppermute x18, starting transfers between devices, shifted(): lax.ppermute(x, 'exp', [(j, (j + step) % count) for j in range(count)])  37.8 us
    ppermute x18, waiting for transfers between devices, shifted(): lax.ppermute(x, 'exp', [(j, (j + step) % count) for j in range(count)])  25.6 us
    dot_general x3, matrix products, expert_mix(): jnp.einsum('becf,efd->becd', hidden, down, preferred_element_type=jnp.flo...  12.3 us
    dot_general x2, matrix products, expert_mix(): jnp.einsum('becd,edf->becf', received, w_gate, preferred_element_type=jnp...  8 us
    dot_general x1, matrix products, expert_mix(): jnp.einsum('becd,edf->becf', received, w_up, preferred_element_type=jnp.f...  5.54 us
    dot_general x3, matrix products, expert_mix(): jnp.einsum('becr,becd->brd', low, result, preferred_element_type=jnp.floa...  4.99 us
    dynamic_slice x15, local copies, waits for them, and re-layouts, columns(): lax.dynamic_slice_in_dim(chunk, start, local, 1)  3.89 us
    sub x1, matrix products, attend(): expo = jnp.exp(score - top)  3.59 us
  transfers between devices with their start and end apart: 19, of which 7 were waited for; matrix products, arithmetic and copies ran while one was open for 32% of the time, Pallas kernels for 0%

profile of v15, /device:TPU:0, one launch (start us, length us, event | category | flops | bytes accessed | tf_op | source)
XLA Modules:
  0.0 132.9 jit_solution(292867948463534627)
XLA Ops:
  0.7 1.8 %constant_dynamic-slice_fusion.15 = bf16[128,1024]{1,0:T(8,128)(2,1)} fusion(bf16[256,1024]{1,0:T(8,128)(2,1)} %param.19, s32[]{:T(128)S(6)} %select_n.176), kind=kLoop, calls=%fused_computation.196 | loop fusion | bytes 524292 | tf_op jit(solution)/shard_map/dynamic_slice | solution.py:132
  2.5 5.1 %collective-permute-start.6 = (bf16[128,1024]{1,0:T(8,128)(2,1)}, bf16[128,1024]{1,0:T(8,128)(2,1)S(1)}, u32[]{:S(2)}, u32[]{:S(2)}) collective-permute-start(bf16[128,1024]{1,0:T(8,128)(2,1)} %constant_dynamic-slice_fusion.15), channel_id=1, source_target_pairs={{0,3},{1,0},{2,1},{3,2},{4,7},{5,4},{6,5},{7,6},{8,11},{9,8},{10,9... | collective-permute-start | bytes 786440 | tf_op jit(solution)/shard_map/ppermute | solution.py:108
  7.6 0.6 multiply_power_fusion
  8.2 0.7 convert_element_type.124
  8.9 1.1 fusion.91
  10.0 1.7 %convolution_convert_fusion.4 = bf16[128,512]{1,0:T(8,128)(2,1)S(1)} fusion(bf16[1024,512]{1,0:T(8,128)(2,1)} %param.18, bf16[128,1024]{1,0:T(8,128)(2,1)} %param.14, f32[1024]{0:T(1024)S(1)} %convert_element_type.124, f32[128]{0:T(128)S(1)} %add_rsqrt_fusion.1), kind=kOutput, calls=%fused_computation.70 | convolution fusion | flops 134807552 | bytes 1446400 | tf_op jit(solution)/shard_map/dot_general | solution.py:169
  11.8 1.9 %fusion.183 = f32[128,512]{0,1:T(8,128)S(1)} fusion(bf16[1024,512]{1,0:T(8,128)(2,1)} %param.17, bf16[128,1024]{1,0:T(8,128)(2,1)} %param.14, f32[1024]{0:T(1024)S(1)} %convert_element_type.124, f32[128]{0:T(128)S(1)} %add_rsqrt_fusion.1), kind=kOutput, calls=%fused_computation.244 | convolution fusion | flops 134742016 | bytes 1577472 | tf_op jit(solution)/shard_map/dot_general | solution.py:166
  13.9 0.3 reduce-window.9
  14.4 0.7 bitcast_subtract_fusion
  15.1 1.0 fusion.185
  16.1 0.8 dynamic-slice_convert_fusion
  16.8 0.8 multiply_cosine_fusion
  17.9 0.5 collective-permute-start.2
  18.4 2.5 %collective-permute-start.1 = (bf16[128,2,256]{0,2,1:T(8,128)(2,1)S(1)}, bf16[128,2,256]{0,2,1:T(8,128)(2,1)S(1)}, u32[]{:S(2)}, u32[]{:S(2)}) collective-permute-start(bf16[128,2,256]{0,2,1:T(8,128)(2,1)S(1)} %get-tuple-element.20), channel_id=1, source_target_pairs={{0,2},{1,3},{2,0},{3,1},{4,6},{5,7},{6,4},{7,5},{8,10},{9,11},{10,... | collective-permute-start | bytes 393224 | tf_op jit(solution)/shard_map/ppermute | solution.py:108
  21.0 1.9 %collective-permute-start = (bf16[128,2,256]{0,2,1:T(8,128)(2,1)S(1)}, bf16[128,2,256]{0,2,1:T(8,128)(2,1)S(1)}, u32[]{:S(2)}, u32[]{:S(2)}) collective-permute-start(bf16[128,2,256]{0,2,1:T(8,128)(2,1)S(1)} %get-tuple-element.21), channel_id=1, source_target_pairs={{0,1},{1,2},{2,3},{3,0},{4,5},{5,6},{6,7},{7,4},{8,9},{9,10},{10,1... | collective-permute-start | bytes 393224 | tf_op jit(solution)/shard_map/ppermute | solution.py:108
  23.3 0.3 compare_and_fusion
  23.8 4.0 %collective-permute-done.2 = bf16[128,2,256]{0,2,1:T(8,128)(2,1)S(1)} collective-permute-done((bf16[128,2,256]{0,2,1:T(8,128)(2,1)S(1)}, bf16[128,2,256]{0,2,1:T(8,128)(2,1)S(1)}, u32[]{:S(2)}, u32[]{:S(2)}) %collective-permute-start.2) | collective-permute-done | bytes 131104 | tf_op jit(solution)/shard_map/ppermute | solution.py:108
  27.8 12.5 %collective-permute-start.4 = (bf16[128,1024]{1,0:T(8,128)(2,1)}, bf16[128,1024]{1,0:T(8,128)(2,1)S(1)}, u32[]{:S(2)}, u32[]{:S(2)}) collective-permute-start(bf16[128,1024]{1,0:T(8,128)(2,1)} %constant_dynamic-slice_fusion.15), channel_id=1, source_target_pairs={{0,1},{1,2},{2,3},{3,0},{4,5},{5,6},{6,7},{7,4},{8,9},{9,10},{10,1... | collective-permute-start | bytes 786440 | tf_op jit(solution)/shard_map/ppermute | solution.py:108
  40.3 1.1 collective-permute-done.1
  41.5 3.6 %fusion.188 = (f32[2,2,512]{2,1,0:T(2,128)S(1)}, f32[2,2,512,512]{2,3,1,0:T(8,128)}) fusion(pred[512,512]{0,1:T(8,128)(4,1)S(1)} %compare_and_fusion, bf16[512,2,2,64]{0,3,2,1:T(8,128)(2,1)S(1)} %bitcast.276, bf16[512,2,256]{0,2,1:T(8,128)(2,1)S(1)} %pad_maximum_fusion.3), kind=kOutput, calls=%fused_computation.247 | convolution fusion | flops 138412544 | bytes 4857856 | tf_op jit(solution)/shard_map/sub | solution.py:44
  45.1 1.0 pad_maximum_fusion
  46.2 2.7 %fusion.73 = bf16[512,2,2,64]{0,3,2,1:T(8,128)(2,1)S(1)} fusion(f32[2,2,512,512]{2,3,1,0:T(8,128)} %get-tuple-element.56, f32[2,2,512]{2,1,0:T(2,128)S(1)} %get-tuple-element.55, bf16[512,2,256]{0,2,1:T(8,128)(2,1)S(1)} %pad_maximum_fusion.3), kind=kOutput, calls=%fused_computation.69 | convolution fusion | flops 136445952 | bytes 4595712 | tf_op jit(solution)/shard_map/kgqt,tkd->qkgd/dot_general | solution.py:46
  49.0 1.8 %collective-permute-start.9 = (bf16[128,256]{0,1:T(8,128)(2,1)S(1)}, bf16[128,256]{0,1:T(8,128)(2,1)S(1)}, u32[]{:S(2)}, u32[]{:S(2)}) collective-permute-start(bf16[128,256]{0,1:T(8,128)(2,1)S(1)} %bitcast.279), channel_id=1, source_target_pairs={{0,1},{1,2},{2,3},{3,0},{4,5},{5,6},{6,7},{7,4},{8,9},{9,10},{10,1... | collective-permute-start | bytes 196616 | tf_op jit(solution)/shard_map/ppermute | solution.py:108
  50.8 2.1 %collective-permute-start.3 = (bf16[128,256]{0,1:T(8,128)(2,1)S(1)}, bf16[128,256]{0,1:T(8,128)(2,1)S(1)}, u32[]{:S(2)}, u32[]{:S(2)}) collective-permute-start(bf16[128,256]{0,1:T(8,128)(2,1)S(1)} %bitcast.280), channel_id=1, source_target_pairs={{0,3},{1,0},{2,1},{3,2},{4,7},{5,4},{6,5},{7,6},{8,11},{9,8},{10,9... | collective-permute-start | bytes 196616 | tf_op jit(solution)/shard_map/ppermute | solution.py:108
  52.9 0.3 convolution_convert_fusion.3
  53.3 1.0 copy.137
  54.2 0.2 fusion.189
  54.5 1.1 broadcast_select_fusion.1
  55.6 1.0 collective-permute-done.3
  56.6 0.3 convolution_add_fusion.1
  56.9 0.2 fusion.101
  57.1 2.0 %collective-permute-done.8 = bf16[128,256]{0,1:T(8,128)(2,1)S(1)} collective-permute-done((bf16[128,256]{0,1:T(8,128)(2,1)S(1)}, bf16[128,256]{0,1:T(8,128)(2,1)S(1)}, u32[]{:S(2)}, u32[]{:S(2)}) %collective-permute-start.8) | collective-permute-done | bytes 65568 | tf_op jit(solution)/shard_map/ppermute | solution.py:108
  59.1 0.4 multiply_reduce_fusion
  60.3 1.8 %collective-permute-start.12 = (bf16[128,1152]{1,0:T(8,128)(2,1)S(1)}, bf16[128,1152]{1,0:T(8,128)(2,1)}, u32[]{:S(2)}, u32[]{:S(2)}) collective-permute-start(bf16[128,1152]{1,0:T(8,128)(2,1)S(1)} %concatenate.44), channel_id=1, source_target_pairs={{0,3},{1,0},{2,1},{3,2},{4,7},{5,4},{6,5},{7,6},{8,11},{9,8},{10,9... | collective-permute-start | bytes 884744 | tf_op jit(solution)/shard_map/ppermute | solution.py:108
  62.2 0.7 collective-permute-start.10
  63.2 0.4 convolution_convert_fusion.2
  63.7 5.9 %convolution_bitcast_fusion.1 = f32[1,8,64,512]{3,2,1,0:T(8,128)} fusion(bf16[8,64,1024]{2,1,0:T(8,128)(2,1)S(1)} %convolution_convert_fusion.2, bf16[8,1024,512]{2,1,0:T(8,128)(2,1)} %param.22), kind=kOutput, calls=%fused_computation.49 | convolution fusion | flops 536870912 | bytes 10485760 | tf_op jit(solution)/shard_map/becd,edf->becf/dot_general | solution.py:86
  69.6 9.1 %convolution_convert_fusion.1 = bf16[8,64,1024]{2,1,0:T(8,128)(2,1)S(1)} fusion(bf16[8,512,1024]{2,1,0:T(8,128)(2,1)} %param.24, bf16[8,64,1024]{2,1,0:T(8,128)(2,1)S(1)} %convolution_convert_fusion.2, bf16[8,1024,512]{2,1,0:T(8,128)(2,1)} %param.23, f32[1,8,64,512]{3,2,1,0:T(8,128)} %convolution_bitcast_fusion.1), kind=kOutput, calls=%fused_computation.37 | convolution fusion | flops 1075838976 | bytes 19922944 | tf_op jit(solution)/shard_map/becf,efd->becd/dot_general | solution.py:96
  78.9 1.2 convolution_bitcast_fusion.2
  80.1 1.0 constant_dynamic-slice_fusion.4
  81.2 5.9 %collective-permute-done.11 = bf16[128,1152]{1,0:T(8,128)(2,1)} collective-permute-done((bf16[128,1152]{1,0:T(8,128)(2,1)S(1)}, bf16[128,1152]{1,0:T(8,128)(2,1)}, u32[]{:S(2)}, u32[]{:S(2)}) %collective-permute-start.11) | collective-permute-done | bytes 294944 | tf_op jit(solution)/shard_map/ppermute | solution.py:108
  87.1 1.0 constant_dynamic-slice_fusion.5
  88.1 1.1 constant_dynamic-slice_fusion.6
  89.4 1.0 slice_bitcast_fusion
  90.4 1.0 slice_bitcast_fusion.1
  91.4 1.0 slice_bitcast_fusion.2
  92.4 1.0 convolution_convert_fusion
  93.4 5.5 %fusion.1 = f32[8,3,64,512]{3,2,1,0:T(8,128)S(1)} fusion(bf16[8,1024,512]{2,1,0:T(8,128)(2,1)} %param.23, bf16[3,8,64,1024]{3,2,1,0:T(8,128)(2,1)S(1)} %convolution_convert_fusion), kind=kOutput, calls=%fused_computation.1 | convolution fusion | flops 1610612736 | bytes 14680064 | tf_op jit(solution)/shard_map/becd,edf->becf/dot_general | solution.py:87
  99.0 2.1 %fusion.12 = bf16[3,8,64,512]{3,2,0,1:T(8,128)(2,1)S(1)} fusion(f32[8,3,64,512]{3,2,1,0:T(8,128)S(1)} %fusion.1, bf16[8,1024,512]{2,1,0:T(8,128)(2,1)S(1)} %bitcast.265, bf16[3,8,64,1024]{3,2,1,0:T(8,128)(2,1)S(1)} %convolution_convert_fusion), kind=kOutput, calls=%fused_computation.16 | convolution fusion | flops 1615331328 | bytes 16252928 | tf_op jit(solution)/shard_map/becd,edf->becf/dot_general | solution.py:86
  101.0 0.3 slice-done.3
  101.3 2.2 %fusion.28 = bf16[3,8,64,512]{3,2,0,1:T(8,128)(2,1)} fusion(bf16[3,8,64,512]{3,2,0,1:T(8,128)(2,1)S(1)} %fusion.12, bf16[8,512,1024]{2,1,0:T(8,128)(2,1)S(1)} %bitcast.267), kind=kOutput, calls=%fused_computation.35 | convolution fusion | flops 806092800 | bytes 7340032 | tf_op jit(solution)/shard_map/becf,efd->becd/dot_general | solution.py:96
  103.5 1.0 fusion.31
  105.0 1.9 %fusion.50 = f32[3,128,512]{2,1,0:T(8,128)S(1)} fusion(bf16[3,8,64,512]{3,2,0,1:T(8,128)(2,1)} %fusion.28, s32[3,8,128]{2,1,0:T(8,128)S(1)} %convolution_convert_fusion.5, pred[3,8,128]{2,1,0:T(8,128)(4,1)S(1)} %compare_bitcast_fusion.1, bf16[3,8,128]{2,1,0:T(8,128)(2,1)S(1)} %maximum_bitcast_fusion.2), kind=kOutput, calls=%fused_computation.53 | convolution fusion | flops 201916416 | bytes 2380800 | tf_op jit(solution)/shard_map/becr,becd->brd/dot_general | solution.py:98
  106.9 1.8 %fusion.65 = bf16[3,128,512]{2,1,0:T(8,128)(2,1)S(1)} fusion(f32[3,128,512]{2,1,0:T(8,128)S(1)} %fusion.50, bf16[3,8,64,512]{3,2,0,1:T(8,128)(2,1)} %fusion.28, s32[3,8,128]{2,1,0:T(8,128)S(1)} %convolution_convert_fusion.5, pred[3,8,128]{2,1,0:T(8,128)(4,1)S(1)} %compare_bitcast_fusion.1, bf16[3,8,128]{2,1,0:T(8,128)(2,1)S(1)} %maximum_bitcast_fusion.3), kind=kOutput, calls=%fused_computation.58 | convolution fusion | flops 202309632 | bytes 2774016 | tf_op jit(solution)/shard_map/becr,becd->brd/dot_general | solution.py:99
  108.8 1.2 collective-permute-start.17
  110.0 2.8 %collective-permute-start.16 = (bf16[128,512]{1,0:T(8,128)(2,1)S(1)}, bf16[128,512]{1,0:T(8,128)(2,1)S(1)}, u32[]{:S(2)}, u32[]{:S(2)}) collective-permute-start(bf16[128,512]{1,0:T(8,128)(2,1)S(1)} %get-tuple-element.25), channel_id=1, source_target_pairs={{0,3},{1,0},{2,1},{3,2},{4,7},{5,4},{6,5},{7,6},{8,11},{9,8},{10,9... | collective-permute-start | bytes 393224 | tf_op jit(solution)/shard_map/ppermute | solution.py:108
  112.9 0.4 fusion.44
  113.3 2.0 %fusion.62 = bf16[3,128,512]{2,1,0:T(8,128)(2,1)S(1)} fusion(f32[3,128,512]{2,1,0:T(8,128)S(1)} %fusion.44, bf16[3,8,64,512]{3,2,0,1:T(8,128)(2,1)} %copy-done.12, s32[3,8,128]{2,1,0:T(8,128)S(1)} %convolution_convert_fusion.5, pred[3,8,128]{2,1,0:T(8,128)(4,1)S(1)} %compare_bitcast_fusion.1, bf16[3,8,128]{2,1,0:T(8,128)(2,1)S(1)} %maximum_bitcast_fusion.3), kind=kOutput, calls=%fused_computation.57 | convolution fusion | flops 202309632 | bytes 2774016 | tf_op jit(solution)/shard_map/becr,becd->brd/dot_general | solution.py:99
  115.3 0.4 collective-permute-start.15
  115.7 1.5 %collective-permute-start.14 = (bf16[128,512]{1,0:T(8,128)(2,1)S(1)}, bf16[128,512]{1,0:T(8,128)(2,1)S(1)}, u32[]{:S(2)}, u32[]{:S(2)}) collective-permute-start(bf16[128,512]{1,0:T(8,128)(2,1)S(1)} %get-tuple-element.24), channel_id=1, source_target_pairs={{0,2},{1,3},{2,0},{3,1},{4,6},{5,7},{6,4},{7,5},{8,10},{9,11},{10,... | collective-permute-start | bytes 393224 | tf_op jit(solution)/shard_map/ppermute | solution.py:108
  117.3 2.8 %collective-permute-start.13 = (bf16[128,512]{1,0:T(8,128)(2,1)S(1)}, bf16[128,512]{1,0:T(8,128)(2,1)S(1)}, u32[]{:S(2)}, u32[]{:S(2)}) collective-permute-start(bf16[128,512]{1,0:T(8,128)(2,1)S(1)} %get-tuple-element.22), channel_id=1, source_target_pairs={{0,3},{1,0},{2,1},{3,2},{4,7},{5,4},{6,5},{7,6},{8,11},{9,8},{10,9... | collective-permute-start | bytes 393224 | tf_op jit(solution)/shard_map/ppermute | solution.py:108
  120.1 4.7 %collective-permute-done.17 = bf16[128,512]{1,0:T(8,128)(2,1)S(1)} collective-permute-done((bf16[128,512]{1,0:T(8,128)(2,1)S(1)}, bf16[128,512]{1,0:T(8,128)(2,1)S(1)}, u32[]{:S(2)}, u32[]{:S(2)}) %collective-permute-start.17) | collective-permute-done | bytes 131104 | tf_op jit(solution)/shard_map/ppermute | solution.py:108
  124.8 6.9 %collective-permute-done.14 = bf16[128,512]{1,0:T(8,128)(2,1)S(1)} collective-permute-done((bf16[128,512]{1,0:T(8,128)(2,1)S(1)}, bf16[128,512]{1,0:T(8,128)(2,1)S(1)}, u32[]{:S(2)}, u32[]{:S(2)}) %collective-permute-start.14) | collective-permute-done | bytes 131104 | tf_op jit(solution)/shard_map/ppermute | solution.py:108
  131.8 1.1 fusion.105
  (119 shorter events, 4.1 us)
Async XLA Ops:
  0.6 14.4 %copy-start = (bf16[1024,1024]{1,0:T(8,128)(2,1)S(1)}, bf16[1024,1024]{1,0:T(8,128)(2,1)}, u32[]{:S(2)}) copy-start(bf16[1024,1024]{1,0:T(8,128)(2,1)} %param.16) | copy-start | bytes 6291460
  0.6 14.4 %copy-start.2 = (bf16[128,1024]{1,0:T(8,128)(2,1)S(1)}, bf16[128,1024]{1,0:T(8,128)(2,1)}, u32[]{:S(2)}) copy-start(bf16[128,1024]{1,0:T(8,128)(2,1)} %param.14) | copy-start | bytes 786436
  0.7 13.0 %copy-start.9 = (s32[1,512]{1,0:T(1,128)S(1)}, s32[1,512]{1,0:T(1,128)}, u32[]{:S(2)}) copy-start(s32[1,512]{1,0:T(1,128)} %param.25) | copy-start | bytes 6148
  2.5 42.6 %collective-permute-start.6 = (bf16[128,1024]{1,0:T(8,128)(2,1)}, bf16[128,1024]{1,0:T(8,128)(2,1)S(1)}, u32[]{:S(2)}, u32[]{:S(2)}) collective-permute-start(bf16[128,1024]{1,0:T(8,128)(2,1)} %constant_dynamic-slice_fusion.15), channel_id=1, source_target_pairs={{0,3},{1,0},{2,1},{3,2},{4,7},{5,4},{6,5},{7,6},{8,11},{9,8},{10,9... | collective-permute-start | bytes 786440 | tf_op jit(solution)/shard_map/ppermute | solution.py:108
  7.6 37.5 %collective-permute-start.5 = (bf16[128,1024]{1,0:T(8,128)(2,1)}, bf16[128,1024]{1,0:T(8,128)(2,1)}, u32[]{:S(2)}, u32[]{:S(2)}) collective-permute-start(bf16[128,1024]{1,0:T(8,128)(2,1)} %constant_dynamic-slice_fusion.15), channel_id=1, source_target_pairs={{0,2},{1,3},{2,0},{3,1},{4,6},{5,7},{6,4},{7,5},{8,10},{9,11},{10,... | collective-permute-start | bytes 786440 | tf_op jit(solution)/shard_map/ppermute | solution.py:108
  15.1 8.2 %copy-start.8 = (s32[128,8]{0,1:T(8,128)S(1)}, s32[128,8]{0,1:T(8,128)}, u32[]{:S(2)}) copy-start(s32[128,8]{0,1:T(8,128)} %param.27) | copy-start | bytes 12292
  16.1 7.5 %copy-start.10 = (s32[1,512]{1,0:T(1,128)S(1)}, s32[1,512]{1,0:T(1,128)}, u32[]{:S(2)}) copy-start(s32[1,512]{1,0:T(1,128)} %param.26) | copy-start | bytes 6148
  16.1 7.6 %copy-start.11 = (bf16[1024]{0:T(1024)(128)(2,1)S(1)}, bf16[1024]{0:T(1024)(128)(2,1)}, u32[]{:S(2)}) copy-start(bf16[1024]{0:T(1024)(128)(2,1)} %param.20) | copy-start | bytes 6148
  17.9 9.9 %collective-permute-start.2 = (bf16[128,2,256]{0,2,1:T(8,128)(2,1)S(1)}, bf16[128,2,256]{0,2,1:T(8,128)(2,1)S(1)}, u32[]{:S(2)}, u32[]{:S(2)}) collective-permute-start(bf16[128,2,256]{0,2,1:T(8,128)(2,1)S(1)} %get-tuple-element.19), channel_id=1, source_target_pairs={{0,3},{1,0},{2,1},{3,2},{4,7},{5,4},{6,5},{7,6},{8,11},{9,8},{10,9... | collective-permute-start | bytes 393224 | tf_op jit(solution)/shard_map/ppermute | solution.py:108
  18.4 22.9 %collective-permute-start.1 = (bf16[128,2,256]{0,2,1:T(8,128)(2,1)S(1)}, bf16[128,2,256]{0,2,1:T(8,128)(2,1)S(1)}, u32[]{:S(2)}, u32[]{:S(2)}) collective-permute-start(bf16[128,2,256]{0,2,1:T(8,128)(2,1)S(1)} %get-tuple-element.20), channel_id=1, source_target_pairs={{0,2},{1,3},{2,0},{3,1},{4,6},{5,7},{6,4},{7,5},{8,10},{9,11},{10,... | collective-permute-start | bytes 393224 | tf_op jit(solution)/shard_map/ppermute | solution.py:108
  21.0 20.4 %collective-permute-start = (bf16[128,2,256]{0,2,1:T(8,128)(2,1)S(1)}, bf16[128,2,256]{0,2,1:T(8,128)(2,1)S(1)}, u32[]{:S(2)}, u32[]{:S(2)}) collective-permute-start(bf16[128,2,256]{0,2,1:T(8,128)(2,1)S(1)} %get-tuple-element.21), channel_id=1, source_target_pairs={{0,1},{1,2},{2,3},{3,0},{4,5},{5,6},{6,7},{7,4},{8,9},{9,10},{10,1... | collective-permute-start | bytes 393224 | tf_op jit(solution)/shard_map/ppermute | solution.py:108
  27.8 17.3 %collective-permute-start.4 = (bf16[128,1024]{1,0:T(8,128)(2,1)}, bf16[128,1024]{1,0:T(8,128)(2,1)S(1)}, u32[]{:S(2)}, u32[]{:S(2)}) collective-permute-start(bf16[128,1024]{1,0:T(8,128)(2,1)} %constant_dynamic-slice_fusion.15), channel_id=1, source_target_pairs={{0,1},{1,2},{2,3},{3,0},{4,5},{5,6},{6,7},{7,4},{8,9},{9,10},{10,1... | collective-permute-start | bytes 786440 | tf_op jit(solution)/shard_map/ppermute | solution.py:108
  46.1 8.4 %collective-permute-start.7 = (bf16[3,128,1024]{2,1,0:T(8,128)(2,1)S(1)}, bf16[3,128,1024]{2,1,0:T(8,128)(2,1)S(1)}, u32[]{:S(2)}, u32[]{:S(2)}) collective-permute-start(bf16[3,128,1024]{2,1,0:T(8,128)(2,1)S(1)} %pad_maximum_fusion), channel_id=1, source_target_pairs={{0,4},{4,0},{8,12},{12,8},{16,20},{20,16},{24,28},{28,24},{1,5},{5... | collective-permute-start | bytes 2359304 | tf_op jit(solution)/shard_map/ppermute | solution.py:134
  46.2 8.0 %copy-start.6 = (bf16[256,1024]{1,0:T(8,128)(2,1)S(1)}, bf16[256,1024]{1,0:T(8,128)(2,1)}, u32[]{:S(2)}) copy-start(bf16[256,1024]{1,0:T(8,128)(2,1)} %param.19) | copy-start | bytes 1572868
  49.0 7.8 %collective-permute-start.9 = (bf16[128,256]{0,1:T(8,128)(2,1)S(1)}, bf16[128,256]{0,1:T(8,128)(2,1)S(1)}, u32[]{:S(2)}, u32[]{:S(2)}) collective-permute-start(bf16[128,256]{0,1:T(8,128)(2,1)S(1)} %bitcast.279), channel_id=1, source_target_pairs={{0,1},{1,2},{2,3},{3,0},{4,5},{5,6},{6,7},{7,4},{8,9},{9,10},{10,1... | collective-permute-start | bytes 196616 | tf_op jit(solution)/shard_map/ppermute | solution.py:108
  50.8 5.7 %collective-permute-start.3 = (bf16[128,256]{0,1:T(8,128)(2,1)S(1)}, bf16[128,256]{0,1:T(8,128)(2,1)S(1)}, u32[]{:S(2)}, u32[]{:S(2)}) collective-permute-start(bf16[128,256]{0,1:T(8,128)(2,1)S(1)} %bitcast.280), channel_id=1, source_target_pairs={{0,3},{1,0},{2,1},{3,2},{4,7},{5,4},{6,5},{7,6},{8,11},{9,8},{10,9... | collective-permute-start | bytes 196616 | tf_op jit(solution)/shard_map/ppermute | solution.py:108
  52.9 6.2 %collective-permute-start.8 = (bf16[128,256]{0,1:T(8,128)(2,1)S(1)}, bf16[128,256]{0,1:T(8,128)(2,1)S(1)}, u32[]{:S(2)}, u32[]{:S(2)}) collective-permute-start(bf16[128,256]{0,1:T(8,128)(2,1)S(1)} %bitcast.278), channel_id=1, source_target_pairs={{0,2},{1,3},{2,0},{3,1},{4,6},{5,7},{6,4},{7,5},{8,10},{9,11},{10,... | collective-permute-start | bytes 196616 | tf_op jit(solution)/shard_map/ppermute | solution.py:108
  56.8 2.8 %copy-start.7 = (bf16[1024,32]{0,1:T(8,128)(2,1)S(1)}, bf16[1024,32]{0,1:T(8,128)(2,1)}, u32[]{:S(2)}) copy-start(bf16[1024,32]{0,1:T(8,128)(2,1)} %param.21) | copy-start | bytes 196612
  59.5 10.2 %copy-start.3 = (f32[128,1024]{1,0:T(8,128)}, f32[128,1024]{1,0:T(8,128)S(1)}, u32[]{:S(2)}) copy-start(f32[128,1024]{1,0:T(8,128)S(1)} %get-tuple-element.58) | copy-start | bytes 1572868
  60.3 19.8 %collective-permute-start.12 = (bf16[128,1152]{1,0:T(8,128)(2,1)S(1)}, bf16[128,1152]{1,0:T(8,128)(2,1)}, u32[]{:S(2)}, u32[]{:S(2)}) collective-permute-start(bf16[128,1152]{1,0:T(8,128)(2,1)S(1)} %concatenate.44), channel_id=1, source_target_pairs={{0,3},{1,0},{2,1},{3,2},{4,7},{5,4},{6,5},{7,6},{8,11},{9,8},{10,9... | collective-permute-start | bytes 884744 | tf_op jit(solution)/shard_map/ppermute | solution.py:108
  62.2 24.9 %collective-permute-start.11 = (bf16[128,1152]{1,0:T(8,128)(2,1)S(1)}, bf16[128,1152]{1,0:T(8,128)(2,1)}, u32[]{:S(2)}, u32[]{:S(2)}) collective-permute-start(bf16[128,1152]{1,0:T(8,128)(2,1)S(1)} %concatenate.44), channel_id=1, source_target_pairs={{0,2},{1,3},{2,0},{3,1},{4,6},{5,7},{6,4},{7,5},{8,10},{9,11},{10,... | collective-permute-start | bytes 884744 | tf_op jit(solution)/shard_map/ppermute | solution.py:108
  62.2 25.9 %collective-permute-start.10 = (bf16[128,1152]{1,0:T(8,128)(2,1)S(1)}, bf16[128,1152]{1,0:T(8,128)(2,1)}, u32[]{:S(2)}, u32[]{:S(2)}) collective-permute-start(bf16[128,1152]{1,0:T(8,128)(2,1)S(1)} %concatenate.44), channel_id=1, source_target_pairs={{0,1},{1,2},{2,3},{3,0},{4,5},{5,6},{6,7},{7,4},{8,9},{9,10},{10,1... | collective-permute-start | bytes 884744 | tf_op jit(solution)/shard_map/ppermute | solution.py:108
  92.4 6.6 %slice-start = ((s8[8388608]{0:T(1024)(128)(4,1)}), s8[4194304]{0:T(1024)(128)(4,1)S(1)}, s32[]{:S(2)}) async-start(s8[8388608]{0:T(1024)(128)(4,1)} %bitcast.264), calls=%async_computation | async-start | bytes 8388608
  93.3 5.6 %slice-start.1 = ((s8[8388608]{0:T(1024)(128)(4,1)}), s8[4194304]{0:T(1024)(128)(4,1)S(1)}, s32[]{:S(2)}) async-start(s8[8388608]{0:T(1024)(128)(4,1)} %bitcast.264), calls=%async_computation.1 | async-start | bytes 8388608
  93.4 7.7 %slice-start.2 = ((s8[8388608]{0:T(1024)(128)(4,1)}), s8[4194304]{0:T(1024)(128)(4,1)S(1)}, s32[]{:S(2)}) async-start(s8[8388608]{0:T(1024)(128)(4,1)} %bitcast.266), calls=%async_computation.2 | async-start | bytes 8388608
  98.9 2.4 %slice-start.3 = ((s8[8388608]{0:T(1024)(128)(4,1)}), s8[4194304]{0:T(1024)(128)(4,1)S(1)}, s32[]{:S(2)}) async-start(s8[8388608]{0:T(1024)(128)(4,1)} %bitcast.266), calls=%async_computation.3 | async-start | bytes 8388608
  104.5 8.4 %copy-start.12 = (bf16[3,8,64,512]{3,2,0,1:T(8,128)(2,1)}, bf16[3,8,64,512]{3,2,0,1:T(8,128)(2,1)S(1)}, u32[]{:S(2)}) copy-start(bf16[3,8,64,512]{3,2,0,1:T(8,128)(2,1)S(1)} %fusion.31) | copy-start | bytes 4718596
  108.7 8.5 %collective-permute-start.18 = (bf16[128,512]{1,0:T(8,128)(2,1)S(1)}, bf16[128,512]{1,0:T(8,128)(2,1)S(1)}, u32[]{:S(2)}, u32[]{:S(2)}) collective-permute-start(bf16[128,512]{1,0:T(8,128)(2,1)S(1)} %get-tuple-element.26), channel_id=1, source_target_pairs={{0,1},{1,2},{2,3},{3,0},{4,5},{5,6},{6,7},{7,4},{8,9},{9,10},{10,1... | collective-permute-start | bytes 393224 | tf_op jit(solution)/shard_map/ppermute | solution.py:108
  108.8 16.0 %collective-permute-start.17 = (bf16[128,512]{1,0:T(8,128)(2,1)S(1)}, bf16[128,512]{1,0:T(8,128)(2,1)S(1)}, u32[]{:S(2)}, u32[]{:S(2)}) collective-permute-start(bf16[128,512]{1,0:T(8,128)(2,1)S(1)} %get-tuple-element.27), channel_id=1, source_target_pairs={{0,2},{1,3},{2,0},{3,1},{4,6},{5,7},{6,4},{7,5},{8,10},{9,11},{10,... | collective-permute-start | bytes 393224 | tf_op jit(solution)/shard_map/ppermute | solution.py:108
  110.0 14.8 %collective-permute-start.16 = (bf16[128,512]{1,0:T(8,128)(2,1)S(1)}, bf16[128,512]{1,0:T(8,128)(2,1)S(1)}, u32[]{:S(2)}, u32[]{:S(2)}) collective-permute-start(bf16[128,512]{1,0:T(8,128)(2,1)S(1)} %get-tuple-element.25), channel_id=1, source_target_pairs={{0,3},{1,0},{2,1},{3,2},{4,7},{5,4},{6,5},{7,6},{8,11},{9,8},{10,9... | collective-permute-start | bytes 393224 | tf_op jit(solution)/shard_map/ppermute | solution.py:108
  113.3 18.5 %copy-start.4 = (f32[128,1024]{1,0:T(8,128)S(1)}, f32[128,1024]{1,0:T(8,128)}, u32[]{:S(2)}) copy-start(f32[128,1024]{1,0:T(8,128)} %copy-done.3) | copy-start | bytes 1572868
  113.3 18.5 %copy-start.5 = (f32[128,1024]{1,0:T(8,128)S(1)}, f32[128,1024]{1,0:T(8,128)}, u32[]{:S(2)}) copy-start(f32[128,1024]{1,0:T(8,128)} %convolution_bitcast_fusion.2) | copy-start | bytes 1572868
  113.3 19.6 %copy-start.1 = (bf16[1024,1024]{1,0:T(8,128)(2,1)S(1)}, bf16[1024,1024]{1,0:T(8,128)(2,1)}, u32[]{:S(2)}) copy-start(bf16[1024,1024]{1,0:T(8,128)(2,1)} %param.16) | copy-start | bytes 6291460
  115.3 9.5 %collective-permute-start.15 = (bf16[128,512]{1,0:T(8,128)(2,1)S(1)}, bf16[128,512]{1,0:T(8,128)(2,1)S(1)}, u32[]{:S(2)}, u32[]{:S(2)}) collective-permute-start(bf16[128,512]{1,0:T(8,128)(2,1)S(1)} %get-tuple-element.23), channel_id=1, source_target_pairs={{0,1},{1,2},{2,3},{3,0},{4,5},{5,6},{6,7},{7,4},{8,9},{9,10},{10,1... | collective-permute-start | bytes 393224 | tf_op jit(solution)/shard_map/ppermute | solution.py:108
  115.7 16.0 %collective-permute-start.14 = (bf16[128,512]{1,0:T(8,128)(2,1)S(1)}, bf16[128,512]{1,0:T(8,128)(2,1)S(1)}, u32[]{:S(2)}, u32[]{:S(2)}) collective-permute-start(bf16[128,512]{1,0:T(8,128)(2,1)S(1)} %get-tuple-element.24), channel_id=1, source_target_pairs={{0,2},{1,3},{2,0},{3,1},{4,6},{5,7},{6,4},{7,5},{8,10},{9,11},{10,... | collective-permute-start | bytes 393224 | tf_op jit(solution)/shard_map/ppermute | solution.py:108
  117.3 14.5 %collective-permute-start.13 = (bf16[128,512]{1,0:T(8,128)(2,1)S(1)}, bf16[128,512]{1,0:T(8,128)(2,1)S(1)}, u32[]{:S(2)}, u32[]{:S(2)}) collective-permute-start(bf16[128,512]{1,0:T(8,128)(2,1)S(1)} %get-tuple-element.22), channel_id=1, source_target_pairs={{0,3},{1,0},{2,1},{3,2},{4,7},{5,4},{6,5},{7,6},{8,11},{9,8},{10,9... | collective-permute-start | bytes 393224 | tf_op jit(solution)/shard_map/ppermute | solution.py:108

commit v16 on v11

--- a/solution.py
+++ b/solution.py
@@ -124,17 +124,18 @@
     return jnp.concatenate(parts)
 
 
-def gather_w_out(w_out):
+def gather_w_out(w_out, extra):
     count = lax.axis_size("exp")
     mates = lax.axis_size("req")
     part = lax.axis_index("req") % 2
     cut = w_out.shape[0] // 2
-    mine = lax.dynamic_slice_in_dim(w_out, part * cut, cut, 0)
+    mine = jnp.concatenate([lax.dynamic_slice_in_dim(w_out, part * cut, cut, 0), extra])
     got = jnp.stack([shifted(mine, step) for step in range(1, count)])
+    names, got = got[:, cut:], got[:, :cut]
     other = lax.ppermute(got, "req", [(j, j ^ 1) for j in range(mates)])
     lower = jnp.where(part == 0, got, other)
     upper = jnp.where(part == 0, other, got)
-    return jnp.concatenate([lower, upper], axis=1)
+    return jnp.concatenate([lower, upper], axis=1), names
 
 
 def shards(
@@ -189,7 +190,10 @@
     seg_rows = step_rows(seg, rows)
     heads_out = attend(query_heads, keyval_heads, seg_rows, seg_rows, where_at, where_at)
     blocks = heads_out.reshape(owners, rows, -1)
-    remote = gather_w_out(w_out)
+    topk = expert_ids.shape[1]
+    flat = expert_ids.T.reshape(-1).astype(jnp.bfloat16)
+    flat = jnp.pad(flat, (0, (-flat.shape[0]) % width)).reshape(-1, width)
+    remote, names = gather_w_out(w_out, flat)
     attention = jnp.dot(blocks[0], w_out, preferred_element_type=jnp.float32)
     for step in range(1, owners):
         got = shifted(blocks[step], -step)
@@ -201,7 +205,11 @@
     packed = routing(normed2, expert_ids, w_router)
     experts = w_router.shape[1]
     moe = expert_mix(packed, 1, width, experts, w_gate, w_up, w_down, 1)[0][0]
-    received = jnp.concatenate([shifted(packed, step) for step in range(1, owners)])
+    received = []
+    for step in range(1, owners):
+        ids = names[step - 1].reshape(-1)[: topk * rows].reshape(topk, rows).T.astype(jnp.int32)
+        received.append(routing(shifted(normed2, step), ids, w_router))
+    received = jnp.concatenate(received)
     pieces = expert_mix(received, owners - 1, width, experts, w_gate, w_up, w_down, 2)
     backs = []
     for piece in pieces:

time: 128 us -> 134 us (1.047)
  local copies, waits for them, and re-layouts: 8.24 us -> 13.3 us
  matrix products: 45.5 us -> 49 us
  starting transfers between devices: 41.7 us -> 39.4 us
    concatenate x1 -> x4, local copies, waits for them, and re-layouts: 0.13 us -> 3.33 us  [routing(): return jnp.concatenate([normed2, high, low, named, fill], axis=1)]
    ppermute x18, starting transfers between devices: 41.6 us -> 39.4 us  [shifted(): lax.ppermute(x, 'exp', [(j, (j + step) % count) for j in range(count)])]
    ppermute x18, waiting for transfers between devices: 22.2 us -> 20.4 us  [shifted(): lax.ppermute(x, 'exp', [(j, (j + step) % count) for j in range(count)])]
    convert_element_type x1 -> x4, local copies, waits for them, and re-layouts: 0.12 us -> 1.66 us  [routing(): named = jnp.any(match, axis=1).astype(jnp.bfloat16)]
    dot_general x1 -> x4, matrix products: 0.17 us -> 1.64 us  [routing(): logits = jnp.dot(normed2, w_router, preferred_element_type=jnp.float32)]
    dynamic_slice x7, local copies, waits for them, and re-layouts: 0.61 us -> 2.06 us  [columns(): lax.dynamic_slice_in_dim(packed, start, local, 1)]
    unnamed x39 -> x54, local copies, waits for them, and re-layouts: 3.35 us -> 2.1 us
  transfers between devices with their start and end apart: 19 -> 19, of which waited for: 7 -> 7; matrix products, arithmetic and copies ran while one was open for 32% -> 36% of each run, Pallas kernels for 0% -> 0%
where the time goes in v16:
time: 134 us
  matrix products  49 us (37%)
  starting transfers between devices  39.4 us (29%)
  waiting for transfers between devices  21.2 us (16%)
  local copies, waits for them, and re-layouts  13.3 us (10%)
  other arithmetic  9.25 us (7%)
  between operations  1.59 us (1%)
    ppermute x18, starting transfers between devices, shifted(): lax.ppermute(x, 'exp', [(j, (j + step) % count) for j in range(count)])  39.4 us
    ppermute x18, waiting for transfers between devices, shifted(): lax.ppermute(x, 'exp', [(j, (j + step) % count) for j in range(count)])  20.4 us
    dot_general x3, matrix products, expert_mix(): jnp.einsum('becf,efd->becd', hidden, down, preferred_element_type=jnp.flo...  12.2 us
    dot_general x2, matrix products, expert_mix(): jnp.einsum('becd,edf->becf', received, w_gate, preferred_element_type=jnp...  8 us
    dot_general x1, matrix products, expert_mix(): jnp.einsum('becd,edf->becf', received, w_up, preferred_element_type=jnp.f...  5.54 us
    dot_general x3, matrix products, expert_mix(): jnp.einsum('becr,becd->brd', low, result, preferred_element_type=jnp.floa...  4.09 us
    sub x1, matrix products, attend(): expo = jnp.exp(score - top)  3.56 us
    concatenate x4, local copies, waits for them, and re-layouts, routing(): return jnp.concatenate([normed2, high, low, named, fill], axis=1)  3.33 us
  transfers between devices with their start and end apart: 19, of which 7 were waited for; matrix products, arithmetic and copies ran while one was open for 36% of the time, Pallas kernels for 0%

profile of v16, /device:TPU:0, one launch (start us, length us, event | category | flops | bytes accessed | tf_op | source)
XLA Modules:
  0.0 133.8 jit_solution(18442188690321151935)
XLA Ops:
  0.7 0.8 convert_bitcast_fusion
  1.5 1.0 constant_dynamic-slice_fusion.9
  2.5 0.7 pad_maximum_fusion.6
  3.2 5.1 %collective-permute-start.6 = (bf16[129,1024]{1,0:T(8,128)(2,1)}, bf16[129,1024]{1,0:T(8,128)(2,1)S(1)}, u32[]{:S(2)}, u32[]{:S(2)}) collective-permute-start(bf16[129,1024]{1,0:T(8,128)(2,1)} %pad_maximum_fusion.6), channel_id=1, source_target_pairs={{0,3},{1,0},{2,1},{3,2},{4,7},{5,4},{6,5},{7,6},{8,11},{9,8},{10,9... | collective-permute-start | bytes 792584 | tf_op jit(solution)/shard_map/ppermute | solution.py:108
  8.4 0.7 convert_element_type.203
  9.0 1.1 fusion.87
  10.1 1.7 %convolution_convert_fusion.4 = bf16[128,512]{1,0:T(8,128)(2,1)S(1)} fusion(bf16[1024,512]{1,0:T(8,128)(2,1)} %param.18, bf16[128,1024]{1,0:T(8,128)(2,1)} %param.14, f32[1024]{0:T(1024)S(1)} %convert_element_type.203, f32[128]{0:T(128)S(1)} %add_rsqrt_fusion.1), kind=kOutput, calls=%fused_computation.70 | convolution fusion | flops 134807552 | bytes 1446400 | tf_op jit(solution)/shard_map/dot_general | solution.py:170
  11.8 0.8 copy.122
  12.6 2.5 %fusion.186 = f32[128,512]{0,1:T(8,128)} fusion(bf16[1024,512]{1,0:T(8,128)(2,1)} %param.17, bf16[128,1024]{1,0:T(8,128)(2,1)S(1)} %copy-done.2, f32[1024]{0:T(1024)S(1)} %convert_element_type.203, f32[128]{0:T(128)S(1)} %add_rsqrt_fusion.1), kind=kOutput, calls=%fused_computation.257 | convolution fusion | flops 134742016 | bytes 1577472 | tf_op jit(solution)/shard_map/dot_general | solution.py:167
  15.3 0.3 reduce-window.9
  15.9 1.0 fusion.188
  17.1 1.0 subtract_convert_fusion.1
  18.3 0.9 pad_maximum_fusion.4
  19.3 0.5 collective-permute-start.2
  19.8 2.5 %collective-permute-start.1 = (bf16[128,2,256]{0,2,1:T(8,128)(2,1)S(1)}, bf16[128,2,256]{0,2,1:T(8,128)(2,1)S(1)}, u32[]{:S(2)}, u32[]{:S(2)}) collective-permute-start(bf16[128,2,256]{0,2,1:T(8,128)(2,1)S(1)} %get-tuple-element.29), channel_id=1, source_target_pairs={{0,2},{1,3},{2,0},{3,1},{4,6},{5,7},{6,4},{7,5},{8,10},{9,11},{10,... | collective-permute-start | bytes 393224 | tf_op jit(solution)/shard_map/ppermute | solution.py:108
  22.3 1.9 %collective-permute-start = (bf16[128,2,256]{0,2,1:T(8,128)(2,1)S(1)}, bf16[128,2,256]{0,2,1:T(8,128)(2,1)S(1)}, u32[]{:S(2)}, u32[]{:S(2)}) collective-permute-start(bf16[128,2,256]{0,2,1:T(8,128)(2,1)S(1)} %get-tuple-element.30), channel_id=1, source_target_pairs={{0,1},{1,2},{2,3},{3,0},{4,5},{5,6},{6,7},{7,4},{8,9},{9,10},{10,1... | collective-permute-start | bytes 393224 | tf_op jit(solution)/shard_map/ppermute | solution.py:108
  25.1 4.4 %collective-permute-done.2 = bf16[128,2,256]{0,2,1:T(8,128)(2,1)S(1)} collective-permute-done((bf16[128,2,256]{0,2,1:T(8,128)(2,1)S(1)}, bf16[128,2,256]{0,2,1:T(8,128)(2,1)S(1)}, u32[]{:S(2)}, u32[]{:S(2)}) %collective-permute-start.2) | collective-permute-done | bytes 131104 | tf_op jit(solution)/shard_map/ppermute | solution.py:108
  29.6 12.8 %collective-permute-start.4 = (bf16[129,1024]{1,0:T(8,128)(2,1)}, bf16[129,1024]{1,0:T(8,128)(2,1)S(1)}, u32[]{:S(2)}, u32[]{:S(2)}) collective-permute-start(bf16[129,1024]{1,0:T(8,128)(2,1)} %pad_maximum_fusion.6), channel_id=1, source_target_pairs={{0,1},{1,2},{2,3},{3,0},{4,5},{5,6},{6,7},{7,4},{8,9},{9,10},{10,1... | collective-permute-start | bytes 792584 | tf_op jit(solution)/shard_map/ppermute | solution.py:108
  42.4 1.1 collective-permute-done.1
  43.6 3.6 %fusion.191 = (f32[2,2,512]{2,1,0:T(2,128)S(1)}, f32[2,2,512,512]{2,3,1,0:T(8,128)}) fusion(pred[512,512]{0,1:T(8,128)(4,1)S(1)} %compare_and_fusion, bf16[512,2,2,64]{0,3,2,1:T(8,128)(2,1)S(1)} %bitcast.297, bf16[512,2,256]{0,2,1:T(8,128)(2,1)S(1)} %pad_maximum_fusion.5), kind=kOutput, calls=%fused_computation.260 | convolution fusion | flops 138412544 | bytes 4857856 | tf_op jit(solution)/shard_map/sub | solution.py:44
  47.2 2.7 %fusion.73 = bf16[512,2,2,64]{0,3,2,1:T(8,128)(2,1)S(1)} fusion(f32[2,2,512,512]{2,3,1,0:T(8,128)} %get-tuple-element.56, f32[2,2,512]{2,1,0:T(2,128)S(1)} %get-tuple-element.55, bf16[512,2,256]{0,2,1:T(8,128)(2,1)S(1)} %pad_maximum_fusion.5), kind=kOutput, calls=%fused_computation.69 | convolution fusion | flops 136445952 | bytes 4595712 | tf_op jit(solution)/shard_map/kgqt,tkd->qkgd/dot_general | solution.py:46
  49.9 0.7 fusion.190
  50.9 3.9 %collective-permute-start.3 = (bf16[128,256]{0,1:T(8,128)(2,1)}, bf16[128,256]{0,1:T(8,128)(2,1)}, u32[]{:S(2)}, u32[]{:S(2)}) collective-permute-start(bf16[128,256]{0,1:T(8,128)(2,1)} %bitcast.18), channel_id=1, source_target_pairs={{0,3},{1,0},{2,1},{3,2},{4,7},{5,4},{6,5},{7,6},{8,11},{9,8},{10,9... | collective-permute-start | bytes 196616 | tf_op jit(solution)/shard_map/ppermute | solution.py:108
  54.7 0.3 convolution_convert_fusion.3
  55.1 1.0 copy.149
  56.5 0.7 copy.135
  57.2 0.7 copy.132
  57.9 0.7 collective-permute-done.7
  58.7 1.5 %broadcast_select_fusion.1 = (bf16[3,128,1024]{2,1,0:T(8,128)(2,1)S(1)}, bf16[3,128,1024]{2,1,0:T(8,128)(2,1)S(1)}) fusion(bf16[3,128,1024]{2,1,0:T(8,128)(2,1)} %collective-permute-done.7, pred[]{:T(512)S(6)} %eq.139, bf16[1,129,1024]{2,1,0:T(8,128)(2,1)S(1)} %bitcast.286, bf16[1,129,1024]{2,1,0:T(8,128)(2,1)S(1)} %bitcast.289, ...), kind=kLoop, calls=%fused_computation.89 | loop fusion | flops 3145728 | bytes 3151873 | tf_op jit(solution)/shard_map/jit(_where)/select_n | solution.py:136
  60.2 1.1 convolution_add_fusion.1
  61.6 0.4 multiply_reduce_fusion
  62.1 0.9 collective-permute-start.12
  63.1 2.1 %collective-permute-start.11 = (bf16[128,1024]{1,0:T(8,128)(2,1)S(1)}, bf16[128,1024]{1,0:T(8,128)(2,1)S(1)}, u32[]{:S(2)}, u32[]{:S(2)}) collective-permute-start(bf16[128,1024]{1,0:T(8,128)(2,1)S(1)} %multiply_convert_fusion), channel_id=1, source_target_pairs={{0,2},{1,3},{2,0},{3,1},{4,6},{5,7},{6,4},{7,5},{8,10},{9,11},{10,... | collective-permute-start | bytes 786440 | tf_op jit(solution)/shard_map/ppermute | solution.py:108
  65.2 1.9 %collective-permute-start.10 = (bf16[128,1024]{1,0:T(8,128)(2,1)S(1)}, bf16[128,1024]{1,0:T(8,128)(2,1)S(1)}, u32[]{:S(2)}, u32[]{:S(2)}) collective-permute-start(bf16[128,1024]{1,0:T(8,128)(2,1)S(1)} %multiply_convert_fusion), channel_id=1, source_target_pairs={{0,1},{1,2},{2,3},{3,0},{4,5},{5,6},{6,7},{7,4},{8,9},{9,10},{10,1... | collective-permute-start | bytes 786440 | tf_op jit(solution)/shard_map/ppermute | solution.py:108
  68.2 0.4 copy-done.10
  68.6 0.4 convolution_convert_fusion.2
  69.2 5.9 %convolution_bitcast_fusion.1 = f32[1,8,64,512]{3,2,1,0:T(8,128)} fusion(bf16[8,64,1024]{2,1,0:T(8,128)(2,1)S(1)} %convolution_convert_fusion.2, bf16[8,1024,512]{2,1,0:T(8,128)(2,1)} %param.22), kind=kOutput, calls=%fused_computation.49 | convolution fusion | flops 536870912 | bytes 10485760 | tf_op jit(solution)/shard_map/becd,edf->becf/dot_general | solution.py:86
  75.1 9.1 %convolution_convert_fusion.1 = bf16[8,64,1024]{2,1,0:T(8,128)(2,1)S(1)} fusion(bf16[8,512,1024]{2,1,0:T(8,128)(2,1)} %param.24, bf16[8,64,1024]{2,1,0:T(8,128)(2,1)S(1)} %convolution_convert_fusion.2, bf16[8,1024,512]{2,1,0:T(8,128)(2,1)} %param.23, f32[1,8,64,512]{3,2,1,0:T(8,128)} %convolution_bitcast_fusion.1), kind=kOutput, calls=%fused_computation.37 | convolution fusion | flops 1075838976 | bytes 19922944 | tf_op jit(solution)/shard_map/becf,efd->becd/dot_general | solution.py:96
  84.3 0.9 constant_dynamic-slice_fusion.8
  85.2 0.7 copy.128
  85.9 1.8 %convolution_bitcast_fusion.2 = f32[128,1024]{1,0:T(8,128)} fusion(bf16[8,64,1024]{2,1,0:T(8,128)(2,1)S(1)} %convolution_convert_fusion.1, s32[8,128]{1,0:T(8,128)S(1)} %convolution_convert_fusion.6, pred[8,128]{1,0:T(8,128)(4,1)} %copy-done.15, bf16[8,128]{1,0:T(8,128)(2,1)S(1)} %bitcast.311), kind=kOutput, calls=%fused_computation.60 | convolution fusion | flops 134414336 | bytes 1580032 | tf_op jit(solution)/shard_map/becr,becd->brd/dot_general | solution.py:99
  87.7 1.1 fusion.196
  90.7 1.1 concatenate.63
  91.8 1.1 concatenate.62
  92.8 1.1 concatenate.61
  94.5 1.0 convolution_convert_fusion
  95.5 5.5 %fusion.1 = f32[8,3,64,512]{3,2,1,0:T(8,128)S(1)} fusion(bf16[8,1024,512]{2,1,0:T(8,128)(2,1)} %param.23, bf16[3,8,64,1024]{3,2,1,0:T(8,128)(2,1)S(1)} %convolution_convert_fusion), kind=kOutput, calls=%fused_computation.1 | convolution fusion | flops 1610612736 | bytes 14680064 | tf_op jit(solution)/shard_map/becd,edf->becf/dot_general | solution.py:87
  101.1 2.1 %fusion.12 = bf16[3,8,64,512]{3,2,0,1:T(8,128)(2,1)S(1)} fusion(f32[8,3,64,512]{3,2,1,0:T(8,128)S(1)} %fusion.1, bf16[8,1024,512]{2,1,0:T(8,128)(2,1)S(1)} %bitcast.279, bf16[3,8,64,1024]{3,2,1,0:T(8,128)(2,1)S(1)} %convolution_convert_fusion), kind=kOutput, calls=%fused_computation.16 | convolution fusion | flops 1615331328 | bytes 16252928 | tf_op jit(solution)/shard_map/becd,edf->becf/dot_general | solution.py:86
  103.5 1.0 fusion.28
  104.5 2.1 %fusion.31 = bf16[3,8,64,512]{3,2,0,1:T(8,128)(2,1)} fusion(bf16[3,8,64,512]{3,2,0,1:T(8,128)(2,1)S(1)} %fusion.12, bf16[8,512,1024]{2,1,0:T(8,128)(2,1)S(1)} %bitcast.281), kind=kOutput, calls=%fused_computation.36 | convolution fusion | flops 806092800 | bytes 7340032 | tf_op jit(solution)/shard_map/becf,efd->becd/dot_general | solution.py:96
  106.8 0.4 fusion.50
  107.2 1.9 %fusion.65 = bf16[3,128,512]{2,1,0:T(8,128)(2,1)S(1)} fusion(f32[3,128,512]{2,1,0:T(8,128)S(1)} %fusion.50, bf16[3,8,64,512]{3,2,0,1:T(8,128)(2,1)} %copy-done.21, s32[3,8,128]{2,1,0:T(8,128)S(1)} %convolution_convert_fusion.5, pred[3,8,128]{2,1,0:T(8,128)(4,1)S(1)} %compare_bitcast_fusion.1, bf16[3,8,128]{2,1,0:T(8,128)(2,1)S(1)} %bitcast.312), kind=kOutput, calls=%fused_computation.58 | convolution fusion | flops 202309632 | bytes 2774016 | tf_op jit(solution)/shard_map/becr,becd->brd/dot_general | solution.py:99
  109.2 2.4 %collective-permute-start.17 = (bf16[128,512]{1,0:T(8,128)(2,1)S(1)}, bf16[128,512]{1,0:T(8,128)(2,1)S(1)}, u32[]{:S(2)}, u32[]{:S(2)}) collective-permute-start(bf16[128,512]{1,0:T(8,128)(2,1)S(1)} %get-tuple-element.36), channel_id=1, source_target_pairs={{0,2},{1,3},{2,0},{3,1},{4,6},{5,7},{6,4},{7,5},{8,10},{9,11},{10,... | collective-permute-start | bytes 393224 | tf_op jit(solution)/shard_map/ppermute | solution.py:108
  111.7 1.4 %collective-permute-start.16 = (bf16[128,512]{1,0:T(8,128)(2,1)S(1)}, bf16[128,512]{1,0:T(8,128)(2,1)S(1)}, u32[]{:S(2)}, u32[]{:S(2)}) collective-permute-start(bf16[128,512]{1,0:T(8,128)(2,1)S(1)} %get-tuple-element.34), channel_id=1, source_target_pairs={{0,3},{1,0},{2,1},{3,2},{4,7},{5,4},{6,5},{7,6},{8,11},{9,8},{10,9... | collective-permute-start | bytes 393224 | tf_op jit(solution)/shard_map/ppermute | solution.py:108
  113.0 0.4 fusion.44
  113.5 0.4 fusion.62
  114.0 0.7 collective-permute-start.15
  114.7 1.5 %collective-permute-start.14 = (bf16[128,512]{1,0:T(8,128)(2,1)S(1)}, bf16[128,512]{1,0:T(8,128)(2,1)S(1)}, u32[]{:S(2)}, u32[]{:S(2)}) collective-permute-start(bf16[128,512]{1,0:T(8,128)(2,1)S(1)} %get-tuple-element.33), channel_id=1, source_target_pairs={{0,2},{1,3},{2,0},{3,1},{4,6},{5,7},{6,4},{7,5},{8,10},{9,11},{10,... | collective-permute-start | bytes 393224 | tf_op jit(solution)/shard_map/ppermute | solution.py:108
  116.1 1.2 collective-permute-done.18
  117.4 1.6 %collective-permute-start.13 = (bf16[128,512]{1,0:T(8,128)(2,1)S(1)}, bf16[128,512]{1,0:T(8,128)(2,1)S(1)}, u32[]{:S(2)}, u32[]{:S(2)}) collective-permute-start(bf16[128,512]{1,0:T(8,128)(2,1)S(1)} %get-tuple-element.31), channel_id=1, source_target_pairs={{0,3},{1,0},{2,1},{3,2},{4,7},{5,4},{6,5},{7,6},{8,11},{9,8},{10,9... | collective-permute-start | bytes 393224 | tf_op jit(solution)/shard_map/ppermute | solution.py:108
  119.0 6.5 %collective-permute-done.17 = bf16[128,512]{1,0:T(8,128)(2,1)S(1)} collective-permute-done((bf16[128,512]{1,0:T(8,128)(2,1)S(1)}, bf16[128,512]{1,0:T(8,128)(2,1)S(1)}, u32[]{:S(2)}, u32[]{:S(2)}) %collective-permute-start.17) | collective-permute-done | bytes 131104 | tf_op jit(solution)/shard_map/ppermute | solution.py:108
  125.5 0.3 collective-permute-done.15
  125.8 6.9 %collective-permute-done.14 = bf16[128,512]{1,0:T(8,128)(2,1)S(1)} collective-permute-done((bf16[128,512]{1,0:T(8,128)(2,1)S(1)}, bf16[128,512]{1,0:T(8,128)(2,1)S(1)}, u32[]{:S(2)}, u32[]{:S(2)}) %collective-permute-start.14) | collective-permute-done | bytes 131104 | tf_op jit(solution)/shard_map/ppermute | solution.py:108
  132.7 1.1 fusion.101
  (171 shorter events, 7.0 us)
Async XLA Ops:
  0.6 15.3 %copy-start = (bf16[1024,1024]{1,0:T(8,128)(2,1)S(1)}, bf16[1024,1024]{1,0:T(8,128)(2,1)}, u32[]{:S(2)}) copy-start(bf16[1024,1024]{1,0:T(8,128)(2,1)} %param.16) | copy-start | bytes 6291460
  0.6 11.9 %copy-start.2 = (bf16[128,1024]{1,0:T(8,128)(2,1)S(1)}, bf16[128,1024]{1,0:T(8,128)(2,1)}, u32[]{:S(2)}) copy-start(bf16[128,1024]{1,0:T(8,128)(2,1)} %param.14) | copy-start | bytes 786436
  0.7 14.5 %copy-start.14 = (s32[1,512]{1,0:T(1,128)S(1)}, s32[1,512]{1,0:T(1,128)}, u32[]{:S(2)}) copy-start(s32[1,512]{1,0:T(1,128)} %param.25) | copy-start | bytes 6148
  3.2 52.8 %collective-permute-start.6 = (bf16[129,1024]{1,0:T(8,128)(2,1)}, bf16[129,1024]{1,0:T(8,128)(2,1)S(1)}, u32[]{:S(2)}, u32[]{:S(2)}) collective-permute-start(bf16[129,1024]{1,0:T(8,128)(2,1)} %pad_maximum_fusion.6), channel_id=1, source_target_pairs={{0,3},{1,0},{2,1},{3,2},{4,7},{5,4},{6,5},{7,6},{8,11},{9,8},{10,9... | collective-permute-start | bytes 792584 | tf_op jit(solution)/shard_map/ppermute | solution.py:108
  8.3 47.8 %collective-permute-start.5 = (bf16[129,1024]{1,0:T(8,128)(2,1)}, bf16[129,1024]{1,0:T(8,128)(2,1)S(1)}, u32[]{:S(2)}, u32[]{:S(2)}) collective-permute-start(bf16[129,1024]{1,0:T(8,128)(2,1)} %pad_maximum_fusion.6), channel_id=1, source_target_pairs={{0,2},{1,3},{2,0},{3,1},{4,6},{5,7},{6,4},{7,5},{8,10},{9,11},{10,... | collective-permute-start | bytes 792584 | tf_op jit(solution)/shard_map/ppermute | solution.py:108
  15.9 8.3 %copy-start.13 = (s32[128,8]{0,1:T(8,128)S(1)}, s32[128,8]{0,1:T(8,128)}, u32[]{:S(2)}) copy-start(s32[128,8]{0,1:T(8,128)} %param.27) | copy-start | bytes 12292
  15.9 9.0 %copy-start.18 = (s32[1,512]{1,0:T(1,128)S(1)}, s32[1,512]{1,0:T(1,128)}, u32[]{:S(2)}) copy-start(s32[1,512]{1,0:T(1,128)} %param.26) | copy-start | bytes 6148
  15.9 9.0 %copy-start.19 = (bf16[1024]{0:T(1024)(128)(2,1)S(1)}, bf16[1024]{0:T(1024)(128)(2,1)}, u32[]{:S(2)}) copy-start(bf16[1024]{0:T(1024)(128)(2,1)} %param.20) | copy-start | bytes 6148
  19.3 10.3 %collective-permute-start.2 = (bf16[128,2,256]{0,2,1:T(8,128)(2,1)S(1)}, bf16[128,2,256]{0,2,1:T(8,128)(2,1)S(1)}, u32[]{:S(2)}, u32[]{:S(2)}) collective-permute-start(bf16[128,2,256]{0,2,1:T(8,128)(2,1)S(1)} %get-tuple-element.28), channel_id=1, source_target_pairs={{0,3},{1,0},{2,1},{3,2},{4,7},{5,4},{6,5},{7,6},{8,11},{9,8},{10,9... | collective-permute-start | bytes 393224 | tf_op jit(solution)/shard_map/ppermute | solution.py:108
  19.8 23.7 %collective-permute-start.1 = (bf16[128,2,256]{0,2,1:T(8,128)(2,1)S(1)}, bf16[128,2,256]{0,2,1:T(8,128)(2,1)S(1)}, u32[]{:S(2)}, u32[]{:S(2)}) collective-permute-start(bf16[128,2,256]{0,2,1:T(8,128)(2,1)S(1)} %get-tuple-element.29), channel_id=1, source_target_pairs={{0,2},{1,3},{2,0},{3,1},{4,6},{5,7},{6,4},{7,5},{8,10},{9,11},{10,... | collective-permute-start | bytes 393224 | tf_op jit(solution)/shard_map/ppermute | solution.py:108
  22.3 21.2 %collective-permute-start = (bf16[128,2,256]{0,2,1:T(8,128)(2,1)S(1)}, bf16[128,2,256]{0,2,1:T(8,128)(2,1)S(1)}, u32[]{:S(2)}, u32[]{:S(2)}) collective-permute-start(bf16[128,2,256]{0,2,1:T(8,128)(2,1)S(1)} %get-tuple-element.30), channel_id=1, source_target_pairs={{0,1},{1,2},{2,3},{3,0},{4,5},{5,6},{6,7},{7,4},{8,9},{9,10},{10,1... | collective-permute-start | bytes 393224 | tf_op jit(solution)/shard_map/ppermute | solution.py:108
  29.6 26.5 %collective-permute-start.4 = (bf16[129,1024]{1,0:T(8,128)(2,1)}, bf16[129,1024]{1,0:T(8,128)(2,1)S(1)}, u32[]{:S(2)}, u32[]{:S(2)}) collective-permute-start(bf16[129,1024]{1,0:T(8,128)(2,1)} %pad_maximum_fusion.6), channel_id=1, source_target_pairs={{0,1},{1,2},{2,3},{3,0},{4,5},{5,6},{6,7},{7,4},{8,9},{9,10},{10,1... | collective-permute-start | bytes 792584 | tf_op jit(solution)/shard_map/ppermute | solution.py:108
  47.2 3.4 %copy-start.6 = (bf16[256,1024]{1,0:T(8,128)(2,1)S(1)}, bf16[256,1024]{1,0:T(8,128)(2,1)}, u32[]{:S(2)}) copy-start(bf16[256,1024]{1,0:T(8,128)(2,1)} %param.19) | copy-start | bytes 1572868
  50.6 10.7 %collective-permute-start.9 = (bf16[128,256]{0,1:T(8,128)(2,1)}, bf16[128,256]{0,1:T(8,128)(2,1)S(1)}, u32[]{:S(2)}, u32[]{:S(2)}) collective-permute-start(bf16[128,256]{0,1:T(8,128)(2,1)} %bitcast.26), channel_id=1, source_target_pairs={{0,1},{1,2},{2,3},{3,0},{4,5},{5,6},{6,7},{7,4},{8,9},{9,10},{10,1... | collective-permute-start | bytes 196616 | tf_op jit(solution)/shard_map/ppermute | solution.py:108
  50.9 9.3 %collective-permute-start.3 = (bf16[128,256]{0,1:T(8,128)(2,1)}, bf16[128,256]{0,1:T(8,128)(2,1)}, u32[]{:S(2)}, u32[]{:S(2)}) collective-permute-start(bf16[128,256]{0,1:T(8,128)(2,1)} %bitcast.18), channel_id=1, source_target_pairs={{0,3},{1,0},{2,1},{3,2},{4,7},{5,4},{6,5},{7,6},{8,11},{9,8},{10,9... | collective-permute-start | bytes 196616 | tf_op jit(solution)/shard_map/ppermute | solution.py:108
  56.1 5.5 %collective-permute-start.8 = (bf16[128,256]{0,1:T(8,128)(2,1)S(1)}, bf16[128,256]{0,1:T(8,128)(2,1)S(1)}, u32[]{:S(2)}, u32[]{:S(2)}) collective-permute-start(bf16[128,256]{0,1:T(8,128)(2,1)S(1)} %bitcast.308), channel_id=1, source_target_pairs={{0,2},{1,3},{2,0},{3,1},{4,6},{5,7},{6,4},{7,5},{8,10},{9,11},{10,... | collective-permute-start | bytes 196616 | tf_op jit(solution)/shard_map/ppermute | solution.py:108
  56.2 2.5 %collective-permute-start.7 = (bf16[3,128,1024]{2,1,0:T(8,128)(2,1)S(1)}, bf16[3,128,1024]{2,1,0:T(8,128)(2,1)}, u32[]{:S(2)}, u32[]{:S(2)}) collective-permute-start(bf16[3,128,1024]{2,1,0:T(8,128)(2,1)S(1)} %pad_maximum_fusion.1), channel_id=1, source_target_pairs={{0,4},{4,0},{8,12},{12,8},{16,20},{20,16},{24,28},{28,24},{1,5},{5... | collective-permute-start | bytes 2359304 | tf_op jit(solution)/shard_map/ppermute | solution.py:135
  61.3 5.8 %copy-start.9 = (bf16[1024,32]{0,1:T(8,128)(2,1)S(1)}, bf16[1024,32]{0,1:T(8,128)(2,1)}, u32[]{:S(2)}) copy-start(bf16[1024,32]{0,1:T(8,128)(2,1)} %param.21) | copy-start | bytes 196612
  62.0 13.2 %copy-start.3 = (f32[128,1024]{1,0:T(8,128)}, f32[128,1024]{1,0:T(8,128)S(1)}, u32[]{:S(2)}) copy-start(f32[128,1024]{1,0:T(8,128)S(1)} %get-tuple-element.58) | copy-start | bytes 1572868
  62.1 25.6 %collective-permute-start.12 = (bf16[128,1024]{1,0:T(8,128)(2,1)S(1)}, bf16[128,1024]{1,0:T(8,128)(2,1)}, u32[]{:S(2)}, u32[]{:S(2)}) collective-permute-start(bf16[128,1024]{1,0:T(8,128)(2,1)S(1)} %multiply_convert_fusion), channel_id=1, source_target_pairs={{0,3},{1,0},{2,1},{3,2},{4,7},{5,4},{6,5},{7,6},{8,11},{9,8},{10,9... | collective-permute-start | bytes 786440 | tf_op jit(solution)/shard_map/ppermute | solution.py:108
  63.1 25.9 %collective-permute-start.11 = (bf16[128,1024]{1,0:T(8,128)(2,1)S(1)}, bf16[128,1024]{1,0:T(8,128)(2,1)S(1)}, u32[]{:S(2)}, u32[]{:S(2)}) collective-permute-start(bf16[128,1024]{1,0:T(8,128)(2,1)S(1)} %multiply_convert_fusion), channel_id=1, source_target_pairs={{0,2},{1,3},{2,0},{3,1},{4,6},{5,7},{6,4},{7,5},{8,10},{9,11},{10,... | collective-permute-start | bytes 786440 | tf_op jit(solution)/shard_map/ppermute | solution.py:108
  65.2 24.7 %collective-permute-start.10 = (bf16[128,1024]{1,0:T(8,128)(2,1)S(1)}, bf16[128,1024]{1,0:T(8,128)(2,1)S(1)}, u32[]{:S(2)}, u32[]{:S(2)}) collective-permute-start(bf16[128,1024]{1,0:T(8,128)(2,1)S(1)} %multiply_convert_fusion), channel_id=1, source_target_pairs={{0,1},{1,2},{2,3},{3,0},{4,5},{5,6},{6,7},{7,4},{8,9},{9,10},{10,1... | collective-permute-start | bytes 786440 | tf_op jit(solution)/shard_map/ppermute | solution.py:108
  67.8 0.7 copy-start.10
  68.6 0.6 copy-start.15
  84.2 7.5 %copy-start.11 = (bf16[128,32]{1,0:T(8,128)(2,1)S(1)}, bf16[128,32]{1,0:T(8,128)(2,1)}, u32[]{:S(2)}) copy-start(bf16[128,32]{1,0:T(8,128)(2,1)} %copy.135) | copy-start | bytes 24580
  84.2 8.6 %copy-start.12 = (bf16[128,32]{1,0:T(8,128)(2,1)S(1)}, bf16[128,32]{1,0:T(8,128)(2,1)}, u32[]{:S(2)}) copy-start(bf16[128,32]{1,0:T(8,128)(2,1)} %copy.132) | copy-start | bytes 24580
  89.0 1.7 %copy-start.8 = (bf16[128,1024]{1,0:T(8,128)(2,1)}, bf16[128,1024]{1,0:T(8,128)(2,1)S(1)}, u32[]{:S(2)}) copy-start(bf16[128,1024]{1,0:T(8,128)(2,1)S(1)} %collective-permute-done.11) | copy-start | bytes 786436
  89.8 0.7 copy-start.7
  94.5 6.6 %slice-start = ((s8[8388608]{0:T(1024)(128)(4,1)}), s8[4194304]{0:T(1024)(128)(4,1)S(1)}, s32[]{:S(2)}) async-start(s8[8388608]{0:T(1024)(128)(4,1)} %bitcast.278), calls=%async_computation | async-start | bytes 8388608
  95.5 5.6 %slice-start.1 = ((s8[8388608]{0:T(1024)(128)(4,1)}), s8[4194304]{0:T(1024)(128)(4,1)S(1)}, s32[]{:S(2)}) async-start(s8[8388608]{0:T(1024)(128)(4,1)} %bitcast.278), calls=%async_computation.1 | async-start | bytes 8388608
  95.5 7.7 %slice-start.2 = ((s8[8388608]{0:T(1024)(128)(4,1)}), s8[4194304]{0:T(1024)(128)(4,1)S(1)}, s32[]{:S(2)}) async-start(s8[8388608]{0:T(1024)(128)(4,1)} %bitcast.280), calls=%async_computation.2 | async-start | bytes 8388608
  101.1 2.4 %slice-start.3 = ((s8[8388608]{0:T(1024)(128)(4,1)}), s8[4194304]{0:T(1024)(128)(4,1)S(1)}, s32[]{:S(2)}) async-start(s8[8388608]{0:T(1024)(128)(4,1)} %bitcast.280), calls=%async_computation.3 | async-start | bytes 8388608
  104.5 2.3 %copy-start.21 = (bf16[3,8,64,512]{3,2,0,1:T(8,128)(2,1)}, bf16[3,8,64,512]{3,2,0,1:T(8,128)(2,1)S(1)}, u32[]{:S(2)}) copy-start(bf16[3,8,64,512]{3,2,0,1:T(8,128)(2,1)S(1)} %fusion.28) | copy-start | bytes 4718596
  106.8 6.2 %copy-start.20 = (bf16[3,8,64,512]{3,2,0,1:T(8,128)(2,1)S(1)}, bf16[3,8,64,512]{3,2,0,1:T(8,128)(2,1)}, u32[]{:S(2)}) copy-start(bf16[3,8,64,512]{3,2,0,1:T(8,128)(2,1)} %fusion.31) | copy-start | bytes 4718596
  109.2 8.2 %collective-permute-start.18 = (bf16[128,512]{1,0:T(8,128)(2,1)S(1)}, bf16[128,512]{1,0:T(8,128)(2,1)S(1)}, u32[]{:S(2)}, u32[]{:S(2)}) collective-permute-start(bf16[128,512]{1,0:T(8,128)(2,1)S(1)} %get-tuple-element.35), channel_id=1, source_target_pairs={{0,1},{1,2},{2,3},{3,0},{4,5},{5,6},{6,7},{7,4},{8,9},{9,10},{10,1... | collective-permute-start | bytes 393224 | tf_op jit(solution)/shard_map/ppermute | solution.py:108
  109.2 16.2 %collective-permute-start.17 = (bf16[128,512]{1,0:T(8,128)(2,1)S(1)}, bf16[128,512]{1,0:T(8,128)(2,1)S(1)}, u32[]{:S(2)}, u32[]{:S(2)}) collective-permute-start(bf16[128,512]{1,0:T(8,128)(2,1)S(1)} %get-tuple-element.36), channel_id=1, source_target_pairs={{0,2},{1,3},{2,0},{3,1},{4,6},{5,7},{6,4},{7,5},{8,10},{9,11},{10,... | collective-permute-start | bytes 393224 | tf_op jit(solution)/shard_map/ppermute | solution.py:108
  111.7 13.8 %collective-permute-start.16 = (bf16[128,512]{1,0:T(8,128)(2,1)S(1)}, bf16[128,512]{1,0:T(8,128)(2,1)S(1)}, u32[]{:S(2)}, u32[]{:S(2)}) collective-permute-start(bf16[128,512]{1,0:T(8,128)(2,1)S(1)} %get-tuple-element.34), channel_id=1, source_target_pairs={{0,3},{1,0},{2,1},{3,2},{4,7},{5,4},{6,5},{7,6},{8,11},{9,8},{10,9... | collective-permute-start | bytes 393224 | tf_op jit(solution)/shard_map/ppermute | solution.py:108
  113.5 19.2 %copy-start.4 = (f32[128,1024]{1,0:T(8,128)S(1)}, f32[128,1024]{1,0:T(8,128)}, u32[]{:S(2)}) copy-start(f32[128,1024]{1,0:T(8,128)} %copy-done.3) | copy-start | bytes 1572868
  113.5 19.2 %copy-start.5 = (f32[128,1024]{1,0:T(8,128)S(1)}, f32[128,1024]{1,0:T(8,128)}, u32[]{:S(2)}) copy-start(f32[128,1024]{1,0:T(8,128)} %convolution_bitcast_fusion.2) | copy-start | bytes 1572868
  113.5 19.2 %copy-start.16 = (pred[8,128]{1,0:T(8,128)(4,1)S(1)}, pred[8,128]{1,0:T(8,128)(4,1)}, u32[]{:S(2)}) copy-start(pred[8,128]{1,0:T(8,128)(4,1)} %copy-done.15) | copy-start | bytes 3076
  113.5 19.2 %copy-start.17 = (bf16[128,8]{0,1:T(8,128)(2,1)S(1)}, bf16[128,8]{0,1:T(8,128)(2,1)}, u32[]{:S(2)}) copy-start(bf16[128,8]{0,1:T(8,128)(2,1)} %copy.128) | copy-start | bytes 6148
  113.5 20.3 %copy-start.1 = (bf16[1024,1024]{1,0:T(8,128)(2,1)S(1)}, bf16[1024,1024]{1,0:T(8,128)(2,1)}, u32[]{:S(2)}) copy-start(bf16[1024,1024]{1,0:T(8,128)(2,1)} %param.16) | copy-start | bytes 6291460
  114.0 11.8 %collective-permute-start.15 = (bf16[128,512]{1,0:T(8,128)(2,1)S(1)}, bf16[128,512]{1,0:T(8,128)(2,1)S(1)}, u32[]{:S(2)}, u32[]{:S(2)}) collective-permute-start(bf16[128,512]{1,0:T(8,128)(2,1)S(1)} %get-tuple-element.32), channel_id=1, source_target_pairs={{0,1},{1,2},{2,3},{3,0},{4,5},{5,6},{6,7},{7,4},{8,9},{9,10},{10,1... | collective-permute-start | bytes 393224 | tf_op jit(solution)/shard_map/ppermute | solution.py:108
  114.7 18.0 %collective-permute-start.14 = (bf16[128,512]{1,0:T(8,128)(2,1)S(1)}, bf16[128,512]{1,0:T(8,128)(2,1)S(1)}, u32[]{:S(2)}, u32[]{:S(2)}) collective-permute-start(bf16[128,512]{1,0:T(8,128)(2,1)S(1)} %get-tuple-element.33), channel_id=1, source_target_pairs={{0,2},{1,3},{2,0},{3,1},{4,6},{5,7},{6,4},{7,5},{8,10},{9,11},{10,... | collective-permute-start | bytes 393224 | tf_op jit(solution)/shard_map/ppermute | solution.py:108
  117.4 15.3 %collective-permute-start.13 = (bf16[128,512]{1,0:T(8,128)(2,1)S(1)}, bf16[128,512]{1,0:T(8,128)(2,1)S(1)}, u32[]{:S(2)}, u32[]{:S(2)}) collective-permute-start(bf16[128,512]{1,0:T(8,128)(2,1)S(1)} %get-tuple-element.31), channel_id=1, source_target_pairs={{0,3},{1,0},{2,1},{3,2},{4,7},{5,4},{6,5},{7,6},{8,11},{9,8},{10,9... | collective-permute-start | bytes 393224 | tf_op jit(solution)/shard_map/ppermute | solution.py:108

commit v17 on v11

--- a/solution.py
+++ b/solution.py
@@ -132,9 +132,7 @@
     mine = lax.dynamic_slice_in_dim(w_out, part * cut, cut, 0)
     got = jnp.stack([shifted(mine, step) for step in range(1, count)])
     other = lax.ppermute(got, "req", [(j, j ^ 1) for j in range(mates)])
-    lower = jnp.where(part == 0, got, other)
-    upper = jnp.where(part == 0, other, got)
-    return jnp.concatenate([lower, upper], axis=1)
+    return got, other
 
 
 def shards(
@@ -191,10 +189,20 @@
     blocks = heads_out.reshape(owners, rows, -1)
     remote = gather_w_out(w_out)
     attention = jnp.dot(blocks[0], w_out, preferred_element_type=jnp.float32)
+    mine, other = remote
+    part = lax.axis_index("req") % 2
+    cut = mine.shape[1]
     for step in range(1, owners):
         got = shifted(blocks[step], -step)
         attention = attention + jnp.dot(
-            got, remote[owners - step - 1], preferred_element_type=jnp.float32
+            lax.dynamic_slice_in_dim(got, part * cut, cut, 1),
+            mine[owners - step - 1],
+            preferred_element_type=jnp.float32,
+        )
+        attention = attention + jnp.dot(
+            lax.dynamic_slice_in_dim(got, (1 - part) * cut, cut, 1),
+            other[owners - step - 1],
+            preferred_element_type=jnp.float32,
         )
     resid = tokens.astype(jnp.float32) + attention
     normed2 = rms_scale(resid, norm_moe)

time: 128 us -> 129 us (level)
  starting transfers between devices: 41.7 us -> 46 us
  waiting for transfers between devices: 22.2 us -> 19.6 us
  other arithmetic: 8.27 us -> 6.97 us
    ppermute x18, starting transfers between devices: 41.6 us -> 46 us  [shifted(): lax.ppermute(x, 'exp', [(j, (j + step) % count) for j in range(count)])]
    ppermute x18, waiting for transfers between devices: 22.2 us -> 19.6 us  [shifted(): lax.ppermute(x, 'exp', [(j, (j + step) % count) for j in range(count)])]
    dot_general x3 -> x6, matrix products: 0.86 us -> 2.63 us  [the longest x3 1.69 us: shards(): jnp.dot(lax.dynamic_slice_in_dim(got, part * cut, cut, 1), mine[owners -...]
where the time goes in v17:
time: 129 us; the launch traced here: 128 us
  starting transfers between devices  46 us (36%)
  matrix products  46 us (36%)
  waiting for transfers between devices  19.6 us (15%)
  local copies, waits for them, and re-layouts  8.25 us (6%)
  other arithmetic  6.97 us (5%)
  between operations  1.38 us (1%)
    ppermute x18, starting transfers between devices, shifted(): lax.ppermute(x, 'exp', [(j, (j + step) % count) for j in range(count)])  46 us
    ppermute x18, waiting for transfers between devices, shifted(): lax.ppermute(x, 'exp', [(j, (j + step) % count) for j in range(count)])  19.6 us
    dot_general x3, matrix products, expert_mix(): jnp.einsum('becf,efd->becd', hidden, down, preferred_element_type=jnp.flo...  11.9 us
    dot_general x2, matrix products, expert_mix(): jnp.einsum('becd,edf->becf', received, w_gate, preferred_element_type=jnp...  7 us
    dot_general x1, matrix products, expert_mix(): jnp.einsum('becd,edf->becf', received, w_up, preferred_element_type=jnp.f...  5.53 us
    sub x1, matrix products, attend(): expo = jnp.exp(score - top)  3.6 us
    dot_general x3, matrix products, expert_mix(): jnp.einsum('becr,becd->brd', low, result, preferred_element_type=jnp.floa...  3.48 us
    unnamed x39, local copies, waits for them, and re-layouts  3.36 us
  transfers between devices with their start and end apart: 19, of which 7 were waited for; matrix products, arithmetic and copies ran while one was open for 32% of the time, Pallas kernels for 0%

profile of v17, /device:TPU:0, one launch (start us, length us, event | category | flops | bytes accessed | tf_op | source)
XLA Modules:
  0.0 128.2 jit_solution(13926131123461210584)
XLA Ops:
  0.7 1.8 %constant_dynamic-slice_fusion.9 = bf16[128,1024]{1,0:T(8,128)(2,1)} fusion(bf16[256,1024]{1,0:T(8,128)(2,1)} %param.19, s32[]{:T(128)S(6)} %select_n.167), kind=kLoop, calls=%fused_computation.192 | loop fusion | bytes 524292 | tf_op jit(solution)/shard_map/dynamic_slice | solution.py:132
  2.5 5.1 %collective-permute-start.4 = (bf16[128,1024]{1,0:T(8,128)(2,1)}, bf16[128,1024]{1,0:T(8,128)(2,1)S(1)}, u32[]{:S(2)}, u32[]{:S(2)}) collective-permute-start(bf16[128,1024]{1,0:T(8,128)(2,1)} %constant_dynamic-slice_fusion.9), channel_id=1, source_target_pairs={{0,3},{1,0},{2,1},{3,2},{4,7},{5,4},{6,5},{7,6},{8,11},{9,8},{10,9... | collective-permute-start | bytes 786440 | tf_op jit(solution)/shard_map/ppermute | solution.py:108
  7.6 0.5 multiply_power_fusion
  8.1 0.7 convert_element_type.124
  8.8 1.1 fusion.90
  9.9 1.7 %convolution_convert_fusion.4 = bf16[128,512]{1,0:T(8,128)(2,1)S(1)} fusion(bf16[1024,512]{1,0:T(8,128)(2,1)} %param.18, bf16[128,1024]{1,0:T(8,128)(2,1)} %param.14, f32[1024]{0:T(1024)S(1)} %convert_element_type.124, f32[128]{0:T(128)S(1)} %add_rsqrt_fusion.1), kind=kOutput, calls=%fused_computation.69 | convolution fusion | flops 134807552 | bytes 1446400 | tf_op jit(solution)/shard_map/dot_general | solution.py:167
  11.7 1.9 %fusion.183 = f32[128,512]{0,1:T(8,128)S(1)} fusion(bf16[1024,512]{1,0:T(8,128)(2,1)} %param.17, bf16[128,1024]{1,0:T(8,128)(2,1)} %param.14, f32[1024]{0:T(1024)S(1)} %convert_element_type.124, f32[128]{0:T(128)S(1)} %add_rsqrt_fusion.1), kind=kOutput, calls=%fused_computation.233 | convolution fusion | flops 134742016 | bytes 1577472 | tf_op jit(solution)/shard_map/dot_general | solution.py:164
  13.8 0.3 reduce-window.9
  14.3 0.7 bitcast_subtract_fusion
  15.0 1.0 fusion.185
  16.0 0.8 dynamic-slice_convert_fusion
  16.7 0.7 multiply_cosine_fusion
  17.7 0.5 collective-permute-start.2
  18.2 2.6 %collective-permute-start.1 = (bf16[128,2,256]{0,2,1:T(8,128)(2,1)S(1)}, bf16[128,2,256]{0,2,1:T(8,128)(2,1)S(1)}, u32[]{:S(2)}, u32[]{:S(2)}) collective-permute-start(bf16[128,2,256]{0,2,1:T(8,128)(2,1)S(1)} %get-tuple-element.21), channel_id=1, source_target_pairs={{0,2},{1,3},{2,0},{3,1},{4,6},{5,7},{6,4},{7,5},{8,10},{9,11},{10,... | collective-permute-start | bytes 393224 | tf_op jit(solution)/shard_map/ppermute | solution.py:108
  20.8 1.9 %collective-permute-start = (bf16[128,2,256]{0,2,1:T(8,128)(2,1)S(1)}, bf16[128,2,256]{0,2,1:T(8,128)(2,1)S(1)}, u32[]{:S(2)}, u32[]{:S(2)}) collective-permute-start(bf16[128,2,256]{0,2,1:T(8,128)(2,1)S(1)} %get-tuple-element.22), channel_id=1, source_target_pairs={{0,1},{1,2},{2,3},{3,0},{4,5},{5,6},{6,7},{7,4},{8,9},{9,10},{10,1... | collective-permute-start | bytes 393224 | tf_op jit(solution)/shard_map/ppermute | solution.py:108
  23.1 0.3 compare_and_fusion
  23.6 4.1 %collective-permute-done.2 = bf16[128,2,256]{0,2,1:T(8,128)(2,1)S(1)} collective-permute-done((bf16[128,2,256]{0,2,1:T(8,128)(2,1)S(1)}, bf16[128,2,256]{0,2,1:T(8,128)(2,1)S(1)}, u32[]{:S(2)}, u32[]{:S(2)}) %collective-permute-start.2) | collective-permute-done | bytes 131104 | tf_op jit(solution)/shard_map/ppermute | solution.py:108
  27.7 12.6 %collective-permute-start.5 = (bf16[128,1024]{1,0:T(8,128)(2,1)}, bf16[128,1024]{1,0:T(8,128)(2,1)S(1)}, u32[]{:S(2)}, u32[]{:S(2)}) collective-permute-start(bf16[128,1024]{1,0:T(8,128)(2,1)} %constant_dynamic-slice_fusion.9), channel_id=1, source_target_pairs={{0,1},{1,2},{2,3},{3,0},{4,5},{5,6},{6,7},{7,4},{8,9},{9,10},{10,1... | collective-permute-start | bytes 786440 | tf_op jit(solution)/shard_map/ppermute | solution.py:108
  40.3 1.1 collective-permute-done.1
  41.5 3.6 %fusion.188 = (f32[2,2,512]{2,1,0:T(2,128)S(1)}, f32[2,2,512,512]{2,3,1,0:T(8,128)}) fusion(pred[512,512]{0,1:T(8,128)(4,1)S(1)} %compare_and_fusion, bf16[512,2,2,64]{0,3,2,1:T(8,128)(2,1)S(1)} %bitcast.268, bf16[512,2,256]{0,2,1:T(8,128)(2,1)S(1)} %pad_maximum_fusion.2), kind=kOutput, calls=%fused_computation.236 | convolution fusion | flops 138412544 | bytes 4857856 | tf_op jit(solution)/shard_map/sub | solution.py:44
  45.1 2.7 %fusion.76 = bf16[512,2,2,64]{0,3,2,1:T(8,128)(2,1)S(1)} fusion(f32[2,2,512,512]{2,3,1,0:T(8,128)} %get-tuple-element.48, f32[2,2,512]{2,1,0:T(2,128)S(1)} %get-tuple-element.47, bf16[512,2,256]{0,2,1:T(8,128)(2,1)S(1)} %pad_maximum_fusion.2), kind=kOutput, calls=%fused_computation.68 | convolution fusion | flops 136445952 | bytes 4595712 | tf_op jit(solution)/shard_map/kgqt,tkd->qkgd/dot_general | solution.py:46
  48.0 0.2 fusion.189
  48.3 3.8 %collective-permute-start.3 = (bf16[128,256]{0,1:T(8,128)(2,1)S(1)}, bf16[128,256]{0,1:T(8,128)(2,1)S(1)}, u32[]{:S(2)}, u32[]{:S(2)}) collective-permute-start(bf16[128,256]{0,1:T(8,128)(2,1)S(1)} %bitcast.270), channel_id=1, source_target_pairs={{0,3},{1,0},{2,1},{3,2},{4,7},{5,4},{6,5},{7,6},{8,11},{9,8},{10,9... | collective-permute-start | bytes 196616 | tf_op jit(solution)/shard_map/ppermute | solution.py:108
  52.1 1.0 pad_maximum_fusion
  53.2 0.3 convolution_convert_fusion.3
  53.6 1.0 copy.113
  54.5 0.2 fusion.148
  54.8 0.4 collective-permute-done.8
  55.2 1.2 fusion.151
  56.4 0.3 convolution_add_fusion.1
  56.6 0.3 fusion.114
  56.9 0.3 fusion.115
  57.2 0.4 multiply_reduce_fusion
  58.5 0.6 collective-permute-start.10
  59.1 1.8 %collective-permute-start.11 = (bf16[128,1152]{1,0:T(8,128)(2,1)S(1)}, bf16[128,1152]{1,0:T(8,128)(2,1)}, u32[]{:S(2)}, u32[]{:S(2)}) collective-permute-start(bf16[128,1152]{1,0:T(8,128)(2,1)S(1)} %concatenate.43), channel_id=1, source_target_pairs={{0,2},{1,3},{2,0},{3,1},{4,6},{5,7},{6,4},{7,5},{8,10},{9,11},{10,... | collective-permute-start | bytes 884744 | tf_op jit(solution)/shard_map/ppermute | solution.py:108
  60.9 2.3 %collective-permute-start.12 = (bf16[128,1152]{1,0:T(8,128)(2,1)S(1)}, bf16[128,1152]{1,0:T(8,128)(2,1)}, u32[]{:S(2)}, u32[]{:S(2)}) collective-permute-start(bf16[128,1152]{1,0:T(8,128)(2,1)S(1)} %concatenate.43), channel_id=1, source_target_pairs={{0,3},{1,0},{2,1},{3,2},{4,7},{5,4},{6,5},{7,6},{8,11},{9,8},{10,9... | collective-permute-start | bytes 884744 | tf_op jit(solution)/shard_map/ppermute | solution.py:108
  63.1 0.2 convolution_convert_fusion.6
  63.6 0.4 convolution_convert_fusion.2
  64.0 5.0 %convolution_bitcast_fusion.1 = f32[1,8,64,512]{3,2,1,0:T(8,128)S(1)} fusion(bf16[8,64,1024]{2,1,0:T(8,128)(2,1)S(1)} %convolution_convert_fusion.2, bf16[8,1024,512]{2,1,0:T(8,128)(2,1)} %param.22), kind=kOutput, calls=%fused_computation.45 | convolution fusion | flops 536870912 | bytes 10485760 | tf_op jit(solution)/shard_map/becd,edf->becf/dot_general | solution.py:86
  69.0 8.8 %convolution_convert_fusion.1 = bf16[8,64,1024]{2,1,0:T(8,128)(2,1)S(1)} fusion(bf16[8,512,1024]{2,1,0:T(8,128)(2,1)} %param.24, bf16[8,64,1024]{2,1,0:T(8,128)(2,1)S(1)} %convolution_convert_fusion.2, bf16[8,1024,512]{2,1,0:T(8,128)(2,1)} %param.23, f32[1,8,64,512]{3,2,1,0:T(8,128)S(1)} %convolution_bitcast_fusion.1), kind=kOutput, calls=%fused_computation.33 | convolution fusion | flops 1075838976 | bytes 19922944 | tf_op jit(solution)/shard_map/becf,efd->becd/dot_general | solution.py:96
  77.9 1.2 convolution_bitcast_fusion.2
  79.1 1.0 constant_dynamic-update-slice_fusion.2
  80.2 2.1 %collective-permute-done.11 = bf16[128,1152]{1,0:T(8,128)(2,1)} collective-permute-done((bf16[128,1152]{1,0:T(8,128)(2,1)S(1)}, bf16[128,1152]{1,0:T(8,128)(2,1)}, u32[]{:S(2)}, u32[]{:S(2)}) %collective-permute-start.11) | collective-permute-done | bytes 294944 | tf_op jit(solution)/shard_map/ppermute | solution.py:108
  82.3 1.0 constant_dynamic-update-slice_fusion.1
  83.3 1.0 constant_dynamic-update-slice_fusion
  84.8 1.0 convolution_convert_fusion
  85.8 5.5 %fusion.1 = f32[8,3,64,512]{3,2,1,0:T(8,128)S(1)} fusion(bf16[8,1024,512]{2,1,0:T(8,128)(2,1)} %param.23, bf16[3,8,64,1024]{3,2,1,0:T(8,128)(2,1)S(1)} %convolution_convert_fusion), kind=kOutput, calls=%fused_computation.1 | convolution fusion | flops 1610612736 | bytes 14680064 | tf_op jit(solution)/shard_map/becd,edf->becf/dot_general | solution.py:87
  91.4 2.1 %fusion.12 = bf16[3,8,64,512]{3,2,0,1:T(8,128)(2,1)S(1)} fusion(f32[8,3,64,512]{3,2,1,0:T(8,128)S(1)} %fusion.1, bf16[8,1024,512]{2,1,0:T(8,128)(2,1)S(1)} %bitcast.257, bf16[3,8,64,1024]{3,2,1,0:T(8,128)(2,1)S(1)} %convolution_convert_fusion), kind=kOutput, calls=%fused_computation.16 | convolution fusion | flops 1615331328 | bytes 16252928 | tf_op jit(solution)/shard_map/becd,edf->becf/dot_general | solution.py:86
  93.5 0.3 slice-done.3
  93.8 1.0 fusion.28
  94.8 2.1 %fusion.31 = bf16[3,8,64,512]{3,2,0,1:T(8,128)(2,1)} fusion(bf16[3,8,64,512]{3,2,0,1:T(8,128)(2,1)S(1)} %fusion.12, bf16[8,512,1024]{2,1,0:T(8,128)(2,1)S(1)} %bitcast.259), kind=kOutput, calls=%fused_computation.32 | convolution fusion | flops 806092800 | bytes 7340032 | tf_op jit(solution)/shard_map/becf,efd->becd/dot_general | solution.py:96
  97.1 0.4 fusion.50
  97.5 1.9 %fusion.65 = bf16[3,128,512]{2,1,0:T(8,128)(2,1)S(1)} fusion(f32[3,128,512]{2,1,0:T(8,128)S(1)} %fusion.50, bf16[3,8,64,512]{3,2,0,1:T(8,128)(2,1)} %copy-done.13, s32[3,8,128]{2,1,0:T(8,128)S(1)} %convolution_convert_fusion.5, pred[3,8,128]{2,1,0:T(8,128)(4,1)S(1)} %compare_bitcast_fusion.1, bf16[3,8,128]{2,1,0:T(8,128)(2,1)S(1)} %bitcast.275), kind=kOutput, calls=%fused_computation.54 | convolution fusion | flops 202309632 | bytes 2774016 | tf_op jit(solution)/shard_map/becr,becd->brd/dot_general | solution.py:99
  99.4 5.3 %collective-permute-start.18 = (bf16[128,512]{1,0:T(8,128)(2,1)S(1)}, bf16[128,512]{1,0:T(8,128)(2,1)S(1)}, u32[]{:S(2)}, u32[]{:S(2)}) collective-permute-start(bf16[128,512]{1,0:T(8,128)(2,1)S(1)} %get-tuple-element.27), channel_id=1, source_target_pairs={{0,1},{1,2},{2,3},{3,0},{4,5},{5,6},{6,7},{7,4},{8,9},{9,10},{10,1... | collective-permute-start | bytes 393224 | tf_op jit(solution)/shard_map/ppermute | solution.py:108
  104.7 2.7 %collective-permute-start.17 = (bf16[128,512]{1,0:T(8,128)(2,1)S(1)}, bf16[128,512]{1,0:T(8,128)(2,1)S(1)}, u32[]{:S(2)}, u32[]{:S(2)}) collective-permute-start(bf16[128,512]{1,0:T(8,128)(2,1)S(1)} %get-tuple-element.28), channel_id=1, source_target_pairs={{0,2},{1,3},{2,0},{3,1},{4,6},{5,7},{6,4},{7,5},{8,10},{9,11},{10,... | collective-permute-start | bytes 393224 | tf_op jit(solution)/shard_map/ppermute | solution.py:108
  107.4 0.4 fusion.44
  107.8 0.4 fusion.62
  108.3 2.1 %collective-permute-start.15 = (bf16[128,512]{1,0:T(8,128)(2,1)S(1)}, bf16[128,512]{1,0:T(8,128)(2,1)S(1)}, u32[]{:S(2)}, u32[]{:S(2)}) collective-permute-start(bf16[128,512]{1,0:T(8,128)(2,1)S(1)} %get-tuple-element.24), channel_id=1, source_target_pairs={{0,1},{1,2},{2,3},{3,0},{4,5},{5,6},{6,7},{7,4},{8,9},{9,10},{10,1... | collective-permute-start | bytes 393224 | tf_op jit(solution)/shard_map/ppermute | solution.py:108
  110.4 0.2 collective-permute-start.14
  110.6 0.6 collective-permute-done.18
  111.2 4.5 %collective-permute-start.13 = (bf16[128,512]{1,0:T(8,128)(2,1)S(1)}, bf16[128,512]{1,0:T(8,128)(2,1)S(1)}, u32[]{:S(2)}, u32[]{:S(2)}) collective-permute-start(bf16[128,512]{1,0:T(8,128)(2,1)S(1)} %get-tuple-element.23), channel_id=1, source_target_pairs={{0,3},{1,0},{2,1},{3,2},{4,7},{5,4},{6,5},{7,6},{8,11},{9,8},{10,9... | collective-permute-start | bytes 393224 | tf_op jit(solution)/shard_map/ppermute | solution.py:108
  115.7 4.8 %collective-permute-done.17 = bf16[128,512]{1,0:T(8,128)(2,1)S(1)} collective-permute-done((bf16[128,512]{1,0:T(8,128)(2,1)S(1)}, bf16[128,512]{1,0:T(8,128)(2,1)S(1)}, u32[]{:S(2)}, u32[]{:S(2)}) %collective-permute-start.17) | collective-permute-done | bytes 131104 | tf_op jit(solution)/shard_map/ppermute | solution.py:108
  120.6 6.5 %collective-permute-done.14 = bf16[128,512]{1,0:T(8,128)(2,1)S(1)} collective-permute-done((bf16[128,512]{1,0:T(8,128)(2,1)S(1)}, bf16[128,512]{1,0:T(8,128)(2,1)S(1)}, u32[]{:S(2)}, u32[]{:S(2)}) %collective-permute-start.14) | collective-permute-done | bytes 131104 | tf_op jit(solution)/shard_map/ppermute | solution.py:108
  127.2 1.1 fusion.94
  (114 shorter events, 3.7 us)
Async XLA Ops:
  0.6 14.3 %copy-start = (bf16[1024,1024]{1,0:T(8,128)(2,1)S(1)}, bf16[1024,1024]{1,0:T(8,128)(2,1)}, u32[]{:S(2)}) copy-start(bf16[1024,1024]{1,0:T(8,128)(2,1)} %param.16) | copy-start | bytes 6291460
  0.6 14.3 %copy-start.2 = (bf16[128,1024]{1,0:T(8,128)(2,1)S(1)}, bf16[128,1024]{1,0:T(8,128)(2,1)}, u32[]{:S(2)}) copy-start(bf16[128,1024]{1,0:T(8,128)(2,1)} %param.14) | copy-start | bytes 786436
  0.7 12.9 %copy-start.9 = (s32[1,512]{1,0:T(1,128)S(1)}, s32[1,512]{1,0:T(1,128)}, u32[]{:S(2)}) copy-start(s32[1,512]{1,0:T(1,128)} %param.25) | copy-start | bytes 6148
  2.5 45.8 %collective-permute-start.4 = (bf16[128,1024]{1,0:T(8,128)(2,1)}, bf16[128,1024]{1,0:T(8,128)(2,1)S(1)}, u32[]{:S(2)}, u32[]{:S(2)}) collective-permute-start(bf16[128,1024]{1,0:T(8,128)(2,1)} %constant_dynamic-slice_fusion.9), channel_id=1, source_target_pairs={{0,3},{1,0},{2,1},{3,2},{4,7},{5,4},{6,5},{7,6},{8,11},{9,8},{10,9... | collective-permute-start | bytes 786440 | tf_op jit(solution)/shard_map/ppermute | solution.py:108
  7.6 44.5 %collective-permute-start.6 = (bf16[128,1024]{1,0:T(8,128)(2,1)}, bf16[128,1024]{1,0:T(8,128)(2,1)}, u32[]{:S(2)}, u32[]{:S(2)}) collective-permute-start(bf16[128,1024]{1,0:T(8,128)(2,1)} %constant_dynamic-slice_fusion.9), channel_id=1, source_target_pairs={{0,2},{1,3},{2,0},{3,1},{4,6},{5,7},{6,4},{7,5},{8,10},{9,11},{10,... | collective-permute-start | bytes 786440 | tf_op jit(solution)/shard_map/ppermute | solution.py:108
  15.0 8.1 %copy-start.8 = (s32[128,8]{0,1:T(8,128)S(1)}, s32[128,8]{0,1:T(8,128)}, u32[]{:S(2)}) copy-start(s32[128,8]{0,1:T(8,128)} %param.27) | copy-start | bytes 12292
  15.9 7.4 %copy-start.10 = (s32[1,512]{1,0:T(1,128)S(1)}, s32[1,512]{1,0:T(1,128)}, u32[]{:S(2)}) copy-start(s32[1,512]{1,0:T(1,128)} %param.26) | copy-start | bytes 6148
  16.0 7.5 %copy-start.11 = (bf16[1024]{0:T(1024)(128)(2,1)S(1)}, bf16[1024]{0:T(1024)(128)(2,1)}, u32[]{:S(2)}) copy-start(bf16[1024]{0:T(1024)(128)(2,1)} %param.20) | copy-start | bytes 6148
  17.7 10.0 %collective-permute-start.2 = (bf16[128,2,256]{0,2,1:T(8,128)(2,1)S(1)}, bf16[128,2,256]{0,2,1:T(8,128)(2,1)S(1)}, u32[]{:S(2)}, u32[]{:S(2)}) collective-permute-start(bf16[128,2,256]{0,2,1:T(8,128)(2,1)S(1)} %get-tuple-element.20), channel_id=1, source_target_pairs={{0,3},{1,0},{2,1},{3,2},{4,7},{5,4},{6,5},{7,6},{8,11},{9,8},{10,9... | collective-permute-start | bytes 393224 | tf_op jit(solution)/shard_map/ppermute | solution.py:108
  18.2 23.2 %collective-permute-start.1 = (bf16[128,2,256]{0,2,1:T(8,128)(2,1)S(1)}, bf16[128,2,256]{0,2,1:T(8,128)(2,1)S(1)}, u32[]{:S(2)}, u32[]{:S(2)}) collective-permute-start(bf16[128,2,256]{0,2,1:T(8,128)(2,1)S(1)} %get-tuple-element.21), channel_id=1, source_target_pairs={{0,2},{1,3},{2,0},{3,1},{4,6},{5,7},{6,4},{7,5},{8,10},{9,11},{10,... | collective-permute-start | bytes 393224 | tf_op jit(solution)/shard_map/ppermute | solution.py:108
  20.8 20.6 %collective-permute-start = (bf16[128,2,256]{0,2,1:T(8,128)(2,1)S(1)}, bf16[128,2,256]{0,2,1:T(8,128)(2,1)S(1)}, u32[]{:S(2)}, u32[]{:S(2)}) collective-permute-start(bf16[128,2,256]{0,2,1:T(8,128)(2,1)S(1)} %get-tuple-element.22), channel_id=1, source_target_pairs={{0,1},{1,2},{2,3},{3,0},{4,5},{5,6},{6,7},{7,4},{8,9},{9,10},{10,1... | collective-permute-start | bytes 393224 | tf_op jit(solution)/shard_map/ppermute | solution.py:108
  27.7 24.4 %collective-permute-start.5 = (bf16[128,1024]{1,0:T(8,128)(2,1)}, bf16[128,1024]{1,0:T(8,128)(2,1)S(1)}, u32[]{:S(2)}, u32[]{:S(2)}) collective-permute-start(bf16[128,1024]{1,0:T(8,128)(2,1)} %constant_dynamic-slice_fusion.9), channel_id=1, source_target_pairs={{0,1},{1,2},{2,3},{3,0},{4,5},{5,6},{6,7},{7,4},{8,9},{9,10},{10,1... | collective-permute-start | bytes 786440 | tf_op jit(solution)/shard_map/ppermute | solution.py:108
  45.1 3.0 %copy-start.6 = (bf16[256,1024]{1,0:T(8,128)(2,1)S(1)}, bf16[256,1024]{1,0:T(8,128)(2,1)}, u32[]{:S(2)}) copy-start(bf16[256,1024]{1,0:T(8,128)(2,1)} %param.19) | copy-start | bytes 1572868
  47.9 6.7 %collective-permute-start.9 = (bf16[128,256]{0,1:T(8,128)(2,1)S(1)}, bf16[128,256]{0,1:T(8,128)(2,1)S(1)}, u32[]{:S(2)}, u32[]{:S(2)}) collective-permute-start(bf16[128,256]{0,1:T(8,128)(2,1)S(1)} %bitcast.272), channel_id=1, source_target_pairs={{0,1},{1,2},{2,3},{3,0},{4,5},{5,6},{6,7},{7,4},{8,9},{9,10},{10,1... | collective-permute-start | bytes 196616 | tf_op jit(solution)/shard_map/ppermute | solution.py:108
  48.0 7.2 %collective-permute-start.8 = (bf16[128,256]{0,1:T(8,128)(2,1)S(1)}, bf16[128,256]{0,1:T(8,128)(2,1)S(1)}, u32[]{:S(2)}, u32[]{:S(2)}) collective-permute-start(bf16[128,256]{0,1:T(8,128)(2,1)S(1)} %bitcast.271), channel_id=1, source_target_pairs={{0,2},{1,3},{2,0},{3,1},{4,6},{5,7},{6,4},{7,5},{8,10},{9,11},{10,... | collective-permute-start | bytes 196616 | tf_op jit(solution)/shard_map/ppermute | solution.py:108
  48.3 8.0 %collective-permute-start.3 = (bf16[128,256]{0,1:T(8,128)(2,1)S(1)}, bf16[128,256]{0,1:T(8,128)(2,1)S(1)}, u32[]{:S(2)}, u32[]{:S(2)}) collective-permute-start(bf16[128,256]{0,1:T(8,128)(2,1)S(1)} %bitcast.270), channel_id=1, source_target_pairs={{0,3},{1,0},{2,1},{3,2},{4,7},{5,4},{6,5},{7,6},{8,11},{9,8},{10,9... | collective-permute-start | bytes 196616 | tf_op jit(solution)/shard_map/ppermute | solution.py:108
  53.1 3.5 %collective-permute-start.7 = (bf16[3,128,1024]{2,1,0:T(8,128)(2,1)S(1)}, bf16[3,128,1024]{2,1,0:T(8,128)(2,1)S(1)}, u32[]{:S(2)}, u32[]{:S(2)}) collective-permute-start(bf16[3,128,1024]{2,1,0:T(8,128)(2,1)S(1)} %pad_maximum_fusion), channel_id=1, source_target_pairs={{0,4},{4,0},{8,12},{12,8},{16,20},{20,16},{24,28},{28,24},{1,5},{5... | collective-permute-start | bytes 2359304 | tf_op jit(solution)/shard_map/ppermute | solution.py:134
  56.6 1.1 copy-start.7
  57.6 5.9 %copy-start.3 = (f32[128,1024]{1,0:T(8,128)}, f32[128,1024]{1,0:T(8,128)S(1)}, u32[]{:S(2)}) copy-start(f32[128,1024]{1,0:T(8,128)S(1)} %get-tuple-element.50) | copy-start | bytes 1572868
  58.5 20.7 %collective-permute-start.10 = (bf16[128,1152]{1,0:T(8,128)(2,1)S(1)}, bf16[128,1152]{1,0:T(8,128)(2,1)}, u32[]{:S(2)}, u32[]{:S(2)}) collective-permute-start(bf16[128,1152]{1,0:T(8,128)(2,1)S(1)} %concatenate.43), channel_id=1, source_target_pairs={{0,1},{1,2},{2,3},{3,0},{4,5},{5,6},{6,7},{7,4},{8,9},{9,10},{10,1... | collective-permute-start | bytes 884744 | tf_op jit(solution)/shard_map/ppermute | solution.py:108
  59.1 23.2 %collective-permute-start.11 = (bf16[128,1152]{1,0:T(8,128)(2,1)S(1)}, bf16[128,1152]{1,0:T(8,128)(2,1)}, u32[]{:S(2)}, u32[]{:S(2)}) collective-permute-start(bf16[128,1152]{1,0:T(8,128)(2,1)S(1)} %concatenate.43), channel_id=1, source_target_pairs={{0,2},{1,3},{2,0},{3,1},{4,6},{5,7},{6,4},{7,5},{8,10},{9,11},{10,... | collective-permute-start | bytes 884744 | tf_op jit(solution)/shard_map/ppermute | solution.py:108
  60.9 22.4 %collective-permute-start.12 = (bf16[128,1152]{1,0:T(8,128)(2,1)S(1)}, bf16[128,1152]{1,0:T(8,128)(2,1)}, u32[]{:S(2)}, u32[]{:S(2)}) collective-permute-start(bf16[128,1152]{1,0:T(8,128)(2,1)S(1)} %concatenate.43), channel_id=1, source_target_pairs={{0,3},{1,0},{2,1},{3,2},{4,7},{5,4},{6,5},{7,6},{8,11},{9,8},{10,9... | collective-permute-start | bytes 884744 | tf_op jit(solution)/shard_map/ppermute | solution.py:108
  84.8 6.6 %slice-start = ((s8[8388608]{0:T(1024)(128)(4,1)}), s8[4194304]{0:T(1024)(128)(4,1)S(1)}, s32[]{:S(2)}) async-start(s8[8388608]{0:T(1024)(128)(4,1)} %bitcast.256), calls=%async_computation | async-start | bytes 8388608
  85.8 5.6 %slice-start.1 = ((s8[8388608]{0:T(1024)(128)(4,1)}), s8[4194304]{0:T(1024)(128)(4,1)S(1)}, s32[]{:S(2)}) async-start(s8[8388608]{0:T(1024)(128)(4,1)} %bitcast.256), calls=%async_computation.1 | async-start | bytes 8388608
  85.8 7.7 %slice-start.2 = ((s8[8388608]{0:T(1024)(128)(4,1)}), s8[4194304]{0:T(1024)(128)(4,1)S(1)}, s32[]{:S(2)}) async-start(s8[8388608]{0:T(1024)(128)(4,1)} %bitcast.258), calls=%async_computation.2 | async-start | bytes 8388608
  91.4 2.4 %slice-start.3 = ((s8[8388608]{0:T(1024)(128)(4,1)}), s8[4194304]{0:T(1024)(128)(4,1)S(1)}, s32[]{:S(2)}) async-start(s8[8388608]{0:T(1024)(128)(4,1)} %bitcast.258), calls=%async_computation.3 | async-start | bytes 8388608
  94.8 2.3 %copy-start.13 = (bf16[3,8,64,512]{3,2,0,1:T(8,128)(2,1)}, bf16[3,8,64,512]{3,2,0,1:T(8,128)(2,1)S(1)}, u32[]{:S(2)}) copy-start(bf16[3,8,64,512]{3,2,0,1:T(8,128)(2,1)S(1)} %fusion.28) | copy-start | bytes 4718596
  97.1 10.3 %copy-start.12 = (bf16[3,8,64,512]{3,2,0,1:T(8,128)(2,1)S(1)}, bf16[3,8,64,512]{3,2,0,1:T(8,128)(2,1)}, u32[]{:S(2)}) copy-start(bf16[3,8,64,512]{3,2,0,1:T(8,128)(2,1)} %fusion.31) | copy-start | bytes 4718596
  99.4 11.8 %collective-permute-start.18 = (bf16[128,512]{1,0:T(8,128)(2,1)S(1)}, bf16[128,512]{1,0:T(8,128)(2,1)S(1)}, u32[]{:S(2)}, u32[]{:S(2)}) collective-permute-start(bf16[128,512]{1,0:T(8,128)(2,1)S(1)} %get-tuple-element.27), channel_id=1, source_target_pairs={{0,1},{1,2},{2,3},{3,0},{4,5},{5,6},{6,7},{7,4},{8,9},{9,10},{10,1... | collective-permute-start | bytes 393224 | tf_op jit(solution)/shard_map/ppermute | solution.py:108
  104.7 15.8 %collective-permute-start.17 = (bf16[128,512]{1,0:T(8,128)(2,1)S(1)}, bf16[128,512]{1,0:T(8,128)(2,1)S(1)}, u32[]{:S(2)}, u32[]{:S(2)}) collective-permute-start(bf16[128,512]{1,0:T(8,128)(2,1)S(1)} %get-tuple-element.28), channel_id=1, source_target_pairs={{0,2},{1,3},{2,0},{3,1},{4,6},{5,7},{6,4},{7,5},{8,10},{9,11},{10,... | collective-permute-start | bytes 393224 | tf_op jit(solution)/shard_map/ppermute | solution.py:108
  107.4 13.2 %collective-permute-start.16 = (bf16[128,512]{1,0:T(8,128)(2,1)S(1)}, bf16[128,512]{1,0:T(8,128)(2,1)S(1)}, u32[]{:S(2)}, u32[]{:S(2)}) collective-permute-start(bf16[128,512]{1,0:T(8,128)(2,1)S(1)} %get-tuple-element.26), channel_id=1, source_target_pairs={{0,3},{1,0},{2,1},{3,2},{4,7},{5,4},{6,5},{7,6},{8,11},{9,8},{10,9... | collective-permute-start | bytes 393224 | tf_op jit(solution)/shard_map/ppermute | solution.py:108
  107.8 19.3 %copy-start.4 = (f32[128,1024]{1,0:T(8,128)S(1)}, f32[128,1024]{1,0:T(8,128)}, u32[]{:S(2)}) copy-start(f32[128,1024]{1,0:T(8,128)} %copy-done.3) | copy-start | bytes 1572868
  107.8 19.3 %copy-start.5 = (f32[128,1024]{1,0:T(8,128)S(1)}, f32[128,1024]{1,0:T(8,128)}, u32[]{:S(2)}) copy-start(f32[128,1024]{1,0:T(8,128)} %convolution_bitcast_fusion.2) | copy-start | bytes 1572868
  107.8 20.4 %copy-start.1 = (bf16[1024,1024]{1,0:T(8,128)(2,1)S(1)}, bf16[1024,1024]{1,0:T(8,128)(2,1)}, u32[]{:S(2)}) copy-start(bf16[1024,1024]{1,0:T(8,128)(2,1)} %param.16) | copy-start | bytes 6291460
  108.3 12.3 %collective-permute-start.15 = (bf16[128,512]{1,0:T(8,128)(2,1)S(1)}, bf16[128,512]{1,0:T(8,128)(2,1)S(1)}, u32[]{:S(2)}, u32[]{:S(2)}) collective-permute-start(bf16[128,512]{1,0:T(8,128)(2,1)S(1)} %get-tuple-element.24), channel_id=1, source_target_pairs={{0,1},{1,2},{2,3},{3,0},{4,5},{5,6},{6,7},{7,4},{8,9},{9,10},{10,1... | collective-permute-start | bytes 393224 | tf_op jit(solution)/shard_map/ppermute | solution.py:108
  110.4 16.7 %collective-permute-start.14 = (bf16[128,512]{1,0:T(8,128)(2,1)S(1)}, bf16[128,512]{1,0:T(8,128)(2,1)S(1)}, u32[]{:S(2)}, u32[]{:S(2)}) collective-permute-start(bf16[128,512]{1,0:T(8,128)(2,1)S(1)} %get-tuple-element.25), channel_id=1, source_target_pairs={{0,2},{1,3},{2,0},{3,1},{4,6},{5,7},{6,4},{7,5},{8,10},{9,11},{10,... | collective-permute-start | bytes 393224 | tf_op jit(solution)/shard_map/ppermute | solution.py:108
  111.2 15.8 %collective-permute-start.13 = (bf16[128,512]{1,0:T(8,128)(2,1)S(1)}, bf16[128,512]{1,0:T(8,128)(2,1)S(1)}, u32[]{:S(2)}, u32[]{:S(2)}) collective-permute-start(bf16[128,512]{1,0:T(8,128)(2,1)S(1)} %get-tuple-element.23), channel_id=1, source_target_pairs={{0,3},{1,0},{2,1},{3,2},{4,7},{5,4},{6,5},{7,6},{8,11},{9,8},{10,9... | collective-permute-start | bytes 393224 | tf_op jit(solution)/shard_map/ppermute | solution.py:108

commit v18 on v11

--- a/solution.py
+++ b/solution.py
@@ -95,9 +95,11 @@
         down = lax.slice_in_dim(w_down, piece * cut, (piece + 1) * cut, axis=2)
         result = jnp.einsum("becf,efd->becd", hidden, down, preferred_element_type=jnp.float32)
         result = result.astype(jnp.bfloat16)
-        partial = jnp.einsum("becr,becd->brd", high, result, preferred_element_type=jnp.float32)
-        partial = partial + jnp.einsum(
-            "becr,becd->brd", low, result, preferred_element_type=jnp.float32
+        partial = jnp.einsum(
+            "becr,becd->brd",
+            jnp.concatenate([high, low], axis=2),
+            jnp.concatenate([result, result], axis=2),
+            preferred_element_type=jnp.float32,
         )
         outs.append(partial)
     return outs

time: 128 us -> 133 us (1.039)
  other arithmetic: 8.27 us -> 11.9 us
  matrix products: 45.5 us -> 47.5 us
    select_n x0 -> x2, other arithmetic: none -> 3.66 us  [expert_mix(): high = jnp.where(picks, jnp.transpose(high, (0, 2, 1))[:, :, None, :], zero)]
    dot_general x2, matrix products: 1.42 us -> 3.44 us  [expert_mix(): jnp.einsum('becr,brd->becd', picks.astype(jnp.bfloat16), rows_all, prefer...]
    dot_general x3, matrix products: 12.2 us -> 14.1 us  [expert_mix(): jnp.einsum('becf,efd->becd', hidden, down, preferred_element_type=jnp.flo...]
    dot_general x6 -> x3, matrix products: 5.39 us -> 4.59 us  [expert_mix(): jnp.einsum('becr,becd->brd', jnp.concatenate([high, low], axis=2), jnp.co...]
    unnamed x39 -> x37, local copies, waits for them, and re-layouts: 3.35 us -> 3.25 us
  transfers between devices with their start and end apart: 19 -> 19, of which waited for: 7 -> 7; matrix products, arithmetic and copies ran while one was open for 32% -> 31% of each run, Pallas kernels for 0% -> 0%
where the time goes in v18:
time: 133 us; the launch traced here: 132 us
  matrix products  47.5 us (36%)
  starting transfers between devices  41.6 us (31%)
  waiting for transfers between devices  22.6 us (17%)
  other arithmetic  11.9 us (9%)
  local copies, waits for them, and re-layouts  7.19 us (5%)
    ppermute x18, starting transfers between devices, shifted(): lax.ppermute(x, 'exp', [(j, (j + step) % count) for j in range(count)])  41.5 us
    ppermute x18, waiting for transfers between devices, shifted(): lax.ppermute(x, 'exp', [(j, (j + step) % count) for j in range(count)])  22.6 us
    dot_general x3, matrix products, expert_mix(): jnp.einsum('becf,efd->becd', hidden, down, preferred_element_type=jnp.flo...  14.1 us
    dot_general x2, matrix products, expert_mix(): jnp.einsum('becd,edf->becf', received, w_gate, preferred_element_type=jnp...  7.01 us
    dot_general x1, matrix products, expert_mix(): jnp.einsum('becd,edf->becf', received, w_up, preferred_element_type=jnp.f...  5.4 us
    dot_general x3, matrix products, expert_mix(): jnp.einsum('becr,becd->brd', jnp.concatenate([high, low], axis=2), jnp.co...  4.59 us
    select_n x2, other arithmetic, expert_mix(): high = jnp.where(picks, jnp.transpose(high, (0, 2, 1))[:, :, None, :], zero)  3.66 us
    sub x1, matrix products, attend(): expo = jnp.exp(score - top)  3.59 us
  transfers between devices with their start and end apart: 19, of which 7 were waited for; matrix products, arithmetic and copies ran while one was open for 31% of the time, Pallas kernels for 0%

profile of v18, /device:TPU:0, one launch (start us, length us, event | category | flops | bytes accessed | tf_op | source)
XLA Modules:
  0.0 132.1 jit_solution(18010514986265298278)
XLA Ops:
  0.7 1.8 %constant_dynamic-slice_fusion.9 = bf16[128,1024]{1,0:T(8,128)(2,1)} fusion(bf16[256,1024]{1,0:T(8,128)(2,1)} %param.19, s32[]{:T(128)S(6)} %select_n.180), kind=kLoop, calls=%fused_computation.165 | loop fusion | bytes 524292 | tf_op jit(solution)/shard_map/dynamic_slice | solution.py:134
  2.5 5.1 %collective-permute-start.6 = (bf16[128,1024]{1,0:T(8,128)(2,1)}, bf16[128,1024]{1,0:T(8,128)(2,1)S(1)}, u32[]{:S(2)}, u32[]{:S(2)}) collective-permute-start(bf16[128,1024]{1,0:T(8,128)(2,1)} %constant_dynamic-slice_fusion.9), channel_id=1, source_target_pairs={{0,3},{1,0},{2,1},{3,2},{4,7},{5,4},{6,5},{7,6},{8,11},{9,8},{10,9... | collective-permute-start | bytes 786440 | tf_op jit(solution)/shard_map/ppermute | solution.py:110
  7.6 0.6 multiply_power_fusion
  8.2 0.7 convert_element_type.130
  8.9 1.1 fusion.80
  10.0 1.7 %convolution_convert_fusion.4 = bf16[128,512]{1,0:T(8,128)(2,1)S(1)} fusion(bf16[1024,512]{1,0:T(8,128)(2,1)} %param.18, bf16[128,1024]{1,0:T(8,128)(2,1)} %param.14, f32[1024]{0:T(1024)S(1)} %convert_element_type.130, f32[128]{0:T(128)S(1)} %add_rsqrt_fusion.1), kind=kOutput, calls=%fused_computation.75 | convolution fusion | flops 134807552 | bytes 1446400 | tf_op jit(solution)/shard_map/dot_general | solution.py:171
  11.8 1.9 %fusion.136 = f32[128,512]{0,1:T(8,128)S(1)} fusion(bf16[1024,512]{1,0:T(8,128)(2,1)} %param.17, bf16[128,1024]{1,0:T(8,128)(2,1)} %param.14, f32[1024]{0:T(1024)S(1)} %convert_element_type.130, f32[128]{0:T(128)S(1)} %add_rsqrt_fusion.1), kind=kOutput, calls=%fused_computation.205 | convolution fusion | flops 134742016 | bytes 1577472 | tf_op jit(solution)/shard_map/dot_general | solution.py:168
  13.9 0.3 reduce-window.9
  14.4 0.7 bitcast_subtract_fusion
  15.1 1.0 fusion.138
  16.1 0.8 dynamic-slice_convert_fusion
  16.8 0.8 multiply_cosine_fusion
  17.9 0.5 collective-permute-start.2
  18.4 2.5 %collective-permute-start.1 = (bf16[128,2,256]{0,2,1:T(8,128)(2,1)S(1)}, bf16[128,2,256]{0,2,1:T(8,128)(2,1)S(1)}, u32[]{:S(2)}, u32[]{:S(2)}) collective-permute-start(bf16[128,2,256]{0,2,1:T(8,128)(2,1)S(1)} %get-tuple-element.23), channel_id=1, source_target_pairs={{0,2},{1,3},{2,0},{3,1},{4,6},{5,7},{6,4},{7,5},{8,10},{9,11},{10,... | collective-permute-start | bytes 393224 | tf_op jit(solution)/shard_map/ppermute | solution.py:110
  21.0 1.9 %collective-permute-start = (bf16[128,2,256]{0,2,1:T(8,128)(2,1)S(1)}, bf16[128,2,256]{0,2,1:T(8,128)(2,1)S(1)}, u32[]{:S(2)}, u32[]{:S(2)}) collective-permute-start(bf16[128,2,256]{0,2,1:T(8,128)(2,1)S(1)} %get-tuple-element.24), channel_id=1, source_target_pairs={{0,1},{1,2},{2,3},{3,0},{4,5},{5,6},{6,7},{7,4},{8,9},{9,10},{10,1... | collective-permute-start | bytes 393224 | tf_op jit(solution)/shard_map/ppermute | solution.py:110
  23.3 0.3 compare_and_fusion
  23.8 4.0 %collective-permute-done.2 = bf16[128,2,256]{0,2,1:T(8,128)(2,1)S(1)} collective-permute-done((bf16[128,2,256]{0,2,1:T(8,128)(2,1)S(1)}, bf16[128,2,256]{0,2,1:T(8,128)(2,1)S(1)}, u32[]{:S(2)}, u32[]{:S(2)}) %collective-permute-start.2) | collective-permute-done | bytes 131104 | tf_op jit(solution)/shard_map/ppermute | solution.py:110
  27.8 12.5 %collective-permute-start.4 = (bf16[128,1024]{1,0:T(8,128)(2,1)}, bf16[128,1024]{1,0:T(8,128)(2,1)S(1)}, u32[]{:S(2)}, u32[]{:S(2)}) collective-permute-start(bf16[128,1024]{1,0:T(8,128)(2,1)} %constant_dynamic-slice_fusion.9), channel_id=1, source_target_pairs={{0,1},{1,2},{2,3},{3,0},{4,5},{5,6},{6,7},{7,4},{8,9},{9,10},{10,1... | collective-permute-start | bytes 786440 | tf_op jit(solution)/shard_map/ppermute | solution.py:110
  40.3 1.1 collective-permute-done.1
  41.5 3.6 %fusion.141 = (f32[2,2,512]{2,1,0:T(2,128)S(1)}, f32[2,2,512,512]{2,3,1,0:T(8,128)}) fusion(pred[512,512]{0,1:T(8,128)(4,1)S(1)} %compare_and_fusion, bf16[512,2,2,64]{0,3,2,1:T(8,128)(2,1)S(1)} %bitcast.266, bf16[512,2,256]{0,2,1:T(8,128)(2,1)S(1)} %pad_maximum_fusion.4), kind=kOutput, calls=%fused_computation.208 | convolution fusion | flops 138412544 | bytes 4857856 | tf_op jit(solution)/shard_map/sub | solution.py:44
  45.1 1.0 pad_maximum_fusion
  46.2 2.7 %fusion.71 = bf16[512,2,2,64]{0,3,2,1:T(8,128)(2,1)S(1)} fusion(f32[2,2,512,512]{2,3,1,0:T(8,128)} %get-tuple-element.54, f32[2,2,512]{2,1,0:T(2,128)S(1)} %get-tuple-element.53, bf16[512,2,256]{0,2,1:T(8,128)(2,1)S(1)} %pad_maximum_fusion.4), kind=kOutput, calls=%fused_computation.74 | convolution fusion | flops 136445952 | bytes 4595712 | tf_op jit(solution)/shard_map/kgqt,tkd->qkgd/dot_general | solution.py:46
  49.0 1.8 %collective-permute-start.9 = (bf16[128,256]{0,1:T(8,128)(2,1)S(1)}, bf16[128,256]{0,1:T(8,128)(2,1)S(1)}, u32[]{:S(2)}, u32[]{:S(2)}) collective-permute-start(bf16[128,256]{0,1:T(8,128)(2,1)S(1)} %bitcast.269), channel_id=1, source_target_pairs={{0,1},{1,2},{2,3},{3,0},{4,5},{5,6},{6,7},{7,4},{8,9},{9,10},{10,1... | collective-permute-start | bytes 196616 | tf_op jit(solution)/shard_map/ppermute | solution.py:110
  50.8 2.1 %collective-permute-start.3 = (bf16[128,256]{0,1:T(8,128)(2,1)S(1)}, bf16[128,256]{0,1:T(8,128)(2,1)S(1)}, u32[]{:S(2)}, u32[]{:S(2)}) collective-permute-start(bf16[128,256]{0,1:T(8,128)(2,1)S(1)} %bitcast.270), channel_id=1, source_target_pairs={{0,3},{1,0},{2,1},{3,2},{4,7},{5,4},{6,5},{7,6},{8,11},{9,8},{10,9... | collective-permute-start | bytes 196616 | tf_op jit(solution)/shard_map/ppermute | solution.py:110
  52.9 0.3 convolution_convert_fusion.3
  53.3 1.0 copy.109
  54.2 0.2 fusion.142
  54.5 1.1 broadcast_select_fusion.1
  55.6 1.0 collective-permute-done.3
  56.6 0.3 convolution_add_fusion.1
  56.9 0.2 fusion.90
  57.1 2.0 %collective-permute-done.8 = bf16[128,256]{0,1:T(8,128)(2,1)S(1)} collective-permute-done((bf16[128,256]{0,1:T(8,128)(2,1)S(1)}, bf16[128,256]{0,1:T(8,128)(2,1)S(1)}, u32[]{:S(2)}, u32[]{:S(2)}) %collective-permute-start.8) | collective-permute-done | bytes 65568 | tf_op jit(solution)/shard_map/ppermute | solution.py:110
  59.1 0.4 multiply_reduce_fusion
  59.6 0.2 fusion.143
  60.4 2.3 %collective-permute-start.11 = (bf16[128,1152]{1,0:T(8,128)(2,1)S(1)}, bf16[128,1152]{1,0:T(8,128)(2,1)}, u32[]{:S(2)}, u32[]{:S(2)}) collective-permute-start(bf16[128,1152]{1,0:T(8,128)(2,1)S(1)} %concatenate.63), channel_id=1, source_target_pairs={{0,2},{1,3},{2,0},{3,1},{4,6},{5,7},{6,4},{7,5},{8,10},{9,11},{10,... | collective-permute-start | bytes 884744 | tf_op jit(solution)/shard_map/ppermute | solution.py:110
  62.7 1.5 %collective-permute-start.12 = (bf16[128,1152]{1,0:T(8,128)(2,1)S(1)}, bf16[128,1152]{1,0:T(8,128)(2,1)S(1)}, u32[]{:S(2)}, u32[]{:S(2)}) collective-permute-start(bf16[128,1152]{1,0:T(8,128)(2,1)S(1)} %concatenate.63), channel_id=1, source_target_pairs={{0,3},{1,0},{2,1},{3,2},{4,7},{5,4},{6,5},{7,6},{8,11},{9,8},{10,9... | collective-permute-start | bytes 884744 | tf_op jit(solution)/shard_map/ppermute | solution.py:110
  64.2 0.2 convolution_convert_fusion.6
  64.6 0.4 convolution_convert_fusion.2
  65.1 5.0 %convolution_bitcast_fusion.1 = f32[1,8,64,512]{3,2,1,0:T(8,128)S(1)} fusion(bf16[8,64,1024]{2,1,0:T(8,128)(2,1)S(1)} %convolution_convert_fusion.2, bf16[8,1024,512]{2,1,0:T(8,128)(2,1)} %param.22), kind=kOutput, calls=%fused_computation.60 | convolution fusion | flops 536870912 | bytes 10485760 | tf_op jit(solution)/shard_map/becd,edf->becf/dot_general | solution.py:86
  70.0 9.8 %fusion.51 = bf16[1,8,64,1024]{3,2,1,0:T(8,128)(2,1)} fusion(bf16[8,512,1024]{2,1,0:T(8,128)(2,1)} %param.24, bf16[8,64,1024]{2,1,0:T(8,128)(2,1)S(1)} %convolution_convert_fusion.2, bf16[8,1024,512]{2,1,0:T(8,128)(2,1)} %param.23, f32[1,8,64,512]{3,2,1,0:T(8,128)S(1)} %convolution_bitcast_fusion.1), kind=kOutput, calls=%fused_computation.57 | convolution fusion | flops 1075838976 | bytes 19922944 | tf_op jit(solution)/shard_map/becf,efd->becd/dot_general | solution.py:96
  80.0 1.4 %fusion.99 = (bf16[1,8,64,128]{2,3,1,0:T(8,128)(2,1)}, bf16[1,8,64,128]{2,3,1,0:T(8,128)(2,1)}) fusion(s32[8,128]{1,0:T(8,128)S(1)} %convolution_convert_fusion.6, pred[8,128]{1,0:T(8,128)(4,1)S(1)} %copy.96, bf16[8,128]{1,0:T(8,128)(2,1)S(1)} %bitcast.273, bf16[8,128]{1,0:T(8,128)(2,1)S(1)} %bitcast.274), kind=kLoop, calls=%fused_computation.112 | loop fusion | flops 262144 | bytes 271360 | tf_op jit(solution)/shard_map/jit(_where)/select_n | solution.py:90
  81.5 1.0 constant_dynamic-update-slice_fusion.2
  82.5 1.2 collective-permute-done.11
  83.6 1.0 constant_dynamic-update-slice_fusion.1
  84.8 0.2 constant_dynamic-slice_fusion.5
  85.0 0.2 convolution_convert_fusion.5
  85.2 3.0 %convolution_convert_fusion = bf16[3,8,64,1024]{3,2,1,0:T(8,128)(2,1)S(1)} fusion(bf16[3,128,1024,1]{2,1,3,0:T(8,128)(2,1)S(1)} %bitcast.256, s32[3,8,128]{2,1,0:T(8,128)S(1)} %convolution_convert_fusion.5, pred[3,8,128]{2,1,0:T(8,128)(4,1)S(1)} %compare_bitcast_fusion.1), kind=kOutput, calls=%fused_computation.32 | convolution fusion | flops 404619264 | bytes 3947520 | tf_op jit(solution)/shard_map/becr,brd->becd/dot_general | solution.py:83
  88.3 5.4 %fusion.1 = f32[8,3,64,512]{3,2,1,0:T(8,128)S(1)} fusion(bf16[8,1024,512]{2,1,0:T(8,128)(2,1)} %param.23, bf16[3,8,64,1024]{3,2,1,0:T(8,128)(2,1)S(1)} %convolution_convert_fusion), kind=kOutput, calls=%fused_computation.1 | convolution fusion | flops 1610612736 | bytes 14680064 | tf_op jit(solution)/shard_map/becd,edf->becf/dot_general | solution.py:87
  93.7 2.1 %fusion.20 = bf16[3,8,64,512]{3,2,0,1:T(8,128)(2,1)S(1)} fusion(f32[8,3,64,512]{3,2,1,0:T(8,128)S(1)} %fusion.1, bf16[8,1024,512]{2,1,0:T(8,128)(2,1)S(1)} %bitcast.253, bf16[3,8,64,1024]{3,2,1,0:T(8,128)(2,1)S(1)} %convolution_convert_fusion), kind=kOutput, calls=%fused_computation.24 | convolution fusion | flops 1615331328 | bytes 16252928 | tf_op jit(solution)/shard_map/becd,edf->becf/dot_general | solution.py:86
  95.8 0.2 slice-done.3
  96.0 2.2 %fusion.43 = bf16[3,8,64,512]{3,2,1,0:T(8,128)(2,1)} fusion(bf16[8,512,1024]{2,1,0:T(8,128)(2,1)S(1)} %bitcast.255, bf16[3,8,64,512]{3,2,0,1:T(8,128)(2,1)S(1)} %fusion.20), kind=kOutput, calls=%fused_computation.51 | convolution fusion | flops 806092800 | bytes 7340032 | tf_op jit(solution)/shard_map/becf,efd->becd/dot_general | solution.py:96
  98.2 2.2 %fusion.46 = bf16[3,8,64,512]{3,2,1,0:T(8,128)(2,1)} fusion(bf16[8,512,1024]{2,1,0:T(8,128)(2,1)S(1)} %bitcast.255, bf16[3,8,64,512]{3,2,0,1:T(8,128)(2,1)S(1)} %fusion.20), kind=kOutput, calls=%fused_computation.52 | convolution fusion | flops 806092800 | bytes 7340032 | tf_op jit(solution)/shard_map/becf,efd->becd/dot_general | solution.py:96
  100.5 2.2 %fusion.42 = (bf16[3,8,64,128]{2,3,1,0:T(8,128)(2,1)S(1)}, bf16[3,8,64,128]{2,3,1,0:T(8,128)(2,1)S(1)}) fusion(s32[3,8,128]{2,1,0:T(8,128)S(1)} %convolution_convert_fusion.5, pred[3,8,128]{2,1,0:T(8,128)(4,1)S(1)} %compare_bitcast_fusion.1, bf16[3,8,128]{2,1,0:T(8,128)(2,1)S(1)} %bitcast.271, bf16[3,8,128]{2,1,0:T(8,128)(2,1)S(1)} %bitcast.272), kind=kLoop, calls=%fused_computation.50 | loop fusion | flops 786432 | bytes 814080 | tf_op jit(solution)/shard_map/jit(_where)/select_n | solution.py:90
  102.8 2.7 %fusion.63 = bf16[3,128,512]{2,1,0:T(8,128)(2,1)S(1)} fusion(bf16[3,8,64,512]{3,2,1,0:T(8,128)(2,1)} %fusion.43, bf16[3,8,64,128]{2,3,1,0:T(8,128)(2,1)S(1)} %get-tuple-element.40, bf16[3,8,64,128]{2,3,1,0:T(8,128)(2,1)S(1)} %get-tuple-element.39), kind=kOutput, calls=%fused_computation.65 | convolution fusion | flops 410714112 | bytes 2752512 | tf_op jit(solution)/shard_map/becr,becd->brd/dot_general | solution.py:98
  105.5 4.9 %collective-permute-start.18 = (bf16[128,512]{1,0:T(8,128)(2,1)S(1)}, bf16[128,512]{1,0:T(8,128)(2,1)S(1)}, u32[]{:S(2)}, u32[]{:S(2)}) collective-permute-start(bf16[128,512]{1,0:T(8,128)(2,1)S(1)} %get-tuple-element.29), channel_id=1, source_target_pairs={{0,1},{1,2},{2,3},{3,0},{4,5},{5,6},{6,7},{7,4},{8,9},{9,10},{10,1... | collective-permute-start | bytes 393224 | tf_op jit(solution)/shard_map/ppermute | solution.py:110
  110.4 1.0 collective-permute-start.17
  111.4 1.4 %collective-permute-start.16 = (bf16[128,512]{1,0:T(8,128)(2,1)S(1)}, bf16[128,512]{1,0:T(8,128)(2,1)S(1)}, u32[]{:S(2)}, u32[]{:S(2)}) collective-permute-start(bf16[128,512]{1,0:T(8,128)(2,1)S(1)} %get-tuple-element.28), channel_id=1, source_target_pairs={{0,3},{1,0},{2,1},{3,2},{4,7},{5,4},{6,5},{7,6},{8,11},{9,8},{10,9... | collective-permute-start | bytes 393224 | tf_op jit(solution)/shard_map/ppermute | solution.py:110
  112.9 0.6 fusion.60
  113.6 0.6 collective-permute-start.15
  114.2 1.9 %collective-permute-start.14 = (bf16[128,512]{1,0:T(8,128)(2,1)S(1)}, bf16[128,512]{1,0:T(8,128)(2,1)S(1)}, u32[]{:S(2)}, u32[]{:S(2)}) collective-permute-start(bf16[128,512]{1,0:T(8,128)(2,1)S(1)} %get-tuple-element.27), channel_id=1, source_target_pairs={{0,2},{1,3},{2,0},{3,1},{4,6},{5,7},{6,4},{7,5},{8,10},{9,11},{10,... | collective-permute-start | bytes 393224 | tf_op jit(solution)/shard_map/ppermute | solution.py:110
  116.2 1.3 collective-permute-start.13
  117.5 6.6 %collective-permute-done.17 = bf16[128,512]{1,0:T(8,128)(2,1)S(1)} collective-permute-done((bf16[128,512]{1,0:T(8,128)(2,1)S(1)}, bf16[128,512]{1,0:T(8,128)(2,1)S(1)}, u32[]{:S(2)}, u32[]{:S(2)}) %collective-permute-start.17) | collective-permute-done | bytes 131104 | tf_op jit(solution)/shard_map/ppermute | solution.py:110
  124.2 6.6 %collective-permute-done.14 = bf16[128,512]{1,0:T(8,128)(2,1)S(1)} collective-permute-done((bf16[128,512]{1,0:T(8,128)(2,1)S(1)}, bf16[128,512]{1,0:T(8,128)(2,1)S(1)}, u32[]{:S(2)}, u32[]{:S(2)}) %collective-permute-start.14) | collective-permute-done | bytes 131104 | tf_op jit(solution)/shard_map/ppermute | solution.py:110
  130.9 1.2 fusion.94
  (109 shorter events, 3.2 us)
Async XLA Ops:
  0.6 14.4 %copy-start = (bf16[1024,1024]{1,0:T(8,128)(2,1)S(1)}, bf16[1024,1024]{1,0:T(8,128)(2,1)}, u32[]{:S(2)}) copy-start(bf16[1024,1024]{1,0:T(8,128)(2,1)} %param.16) | copy-start | bytes 6291460
  0.6 14.4 %copy-start.2 = (bf16[128,1024]{1,0:T(8,128)(2,1)S(1)}, bf16[128,1024]{1,0:T(8,128)(2,1)}, u32[]{:S(2)}) copy-start(bf16[128,1024]{1,0:T(8,128)(2,1)} %param.14) | copy-start | bytes 786436
  0.7 13.0 %copy-start.9 = (s32[1,512]{1,0:T(1,128)S(1)}, s32[1,512]{1,0:T(1,128)}, u32[]{:S(2)}) copy-start(s32[1,512]{1,0:T(1,128)} %param.25) | copy-start | bytes 6148
  2.5 42.6 %collective-permute-start.6 = (bf16[128,1024]{1,0:T(8,128)(2,1)}, bf16[128,1024]{1,0:T(8,128)(2,1)S(1)}, u32[]{:S(2)}, u32[]{:S(2)}) collective-permute-start(bf16[128,1024]{1,0:T(8,128)(2,1)} %constant_dynamic-slice_fusion.9), channel_id=1, source_target_pairs={{0,3},{1,0},{2,1},{3,2},{4,7},{5,4},{6,5},{7,6},{8,11},{9,8},{10,9... | collective-permute-start | bytes 786440 | tf_op jit(solution)/shard_map/ppermute | solution.py:110
  7.6 37.5 %collective-permute-start.5 = (bf16[128,1024]{1,0:T(8,128)(2,1)}, bf16[128,1024]{1,0:T(8,128)(2,1)}, u32[]{:S(2)}, u32[]{:S(2)}) collective-permute-start(bf16[128,1024]{1,0:T(8,128)(2,1)} %constant_dynamic-slice_fusion.9), channel_id=1, source_target_pairs={{0,2},{1,3},{2,0},{3,1},{4,6},{5,7},{6,4},{7,5},{8,10},{9,11},{10,... | collective-permute-start | bytes 786440 | tf_op jit(solution)/shard_map/ppermute | solution.py:110
  15.1 8.2 %copy-start.8 = (s32[128,8]{0,1:T(8,128)S(1)}, s32[128,8]{0,1:T(8,128)}, u32[]{:S(2)}) copy-start(s32[128,8]{0,1:T(8,128)} %param.27) | copy-start | bytes 12292
  16.1 7.5 %copy-start.10 = (s32[1,512]{1,0:T(1,128)S(1)}, s32[1,512]{1,0:T(1,128)}, u32[]{:S(2)}) copy-start(s32[1,512]{1,0:T(1,128)} %param.26) | copy-start | bytes 6148
  16.1 7.6 %copy-start.11 = (bf16[1024]{0:T(1024)(128)(2,1)S(1)}, bf16[1024]{0:T(1024)(128)(2,1)}, u32[]{:S(2)}) copy-start(bf16[1024]{0:T(1024)(128)(2,1)} %param.20) | copy-start | bytes 6148
  17.9 9.9 %collective-permute-start.2 = (bf16[128,2,256]{0,2,1:T(8,128)(2,1)S(1)}, bf16[128,2,256]{0,2,1:T(8,128)(2,1)S(1)}, u32[]{:S(2)}, u32[]{:S(2)}) collective-permute-start(bf16[128,2,256]{0,2,1:T(8,128)(2,1)S(1)} %get-tuple-element.22), channel_id=1, source_target_pairs={{0,3},{1,0},{2,1},{3,2},{4,7},{5,4},{6,5},{7,6},{8,11},{9,8},{10,9... | collective-permute-start | bytes 393224 | tf_op jit(solution)/shard_map/ppermute | solution.py:110
  18.4 22.9 %collective-permute-start.1 = (bf16[128,2,256]{0,2,1:T(8,128)(2,1)S(1)}, bf16[128,2,256]{0,2,1:T(8,128)(2,1)S(1)}, u32[]{:S(2)}, u32[]{:S(2)}) collective-permute-start(bf16[128,2,256]{0,2,1:T(8,128)(2,1)S(1)} %get-tuple-element.23), channel_id=1, source_target_pairs={{0,2},{1,3},{2,0},{3,1},{4,6},{5,7},{6,4},{7,5},{8,10},{9,11},{10,... | collective-permute-start | bytes 393224 | tf_op jit(solution)/shard_map/ppermute | solution.py:110
  21.0 20.4 %collective-permute-start = (bf16[128,2,256]{0,2,1:T(8,128)(2,1)S(1)}, bf16[128,2,256]{0,2,1:T(8,128)(2,1)S(1)}, u32[]{:S(2)}, u32[]{:S(2)}) collective-permute-start(bf16[128,2,256]{0,2,1:T(8,128)(2,1)S(1)} %get-tuple-element.24), channel_id=1, source_target_pairs={{0,1},{1,2},{2,3},{3,0},{4,5},{5,6},{6,7},{7,4},{8,9},{9,10},{10,1... | collective-permute-start | bytes 393224 | tf_op jit(solution)/shard_map/ppermute | solution.py:110
  27.8 17.3 %collective-permute-start.4 = (bf16[128,1024]{1,0:T(8,128)(2,1)}, bf16[128,1024]{1,0:T(8,128)(2,1)S(1)}, u32[]{:S(2)}, u32[]{:S(2)}) collective-permute-start(bf16[128,1024]{1,0:T(8,128)(2,1)} %constant_dynamic-slice_fusion.9), channel_id=1, source_target_pairs={{0,1},{1,2},{2,3},{3,0},{4,5},{5,6},{6,7},{7,4},{8,9},{9,10},{10,1... | collective-permute-start | bytes 786440 | tf_op jit(solution)/shard_map/ppermute | solution.py:110
  46.1 8.4 %collective-permute-start.7 = (bf16[3,128,1024]{2,1,0:T(8,128)(2,1)S(1)}, bf16[3,128,1024]{2,1,0:T(8,128)(2,1)S(1)}, u32[]{:S(2)}, u32[]{:S(2)}) collective-permute-start(bf16[3,128,1024]{2,1,0:T(8,128)(2,1)S(1)} %pad_maximum_fusion), channel_id=1, source_target_pairs={{0,4},{4,0},{8,12},{12,8},{16,20},{20,16},{24,28},{28,24},{1,5},{5... | collective-permute-start | bytes 2359304 | tf_op jit(solution)/shard_map/ppermute | solution.py:136
  46.2 8.0 %copy-start.3 = (bf16[256,1024]{1,0:T(8,128)(2,1)S(1)}, bf16[256,1024]{1,0:T(8,128)(2,1)}, u32[]{:S(2)}) copy-start(bf16[256,1024]{1,0:T(8,128)(2,1)} %param.19) | copy-start | bytes 1572868
  49.0 7.8 %collective-permute-start.9 = (bf16[128,256]{0,1:T(8,128)(2,1)S(1)}, bf16[128,256]{0,1:T(8,128)(2,1)S(1)}, u32[]{:S(2)}, u32[]{:S(2)}) collective-permute-start(bf16[128,256]{0,1:T(8,128)(2,1)S(1)} %bitcast.269), channel_id=1, source_target_pairs={{0,1},{1,2},{2,3},{3,0},{4,5},{5,6},{6,7},{7,4},{8,9},{9,10},{10,1... | collective-permute-start | bytes 196616 | tf_op jit(solution)/shard_map/ppermute | solution.py:110
  50.8 5.7 %collective-permute-start.3 = (bf16[128,256]{0,1:T(8,128)(2,1)S(1)}, bf16[128,256]{0,1:T(8,128)(2,1)S(1)}, u32[]{:S(2)}, u32[]{:S(2)}) collective-permute-start(bf16[128,256]{0,1:T(8,128)(2,1)S(1)} %bitcast.270), channel_id=1, source_target_pairs={{0,3},{1,0},{2,1},{3,2},{4,7},{5,4},{6,5},{7,6},{8,11},{9,8},{10,9... | collective-permute-start | bytes 196616 | tf_op jit(solution)/shard_map/ppermute | solution.py:110
  52.9 6.2 %collective-permute-start.8 = (bf16[128,256]{0,1:T(8,128)(2,1)S(1)}, bf16[128,256]{0,1:T(8,128)(2,1)S(1)}, u32[]{:S(2)}, u32[]{:S(2)}) collective-permute-start(bf16[128,256]{0,1:T(8,128)(2,1)S(1)} %bitcast.268), channel_id=1, source_target_pairs={{0,2},{1,3},{2,0},{3,1},{4,6},{5,7},{6,4},{7,5},{8,10},{9,11},{10,... | collective-permute-start | bytes 196616 | tf_op jit(solution)/shard_map/ppermute | solution.py:110
  56.8 2.8 %copy-start.7 = (bf16[1024,32]{0,1:T(8,128)(2,1)S(1)}, bf16[1024,32]{0,1:T(8,128)(2,1)}, u32[]{:S(2)}) copy-start(bf16[1024,32]{0,1:T(8,128)(2,1)} %param.21) | copy-start | bytes 196612
  60.3 21.1 %collective-permute-start.10 = (bf16[128,1152]{1,0:T(8,128)(2,1)S(1)}, bf16[128,1152]{1,0:T(8,128)(2,1)}, u32[]{:S(2)}, u32[]{:S(2)}) collective-permute-start(bf16[128,1152]{1,0:T(8,128)(2,1)S(1)} %concatenate.63), channel_id=1, source_target_pairs={{0,1},{1,2},{2,3},{3,0},{4,5},{5,6},{6,7},{7,4},{8,9},{9,10},{10,1... | collective-permute-start | bytes 884744 | tf_op jit(solution)/shard_map/ppermute | solution.py:110
  60.4 23.2 %collective-permute-start.11 = (bf16[128,1152]{1,0:T(8,128)(2,1)S(1)}, bf16[128,1152]{1,0:T(8,128)(2,1)}, u32[]{:S(2)}, u32[]{:S(2)}) collective-permute-start(bf16[128,1152]{1,0:T(8,128)(2,1)S(1)} %concatenate.63), channel_id=1, source_target_pairs={{0,2},{1,3},{2,0},{3,1},{4,6},{5,7},{6,4},{7,5},{8,10},{9,11},{10,... | collective-permute-start | bytes 884744 | tf_op jit(solution)/shard_map/ppermute | solution.py:110
  62.7 21.9 %collective-permute-start.12 = (bf16[128,1152]{1,0:T(8,128)(2,1)S(1)}, bf16[128,1152]{1,0:T(8,128)(2,1)S(1)}, u32[]{:S(2)}, u32[]{:S(2)}) collective-permute-start(bf16[128,1152]{1,0:T(8,128)(2,1)S(1)} %concatenate.63), channel_id=1, source_target_pairs={{0,3},{1,0},{2,1},{3,2},{4,7},{5,4},{6,5},{7,6},{8,11},{9,8},{10,9... | collective-permute-start | bytes 884744 | tf_op jit(solution)/shard_map/ppermute | solution.py:110
  85.2 8.4 %slice-start = ((s8[8388608]{0:T(1024)(128)(4,1)}), s8[4194304]{0:T(1024)(128)(4,1)S(1)}, s32[]{:S(2)}) async-start(s8[8388608]{0:T(1024)(128)(4,1)} %bitcast.252), calls=%async_computation | async-start | bytes 8388608
  88.2 5.4 %slice-start.1 = ((s8[8388608]{0:T(1024)(128)(4,1)}), s8[4194304]{0:T(1024)(128)(4,1)S(1)}, s32[]{:S(2)}) async-start(s8[8388608]{0:T(1024)(128)(4,1)} %bitcast.252), calls=%async_computation.1 | async-start | bytes 8388608
  88.2 7.5 %slice-start.2 = ((s8[8388608]{0:T(1024)(128)(4,1)}), s8[4194304]{0:T(1024)(128)(4,1)S(1)}, s32[]{:S(2)}) async-start(s8[8388608]{0:T(1024)(128)(4,1)} %bitcast.254), calls=%async_computation.2 | async-start | bytes 8388608
  93.7 2.3 %slice-start.3 = ((s8[8388608]{0:T(1024)(128)(4,1)}), s8[4194304]{0:T(1024)(128)(4,1)S(1)}, s32[]{:S(2)}) async-start(s8[8388608]{0:T(1024)(128)(4,1)} %bitcast.254), calls=%async_computation.3 | async-start | bytes 8388608
  102.8 10.1 %copy-start.12 = (bf16[3,8,64,512]{3,2,1,0:T(8,128)(2,1)S(1)}, bf16[3,8,64,512]{3,2,1,0:T(8,128)(2,1)}, u32[]{:S(2)}) copy-start(bf16[3,8,64,512]{3,2,1,0:T(8,128)(2,1)} %fusion.46) | copy-start | bytes 4718596
  105.5 10.7 %collective-permute-start.18 = (bf16[128,512]{1,0:T(8,128)(2,1)S(1)}, bf16[128,512]{1,0:T(8,128)(2,1)S(1)}, u32[]{:S(2)}, u32[]{:S(2)}) collective-permute-start(bf16[128,512]{1,0:T(8,128)(2,1)S(1)} %get-tuple-element.29), channel_id=1, source_target_pairs={{0,1},{1,2},{2,3},{3,0},{4,5},{5,6},{6,7},{7,4},{8,9},{9,10},{10,1... | collective-permute-start | bytes 393224 | tf_op jit(solution)/shard_map/ppermute | solution.py:110
  110.4 13.7 %collective-permute-start.17 = (bf16[128,512]{1,0:T(8,128)(2,1)S(1)}, bf16[128,512]{1,0:T(8,128)(2,1)S(1)}, u32[]{:S(2)}, u32[]{:S(2)}) collective-permute-start(bf16[128,512]{1,0:T(8,128)(2,1)S(1)} %get-tuple-element.30), channel_id=1, source_target_pairs={{0,2},{1,3},{2,0},{3,1},{4,6},{5,7},{6,4},{7,5},{8,10},{9,11},{10,... | collective-permute-start | bytes 393224 | tf_op jit(solution)/shard_map/ppermute | solution.py:110
  111.4 19.4 %copy-start.4 = (bf16[1,8,64,1024]{3,2,1,0:T(8,128)(2,1)S(1)}, bf16[1,8,64,1024]{3,2,1,0:T(8,128)(2,1)}, u32[]{:S(2)}) copy-start(bf16[1,8,64,1024]{3,2,1,0:T(8,128)(2,1)} %fusion.51) | copy-start | bytes 3145732
  111.4 19.4 %copy-start.5 = (bf16[1,8,64,128]{2,3,1,0:T(8,128)(2,1)S(1)}, bf16[1,8,64,128]{2,3,1,0:T(8,128)(2,1)}, u32[]{:S(2)}) copy-start(bf16[1,8,64,128]{2,3,1,0:T(8,128)(2,1)} %get-tuple-element.41) | copy-start | bytes 393220
  111.4 19.5 %copy-start.6 = (bf16[1,8,64,128]{2,3,1,0:T(8,128)(2,1)S(1)}, bf16[1,8,64,128]{2,3,1,0:T(8,128)(2,1)}, u32[]{:S(2)}) copy-start(bf16[1,8,64,128]{2,3,1,0:T(8,128)(2,1)} %get-tuple-element.42) | copy-start | bytes 393220
  111.4 12.7 %collective-permute-start.16 = (bf16[128,512]{1,0:T(8,128)(2,1)S(1)}, bf16[128,512]{1,0:T(8,128)(2,1)S(1)}, u32[]{:S(2)}, u32[]{:S(2)}) collective-permute-start(bf16[128,512]{1,0:T(8,128)(2,1)S(1)} %get-tuple-element.28), channel_id=1, source_target_pairs={{0,3},{1,0},{2,1},{3,2},{4,7},{5,4},{6,5},{7,6},{8,11},{9,8},{10,9... | collective-permute-start | bytes 393224 | tf_op jit(solution)/shard_map/ppermute | solution.py:110
  113.6 18.6 %copy-start.1 = (bf16[1024,1024]{1,0:T(8,128)(2,1)S(1)}, bf16[1024,1024]{1,0:T(8,128)(2,1)}, u32[]{:S(2)}) copy-start(bf16[1024,1024]{1,0:T(8,128)(2,1)} %param.16) | copy-start | bytes 6291460
  113.6 10.6 %collective-permute-start.15 = (bf16[128,512]{1,0:T(8,128)(2,1)S(1)}, bf16[128,512]{1,0:T(8,128)(2,1)S(1)}, u32[]{:S(2)}, u32[]{:S(2)}) collective-permute-start(bf16[128,512]{1,0:T(8,128)(2,1)S(1)} %get-tuple-element.26), channel_id=1, source_target_pairs={{0,1},{1,2},{2,3},{3,0},{4,5},{5,6},{6,7},{7,4},{8,9},{9,10},{10,1... | collective-permute-start | bytes 393224 | tf_op jit(solution)/shard_map/ppermute | solution.py:110
  114.2 16.6 %collective-permute-start.14 = (bf16[128,512]{1,0:T(8,128)(2,1)S(1)}, bf16[128,512]{1,0:T(8,128)(2,1)S(1)}, u32[]{:S(2)}, u32[]{:S(2)}) collective-permute-start(bf16[128,512]{1,0:T(8,128)(2,1)S(1)} %get-tuple-element.27), channel_id=1, source_target_pairs={{0,2},{1,3},{2,0},{3,1},{4,6},{5,7},{6,4},{7,5},{8,10},{9,11},{10,... | collective-permute-start | bytes 393224 | tf_op jit(solution)/shard_map/ppermute | solution.py:110
  116.2 14.6 %collective-permute-start.13 = (bf16[128,512]{1,0:T(8,128)(2,1)S(1)}, bf16[128,512]{1,0:T(8,128)(2,1)S(1)}, u32[]{:S(2)}, u32[]{:S(2)}) collective-permute-start(bf16[128,512]{1,0:T(8,128)(2,1)S(1)} %get-tuple-element.25), channel_id=1, source_target_pairs={{0,3},{1,0},{2,1},{3,2},{4,7},{5,4},{6,5},{7,6},{8,11},{9,8},{10,9... | collective-permute-start | bytes 393224 | tf_op jit(solution)/shard_map/ppermute | solution.py:110

commit v19 on v11

--- a/solution.py
+++ b/solution.py
@@ -202,7 +202,7 @@
     experts = w_router.shape[1]
     moe = expert_mix(packed, 1, width, experts, w_gate, w_up, w_down, 1)[0][0]
     received = jnp.concatenate([shifted(packed, step) for step in range(1, owners)])
-    pieces = expert_mix(received, owners - 1, width, experts, w_gate, w_up, w_down, 2)
+    pieces = expert_mix(received, owners - 1, width, experts, w_gate, w_up, w_down, 4)
     backs = []
     for piece in pieces:
         piece = piece.astype(jnp.bfloat16)

time: 128 us -> 134 us (1.047)
  starting transfers between devices: 41.7 us -> 53.1 us
  waiting for transfers between devices: 22.2 us -> 12.1 us
  matrix products: 45.5 us -> 50.6 us
    ppermute x18 -> x24, starting transfers between devices: 41.6 us -> 53 us  [shifted(): lax.ppermute(x, 'exp', [(j, (j + step) % count) for j in range(count)])]
    ppermute x18 -> x24, waiting for transfers between devices: 22.2 us -> 12 us  [shifted(): lax.ppermute(x, 'exp', [(j, (j + step) % count) for j in range(count)])]
    dot_general x3 -> x5, matrix products: 12.2 us -> 15.3 us  [expert_mix(): jnp.einsum('becf,efd->becd', hidden, down, preferred_element_type=jnp.flo...]
    dot_general x3 -> x5, matrix products: 1.91 us -> 3.65 us  [expert_mix(): jnp.einsum('becr,becd->brd', high, result, preferred_element_type=jnp.flo...]
    dot_general x3 -> x5, matrix products: 3.47 us -> 3.74 us  [expert_mix(): jnp.einsum('becr,becd->brd', low, result, preferred_element_type=jnp.floa...]
    unnamed x39 -> x41, local copies, waits for them, and re-layouts: 3.35 us -> 3.35 us
  transfers between devices with their start and end apart: 19 -> 25, of which waited for: 7 -> 6; matrix products, arithmetic and copies ran while one was open for 32% -> 31% of each run, Pallas kernels for 0% -> 0%
where the time goes in v19:
time: 134 us
  starting transfers between devices  53.1 us (40%)
  matrix products  50.6 us (38%)
  waiting for transfers between devices  12.1 us (9%)
  local copies, waits for them, and re-layouts  8.25 us (6%)
  other arithmetic  8.25 us (6%)
  between operations  1.41 us (1%)
    ppermute x24, starting transfers between devices, shifted(): lax.ppermute(x, 'exp', [(j, (j + step) % count) for j in range(count)])  53 us
    dot_general x5, matrix products, expert_mix(): jnp.einsum('becf,efd->becd', hidden, down, preferred_element_type=jnp.flo...  15.3 us
    ppermute x24, waiting for transfers between devices, shifted(): lax.ppermute(x, 'exp', [(j, (j + step) % count) for j in range(count)])  12 us
    dot_general x2, matrix products, expert_mix(): jnp.einsum('becd,edf->becf', received, w_gate, preferred_element_type=jnp...  8.03 us
    dot_general x1, matrix products, expert_mix(): jnp.einsum('becd,edf->becf', received, w_up, preferred_element_type=jnp.f...  5.54 us
    dot_general x5, matrix products, expert_mix(): jnp.einsum('becr,becd->brd', low, result, preferred_element_type=jnp.floa...  3.74 us
    dot_general x5, matrix products, expert_mix(): jnp.einsum('becr,becd->brd', high, result, preferred_element_type=jnp.flo...  3.65 us
    sub x1, matrix products, attend(): expo = jnp.exp(score - top)  3.58 us
  transfers between devices with their start and end apart: 25, of which 6 were waited for; matrix products, arithmetic and copies ran while one was open for 31% of the time, Pallas kernels for 0%

profile of v19, /device:TPU:0, one launch (start us, length us, event | category | flops | bytes accessed | tf_op | source)
XLA Modules:
  0.0 133.7 jit_solution(16226760929902072692)
XLA Ops:
  0.7 1.8 %constant_dynamic-slice_fusion.9 = bf16[128,1024]{1,0:T(8,128)(2,1)} fusion(bf16[256,1024]{1,0:T(8,128)(2,1)} %param.19, s32[]{:T(128)S(6)} %select_n.170), kind=kLoop, calls=%fused_computation.227 | loop fusion | bytes 524292 | tf_op jit(solution)/shard_map/dynamic_slice | solution.py:132
  2.5 5.1 %collective-permute-start.6 = (bf16[128,1024]{1,0:T(8,128)(2,1)}, bf16[128,1024]{1,0:T(8,128)(2,1)S(1)}, u32[]{:S(2)}, u32[]{:S(2)}) collective-permute-start(bf16[128,1024]{1,0:T(8,128)(2,1)} %constant_dynamic-slice_fusion.9), channel_id=1, source_target_pairs={{0,3},{1,0},{2,1},{3,2},{4,7},{5,4},{6,5},{7,6},{8,11},{9,8},{10,9... | collective-permute-start | bytes 786440 | tf_op jit(solution)/shard_map/ppermute | solution.py:108
  7.6 0.6 multiply_power_fusion
  8.2 0.7 convert_element_type.160
  8.9 1.1 fusion.97
  10.0 1.7 %convolution_convert_fusion.4 = bf16[128,512]{1,0:T(8,128)(2,1)S(1)} fusion(bf16[1024,512]{1,0:T(8,128)(2,1)} %param.18, bf16[128,1024]{1,0:T(8,128)(2,1)} %param.14, f32[1024]{0:T(1024)S(1)} %convert_element_type.160, f32[128]{0:T(128)S(1)} %add_rsqrt_fusion.1), kind=kOutput, calls=%fused_computation.80 | convolution fusion | flops 134807552 | bytes 1446400 | tf_op jit(solution)/shard_map/dot_general | solution.py:169
  11.8 1.9 %fusion.203 = f32[128,512]{0,1:T(8,128)S(1)} fusion(bf16[1024,512]{1,0:T(8,128)(2,1)} %param.17, bf16[128,1024]{1,0:T(8,128)(2,1)} %param.14, f32[1024]{0:T(1024)S(1)} %convert_element_type.160, f32[128]{0:T(128)S(1)} %add_rsqrt_fusion.1), kind=kOutput, calls=%fused_computation.274 | convolution fusion | flops 134742016 | bytes 1577472 | tf_op jit(solution)/shard_map/dot_general | solution.py:166
  14.4 0.7 bitcast_subtract_fusion
  15.1 1.0 fusion.205
  16.1 0.8 dynamic-slice_convert_fusion
  16.8 0.8 multiply_cosine_fusion
  17.9 0.5 collective-permute-start.2
  18.4 2.6 %collective-permute-start.1 = (bf16[128,2,256]{0,2,1:T(8,128)(2,1)S(1)}, bf16[128,2,256]{0,2,1:T(8,128)(2,1)S(1)}, u32[]{:S(2)}, u32[]{:S(2)}) collective-permute-start(bf16[128,2,256]{0,2,1:T(8,128)(2,1)S(1)} %get-tuple-element.23), channel_id=1, source_target_pairs={{0,2},{1,3},{2,0},{3,1},{4,6},{5,7},{6,4},{7,5},{8,10},{9,11},{10,... | collective-permute-start | bytes 393224 | tf_op jit(solution)/shard_map/ppermute | solution.py:108
  21.0 1.9 %collective-permute-start = (bf16[128,2,256]{0,2,1:T(8,128)(2,1)S(1)}, bf16[128,2,256]{0,2,1:T(8,128)(2,1)S(1)}, u32[]{:S(2)}, u32[]{:S(2)}) collective-permute-start(bf16[128,2,256]{0,2,1:T(8,128)(2,1)S(1)} %get-tuple-element.24), channel_id=1, source_target_pairs={{0,1},{1,2},{2,3},{3,0},{4,5},{5,6},{6,7},{7,4},{8,9},{9,10},{10,1... | collective-permute-start | bytes 393224 | tf_op jit(solution)/shard_map/ppermute | solution.py:108
  23.8 4.0 %collective-permute-done.2 = bf16[128,2,256]{0,2,1:T(8,128)(2,1)S(1)} collective-permute-done((bf16[128,2,256]{0,2,1:T(8,128)(2,1)S(1)}, bf16[128,2,256]{0,2,1:T(8,128)(2,1)S(1)}, u32[]{:S(2)}, u32[]{:S(2)}) %collective-permute-start.2) | collective-permute-done | bytes 131104 | tf_op jit(solution)/shard_map/ppermute | solution.py:108
  27.8 12.5 %collective-permute-start.4 = (bf16[128,1024]{1,0:T(8,128)(2,1)}, bf16[128,1024]{1,0:T(8,128)(2,1)S(1)}, u32[]{:S(2)}, u32[]{:S(2)}) collective-permute-start(bf16[128,1024]{1,0:T(8,128)(2,1)} %constant_dynamic-slice_fusion.9), channel_id=1, source_target_pairs={{0,1},{1,2},{2,3},{3,0},{4,5},{5,6},{6,7},{7,4},{8,9},{9,10},{10,1... | collective-permute-start | bytes 786440 | tf_op jit(solution)/shard_map/ppermute | solution.py:108
  40.3 1.1 collective-permute-done.1
  41.5 3.6 %fusion.208 = (f32[2,2,512]{2,1,0:T(2,128)S(1)}, f32[2,2,512,512]{2,3,1,0:T(8,128)}) fusion(pred[512,512]{0,1:T(8,128)(4,1)S(1)} %compare_and_fusion, bf16[512,2,2,64]{0,3,2,1:T(8,128)(2,1)S(1)} %bitcast.326, bf16[512,2,256]{0,2,1:T(8,128)(2,1)S(1)} %pad_maximum_fusion.3), kind=kOutput, calls=%fused_computation.277 | convolution fusion | flops 138412544 | bytes 4857856 | tf_op jit(solution)/shard_map/sub | solution.py:44
  45.1 1.0 pad_maximum_fusion
  46.2 2.7 %fusion.67 = bf16[512,2,2,64]{0,3,2,1:T(8,128)(2,1)S(1)} fusion(f32[2,2,512,512]{2,3,1,0:T(8,128)} %get-tuple-element.56, f32[2,2,512]{2,1,0:T(2,128)S(1)} %get-tuple-element.55, bf16[512,2,256]{0,2,1:T(8,128)(2,1)S(1)} %pad_maximum_fusion.3), kind=kOutput, calls=%fused_computation.79 | convolution fusion | flops 136445952 | bytes 4595712 | tf_op jit(solution)/shard_map/kgqt,tkd->qkgd/dot_general | solution.py:46
  49.0 1.8 %collective-permute-start.9 = (bf16[128,256]{0,1:T(8,128)(2,1)S(1)}, bf16[128,256]{0,1:T(8,128)(2,1)S(1)}, u32[]{:S(2)}, u32[]{:S(2)}) collective-permute-start(bf16[128,256]{0,1:T(8,128)(2,1)S(1)} %bitcast.329), channel_id=1, source_target_pairs={{0,1},{1,2},{2,3},{3,0},{4,5},{5,6},{6,7},{7,4},{8,9},{9,10},{10,1... | collective-permute-start | bytes 196616 | tf_op jit(solution)/shard_map/ppermute | solution.py:108
  50.8 2.1 %collective-permute-start.3 = (bf16[128,256]{0,1:T(8,128)(2,1)S(1)}, bf16[128,256]{0,1:T(8,128)(2,1)S(1)}, u32[]{:S(2)}, u32[]{:S(2)}) collective-permute-start(bf16[128,256]{0,1:T(8,128)(2,1)S(1)} %bitcast.330), channel_id=1, source_target_pairs={{0,3},{1,0},{2,1},{3,2},{4,7},{5,4},{6,5},{7,6},{8,11},{9,8},{10,9... | collective-permute-start | bytes 196616 | tf_op jit(solution)/shard_map/ppermute | solution.py:108
  52.9 0.3 convolution_convert_fusion.3
  53.3 1.0 copy.133
  54.5 1.1 broadcast_select_fusion.1
  55.6 1.0 collective-permute-done.3
  57.1 2.0 %collective-permute-done.8 = bf16[128,256]{0,1:T(8,128)(2,1)S(1)} collective-permute-done((bf16[128,256]{0,1:T(8,128)(2,1)S(1)}, bf16[128,256]{0,1:T(8,128)(2,1)S(1)}, u32[]{:S(2)}, u32[]{:S(2)}) %collective-permute-start.8) | collective-permute-done | bytes 65568 | tf_op jit(solution)/shard_map/ppermute | solution.py:108
  59.1 0.4 multiply_reduce_fusion
  60.4 2.3 %collective-permute-start.11 = (bf16[128,1152]{1,0:T(8,128)(2,1)S(1)}, bf16[128,1152]{1,0:T(8,128)(2,1)}, u32[]{:S(2)}, u32[]{:S(2)}) collective-permute-start(bf16[128,1152]{1,0:T(8,128)(2,1)S(1)} %concatenate.47), channel_id=1, source_target_pairs={{0,2},{1,3},{2,0},{3,1},{4,6},{5,7},{6,4},{7,5},{8,10},{9,11},{10,... | collective-permute-start | bytes 884744 | tf_op jit(solution)/shard_map/ppermute | solution.py:108
  62.7 1.5 %collective-permute-start.12 = (bf16[128,1152]{1,0:T(8,128)(2,1)S(1)}, bf16[128,1152]{1,0:T(8,128)(2,1)}, u32[]{:S(2)}, u32[]{:S(2)}) collective-permute-start(bf16[128,1152]{1,0:T(8,128)(2,1)S(1)} %concatenate.47), channel_id=1, source_target_pairs={{0,3},{1,0},{2,1},{3,2},{4,7},{5,4},{6,5},{7,6},{8,11},{9,8},{10,9... | collective-permute-start | bytes 884744 | tf_op jit(solution)/shard_map/ppermute | solution.py:108
  64.6 0.5 convolution_convert_fusion.2
  65.1 6.0 %convolution_bitcast_fusion.1 = f32[1,8,64,512]{3,2,1,0:T(8,128)} fusion(bf16[8,64,1024]{2,1,0:T(8,128)(2,1)S(1)} %convolution_convert_fusion.2, bf16[8,1024,512]{2,1,0:T(8,128)(2,1)} %param.22), kind=kOutput, calls=%fused_computation.47 | convolution fusion | flops 536870912 | bytes 10485760 | tf_op jit(solution)/shard_map/becd,edf->becf/dot_general | solution.py:86
  71.1 9.1 %convolution_convert_fusion.1 = bf16[8,64,1024]{2,1,0:T(8,128)(2,1)S(1)} fusion(bf16[8,512,1024]{2,1,0:T(8,128)(2,1)} %param.24, bf16[8,64,1024]{2,1,0:T(8,128)(2,1)S(1)} %convolution_convert_fusion.2, bf16[8,1024,512]{2,1,0:T(8,128)(2,1)} %param.23, f32[1,8,64,512]{3,2,1,0:T(8,128)} %convolution_bitcast_fusion.1), kind=kOutput, calls=%fused_computation.39 | convolution fusion | flops 1075838976 | bytes 19922944 | tf_op jit(solution)/shard_map/becf,efd->becd/dot_general | solution.py:96
  80.3 1.2 convolution_bitcast_fusion.2
  81.6 1.0 constant_dynamic-update-slice_fusion.2
  82.6 1.0 collective-permute-done.11
  83.5 1.0 constant_dynamic-update-slice_fusion.1
  84.6 1.0 constant_dynamic-update-slice_fusion
  86.1 1.0 convolution_convert_fusion
  87.1 5.5 %fusion.1 = f32[8,3,64,512]{3,2,1,0:T(8,128)S(1)} fusion(bf16[8,1024,512]{2,1,0:T(8,128)(2,1)} %param.23, bf16[3,8,64,1024]{3,2,1,0:T(8,128)(2,1)S(1)} %convolution_convert_fusion), kind=kOutput, calls=%fused_computation.1 | convolution fusion | flops 1610612736 | bytes 14680064 | tf_op jit(solution)/shard_map/becd,edf->becf/dot_general | solution.py:87
  92.7 2.1 %fusion.6 = bf16[3,8,64,512]{3,2,0,1:T(8,128)(2,1)S(1)} fusion(f32[8,3,64,512]{3,2,1,0:T(8,128)S(1)} %fusion.1, bf16[8,1024,512]{2,1,0:T(8,128)(2,1)S(1)} %bitcast.313, bf16[3,8,64,1024]{3,2,1,0:T(8,128)(2,1)S(1)} %convolution_convert_fusion), kind=kOutput, calls=%fused_computation.10 | convolution fusion | flops 1615331328 | bytes 16252928 | tf_op jit(solution)/shard_map/becd,edf->becf/dot_general | solution.py:86
  95.1 1.5 %fusion.42 = bf16[3,8,64,256]{3,2,0,1:T(8,128)(2,1)} fusion(bf16[3,8,64,512]{3,2,0,1:T(8,128)(2,1)S(1)} %fusion.6, bf16[8,512,1024]{2,1,0:T(8,128)(2,1)S(1)} %bitcast.315), kind=kOutput, calls=%fused_computation.49 | convolution fusion | flops 403046400 | bytes 4456448 | tf_op jit(solution)/shard_map/becf,efd->becd/dot_general | solution.py:96
  96.6 1.6 %fusion.45 = bf16[3,8,64,256]{3,2,0,1:T(8,128)(2,1)} fusion(bf16[3,8,64,512]{3,2,0,1:T(8,128)(2,1)S(1)} %fusion.6, bf16[8,512,1024]{2,1,0:T(8,128)(2,1)S(1)} %bitcast.315), kind=kOutput, calls=%fused_computation.50 | convolution fusion | flops 403046400 | bytes 4456448 | tf_op jit(solution)/shard_map/becf,efd->becd/dot_general | solution.py:96
  98.2 1.5 %fusion.48 = bf16[3,8,64,256]{3,2,0,1:T(8,128)(2,1)} fusion(bf16[3,8,64,512]{3,2,0,1:T(8,128)(2,1)S(1)} %fusion.6, bf16[8,512,1024]{2,1,0:T(8,128)(2,1)S(1)} %bitcast.315), kind=kOutput, calls=%fused_computation.51 | convolution fusion | flops 403046400 | bytes 4456448 | tf_op jit(solution)/shard_map/becf,efd->becd/dot_general | solution.py:96
  99.7 1.5 %fusion.51 = bf16[3,8,64,256]{3,2,0,1:T(8,128)(2,1)} fusion(bf16[3,8,64,512]{3,2,0,1:T(8,128)(2,1)S(1)} %fusion.6, bf16[8,512,1024]{2,1,0:T(8,128)(2,1)S(1)} %bitcast.315), kind=kOutput, calls=%fused_computation.52 | convolution fusion | flops 403046400 | bytes 4456448 | tf_op jit(solution)/shard_map/becf,efd->becd/dot_general | solution.py:96
  101.4 1.5 %convolution_bitcast_fusion.4 = f32[3,128,256]{2,1,0:T(8,128)S(1)} fusion(bf16[3,8,64,256]{3,2,0,1:T(8,128)(2,1)} %fusion.42, s32[3,8,128]{2,1,0:T(8,128)S(1)} %convolution_convert_fusion.5, pred[3,8,128]{2,1,0:T(8,128)(4,1)S(1)} %compare_bitcast_fusion.1, bf16[3,8,128]{2,1,0:T(8,128)(2,1)S(1)} %bitcast.337), kind=kOutput, calls=%fused_computation.62 | convolution fusion | flops 101253120 | bytes 1201152 | tf_op jit(solution)/shard_map/becr,becd->brd/dot_general | solution.py:99
  103.0 1.5 %fusion.63 = bf16[3,128,256]{2,1,0:T(8,128)(2,1)S(1)} fusion(f32[3,128,256]{2,1,0:T(8,128)S(1)} %convolution_bitcast_fusion.4, bf16[3,8,64,256]{3,2,0,1:T(8,128)(2,1)} %fusion.42, s32[3,8,128]{2,1,0:T(8,128)S(1)} %convolution_convert_fusion.5, pred[3,8,128]{2,1,0:T(8,128)(4,1)S(1)} %compare_bitcast_fusion.1, bf16[3,8,128]{2,1,0:T(8,128)(2,1)S(1)} %bitcast.333), kind=kOutput, calls=%fused_computation.75 | convolution fusion | flops 101449728 | bytes 1397760 | tf_op jit(solution)/shard_map/becr,becd->brd/dot_general | solution.py:98
  104.6 5.0 %collective-permute-start.24 = (bf16[128,256]{1,0:T(8,128)(2,1)S(1)}, bf16[128,256]{1,0:T(8,128)(2,1)S(1)}, u32[]{:S(2)}, u32[]{:S(2)}) collective-permute-start(bf16[128,256]{1,0:T(8,128)(2,1)S(1)} %get-tuple-element.43), channel_id=1, source_target_pairs={{0,1},{1,2},{2,3},{3,0},{4,5},{5,6},{6,7},{7,4},{8,9},{9,10},{10,1... | collective-permute-start | bytes 196616 | tf_op jit(solution)/shard_map/ppermute | solution.py:108
  109.6 1.0 collective-permute-start.23
  110.5 1.5 %collective-permute-start.22 = (bf16[128,256]{1,0:T(8,128)(2,1)S(1)}, bf16[128,256]{1,0:T(8,128)(2,1)S(1)}, u32[]{:S(2)}, u32[]{:S(2)}) collective-permute-start(bf16[128,256]{1,0:T(8,128)(2,1)S(1)} %get-tuple-element.42), channel_id=1, source_target_pairs={{0,3},{1,0},{2,1},{3,2},{4,7},{5,4},{6,5},{7,6},{8,11},{9,8},{10,9... | collective-permute-start | bytes 196616 | tf_op jit(solution)/shard_map/ppermute | solution.py:108
  112.4 0.3 fusion.64
  112.7 0.6 collective-permute-start.21
  113.3 2.0 %collective-permute-start.20 = (bf16[128,256]{1,0:T(8,128)(2,1)S(1)}, bf16[128,256]{1,0:T(8,128)(2,1)S(1)}, u32[]{:S(2)}, u32[]{:S(2)}) collective-permute-start(bf16[128,256]{1,0:T(8,128)(2,1)S(1)} %get-tuple-element.41), channel_id=1, source_target_pairs={{0,2},{1,3},{2,0},{3,1},{4,6},{5,7},{6,4},{7,5},{8,10},{9,11},{10,... | collective-permute-start | bytes 196616 | tf_op jit(solution)/shard_map/ppermute | solution.py:108
  115.7 0.3 fusion.65
  116.1 0.3 convolution_bitcast_fusion.10
  116.4 0.3 fusion.66
  116.8 1.4 %collective-permute-start.19 = (bf16[128,256]{1,0:T(8,128)(2,1)S(1)}, bf16[128,256]{1,0:T(8,128)(2,1)S(1)}, u32[]{:S(2)}, u32[]{:S(2)}) collective-permute-start(bf16[128,256]{1,0:T(8,128)(2,1)S(1)} %get-tuple-element.39), channel_id=1, source_target_pairs={{0,3},{1,0},{2,1},{3,2},{4,7},{5,4},{6,5},{7,6},{8,11},{9,8},{10,9... | collective-permute-start | bytes 196616 | tf_op jit(solution)/shard_map/ppermute | solution.py:108
  118.2 0.7 collective-permute-start.18
  118.9 1.4 %collective-permute-start.17 = (bf16[128,256]{1,0:T(8,128)(2,1)S(1)}, bf16[128,256]{1,0:T(8,128)(2,1)S(1)}, u32[]{:S(2)}, u32[]{:S(2)}) collective-permute-start(bf16[128,256]{1,0:T(8,128)(2,1)S(1)} %get-tuple-element.38), channel_id=1, source_target_pairs={{0,2},{1,3},{2,0},{3,1},{4,6},{5,7},{6,4},{7,5},{8,10},{9,11},{10,... | collective-permute-start | bytes 196616 | tf_op jit(solution)/shard_map/ppermute | solution.py:108
  120.3 2.9 %collective-permute-start.16 = (bf16[128,256]{1,0:T(8,128)(2,1)S(1)}, bf16[128,256]{1,0:T(8,128)(2,1)S(1)}, u32[]{:S(2)}, u32[]{:S(2)}) collective-permute-start(bf16[128,256]{1,0:T(8,128)(2,1)S(1)} %get-tuple-element.36), channel_id=1, source_target_pairs={{0,3},{1,0},{2,1},{3,2},{4,7},{5,4},{6,5},{7,6},{8,11},{9,8},{10,9... | collective-permute-start | bytes 196616 | tf_op jit(solution)/shard_map/ppermute | solution.py:108
  123.2 2.2 %collective-permute-start.14 = (bf16[128,256]{1,0:T(8,128)(2,1)S(1)}, bf16[128,256]{1,0:T(8,128)(2,1)S(1)}, u32[]{:S(2)}, u32[]{:S(2)}) collective-permute-start(bf16[128,256]{1,0:T(8,128)(2,1)S(1)} %get-tuple-element.35), channel_id=1, source_target_pairs={{0,2},{1,3},{2,0},{3,1},{4,6},{5,7},{6,4},{7,5},{8,10},{9,11},{10,... | collective-permute-start | bytes 196616 | tf_op jit(solution)/shard_map/ppermute | solution.py:108
  125.5 4.2 %collective-permute-start.13 = (bf16[128,256]{1,0:T(8,128)(2,1)S(1)}, bf16[128,256]{1,0:T(8,128)(2,1)S(1)}, u32[]{:S(2)}, u32[]{:S(2)}) collective-permute-start(bf16[128,256]{1,0:T(8,128)(2,1)S(1)} %get-tuple-element.33), channel_id=1, source_target_pairs={{0,3},{1,0},{2,1},{3,2},{4,7},{5,4},{6,5},{7,6},{8,11},{9,8},{10,9... | collective-permute-start | bytes 196616 | tf_op jit(solution)/shard_map/ppermute | solution.py:108
  129.7 2.9 %collective-permute-done.14 = bf16[128,256]{1,0:T(8,128)(2,1)S(1)} collective-permute-done((bf16[128,256]{1,0:T(8,128)(2,1)S(1)}, bf16[128,256]{1,0:T(8,128)(2,1)S(1)}, u32[]{:S(2)}, u32[]{:S(2)}) %collective-permute-start.14) | collective-permute-done | bytes 65568 | tf_op jit(solution)/shard_map/ppermute | solution.py:108
  132.6 1.1 fusion.111
  (136 shorter events, 6.2 us)
Async XLA Ops:
  0.6 14.4 %copy-start = (bf16[1024,1024]{1,0:T(8,128)(2,1)S(1)}, bf16[1024,1024]{1,0:T(8,128)(2,1)}, u32[]{:S(2)}) copy-start(bf16[1024,1024]{1,0:T(8,128)(2,1)} %param.16) | copy-start | bytes 6291460
  0.6 14.4 %copy-start.2 = (bf16[128,1024]{1,0:T(8,128)(2,1)S(1)}, bf16[128,1024]{1,0:T(8,128)(2,1)}, u32[]{:S(2)}) copy-start(bf16[128,1024]{1,0:T(8,128)(2,1)} %param.14) | copy-start | bytes 786436
  0.7 13.0 %copy-start.9 = (s32[1,512]{1,0:T(1,128)S(1)}, s32[1,512]{1,0:T(1,128)}, u32[]{:S(2)}) copy-start(s32[1,512]{1,0:T(1,128)} %param.25) | copy-start | bytes 6148
  2.5 42.6 %collective-permute-start.6 = (bf16[128,1024]{1,0:T(8,128)(2,1)}, bf16[128,1024]{1,0:T(8,128)(2,1)S(1)}, u32[]{:S(2)}, u32[]{:S(2)}) collective-permute-start(bf16[128,1024]{1,0:T(8,128)(2,1)} %constant_dynamic-slice_fusion.9), channel_id=1, source_target_pairs={{0,3},{1,0},{2,1},{3,2},{4,7},{5,4},{6,5},{7,6},{8,11},{9,8},{10,9... | collective-permute-start | bytes 786440 | tf_op jit(solution)/shard_map/ppermute | solution.py:108
  7.6 37.5 %collective-permute-start.5 = (bf16[128,1024]{1,0:T(8,128)(2,1)}, bf16[128,1024]{1,0:T(8,128)(2,1)}, u32[]{:S(2)}, u32[]{:S(2)}) collective-permute-start(bf16[128,1024]{1,0:T(8,128)(2,1)} %constant_dynamic-slice_fusion.9), channel_id=1, source_target_pairs={{0,2},{1,3},{2,0},{3,1},{4,6},{5,7},{6,4},{7,5},{8,10},{9,11},{10,... | collective-permute-start | bytes 786440 | tf_op jit(solution)/shard_map/ppermute | solution.py:108
  15.1 8.2 %copy-start.8 = (s32[128,8]{0,1:T(8,128)S(1)}, s32[128,8]{0,1:T(8,128)}, u32[]{:S(2)}) copy-start(s32[128,8]{0,1:T(8,128)} %param.27) | copy-start | bytes 12292
  16.0 7.5 %copy-start.10 = (s32[1,512]{1,0:T(1,128)S(1)}, s32[1,512]{1,0:T(1,128)}, u32[]{:S(2)}) copy-start(s32[1,512]{1,0:T(1,128)} %param.26) | copy-start | bytes 6148
  16.1 7.5 %copy-start.11 = (bf16[1024]{0:T(1024)(128)(2,1)S(1)}, bf16[1024]{0:T(1024)(128)(2,1)}, u32[]{:S(2)}) copy-start(bf16[1024]{0:T(1024)(128)(2,1)} %param.20) | copy-start | bytes 6148
  17.9 9.9 %collective-permute-start.2 = (bf16[128,2,256]{0,2,1:T(8,128)(2,1)S(1)}, bf16[128,2,256]{0,2,1:T(8,128)(2,1)S(1)}, u32[]{:S(2)}, u32[]{:S(2)}) collective-permute-start(bf16[128,2,256]{0,2,1:T(8,128)(2,1)S(1)} %get-tuple-element.22), channel_id=1, source_target_pairs={{0,3},{1,0},{2,1},{3,2},{4,7},{5,4},{6,5},{7,6},{8,11},{9,8},{10,9... | collective-permute-start | bytes 393224 | tf_op jit(solution)/shard_map/ppermute | solution.py:108
  18.4 23.0 %collective-permute-start.1 = (bf16[128,2,256]{0,2,1:T(8,128)(2,1)S(1)}, bf16[128,2,256]{0,2,1:T(8,128)(2,1)S(1)}, u32[]{:S(2)}, u32[]{:S(2)}) collective-permute-start(bf16[128,2,256]{0,2,1:T(8,128)(2,1)S(1)} %get-tuple-element.23), channel_id=1, source_target_pairs={{0,2},{1,3},{2,0},{3,1},{4,6},{5,7},{6,4},{7,5},{8,10},{9,11},{10,... | collective-permute-start | bytes 393224 | tf_op jit(solution)/shard_map/ppermute | solution.py:108
  21.0 20.4 %collective-permute-start = (bf16[128,2,256]{0,2,1:T(8,128)(2,1)S(1)}, bf16[128,2,256]{0,2,1:T(8,128)(2,1)S(1)}, u32[]{:S(2)}, u32[]{:S(2)}) collective-permute-start(bf16[128,2,256]{0,2,1:T(8,128)(2,1)S(1)} %get-tuple-element.24), channel_id=1, source_target_pairs={{0,1},{1,2},{2,3},{3,0},{4,5},{5,6},{6,7},{7,4},{8,9},{9,10},{10,1... | collective-permute-start | bytes 393224 | tf_op jit(solution)/shard_map/ppermute | solution.py:108
  27.8 17.3 %collective-permute-start.4 = (bf16[128,1024]{1,0:T(8,128)(2,1)}, bf16[128,1024]{1,0:T(8,128)(2,1)S(1)}, u32[]{:S(2)}, u32[]{:S(2)}) collective-permute-start(bf16[128,1024]{1,0:T(8,128)(2,1)} %constant_dynamic-slice_fusion.9), channel_id=1, source_target_pairs={{0,1},{1,2},{2,3},{3,0},{4,5},{5,6},{6,7},{7,4},{8,9},{9,10},{10,1... | collective-permute-start | bytes 786440 | tf_op jit(solution)/shard_map/ppermute | solution.py:108
  46.1 8.4 %collective-permute-start.7 = (bf16[3,128,1024]{2,1,0:T(8,128)(2,1)S(1)}, bf16[3,128,1024]{2,1,0:T(8,128)(2,1)S(1)}, u32[]{:S(2)}, u32[]{:S(2)}) collective-permute-start(bf16[3,128,1024]{2,1,0:T(8,128)(2,1)S(1)} %pad_maximum_fusion), channel_id=1, source_target_pairs={{0,4},{4,0},{8,12},{12,8},{16,20},{20,16},{24,28},{28,24},{1,5},{5... | collective-permute-start | bytes 2359304 | tf_op jit(solution)/shard_map/ppermute | solution.py:134
  46.2 8.0 %copy-start.6 = (bf16[256,1024]{1,0:T(8,128)(2,1)S(1)}, bf16[256,1024]{1,0:T(8,128)(2,1)}, u32[]{:S(2)}) copy-start(bf16[256,1024]{1,0:T(8,128)(2,1)} %param.19) | copy-start | bytes 1572868
  49.0 7.8 %collective-permute-start.9 = (bf16[128,256]{0,1:T(8,128)(2,1)S(1)}, bf16[128,256]{0,1:T(8,128)(2,1)S(1)}, u32[]{:S(2)}, u32[]{:S(2)}) collective-permute-start(bf16[128,256]{0,1:T(8,128)(2,1)S(1)} %bitcast.329), channel_id=1, source_target_pairs={{0,1},{1,2},{2,3},{3,0},{4,5},{5,6},{6,7},{7,4},{8,9},{9,10},{10,1... | collective-permute-start | bytes 196616 | tf_op jit(solution)/shard_map/ppermute | solution.py:108
  50.8 5.7 %collective-permute-start.3 = (bf16[128,256]{0,1:T(8,128)(2,1)S(1)}, bf16[128,256]{0,1:T(8,128)(2,1)S(1)}, u32[]{:S(2)}, u32[]{:S(2)}) collective-permute-start(bf16[128,256]{0,1:T(8,128)(2,1)S(1)} %bitcast.330), channel_id=1, source_target_pairs={{0,3},{1,0},{2,1},{3,2},{4,7},{5,4},{6,5},{7,6},{8,11},{9,8},{10,9... | collective-permute-start | bytes 196616 | tf_op jit(solution)/shard_map/ppermute | solution.py:108
  52.9 6.2 %collective-permute-start.8 = (bf16[128,256]{0,1:T(8,128)(2,1)S(1)}, bf16[128,256]{0,1:T(8,128)(2,1)S(1)}, u32[]{:S(2)}, u32[]{:S(2)}) collective-permute-start(bf16[128,256]{0,1:T(8,128)(2,1)S(1)} %bitcast.328), channel_id=1, source_target_pairs={{0,2},{1,3},{2,0},{3,1},{4,6},{5,7},{6,4},{7,5},{8,10},{9,11},{10,... | collective-permute-start | bytes 196616 | tf_op jit(solution)/shard_map/ppermute | solution.py:108
  56.8 2.8 %copy-start.7 = (bf16[1024,32]{0,1:T(8,128)(2,1)S(1)}, bf16[1024,32]{0,1:T(8,128)(2,1)}, u32[]{:S(2)}) copy-start(bf16[1024,32]{0,1:T(8,128)(2,1)} %param.21) | copy-start | bytes 196612
  59.5 11.6 %copy-start.3 = (f32[128,1024]{1,0:T(8,128)}, f32[128,1024]{1,0:T(8,128)S(1)}, u32[]{:S(2)}) copy-start(f32[128,1024]{1,0:T(8,128)S(1)} %get-tuple-element.58) | copy-start | bytes 1572868
  60.3 21.2 %collective-permute-start.10 = (bf16[128,1152]{1,0:T(8,128)(2,1)S(1)}, bf16[128,1152]{1,0:T(8,128)(2,1)}, u32[]{:S(2)}, u32[]{:S(2)}) collective-permute-start(bf16[128,1152]{1,0:T(8,128)(2,1)S(1)} %concatenate.47), channel_id=1, source_target_pairs={{0,1},{1,2},{2,3},{3,0},{4,5},{5,6},{6,7},{7,4},{8,9},{9,10},{10,1... | collective-permute-start | bytes 884744 | tf_op jit(solution)/shard_map/ppermute | solution.py:108
  60.4 23.1 %collective-permute-start.11 = (bf16[128,1152]{1,0:T(8,128)(2,1)S(1)}, bf16[128,1152]{1,0:T(8,128)(2,1)}, u32[]{:S(2)}, u32[]{:S(2)}) collective-permute-start(bf16[128,1152]{1,0:T(8,128)(2,1)S(1)} %concatenate.47), channel_id=1, source_target_pairs={{0,2},{1,3},{2,0},{3,1},{4,6},{5,7},{6,4},{7,5},{8,10},{9,11},{10,... | collective-permute-start | bytes 884744 | tf_op jit(solution)/shard_map/ppermute | solution.py:108
  62.7 21.8 %collective-permute-start.12 = (bf16[128,1152]{1,0:T(8,128)(2,1)S(1)}, bf16[128,1152]{1,0:T(8,128)(2,1)}, u32[]{:S(2)}, u32[]{:S(2)}) collective-permute-start(bf16[128,1152]{1,0:T(8,128)(2,1)S(1)} %concatenate.47), channel_id=1, source_target_pairs={{0,3},{1,0},{2,1},{3,2},{4,7},{5,4},{6,5},{7,6},{8,11},{9,8},{10,9... | collective-permute-start | bytes 884744 | tf_op jit(solution)/shard_map/ppermute | solution.py:108
  86.1 6.6 %slice-start = ((s8[8388608]{0:T(1024)(128)(4,1)}), s8[4194304]{0:T(1024)(128)(4,1)S(1)}, s32[]{:S(2)}) async-start(s8[8388608]{0:T(1024)(128)(4,1)} %bitcast.312), calls=%async_computation | async-start | bytes 8388608
  87.1 5.6 %slice-start.1 = ((s8[8388608]{0:T(1024)(128)(4,1)}), s8[4194304]{0:T(1024)(128)(4,1)S(1)}, s32[]{:S(2)}) async-start(s8[8388608]{0:T(1024)(128)(4,1)} %bitcast.312), calls=%async_computation.1 | async-start | bytes 8388608
  87.1 7.7 %slice-start.2 = ((s8[8388608]{0:T(1024)(128)(4,1)}), s8[4194304]{0:T(1024)(128)(4,1)S(1)}, s32[]{:S(2)}) async-start(s8[8388608]{0:T(1024)(128)(4,1)} %bitcast.314), calls=%async_computation.2 | async-start | bytes 8388608
  92.7 2.4 %slice-start.3 = ((s8[8388608]{0:T(1024)(128)(4,1)}), s8[4194304]{0:T(1024)(128)(4,1)S(1)}, s32[]{:S(2)}) async-start(s8[8388608]{0:T(1024)(128)(4,1)} %bitcast.314), calls=%async_computation.3 | async-start | bytes 8388608
  101.2 10.8 %copy-start.14 = (bf16[3,8,64,256]{3,2,0,1:T(8,128)(2,1)S(1)}, bf16[3,8,64,256]{3,2,0,1:T(8,128)(2,1)}, u32[]{:S(2)}) copy-start(bf16[3,8,64,256]{3,2,0,1:T(8,128)(2,1)} %fusion.45) | copy-start | bytes 2359300
  103.0 12.3 %copy-start.13 = (bf16[3,8,64,256]{3,2,0,1:T(8,128)(2,1)S(1)}, bf16[3,8,64,256]{3,2,0,1:T(8,128)(2,1)}, u32[]{:S(2)}) copy-start(bf16[3,8,64,256]{3,2,0,1:T(8,128)(2,1)} %fusion.48) | copy-start | bytes 2359300
  104.6 12.2 %collective-permute-start.24 = (bf16[128,256]{1,0:T(8,128)(2,1)S(1)}, bf16[128,256]{1,0:T(8,128)(2,1)S(1)}, u32[]{:S(2)}, u32[]{:S(2)}) collective-permute-start(bf16[128,256]{1,0:T(8,128)(2,1)S(1)} %get-tuple-element.43), channel_id=1, source_target_pairs={{0,1},{1,2},{2,3},{3,0},{4,5},{5,6},{6,7},{7,4},{8,9},{9,10},{10,1... | collective-permute-start | bytes 196616 | tf_op jit(solution)/shard_map/ppermute | solution.py:108
  109.6 8.6 %collective-permute-start.23 = (bf16[128,256]{1,0:T(8,128)(2,1)S(1)}, bf16[128,256]{1,0:T(8,128)(2,1)S(1)}, u32[]{:S(2)}, u32[]{:S(2)}) collective-permute-start(bf16[128,256]{1,0:T(8,128)(2,1)S(1)} %get-tuple-element.44), channel_id=1, source_target_pairs={{0,2},{1,3},{2,0},{3,1},{4,6},{5,7},{6,4},{7,5},{8,10},{9,11},{10,... | collective-permute-start | bytes 196616 | tf_op jit(solution)/shard_map/ppermute | solution.py:108
  110.5 8.4 %collective-permute-start.22 = (bf16[128,256]{1,0:T(8,128)(2,1)S(1)}, bf16[128,256]{1,0:T(8,128)(2,1)S(1)}, u32[]{:S(2)}, u32[]{:S(2)}) collective-permute-start(bf16[128,256]{1,0:T(8,128)(2,1)S(1)} %get-tuple-element.42), channel_id=1, source_target_pairs={{0,3},{1,0},{2,1},{3,2},{4,7},{5,4},{6,5},{7,6},{8,11},{9,8},{10,9... | collective-permute-start | bytes 196616 | tf_op jit(solution)/shard_map/ppermute | solution.py:108
  112.4 3.7 %copy-start.12 = (bf16[3,8,64,256]{3,2,0,1:T(8,128)(2,1)S(1)}, bf16[3,8,64,256]{3,2,0,1:T(8,128)(2,1)}, u32[]{:S(2)}) copy-start(bf16[3,8,64,256]{3,2,0,1:T(8,128)(2,1)} %fusion.51) | copy-start | bytes 2359300
  112.7 7.6 %collective-permute-start.21 = (bf16[128,256]{1,0:T(8,128)(2,1)S(1)}, bf16[128,256]{1,0:T(8,128)(2,1)S(1)}, u32[]{:S(2)}, u32[]{:S(2)}) collective-permute-start(bf16[128,256]{1,0:T(8,128)(2,1)S(1)} %get-tuple-element.40), channel_id=1, source_target_pairs={{0,1},{1,2},{2,3},{3,0},{4,5},{5,6},{6,7},{7,4},{8,9},{9,10},{10,1... | collective-permute-start | bytes 196616 | tf_op jit(solution)/shard_map/ppermute | solution.py:108
  113.3 9.9 %collective-permute-start.20 = (bf16[128,256]{1,0:T(8,128)(2,1)S(1)}, bf16[128,256]{1,0:T(8,128)(2,1)S(1)}, u32[]{:S(2)}, u32[]{:S(2)}) collective-permute-start(bf16[128,256]{1,0:T(8,128)(2,1)S(1)} %get-tuple-element.41), channel_id=1, source_target_pairs={{0,2},{1,3},{2,0},{3,1},{4,6},{5,7},{6,4},{7,5},{8,10},{9,11},{10,... | collective-permute-start | bytes 196616 | tf_op jit(solution)/shard_map/ppermute | solution.py:108
  116.0 16.6 %copy-start.4 = (f32[128,1024]{1,0:T(8,128)S(1)}, f32[128,1024]{1,0:T(8,128)}, u32[]{:S(2)}) copy-start(f32[128,1024]{1,0:T(8,128)} %copy-done.3) | copy-start | bytes 1572868
  116.0 16.6 %copy-start.5 = (f32[128,1024]{1,0:T(8,128)S(1)}, f32[128,1024]{1,0:T(8,128)}, u32[]{:S(2)}) copy-start(f32[128,1024]{1,0:T(8,128)} %convolution_bitcast_fusion.2) | copy-start | bytes 1572868
  116.1 17.6 %copy-start.1 = (bf16[1024,1024]{1,0:T(8,128)(2,1)S(1)}, bf16[1024,1024]{1,0:T(8,128)(2,1)}, u32[]{:S(2)}) copy-start(bf16[1024,1024]{1,0:T(8,128)(2,1)} %param.16) | copy-start | bytes 6291460
  116.8 6.4 %collective-permute-start.19 = (bf16[128,256]{1,0:T(8,128)(2,1)S(1)}, bf16[128,256]{1,0:T(8,128)(2,1)S(1)}, u32[]{:S(2)}, u32[]{:S(2)}) collective-permute-start(bf16[128,256]{1,0:T(8,128)(2,1)S(1)} %get-tuple-element.39), channel_id=1, source_target_pairs={{0,3},{1,0},{2,1},{3,2},{4,7},{5,4},{6,5},{7,6},{8,11},{9,8},{10,9... | collective-permute-start | bytes 196616 | tf_op jit(solution)/shard_map/ppermute | solution.py:108
  118.2 7.3 %collective-permute-start.18 = (bf16[128,256]{1,0:T(8,128)(2,1)S(1)}, bf16[128,256]{1,0:T(8,128)(2,1)S(1)}, u32[]{:S(2)}, u32[]{:S(2)}) collective-permute-start(bf16[128,256]{1,0:T(8,128)(2,1)S(1)} %get-tuple-element.37), channel_id=1, source_target_pairs={{0,1},{1,2},{2,3},{3,0},{4,5},{5,6},{6,7},{7,4},{8,9},{9,10},{10,1... | collective-permute-start | bytes 196616 | tf_op jit(solution)/shard_map/ppermute | solution.py:108
  118.9 10.7 %collective-permute-start.17 = (bf16[128,256]{1,0:T(8,128)(2,1)S(1)}, bf16[128,256]{1,0:T(8,128)(2,1)S(1)}, u32[]{:S(2)}, u32[]{:S(2)}) collective-permute-start(bf16[128,256]{1,0:T(8,128)(2,1)S(1)} %get-tuple-element.38), channel_id=1, source_target_pairs={{0,2},{1,3},{2,0},{3,1},{4,6},{5,7},{6,4},{7,5},{8,10},{9,11},{10,... | collective-permute-start | bytes 196616 | tf_op jit(solution)/shard_map/ppermute | solution.py:108
  120.3 9.3 %collective-permute-start.16 = (bf16[128,256]{1,0:T(8,128)(2,1)S(1)}, bf16[128,256]{1,0:T(8,128)(2,1)S(1)}, u32[]{:S(2)}, u32[]{:S(2)}) collective-permute-start(bf16[128,256]{1,0:T(8,128)(2,1)S(1)} %get-tuple-element.36), channel_id=1, source_target_pairs={{0,3},{1,0},{2,1},{3,2},{4,7},{5,4},{6,5},{7,6},{8,11},{9,8},{10,9... | collective-permute-start | bytes 196616 | tf_op jit(solution)/shard_map/ppermute | solution.py:108
  123.2 6.4 %collective-permute-start.15 = (bf16[128,256]{1,0:T(8,128)(2,1)S(1)}, bf16[128,256]{1,0:T(8,128)(2,1)S(1)}, u32[]{:S(2)}, u32[]{:S(2)}) collective-permute-start(bf16[128,256]{1,0:T(8,128)(2,1)S(1)} %get-tuple-element.34), channel_id=1, source_target_pairs={{0,1},{1,2},{2,3},{3,0},{4,5},{5,6},{6,7},{7,4},{8,9},{9,10},{10,1... | collective-permute-start | bytes 196616 | tf_op jit(solution)/shard_map/ppermute | solution.py:108
  123.2 9.3 %collective-permute-start.14 = (bf16[128,256]{1,0:T(8,128)(2,1)S(1)}, bf16[128,256]{1,0:T(8,128)(2,1)S(1)}, u32[]{:S(2)}, u32[]{:S(2)}) collective-permute-start(bf16[128,256]{1,0:T(8,128)(2,1)S(1)} %get-tuple-element.35), channel_id=1, source_target_pairs={{0,2},{1,3},{2,0},{3,1},{4,6},{5,7},{6,4},{7,5},{8,10},{9,11},{10,... | collective-permute-start | bytes 196616 | tf_op jit(solution)/shard_map/ppermute | solution.py:108
  125.5 7.1 %collective-permute-start.13 = (bf16[128,256]{1,0:T(8,128)(2,1)S(1)}, bf16[128,256]{1,0:T(8,128)(2,1)S(1)}, u32[]{:S(2)}, u32[]{:S(2)}) collective-permute-start(bf16[128,256]{1,0:T(8,128)(2,1)S(1)} %get-tuple-element.33), channel_id=1, source_target_pairs={{0,3},{1,0},{2,1},{3,2},{4,7},{5,4},{6,5},{7,6},{8,11},{9,8},{10,9... | collective-permute-start | bytes 196616 | tf_op jit(solution)/shard_map/ppermute | solution.py:108

commit v20 on v11

--- a/solution.py
+++ b/solution.py
@@ -96,9 +96,10 @@
         result = jnp.einsum("becf,efd->becd", hidden, down, preferred_element_type=jnp.float32)
         result = result.astype(jnp.bfloat16)
         partial = jnp.einsum("becr,becd->brd", high, result, preferred_element_type=jnp.float32)
-        partial = partial + jnp.einsum(
-            "becr,becd->brd", low, result, preferred_element_type=jnp.float32
-        )
+        if pieces == 1:
+            partial = partial + jnp.einsum(
+                "becr,becd->brd", low, result, preferred_element_type=jnp.float32
+            )
         outs.append(partial)
     return outs
 

time: 128 us -> 138 us (1.078)
  matrix products: 45.5 us -> 51.5 us
  other arithmetic: 8.27 us -> 12.9 us
  local copies, waits for them, and re-layouts: 8.24 us -> 12.8 us
  waiting for transfers between devices: 22.2 us -> 18.9 us
  starting transfers between devices: 41.7 us -> 39.3 us
    dot_general x3, matrix products: 1.91 us -> 8.95 us  [expert_mix(): jnp.einsum('becr,becd->brd', high, result, preferred_element_type=jnp.flo...]
    ppermute x18, waiting for transfers between devices: 22.2 us -> 18.9 us  [shifted(): lax.ppermute(x, 'exp', [(j, (j + step) % count) for j in range(count)])]
    ppermute x18, starting transfers between devices: 41.6 us -> 39.2 us  [shifted(): lax.ppermute(x, 'exp', [(j, (j + step) % count) for j in range(count)])]
    dot_general x3 -> x1, matrix products: 12.2 us -> 10.1 us  [expert_mix(): jnp.einsum('becf,efd->becd', hidden, down, preferred_element_type=jnp.flo...]
    dot_general x3 -> x1, matrix products: 3.47 us -> 1.59 us  [expert_mix(): jnp.einsum('becr,becd->brd', low, result, preferred_element_type=jnp.floa...]
    unnamed x39 -> x35, local copies, waits for them, and re-layouts: 3.35 us -> 4.49 us
  transfers between devices with their start and end apart: 19 -> 19, of which waited for: 7 -> 7; matrix products, arithmetic and copies ran while one was open for 32% -> 37% of each run, Pallas kernels for 0% -> 0%
where the time goes in v20:
time: 138 us; the launch traced here: 137 us
  matrix products  51.5 us (37%)
  starting transfers between devices  39.3 us (28%)
  waiting for transfers between devices  18.9 us (14%)
  other arithmetic  12.9 us (9%)
  local copies, waits for them, and re-layouts  12.8 us (9%)
    ppermute x18, starting transfers between devices, shifted(): lax.ppermute(x, 'exp', [(j, (j + step) % count) for j in range(count)])  39.2 us
    ppermute x18, waiting for transfers between devices, shifted(): lax.ppermute(x, 'exp', [(j, (j + step) % count) for j in range(count)])  18.9 us
    dot_general x1, matrix products, expert_mix(): jnp.einsum('becf,efd->becd', hidden, down, preferred_element_type=jnp.flo...  10.1 us
    dot_general x2, matrix products, expert_mix(): jnp.einsum('becd,edf->becf', received, w_gate, preferred_element_type=jnp...  9.2 us
    dot_general x3, matrix products, expert_mix(): jnp.einsum('becr,becd->brd', high, result, preferred_element_type=jnp.flo...  8.95 us
    dot_general x1, matrix products, expert_mix(): jnp.einsum('becd,edf->becf', received, w_up, preferred_element_type=jnp.f...  5.54 us
    sub x1, matrix products, attend(): expo = jnp.exp(score - top)  4.62 us
    unnamed x35, local copies, waits for them, and re-layouts  4.49 us
  transfers between devices with their start and end apart: 19, of which 7 were waited for; matrix products, arithmetic and copies ran while one was open for 37% of the time, Pallas kernels for 0%

profile of v20, /device:TPU:0, one launch (start us, length us, event | category | flops | bytes accessed | tf_op | source)
XLA Modules:
  0.0 136.5 jit_solution(6296606837163633379)
XLA Ops:
  0.7 1.8 %constant_dynamic-slice_fusion.8 = bf16[128,1024]{1,0:T(8,128)(2,1)} fusion(bf16[256,1024]{1,0:T(8,128)(2,1)} %param.19, s32[]{:T(128)S(6)} %select_n.166), kind=kLoop, calls=%fused_computation.167 | loop fusion | bytes 524292 | tf_op jit(solution)/shard_map/dynamic_slice | solution.py:133
  2.5 5.1 %collective-permute-start.6 = (bf16[128,1024]{1,0:T(8,128)(2,1)}, bf16[128,1024]{1,0:T(8,128)(2,1)S(1)}, u32[]{:S(2)}, u32[]{:S(2)}) collective-permute-start(bf16[128,1024]{1,0:T(8,128)(2,1)} %constant_dynamic-slice_fusion.8), channel_id=1, source_target_pairs={{0,3},{1,0},{2,1},{3,2},{4,7},{5,4},{6,5},{7,6},{8,11},{9,8},{10,9... | collective-permute-start | bytes 786440 | tf_op jit(solution)/shard_map/ppermute | solution.py:109
  7.6 0.5 multiply_power_fusion
  8.1 0.7 convert_element_type.124
  8.8 1.1 fusion.98
  9.9 1.7 %convolution_convert_fusion.4 = bf16[128,512]{1,0:T(8,128)(2,1)S(1)} fusion(bf16[1024,512]{1,0:T(8,128)(2,1)} %param.18, bf16[128,1024]{1,0:T(8,128)(2,1)} %param.14, f32[1024]{0:T(1024)S(1)} %convert_element_type.124, f32[128]{0:T(128)S(1)} %add_rsqrt_fusion.1), kind=kOutput, calls=%fused_computation.62 | convolution fusion | flops 134807552 | bytes 1446400 | tf_op jit(solution)/shard_map/dot_general | solution.py:170
  11.7 1.9 %fusion.176 = f32[128,512]{0,1:T(8,128)S(1)} fusion(bf16[1024,512]{1,0:T(8,128)(2,1)} %param.17, bf16[128,1024]{1,0:T(8,128)(2,1)} %param.14, f32[1024]{0:T(1024)S(1)} %convert_element_type.124, f32[128]{0:T(128)S(1)} %add_rsqrt_fusion.1), kind=kOutput, calls=%fused_computation.208 | convolution fusion | flops 134742016 | bytes 1577472 | tf_op jit(solution)/shard_map/dot_general | solution.py:167
  14.4 0.7 bitcast_subtract_fusion
  15.0 1.0 fusion.178
  16.0 0.8 dynamic-slice_convert_fusion
  16.8 0.8 multiply_cosine_fusion
  17.6 0.7 subtract_convert_fusion.1
  18.4 0.9 pad_maximum_fusion.2
  19.4 0.5 collective-permute-start.2
  19.8 2.6 %collective-permute-start.1 = (bf16[128,2,256]{0,2,1:T(8,128)(2,1)S(1)}, bf16[128,2,256]{0,2,1:T(8,128)(2,1)S(1)}, u32[]{:S(2)}, u32[]{:S(2)}) collective-permute-start(bf16[128,2,256]{0,2,1:T(8,128)(2,1)S(1)} %get-tuple-element.22), channel_id=1, source_target_pairs={{0,2},{1,3},{2,0},{3,1},{4,6},{5,7},{6,4},{7,5},{8,10},{9,11},{10,... | collective-permute-start | bytes 393224 | tf_op jit(solution)/shard_map/ppermute | solution.py:109
  22.4 1.9 %collective-permute-start = (bf16[128,2,256]{0,2,1:T(8,128)(2,1)S(1)}, bf16[128,2,256]{0,2,1:T(8,128)(2,1)}, u32[]{:S(2)}, u32[]{:S(2)}) collective-permute-start(bf16[128,2,256]{0,2,1:T(8,128)(2,1)S(1)} %get-tuple-element.23), channel_id=1, source_target_pairs={{0,1},{1,2},{2,3},{3,0},{4,5},{5,6},{6,7},{7,4},{8,9},{9,10},{10,1... | collective-permute-start | bytes 393224 | tf_op jit(solution)/shard_map/ppermute | solution.py:109
  24.7 1.0 compare_and_fusion
  25.7 0.7 convert_element_type.132
  26.4 0.7 copy.84
  27.3 13.0 %collective-permute-start.4 = (bf16[128,1024]{1,0:T(8,128)(2,1)}, bf16[128,1024]{1,0:T(8,128)(2,1)S(1)}, u32[]{:S(2)}, u32[]{:S(2)}) collective-permute-start(bf16[128,1024]{1,0:T(8,128)(2,1)} %constant_dynamic-slice_fusion.8), channel_id=1, source_target_pairs={{0,1},{1,2},{2,3},{3,0},{4,5},{5,6},{6,7},{7,4},{8,9},{9,10},{10,1... | collective-permute-start | bytes 786440 | tf_op jit(solution)/shard_map/ppermute | solution.py:109
  40.3 1.1 collective-permute-done.1
  41.4 0.6 copy-done.8
  42.0 1.1 pad_maximum_fusion.3
  43.1 0.7 slice.127
  43.9 4.6 %fusion.181 = (f32[2,2,512]{2,1,0:T(2,128)S(1)}, f32[2,2,512,512]{2,3,1,0:T(8,128)}) fusion(pred[512,512]{0,1:T(8,128)(4,1)} %compare_and_fusion, bf16[512,2,2,64]{0,3,2,1:T(8,128)(2,1)} %bitcast.271, bf16[512,2,256]{0,2,1:T(8,128)(2,1)S(1)} %pad_maximum_fusion.3), kind=kOutput, calls=%fused_computation.211 | convolution fusion | flops 138412544 | bytes 4857856 | tf_op jit(solution)/shard_map/sub | solution.py:44
  48.5 1.0 pad_maximum_fusion
  49.6 2.7 %fusion.85 = bf16[512,2,2,64]{0,3,2,1:T(8,128)(2,1)S(1)} fusion(f32[2,2,512,512]{2,3,1,0:T(8,128)} %get-tuple-element.49, f32[2,2,512]{2,1,0:T(2,128)S(1)} %get-tuple-element.48, bf16[512,2,256]{0,2,1:T(8,128)(2,1)S(1)} %pad_maximum_fusion.3), kind=kOutput, calls=%fused_computation.61 | convolution fusion | flops 136445952 | bytes 4595712 | tf_op jit(solution)/shard_map/kgqt,tkd->qkgd/dot_general | solution.py:46
  52.5 3.8 %collective-permute-start.3 = (bf16[128,256]{0,1:T(8,128)(2,1)S(1)}, bf16[128,256]{0,1:T(8,128)(2,1)S(1)}, u32[]{:S(2)}, u32[]{:S(2)}) collective-permute-start(bf16[128,256]{0,1:T(8,128)(2,1)S(1)} %bitcast.275), channel_id=1, source_target_pairs={{0,3},{1,0},{2,1},{3,2},{4,7},{5,4},{6,5},{7,6},{8,11},{9,8},{10,9... | collective-permute-start | bytes 196616 | tf_op jit(solution)/shard_map/ppermute | solution.py:109
  56.3 0.3 convolution_convert_fusion.3
  56.7 1.0 copy.95
  57.9 1.1 broadcast_select_fusion.1
  59.5 3.0 %collective-permute-done.8 = bf16[128,256]{0,1:T(8,128)(2,1)S(1)} collective-permute-done((bf16[128,256]{0,1:T(8,128)(2,1)S(1)}, bf16[128,256]{0,1:T(8,128)(2,1)S(1)}, u32[]{:S(2)}, u32[]{:S(2)}) %collective-permute-start.8) | collective-permute-done | bytes 65568 | tf_op jit(solution)/shard_map/ppermute | solution.py:109
  62.5 0.4 multiply_reduce_fusion
  62.9 0.8 copy-done.3
  64.4 0.9 concatenate.47
  65.3 2.3 %collective-permute-start.11 = (bf16[128,1152]{1,0:T(8,128)(2,1)}, bf16[128,1152]{1,0:T(8,128)(2,1)}, u32[]{:S(2)}, u32[]{:S(2)}) collective-permute-start(bf16[128,1152]{1,0:T(8,128)(2,1)} %concatenate.47), channel_id=1, source_target_pairs={{0,2},{1,3},{2,0},{3,1},{4,6},{5,7},{6,4},{7,5},{8,10},{9,11},{10,... | collective-permute-start | bytes 884744 | tf_op jit(solution)/shard_map/ppermute | solution.py:109
  67.6 1.5 %collective-permute-start.12 = (bf16[128,1152]{1,0:T(8,128)(2,1)}, bf16[128,1152]{1,0:T(8,128)(2,1)}, u32[]{:S(2)}, u32[]{:S(2)}) collective-permute-start(bf16[128,1152]{1,0:T(8,128)(2,1)} %concatenate.47), channel_id=1, source_target_pairs={{0,3},{1,0},{2,1},{3,2},{4,7},{5,4},{6,5},{7,6},{8,11},{9,8},{10,9... | collective-permute-start | bytes 884744 | tf_op jit(solution)/shard_map/ppermute | solution.py:109
  69.1 1.0 convolution_convert_fusion.6
  70.1 0.9 compare_bitcast_fusion
  71.0 0.5 convolution_convert_fusion.2
  71.5 5.9 %convolution_bitcast_fusion.1 = f32[1,8,64,512]{3,2,1,0:T(8,128)} fusion(bf16[8,64,1024]{2,1,0:T(8,128)(2,1)S(1)} %convolution_convert_fusion.2, bf16[8,1024,512]{2,1,0:T(8,128)(2,1)} %param.22), kind=kOutput, calls=%fused_computation.45 | convolution fusion | flops 536870912 | bytes 10485760 | tf_op jit(solution)/shard_map/becd,edf->becf/dot_general | solution.py:86
  77.4 10.1 %convolution_convert_fusion.1 = bf16[8,64,1024]{2,1,0:T(8,128)(2,1)} fusion(bf16[8,512,1024]{2,1,0:T(8,128)(2,1)} %param.24, bf16[8,64,1024]{2,1,0:T(8,128)(2,1)S(1)} %convolution_convert_fusion.2, bf16[8,1024,512]{2,1,0:T(8,128)(2,1)} %param.23, f32[1,8,64,512]{3,2,1,0:T(8,128)} %convolution_bitcast_fusion.1), kind=kOutput, calls=%fused_computation.39 | convolution fusion | flops 1075838976 | bytes 19922944 | tf_op jit(solution)/shard_map/becf,efd->becd/dot_general | solution.py:96
  87.5 0.9 constant_dynamic-slice_fusion.7
  88.5 1.6 %convolution_bitcast_fusion.2 = f32[128,1024]{1,0:T(8,128)S(1)} fusion(bf16[8,64,1024]{2,1,0:T(8,128)(2,1)} %convolution_convert_fusion.1, s32[8,128]{1,0:T(8,128)S(1)} %convolution_convert_fusion.6, pred[8,128]{1,0:T(8,128)(4,1)S(1)} %copy.85, bf16[8,128]{1,0:T(8,128)(2,1)S(1)} %bitcast.277), kind=kOutput, calls=%fused_computation.52 | convolution fusion | flops 134414336 | bytes 1580032 | tf_op jit(solution)/shard_map/becr,becd->brd/dot_general | solution.py:100
  90.2 1.0 constant_dynamic-update-slice_fusion.2
  91.2 1.0 constant_dynamic-update-slice_fusion.1
  92.2 1.0 constant_dynamic-update-slice_fusion
  93.3 0.8 constant_dynamic-slice_fusion.4
  94.3 1.0 convolution_convert_fusion
  95.3 5.5 %fusion.1 = f32[8,3,64,512]{3,2,1,0:T(8,128)S(1)} fusion(bf16[8,1024,512]{2,1,0:T(8,128)(2,1)} %param.23, bf16[3,8,64,1024]{3,2,1,0:T(8,128)(2,1)S(1)} %convolution_convert_fusion), kind=kOutput, calls=%fused_computation.1 | convolution fusion | flops 1610612736 | bytes 14680064 | tf_op jit(solution)/shard_map/becd,edf->becf/dot_general | solution.py:87
  100.9 3.3 %fusion.12 = bf16[3,8,64,512]{3,2,0,1:T(8,128)(2,1)} fusion(f32[8,3,64,512]{3,2,1,0:T(8,128)S(1)} %fusion.1, bf16[8,1024,512]{2,1,0:T(8,128)(2,1)S(1)} %bitcast.260, bf16[3,8,64,1024]{3,2,1,0:T(8,128)(2,1)S(1)} %convolution_convert_fusion), kind=kOutput, calls=%fused_computation.16 | convolution fusion | flops 1615331328 | bytes 16252928 | tf_op jit(solution)/shard_map/becd,edf->becf/dot_general | solution.py:86
  104.3 4.0 %fusion.66 = bf16[3,128,512]{2,1,0:T(8,128)(2,1)S(1)} fusion(bf16[8,512,1024]{2,1,0:T(8,128)(2,1)} %param.24, bf16[3,8,64,512]{3,2,0,1:T(8,128)(2,1)} %fusion.12, s32[3,8,128]{2,1,0:T(8,128)S(1)} %convolution_convert_fusion.5, pred[3,8,128]{2,1,0:T(8,128)(4,1)S(1)} %compare_bitcast_fusion.1, bf16[3,8,128]{2,1,0:T(8,128)(2,1)S(1)} %bitcast.278), kind=kOutput, calls=%fused_computation.49 | convolution fusion | flops 1008205824 | bytes 6181888 | tf_op jit(solution)/shard_map/becr,becd->brd/dot_general | solution.py:98
  108.2 3.9 %fusion.73 = bf16[3,128,512]{2,1,0:T(8,128)(2,1)S(1)} fusion(bf16[8,512,1024]{2,1,0:T(8,128)(2,1)} %param.24, bf16[3,8,64,512]{3,2,0,1:T(8,128)(2,1)} %fusion.12, s32[3,8,128]{2,1,0:T(8,128)S(1)} %convolution_convert_fusion.5, pred[3,8,128]{2,1,0:T(8,128)(4,1)S(1)} %compare_bitcast_fusion.1, bf16[3,8,128]{2,1,0:T(8,128)(2,1)S(1)} %bitcast.279), kind=kOutput, calls=%fused_computation.50 | convolution fusion | flops 1008205824 | bytes 6181888 | tf_op jit(solution)/shard_map/becr,becd->brd/dot_general | solution.py:98
  112.2 2.4 %collective-permute-start.18 = (bf16[128,512]{1,0:T(8,128)(2,1)S(1)}, bf16[128,512]{1,0:T(8,128)(2,1)S(1)}, u32[]{:S(2)}, u32[]{:S(2)}) collective-permute-start(bf16[128,512]{1,0:T(8,128)(2,1)S(1)} %get-tuple-element.28), channel_id=1, source_target_pairs={{0,1},{1,2},{2,3},{3,0},{4,5},{5,6},{6,7},{7,4},{8,9},{9,10},{10,1... | collective-permute-start | bytes 393224 | tf_op jit(solution)/shard_map/ppermute | solution.py:109
  114.6 1.0 collective-permute-start.17
  115.6 1.6 %collective-permute-start.16 = (bf16[128,512]{1,0:T(8,128)(2,1)S(1)}, bf16[128,512]{1,0:T(8,128)(2,1)S(1)}, u32[]{:S(2)}, u32[]{:S(2)}) collective-permute-start(bf16[128,512]{1,0:T(8,128)(2,1)S(1)} %get-tuple-element.27), channel_id=1, source_target_pairs={{0,3},{1,0},{2,1},{3,2},{4,7},{5,4},{6,5},{7,6},{8,11},{9,8},{10,9... | collective-permute-start | bytes 393224 | tf_op jit(solution)/shard_map/ppermute | solution.py:109
  117.3 0.5 collective-permute-start.15
  117.7 1.9 %collective-permute-start.14 = (bf16[128,512]{1,0:T(8,128)(2,1)S(1)}, bf16[128,512]{1,0:T(8,128)(2,1)S(1)}, u32[]{:S(2)}, u32[]{:S(2)}) collective-permute-start(bf16[128,512]{1,0:T(8,128)(2,1)S(1)} %get-tuple-element.26), channel_id=1, source_target_pairs={{0,2},{1,3},{2,0},{3,1},{4,6},{5,7},{6,4},{7,5},{8,10},{9,11},{10,... | collective-permute-start | bytes 393224 | tf_op jit(solution)/shard_map/ppermute | solution.py:109
  119.6 0.9 collective-permute-done.18
  120.5 1.1 collective-permute-start.13
  121.6 6.2 %collective-permute-done.17 = bf16[128,512]{1,0:T(8,128)(2,1)S(1)} collective-permute-done((bf16[128,512]{1,0:T(8,128)(2,1)S(1)}, bf16[128,512]{1,0:T(8,128)(2,1)S(1)}, u32[]{:S(2)}, u32[]{:S(2)}) %collective-permute-start.17) | collective-permute-done | bytes 131104 | tf_op jit(solution)/shard_map/ppermute | solution.py:109
  127.9 1.0 collective-permute-done.15
  128.9 6.5 %collective-permute-done.14 = bf16[128,512]{1,0:T(8,128)(2,1)S(1)} collective-permute-done((bf16[128,512]{1,0:T(8,128)(2,1)S(1)}, bf16[128,512]{1,0:T(8,128)(2,1)S(1)}, u32[]{:S(2)}, u32[]{:S(2)}) %collective-permute-start.14) | collective-permute-done | bytes 131104 | tf_op jit(solution)/shard_map/ppermute | solution.py:109
  135.5 1.1 fusion.112
  (102 shorter events, 4.0 us)
Async XLA Ops:
  0.6 14.4 %copy-start = (bf16[1024,1024]{1,0:T(8,128)(2,1)S(1)}, bf16[1024,1024]{1,0:T(8,128)(2,1)}, u32[]{:S(2)}) copy-start(bf16[1024,1024]{1,0:T(8,128)(2,1)} %param.16) | copy-start | bytes 6291460
  0.6 14.4 %copy-start.2 = (bf16[128,1024]{1,0:T(8,128)(2,1)S(1)}, bf16[128,1024]{1,0:T(8,128)(2,1)}, u32[]{:S(2)}) copy-start(bf16[128,1024]{1,0:T(8,128)(2,1)} %param.14) | copy-start | bytes 786436
  0.7 13.0 %copy-start.12 = (s32[1,512]{1,0:T(1,128)S(1)}, s32[1,512]{1,0:T(1,128)}, u32[]{:S(2)}) copy-start(s32[1,512]{1,0:T(1,128)} %param.25) | copy-start | bytes 6148
  2.5 46.0 %collective-permute-start.6 = (bf16[128,1024]{1,0:T(8,128)(2,1)}, bf16[128,1024]{1,0:T(8,128)(2,1)S(1)}, u32[]{:S(2)}, u32[]{:S(2)}) collective-permute-start(bf16[128,1024]{1,0:T(8,128)(2,1)} %constant_dynamic-slice_fusion.8), channel_id=1, source_target_pairs={{0,3},{1,0},{2,1},{3,2},{4,7},{5,4},{6,5},{7,6},{8,11},{9,8},{10,9... | collective-permute-start | bytes 786440 | tf_op jit(solution)/shard_map/ppermute | solution.py:109
  7.6 40.9 %collective-permute-start.5 = (bf16[128,1024]{1,0:T(8,128)(2,1)}, bf16[128,1024]{1,0:T(8,128)(2,1)}, u32[]{:S(2)}, u32[]{:S(2)}) collective-permute-start(bf16[128,1024]{1,0:T(8,128)(2,1)} %constant_dynamic-slice_fusion.8), channel_id=1, source_target_pairs={{0,2},{1,3},{2,0},{3,1},{4,6},{5,7},{6,4},{7,5},{8,10},{9,11},{10,... | collective-permute-start | bytes 786440 | tf_op jit(solution)/shard_map/ppermute | solution.py:109
  15.0 9.7 %copy-start.11 = (s32[128,8]{0,1:T(8,128)S(1)}, s32[128,8]{0,1:T(8,128)}, u32[]{:S(2)}) copy-start(s32[128,8]{0,1:T(8,128)} %param.27) | copy-start | bytes 12292
  16.0 9.7 %copy-start.13 = (s32[1,512]{1,0:T(1,128)S(1)}, s32[1,512]{1,0:T(1,128)}, u32[]{:S(2)}) copy-start(s32[1,512]{1,0:T(1,128)} %param.26) | copy-start | bytes 6148
  19.4 8.0 %collective-permute-start.2 = (bf16[128,2,256]{0,2,1:T(8,128)(2,1)S(1)}, bf16[128,2,256]{0,2,1:T(8,128)(2,1)S(1)}, u32[]{:S(2)}, u32[]{:S(2)}) collective-permute-start(bf16[128,2,256]{0,2,1:T(8,128)(2,1)S(1)} %get-tuple-element.21), channel_id=1, source_target_pairs={{0,3},{1,0},{2,1},{3,2},{4,7},{5,4},{6,5},{7,6},{8,11},{9,8},{10,9... | collective-permute-start | bytes 393224 | tf_op jit(solution)/shard_map/ppermute | solution.py:109
  19.8 21.5 %collective-permute-start.1 = (bf16[128,2,256]{0,2,1:T(8,128)(2,1)S(1)}, bf16[128,2,256]{0,2,1:T(8,128)(2,1)S(1)}, u32[]{:S(2)}, u32[]{:S(2)}) collective-permute-start(bf16[128,2,256]{0,2,1:T(8,128)(2,1)S(1)} %get-tuple-element.22), channel_id=1, source_target_pairs={{0,2},{1,3},{2,0},{3,1},{4,6},{5,7},{6,4},{7,5},{8,10},{9,11},{10,... | collective-permute-start | bytes 393224 | tf_op jit(solution)/shard_map/ppermute | solution.py:109
  22.4 19.0 %collective-permute-start = (bf16[128,2,256]{0,2,1:T(8,128)(2,1)S(1)}, bf16[128,2,256]{0,2,1:T(8,128)(2,1)}, u32[]{:S(2)}, u32[]{:S(2)}) collective-permute-start(bf16[128,2,256]{0,2,1:T(8,128)(2,1)S(1)} %get-tuple-element.23), channel_id=1, source_target_pairs={{0,1},{1,2},{2,3},{3,0},{4,5},{5,6},{6,7},{7,4},{8,9},{9,10},{10,1... | collective-permute-start | bytes 393224 | tf_op jit(solution)/shard_map/ppermute | solution.py:109
  27.3 14.1 %copy-start.7 = (bf16[128,2,256]{0,2,1:T(8,128)(2,1)}, bf16[128,2,256]{0,2,1:T(8,128)(2,1)S(1)}, u32[]{:S(2)}) copy-start(bf16[128,2,256]{0,2,1:T(8,128)(2,1)S(1)} %collective-permute-done.2) | copy-start | bytes 393220
  27.3 21.2 %collective-permute-start.4 = (bf16[128,1024]{1,0:T(8,128)(2,1)}, bf16[128,1024]{1,0:T(8,128)(2,1)S(1)}, u32[]{:S(2)}, u32[]{:S(2)}) collective-permute-start(bf16[128,1024]{1,0:T(8,128)(2,1)} %constant_dynamic-slice_fusion.8), channel_id=1, source_target_pairs={{0,1},{1,2},{2,3},{3,0},{4,5},{5,6},{6,7},{7,4},{8,9},{9,10},{10,1... | collective-permute-start | bytes 786440 | tf_op jit(solution)/shard_map/ppermute | solution.py:109
  41.4 0.6 copy-start.8
  49.5 8.4 %collective-permute-start.7 = (bf16[3,128,1024]{2,1,0:T(8,128)(2,1)S(1)}, bf16[3,128,1024]{2,1,0:T(8,128)(2,1)S(1)}, u32[]{:S(2)}, u32[]{:S(2)}) collective-permute-start(bf16[3,128,1024]{2,1,0:T(8,128)(2,1)S(1)} %pad_maximum_fusion), channel_id=1, source_target_pairs={{0,4},{4,0},{8,12},{12,8},{16,20},{20,16},{24,28},{28,24},{1,5},{5... | collective-permute-start | bytes 2359304 | tf_op jit(solution)/shard_map/ppermute | solution.py:135
  49.6 8.0 %copy-start.5 = (bf16[256,1024]{1,0:T(8,128)(2,1)S(1)}, bf16[256,1024]{1,0:T(8,128)(2,1)}, u32[]{:S(2)}) copy-start(bf16[256,1024]{1,0:T(8,128)(2,1)} %param.19) | copy-start | bytes 1572868
  52.4 6.9 %collective-permute-start.9 = (bf16[128,256]{0,1:T(8,128)(2,1)S(1)}, bf16[128,256]{0,1:T(8,128)(2,1)S(1)}, u32[]{:S(2)}, u32[]{:S(2)}) collective-permute-start(bf16[128,256]{0,1:T(8,128)(2,1)S(1)} %bitcast.274), channel_id=1, source_target_pairs={{0,1},{1,2},{2,3},{3,0},{4,5},{5,6},{6,7},{7,4},{8,9},{9,10},{10,1... | collective-permute-start | bytes 196616 | tf_op jit(solution)/shard_map/ppermute | solution.py:109
  52.5 6.5 %collective-permute-start.3 = (bf16[128,256]{0,1:T(8,128)(2,1)S(1)}, bf16[128,256]{0,1:T(8,128)(2,1)S(1)}, u32[]{:S(2)}, u32[]{:S(2)}) collective-permute-start(bf16[128,256]{0,1:T(8,128)(2,1)S(1)} %bitcast.275), channel_id=1, source_target_pairs={{0,3},{1,0},{2,1},{3,2},{4,7},{5,4},{6,5},{7,6},{8,11},{9,8},{10,9... | collective-permute-start | bytes 196616 | tf_op jit(solution)/shard_map/ppermute | solution.py:109
  56.3 6.2 %collective-permute-start.8 = (bf16[128,256]{0,1:T(8,128)(2,1)S(1)}, bf16[128,256]{0,1:T(8,128)(2,1)S(1)}, u32[]{:S(2)}, u32[]{:S(2)}) collective-permute-start(bf16[128,256]{0,1:T(8,128)(2,1)S(1)} %bitcast.273), channel_id=1, source_target_pairs={{0,2},{1,3},{2,0},{3,1},{4,6},{5,7},{6,4},{7,5},{8,10},{9,11},{10,... | collective-permute-start | bytes 196616 | tf_op jit(solution)/shard_map/ppermute | solution.py:109
  59.3 4.5 %copy-start.10 = (bf16[1024,32]{0,1:T(8,128)(2,1)S(1)}, bf16[1024,32]{0,1:T(8,128)(2,1)}, u32[]{:S(2)}) copy-start(bf16[1024,32]{0,1:T(8,128)(2,1)} %param.21) | copy-start | bytes 196612
  59.3 5.1 %copy-start.9 = (bf16[128,32]{1,0:T(8,128)(2,1)S(1)}, bf16[128,32]{1,0:T(8,128)(2,1)}, u32[]{:S(2)}) copy-start(bf16[128,32]{1,0:T(8,128)(2,1)} %copy.84) | copy-start | bytes 24580
  62.9 0.8 copy-start.3
  65.3 24.9 %collective-permute-start.10 = (bf16[128,1152]{1,0:T(8,128)(2,1)}, bf16[128,1152]{1,0:T(8,128)(2,1)}, u32[]{:S(2)}, u32[]{:S(2)}) collective-permute-start(bf16[128,1152]{1,0:T(8,128)(2,1)} %concatenate.47), channel_id=1, source_target_pairs={{0,1},{1,2},{2,3},{3,0},{4,5},{5,6},{6,7},{7,4},{8,9},{9,10},{10,1... | collective-permute-start | bytes 884744 | tf_op jit(solution)/shard_map/ppermute | solution.py:109
  65.3 25.9 %collective-permute-start.11 = (bf16[128,1152]{1,0:T(8,128)(2,1)}, bf16[128,1152]{1,0:T(8,128)(2,1)}, u32[]{:S(2)}, u32[]{:S(2)}) collective-permute-start(bf16[128,1152]{1,0:T(8,128)(2,1)} %concatenate.47), channel_id=1, source_target_pairs={{0,2},{1,3},{2,0},{3,1},{4,6},{5,7},{6,4},{7,5},{8,10},{9,11},{10,... | collective-permute-start | bytes 884744 | tf_op jit(solution)/shard_map/ppermute | solution.py:109
  67.6 24.6 %collective-permute-start.12 = (bf16[128,1152]{1,0:T(8,128)(2,1)}, bf16[128,1152]{1,0:T(8,128)(2,1)}, u32[]{:S(2)}, u32[]{:S(2)}) collective-permute-start(bf16[128,1152]{1,0:T(8,128)(2,1)} %concatenate.47), channel_id=1, source_target_pairs={{0,3},{1,0},{2,1},{3,2},{4,7},{5,4},{6,5},{7,6},{8,11},{9,8},{10,9... | collective-permute-start | bytes 884744 | tf_op jit(solution)/shard_map/ppermute | solution.py:109
  94.3 6.6 %slice-start = ((s8[8388608]{0:T(1024)(128)(4,1)}), s8[4194304]{0:T(1024)(128)(4,1)S(1)}, s32[]{:S(2)}) async-start(s8[8388608]{0:T(1024)(128)(4,1)} %bitcast.259), calls=%async_computation | async-start | bytes 8388608
  95.3 5.6 %slice-start.1 = ((s8[8388608]{0:T(1024)(128)(4,1)}), s8[4194304]{0:T(1024)(128)(4,1)S(1)}, s32[]{:S(2)}) async-start(s8[8388608]{0:T(1024)(128)(4,1)} %bitcast.259), calls=%async_computation.1 | async-start | bytes 8388608
  100.9 3.3 %copy-start.6 = (bf16[384,8]{1,0:T(8,128)(2,1)S(1)}, bf16[384,8]{1,0:T(8,128)(2,1)}, u32[]{:S(2)}) copy-start(bf16[384,8]{1,0:T(8,128)(2,1)} %get-tuple-element.16) | copy-start | bytes 18436
  112.2 23.3 %copy-start.1 = (bf16[8,64,1024]{2,1,0:T(8,128)(2,1)S(1)}, bf16[8,64,1024]{2,1,0:T(8,128)(2,1)}, u32[]{:S(2)}) copy-start(bf16[8,64,1024]{2,1,0:T(8,128)(2,1)} %convolution_convert_fusion.1) | copy-start | bytes 3145732
  112.2 23.3 %copy-start.4 = (f32[128,1024]{1,0:T(8,128)S(1)}, f32[128,1024]{1,0:T(8,128)}, u32[]{:S(2)}) copy-start(f32[128,1024]{1,0:T(8,128)} %copy-done.3) | copy-start | bytes 1572868
  112.2 8.3 %collective-permute-start.18 = (bf16[128,512]{1,0:T(8,128)(2,1)S(1)}, bf16[128,512]{1,0:T(8,128)(2,1)S(1)}, u32[]{:S(2)}, u32[]{:S(2)}) collective-permute-start(bf16[128,512]{1,0:T(8,128)(2,1)S(1)} %get-tuple-element.28), channel_id=1, source_target_pairs={{0,1},{1,2},{2,3},{3,0},{4,5},{5,6},{6,7},{7,4},{8,9},{9,10},{10,1... | collective-permute-start | bytes 393224 | tf_op jit(solution)/shard_map/ppermute | solution.py:109
  114.6 13.3 %collective-permute-start.17 = (bf16[128,512]{1,0:T(8,128)(2,1)S(1)}, bf16[128,512]{1,0:T(8,128)(2,1)S(1)}, u32[]{:S(2)}, u32[]{:S(2)}) collective-permute-start(bf16[128,512]{1,0:T(8,128)(2,1)S(1)} %get-tuple-element.29), channel_id=1, source_target_pairs={{0,2},{1,3},{2,0},{3,1},{4,6},{5,7},{6,4},{7,5},{8,10},{9,11},{10,... | collective-permute-start | bytes 393224 | tf_op jit(solution)/shard_map/ppermute | solution.py:109
  115.6 12.2 %collective-permute-start.16 = (bf16[128,512]{1,0:T(8,128)(2,1)S(1)}, bf16[128,512]{1,0:T(8,128)(2,1)S(1)}, u32[]{:S(2)}, u32[]{:S(2)}) collective-permute-start(bf16[128,512]{1,0:T(8,128)(2,1)S(1)} %get-tuple-element.27), channel_id=1, source_target_pairs={{0,3},{1,0},{2,1},{3,2},{4,7},{5,4},{6,5},{7,6},{8,11},{9,8},{10,9... | collective-permute-start | bytes 393224 | tf_op jit(solution)/shard_map/ppermute | solution.py:109
  117.3 11.7 %collective-permute-start.15 = (bf16[128,512]{1,0:T(8,128)(2,1)S(1)}, bf16[128,512]{1,0:T(8,128)(2,1)S(1)}, u32[]{:S(2)}, u32[]{:S(2)}) collective-permute-start(bf16[128,512]{1,0:T(8,128)(2,1)S(1)} %get-tuple-element.25), channel_id=1, source_target_pairs={{0,1},{1,2},{2,3},{3,0},{4,5},{5,6},{6,7},{7,4},{8,9},{9,10},{10,1... | collective-permute-start | bytes 393224 | tf_op jit(solution)/shard_map/ppermute | solution.py:109
  117.7 17.7 %collective-permute-start.14 = (bf16[128,512]{1,0:T(8,128)(2,1)S(1)}, bf16[128,512]{1,0:T(8,128)(2,1)S(1)}, u32[]{:S(2)}, u32[]{:S(2)}) collective-permute-start(bf16[128,512]{1,0:T(8,128)(2,1)S(1)} %get-tuple-element.26), channel_id=1, source_target_pairs={{0,2},{1,3},{2,0},{3,1},{4,6},{5,7},{6,4},{7,5},{8,10},{9,11},{10,... | collective-permute-start | bytes 393224 | tf_op jit(solution)/shard_map/ppermute | solution.py:109
  120.5 14.9 %collective-permute-start.13 = (bf16[128,512]{1,0:T(8,128)(2,1)S(1)}, bf16[128,512]{1,0:T(8,128)(2,1)S(1)}, u32[]{:S(2)}, u32[]{:S(2)}) collective-permute-start(bf16[128,512]{1,0:T(8,128)(2,1)S(1)} %get-tuple-element.24), channel_id=1, source_target_pairs={{0,3},{1,0},{2,1},{3,2},{4,7},{5,4},{6,5},{7,6},{8,11},{9,8},{10,9... | collective-permute-start | bytes 393224 | tf_op jit(solution)/shard_map/ppermute | solution.py:109
